TPU v7x, 512 devices: a whole 4x8x8 slice. The times are simulated.
512 devices in a mesh: tm: 16 (over y, core), pre: 32 (over z, x).
Axes of the slice: x: 4, y: 8, z: 8, core: 2. Of those that a mesh axis runs over, the one named last changes fastest.
Arguments:
- spikes: int32 [3072, 16384], P('tm', 'pre'), may hold values from 0 to 1
- trace_decay: float32 [16384], P('pre'), may hold values from 0.96 to 1
- pseudo_deriv: bfloat16 [3072, 16384], P('pre', 'tm'), may hold values from 0 to 0.29882812
- readout_weight: bfloat16 [16384, 512], P('pre'), may hold values from -2 to 2
- feedback_weight: bfloat16 [16384, 512], P('tm'), may hold values from -6 to 6
- targets: int32 [3072], P('tm'), may hold values from 0 to 511
Outputs:
- gradient: float32 [16384, 16384], P('pre', 'tm')
All inputs are finite; a program needn't handle non-finite values.
Results may differ from a plain program's by a relative error of at most 0.0022.
Values may be sent and summed in bfloat16 or wider, within the bound.
No kernel may reach another device: no remote copies, remote signals or barrier semaphores. Data moves between devices by JAX's collectives and lax.ppermute only.
A program may use at most 64 MiB of HBM per device.

v0:
```python
import jax
import jax.numpy as jnp
from jax import lax
from jax.sharding import PartitionSpec as P


def prefix(value, axis, combine, identity):
    count, index = (lax.axis_size(axis), lax.axis_index(axis))
    everything = jax.tree.map(lambda part: lax.all_gather(part, axis), value)
    start = jax.tree.map(
        lambda part, zero: jnp.broadcast_to(jnp.asarray(zero, part.dtype), part.shape),
        value,
        identity,
    )

    def step(k, before):
        reached = k < index
        new = combine(before, jax.tree.map(lambda part: part[k], everything))
        return jax.tree.map(lambda a, b: jnp.where(reached, a, b), new, before)

    return lax.fori_loop(0, count, step, start)


def combine_pairs(earlier, later):
    return (earlier[0] * later[0], later[1] + later[0] * earlier[1])


def local_traces(spikes, decays):
    factor = jnp.broadcast_to(decays[None, :], spikes.shape)
    source = (1.0 - decays)[None, :] * spikes.astype(jnp.float32)
    return lax.associative_scan(combine_pairs, (factor, source), axis=0)


def error_rows(spikes, readout_weight, targets):
    partial_logits = jnp.dot(
        spikes.astype(jnp.bfloat16), readout_weight, preferred_element_type=jnp.float32
    )
    logits = lax.psum(partial_logits, "pre")
    class_prob = jax.nn.softmax(logits, axis=-1)
    classes = lax.broadcasted_iota(jnp.int32, logits.shape, 1)
    onehot = (targets[:, None] == classes).astype(jnp.float32)
    return (class_prob - onehot).astype(jnp.bfloat16)


def make_signal(errors_all, feedback_weight, derivs, offset):
    err_rows = lax.dynamic_slice_in_dim(errors_all, offset, derivs.shape[0], 0)
    signal = lax.dot_general(
        err_rows, feedback_weight, (((1,), (1,)), ((), ())), preferred_element_type=jnp.float32
    )
    return (signal * derivs.astype(jnp.float32)).astype(jnp.bfloat16)


def outer_sum(left_rows, right_rows):
    return lax.dot_general(
        left_rows, right_rows, (((0,), (0,)), ((), ())), preferred_element_type=jnp.float32
    )


def shards(spikes, trace_decay, pseudo_deriv, readout_weight, feedback_weight, targets):
    errors = error_rows(spikes, readout_weight, targets)
    errors_all = lax.all_gather(errors, "tm", axis=0, tiled=True)
    powers, states = local_traces(spikes, trace_decay)
    carried = prefix(
        (powers[-1], states[-1]),
        "tm",
        combine_pairs,
        (jnp.ones_like(trace_decay), jnp.zeros_like(trace_decay)),
    )
    incoming = carried[1]
    traces = (states + powers * incoming[None, :]).astype(jnp.bfloat16)
    offset = lax.axis_index("pre") * pseudo_deriv.shape[0]
    sources = make_signal(errors_all, feedback_weight, pseudo_deriv, offset)
    signal_all = lax.all_gather(sources, "pre", axis=0, tiled=True)
    return outer_sum(lax.all_gather(traces, "tm", axis=0, tiled=True), signal_all)


def solution(mesh):
    placed = (P("tm", "pre"), P("pre"), P("pre", "tm"), P("pre", None), P("tm", None), P("tm"))
    return jax.shard_map(
        shards, mesh=mesh, in_specs=placed, out_specs=P("pre", "tm"), check_vma=False
    )
```

profile of v0, /device:TPU:6, one launch (start us, length us, event | category | flops | bytes accessed | tf_op | source)
XLA Modules:
  0.0 372.4 jit_solution(8021454056844879361)
XLA Ops:
  6.5 0.0 copy-start
  6.5 0.0 copy-start.3
  6.5 0.0 all-reduce.30.cloned.1.call-start
  6.5 2.3 fusion.3
  8.8 0.0 all-reduce.30.cloned.1.call-update
  8.8 0.0 all-gather.8.cloned.1.call-start
  8.9 0.7 broadcast_subtract_fusion
  9.6 1.0 convert_multiply_fusion
  10.6 0.0 copy-start.1
  10.6 0.1 slice.194
  10.8 0.1 slice.192
  10.9 0.2 slice.190
  11.2 0.0 copy-done.3
  12.4 0.0 copy-done.1
  12.4 0.0 slice-start
  12.7 0.0 copy-start.4
  12.8 0.1 fusion.2
  12.9 0.2 slice-done
  13.2 0.1 pad.98
  13.3 0.0 copy-start.2
  13.3 0.1 pad.99
  13.4 17.7 %all-gather = f32[16,1,512]{2,1,0:T(1,128)S(1)} all-gather(f32[1,1,512]{2,1,0:T(1,128)S(1)} %add_bitcast_fusion.1), channel_id=1, replica_groups=mesh['tm'=16,'pre'=32] {'tm'}, dimensions={0}, use_global_device_ids=true | all-gather | bytes 34816 | tf_op jit(solution)/shard_map/all_gather | solution.py:9
  31.0 0.1 pad.113
  31.1 0.1 pad.112
  31.2 139.8 %all-reduce.30.cloned.1.call-done = f32[192,512]{1,0:T(8,128)} async-done(((f32[192,512]{1,0:T(8,128)}), f32[192,512]{1,0:T(8,128)}) %all-reduce.30.cloned.1.call-update) | async-done | bytes 393232 | tf_op jit(solution)/shard_map/psum | solution.py:38
  170.9 1.1 reduce_max.9
  172.0 1.2 fusion.1
  173.2 0.0 copy-done.4
  173.3 1.9 subtract_convert_fusion
  175.1 0.0 all-gather.8.cloned.1.call-update
  175.1 0.0 all-gather.6.cloned.1.call-start
  175.2 17.0 %all-gather.1 = f32[16,1,512]{2,1,0:T(1,128)S(1)} all-gather(f32[1,1,512]{2,1,0:T(1,128)S(1)} %add_bitcast_fusion), channel_id=1, replica_groups=mesh['tm'=16,'pre'=32] {'tm'}, dimensions={0}, use_global_device_ids=true | all-gather | bytes 34816 | tf_op jit(solution)/shard_map/all_gather | solution.py:9
  192.2 0.9 while.14
  193.1 0.8 add_convert_fusion
  194.0 0.0 all-gather.6.cloned.1.call-update
  194.0 0.0 all-gather.10.cloned.1.call-start
  194.1 23.2 %all-gather.8.cloned.1.call-done = bf16[3072,512]{1,0:T(8,128)(2,1)} async-done(((bf16[192,512]{1,0:T(8,128)(2,1)}), bf16[3072,512]{1,0:T(8,128)(2,1)}) %all-gather.8.cloned.1.call-update) | async-done | bytes 3145744 | tf_op jit(solution)/shard_map/all_gather | solution.py:61
  217.3 0.0 copy-done
  217.3 0.0 copy-done.2
  217.3 2.0 fusion
  219.3 0.0 all-gather.10.cloned.1.call-update
  219.3 42.7 %all-gather.6.cloned.1.call-done = bf16[3072,512]{1,0:T(8,128)(2,1)} async-done(((bf16[192,512]{1,0:T(8,128)(2,1)}), bf16[3072,512]{1,0:T(8,128)(2,1)}) %all-gather.6.cloned.1.call-update) | async-done | bytes 3145744 | tf_op jit(solution)/shard_map/all_gather | solution.py:74
  262.1 95.3 %all-gather.10.cloned.1.call-done = bf16[3072,1024]{1,0:T(8,128)(2,1)} async-done(((bf16[96,1024]{1,0:T(8,128)(2,1)}), bf16[3072,1024]{1,0:T(8,128)(2,1)}) %all-gather.10.cloned.1.call-update) | async-done | bytes 6291472 | tf_op jit(solution)/shard_map/all_gather | solution.py:73
  357.4 8.5 %fusion.19 = f32[512,1024]{1,0:T(8,128)} fusion(bf16[3072,512]{1,0:T(8,128)(2,1)} %all-gather.6.cloned.1.call-done, bf16[3072,1024]{1,0:T(8,128)(2,1)} %all-gather.10.cloned.1.call-done), kind=kOutput, calls=%fused_computation.73 | convolution fusion | flops 3221225472 | bytes 11534336 | tf_op jit(solution)/shard_map/dot_general | solution.py:54
  (116 shorter events, 1.6 us)
Async XLA Ops:
  6.5 210.7 %copy-start = (bf16[1024,512]{1,0:T(8,128)(2,1)S(1)}, bf16[1024,512]{1,0:T(8,128)(2,1)}, u32[]{:S(2)}) copy-start(bf16[1024,512]{1,0:T(8,128)(2,1)} %param.12) | copy-start | bytes 3145732
  6.5 4.6 %copy-start.3 = (f32[512]{0:T(512)S(1)}, f32[512]{0:T(512)}, u32[]{:S(2)}) copy-start(f32[512]{0:T(512)} %param.9) | copy-start | bytes 6148
  6.5 164.4 %all-reduce.30.cloned.1.call-start = ((), (), s32[]{:S(2)}) async-start(), calls=%async_computation.1 | async-start | bytes 786432 | tf_op jit(solution)/shard_map/psum | solution.py:38
  8.8 208.4 %all-gather.8.cloned.1.call-start = ((), (), s32[]{:S(2)}) async-start(), calls=%async_computation.2 | async-start | bytes 3342336 | tf_op jit(solution)/shard_map/all_gather | solution.py:61
  10.6 1.7 copy-start.1
  12.4 0.7 slice-start
  12.7 160.5 %copy-start.4 = (s32[192]{0:T(256)S(1)}, s32[192]{0:T(256)}, u32[]{:S(2)}) copy-start(s32[192]{0:T(256)} %param.13) | copy-start | bytes 2308
  13.3 204.0 %copy-start.2 = (bf16[96,1024]{1,0:T(8,128)(2,1)S(1)}, bf16[96,1024]{1,0:T(8,128)(2,1)}, u32[]{:S(2)}) copy-start(bf16[96,1024]{1,0:T(8,128)(2,1)} %param.10) | copy-start | bytes 589828
  175.1 86.9 %all-gather.6.cloned.1.call-start = ((), (), s32[]{:S(2)}) async-start(), calls=%async_computation | async-start | bytes 3342336 | tf_op jit(solution)/shard_map/all_gather | solution.py:74
  194.0 163.4 %all-gather.10.cloned.1.call-start = ((), (), s32[]{:S(2)}) async-start(), calls=%async_computation.3 | async-start | bytes 6488064 | tf_op jit(solution)/shard_map/all_gather | solution.py:73
Sparse Core Ops, SparseCore 0:
  10.8 160.1 all-reduce.29
  175.3 41.9 all-gather.7
  219.6 42.4 all-gather.5
  265.6 91.7 all-gather.9
where the time goes:
time: 375 us; the launch traced here: 372 us
  waiting for transfers between devices  301 us (80%)
  blocking collectives  34.7 us (9%)
  between operations  13.8 us (4%)
  matrix products  12.8 us (3%)
  other arithmetic  7.6 us (2%)
    psum x1, waiting for transfers between devices, error_rows(): logits = lax.psum(partial_logits, 'pre')  140 us
    all_gather x1, waiting for transfers between devices, shards(): signal_all = lax.all_gather(sources, 'pre', axis=0, tiled=True)  95.3 us
    all_gather x1, waiting for transfers between devices, shards(): lax.all_gather(traces, 'tm', axis=0, tiled=True)  42.7 us
    all_gather x2, blocking collectives, prefix(): everything = jax.tree.map(lambda part: lax.all_gather(part, axis), value)  34.7 us
    all_gather x1, waiting for transfers between devices, shards(): errors_all = lax.all_gather(errors, 'tm', axis=0, tiled=True)  23.2 us
    dot_general x1, matrix products, outer_sum(): lax.dot_general(left_rows, right_rows, (((0,), (0,)), ((), ())), preferre...  8.49 us
  transfers between devices with their start and end apart: 4, of which 4 were waited for; matrix products, arithmetic and copies ran while one was open for 2% of the time, Pallas kernels for 0%

commit v1 on v0

v1 whole, which is shorter than its diff:
```python
import jax
import jax.numpy as jnp
from jax import lax
from jax.sharding import PartitionSpec as P


def combine_pairs(earlier, later):
    return (earlier[0] * later[0], later[1] + later[0] * earlier[1])


def local_traces(spikes, decays):
    factor = jnp.broadcast_to(decays[None, :], spikes.shape)
    source = (1.0 - decays)[None, :] * spikes.astype(jnp.float32)
    return lax.associative_scan(combine_pairs, (factor, source), axis=0)


def owned_errors(spikes, readout_weight, targets):
    npre = lax.axis_size("pre")
    b = lax.axis_index("pre")
    partial_logits = jnp.dot(
        spikes.astype(jnp.bfloat16), readout_weight, preferred_element_type=jnp.float32
    )
    rows = partial_logits.shape[0] // npre
    pieces = lax.all_to_all(partial_logits, "pre", 0, 0, tiled=True)
    logits = pieces.reshape(npre, rows, -1).sum(0)
    class_prob = jax.nn.softmax(logits, axis=-1)
    classes = lax.broadcasted_iota(jnp.int32, logits.shape, 1)
    mine = lax.dynamic_slice_in_dim(targets, b * rows, rows, 0)
    onehot = (mine[:, None] == classes).astype(jnp.float32)
    return (class_prob - onehot).astype(jnp.bfloat16)


def route_errors(errors, ntm, npre, deriv_rows):
    rows = errors.shape[0]
    tstep = rows * npre
    per = deriv_rows // rows
    perm = []
    for a in range(ntm):
        for b in range(npre):
            start = tstep * a + rows * b
            dst_b = start // deriv_rows
            dst_a = (start % deriv_rows) // rows
            perm.append((a * npre + b, dst_a * npre + dst_b))
    moved = lax.ppermute(errors, ("tm", "pre"), perm)
    assert per == ntm
    return lax.all_gather(moved, "tm", axis=0, tiled=True)


def ring_gather(block, axis, count):
    index = lax.axis_index(axis)
    fwd = [(i, (i + 1) % count) for i in range(count)]
    bwd = [(i, (i - 1) % count) for i in range(count)]
    out = jnp.zeros((count,) + block.shape, block.dtype)
    out = lax.dynamic_update_slice_in_dim(out, block[None], index, 0)
    f = block
    b = block
    for s in range(1, count // 2 + 1):
        f = lax.ppermute(f, axis, fwd)
        out = lax.dynamic_update_slice_in_dim(out, f[None], (index - s) % count, 0)
        if s < count - count // 2:
            b = lax.ppermute(b, axis, bwd)
            out = lax.dynamic_update_slice_in_dim(out, b[None], (index + s) % count, 0)
    return out.reshape((count * block.shape[0],) + block.shape[1:])


def shards(spikes, trace_decay, pseudo_deriv, readout_weight, feedback_weight, targets):
    ntm = lax.axis_size("tm")
    npre = lax.axis_size("pre")
    a = lax.axis_index("tm")

    errors = owned_errors(spikes, readout_weight, targets)
    err_rows = route_errors(errors, ntm, npre, pseudo_deriv.shape[0])
    signal = lax.dot_general(
        err_rows, feedback_weight, (((1,), (1,)), ((), ())), preferred_element_type=jnp.float32
    )
    weighted = (signal * pseudo_deriv.astype(jnp.float32)).astype(jnp.bfloat16)
    weighted_all = lax.all_gather(weighted, "pre", axis=0, tiled=True)

    powers, states = local_traces(spikes, trace_decay)
    ends = lax.all_gather(states[-1], "tm", axis=0)
    span = powers[-1]

    def step(k, carry):
        return jnp.where(k < a, span * carry + ends[k], carry)

    incoming = lax.fori_loop(0, ntm, step, jnp.zeros_like(trace_decay))
    traces = (states + powers * incoming[None, :]).astype(jnp.bfloat16)
    traces_all = ring_gather(traces, "tm", ntm)

    return lax.dot_general(
        traces_all, weighted_all, (((0,), (0,)), ((), ())), preferred_element_type=jnp.float32
    )


def solution(mesh):
    placed = (P("tm", "pre"), P("pre"), P("pre", "tm"), P("pre", None), P("tm", None), P("tm"))
    return jax.shard_map(
        shards, mesh=mesh, in_specs=placed, out_specs=P("pre", "tm"), check_vma=False
    )
```

time: 375 us -> 177 us (0.47)
  waiting for transfers between devices: 301 us -> 58.3 us
  starting transfers between devices: 0.13 us -> 37 us
  local copies, waits for them, and re-layouts: 1.85 us -> 15 us
  other arithmetic: 7.6 us -> 2.2 us
    all_gather x3 -> x1, waiting for transfers between devices: 161 us -> 14.3 us  [shards(): weighted_all = lax.all_gather(weighted, 'pre', axis=0, tiled=True)]
    psum x1 -> x0, waiting for transfers between devices: 140 us -> none  [error_rows(): logits = lax.psum(partial_logits, 'pre')]
    ppermute x0 -> x16, waiting for transfers between devices: none -> 28.2 us  [the longest x8 18.9 us: ring_gather(): f = lax.ppermute(f, axis, fwd)]
    ppermute x0 -> x16, starting transfers between devices: none -> 23.6 us  [the longest x7 21.3 us: ring_gather(): b = lax.ppermute(b, axis, bwd)]
    all_to_all x0 -> x1, waiting for transfers between devices: none -> 15.8 us  [owned_errors(): pieces = lax.all_to_all(partial_logits, 'pre', 0, 0, tiled=True)]
    all_to_all x0 -> x1, starting transfers between devices: none -> 13.4 us  [owned_errors(): pieces = lax.all_to_all(partial_logits, 'pre', 0, 0, tiled=True)]
    dynamic_update_slice x0 -> x15, local copies, waits for them, and re-layouts: none -> 10.3 us  [the longest x8 5.53 us: ring_gather(): out = lax.dynamic_update_slice_in_dim(out, f[None], (index - s) % count, 0)]
  transfers between devices with their start and end apart: 4 -> 18, of which waited for: 4 -> 12; matrix products, arithmetic and copies ran while one was open for 2% -> 9% of each run, Pallas kernels for 0% -> 0%
where the time goes in v1:
time: 177 us; the launch traced here: 174 us
  waiting for transfers between devices  58.3 us (33%)
  starting transfers between devices  37 us (21%)
  blocking collectives  35.9 us (20%)
  local copies, waits for them, and re-layouts  15 us (8%)
  between operations  14.1 us (8%)
  matrix products  11.2 us (6%)
  other arithmetic  2.2 us (1%)
    ppermute x7, starting transfers between devices, ring_gather(): b = lax.ppermute(b, axis, bwd)  21.3 us
    ppermute x8, waiting for transfers between devices, ring_gather(): f = lax.ppermute(f, axis, fwd)  18.9 us
    all_gather x1, blocking collectives, route_errors(): return lax.all_gather(moved, 'tm', axis=0, tiled=True)  18.5 us
    all_gather x1, blocking collectives, shards(): ends = lax.all_gather(states[-1], 'tm', axis=0)  17.4 us
    all_to_all x1, waiting for transfers between devices, owned_errors(): pieces = lax.all_to_all(partial_logits, 'pre', 0, 0, tiled=True)  15.8 us
    all_gather x1, waiting for transfers between devices, shards(): weighted_all = lax.all_gather(weighted, 'pre', axis=0, tiled=True)  14.3 us
    all_to_all x1, starting transfers between devices, owned_errors(): pieces = lax.all_to_all(partial_logits, 'pre', 0, 0, tiled=True)  13.4 us
    ppermute x1, waiting for transfers between devices, route_errors(): moved = lax.ppermute(errors, ('tm', 'pre'), perm)  9.04 us
  transfers between devices with their start and end apart: 18, of which 12 were waited for; matrix products, arithmetic and copies ran while one was open for 9% of the time, Pallas kernels for 0%

profile of v1, /device:TPU:6, one launch (start us, length us, event | category | flops | bytes accessed | tf_op | source)
XLA Modules:
  0.0 174.2 jit_solution(5760002937118521136)
XLA Ops:
  6.5 1.6 fusion.2
  8.1 0.0 copy-start.5
  8.1 0.0 copy-start.3
  8.1 0.8 all_to_all.6
  9.0 13.4 %all-to-all-start = ((f32[32,6,512]{2,1,0:T(8,128)}), f32[32,6,512]{2,1,0:T(8,128)S(1)}, u32[]{:S(2)}, u32[]{:S(2)}) async-start(f32[32,6,512]{2,1,0:T(8,128)} %all_to_all.6), calls=%async_computation | async-start | bytes 1048576 | tf_op jit(solution)/shard_map/all_to_all | solution.py:24
  22.4 0.0 all-gather.4.cloned.1.call-start
  22.5 0.1 slice.192
  22.7 0.1 slice.194
  23.3 0.1 dynamic_slice.10
  23.4 15.8 %all-to-all-done = f32[32,6,512]{2,1,0:T(8,128)S(1)} async-done(((f32[32,6,512]{2,1,0:T(8,128)}), f32[32,6,512]{2,1,0:T(8,128)S(1)}, u32[]{:S(2)}, u32[]{:S(2)}) %all-to-all-start) | async-done | bytes 393248 | tf_op jit(solution)/shard_map/all_to_all | solution.py:24
  39.2 0.1 reduce_sum.18
  39.3 0.1 reduce_max.9
  39.4 0.2 fusion.8
  39.6 0.1 subtract_convert_fusion
  39.7 1.9 %collective-permute-start.15 = (bf16[6,512]{1,0:T(8,128)(2,1)S(1)}, bf16[6,512]{1,0:T(8,128)(2,1)S(1)}, u32[]{:S(2)}, u32[]{:S(2)}) collective-permute-start(bf16[6,512]{1,0:T(8,128)(2,1)S(1)} %subtract_convert_fusion), channel_id=1, source_target_pairs={{0,0},{1,32},{2,64},{3,96},{4,128},{5,160},{6,192},{7,224},{8,256}... | collective-permute-start | bytes 18440 | tf_op jit(solution)/shard_map/ppermute | solution.py:44
  41.6 9.0 %collective-permute-done.15 = bf16[6,512]{1,0:T(8,128)(2,1)S(1)} collective-permute-done((bf16[6,512]{1,0:T(8,128)(2,1)S(1)}, bf16[6,512]{1,0:T(8,128)(2,1)S(1)}, u32[]{:S(2)}, u32[]{:S(2)}) %collective-permute-start.15) | collective-permute-done | bytes 6176 | tf_op jit(solution)/shard_map/ppermute | solution.py:44
  50.7 18.5 %all-gather.1 = bf16[16,6,512]{2,1,0:T(8,128)(2,1)S(1)} all-gather(bf16[1,6,512]{2,1,0:T(8,128)(2,1)S(1)} %bitcast.70), channel_id=1, replica_groups=mesh['tm'=16,'pre'=32] {'tm'}, dimensions={0}, use_global_device_ids=true | all-gather | bytes 104448 | tf_op jit(solution)/shard_map/all_gather | solution.py:46
  69.3 1.1 fusion
  70.4 0.0 all-gather.4.cloned.1.call-update
  70.6 0.2 slice.190
  71.6 0.1 pad.99
  71.8 0.1 fusion.1
  71.9 0.1 slice-done
  72.1 0.1 pad.98
  72.1 17.4 %all-gather = f32[16,1,512]{2,1,0:T(1,128)S(1)} all-gather(f32[1,1,512]{2,1,0:T(1,128)S(1)} %add_bitcast_fusion), channel_id=1, replica_groups=mesh['tm'=16,'pre'=32] {'tm'}, dimensions={0}, use_global_device_ids=true | all-gather | bytes 34816 | tf_op jit(solution)/shard_map/all_gather | solution.py:80
  89.6 0.1 pad.112
  89.6 0.1 pad.113
  89.7 0.9 while.14
  90.6 2.0 %broadcast_in_dim.65 = bf16[16,192,512]{2,1,0:T(8,128)(2,1)} broadcast(bf16[]{:T(256)} %constant.118.clone.1), dimensions={} | broadcast | bytes 3145730 | tf_op jit(solution)/shard_map/broadcast_in_dim | solution.py:53
  92.6 0.9 bitcast_dynamic-update-slice_fusion.15
  93.5 0.3 collective-permute-start
  93.8 2.6 %collective-permute-start.1 = (bf16[192,512]{1,0:T(8,128)(2,1)S(1)}, bf16[192,512]{1,0:T(8,128)(2,1)S(1)}, u32[]{:S(2)}, u32[]{:S(2)}) collective-permute-start(bf16[192,512]{1,0:T(8,128)(2,1)S(1)} %get-tuple-element.129), channel_id=1, source_target_pairs={{0,480},{32,0},{64,32},{96,64},{128,96},{160,128},{192,160},{224,1... | collective-permute-start | bytes 589832 | tf_op jit(solution)/shard_map/ppermute | solution.py:61
  96.4 3.3 %collective-permute-done = bf16[192,512]{1,0:T(8,128)(2,1)S(1)} collective-permute-done((bf16[192,512]{1,0:T(8,128)(2,1)S(1)}, bf16[192,512]{1,0:T(8,128)(2,1)S(1)}, u32[]{:S(2)}, u32[]{:S(2)}) %collective-permute-start) | collective-permute-done | bytes 196640 | tf_op jit(solution)/shard_map/ppermute | solution.py:58
  99.8 3.0 %collective-permute-start.3 = (bf16[192,512]{1,0:T(8,128)(2,1)S(1)}, bf16[192,512]{1,0:T(8,128)(2,1)S(1)}, u32[]{:S(2)}, u32[]{:S(2)}) collective-permute-start(bf16[192,512]{1,0:T(8,128)(2,1)S(1)} %collective-permute-done.1), channel_id=1, source_target_pairs={{0,480},{32,0},{64,32},{96,64},{128,96},{160,128},{192,160},{224,1... | collective-permute-start | bytes 589832 | tf_op jit(solution)/shard_map/ppermute | solution.py:61
  102.7 0.7 bitcast_dynamic-update-slice_fusion.14
  103.4 0.7 bitcast_dynamic-update-slice_fusion.13
  104.1 2.0 %collective-permute-done.2 = bf16[192,512]{1,0:T(8,128)(2,1)S(1)} collective-permute-done((bf16[192,512]{1,0:T(8,128)(2,1)S(1)}, bf16[192,512]{1,0:T(8,128)(2,1)S(1)}, u32[]{:S(2)}, u32[]{:S(2)}) %collective-permute-start.2) | collective-permute-done | bytes 196640 | tf_op jit(solution)/shard_map/ppermute | solution.py:58
  106.1 3.0 %collective-permute-start.5 = (bf16[192,512]{1,0:T(8,128)(2,1)S(1)}, bf16[192,512]{1,0:T(8,128)(2,1)S(1)}, u32[]{:S(2)}, u32[]{:S(2)}) collective-permute-start(bf16[192,512]{1,0:T(8,128)(2,1)S(1)} %collective-permute-done.3), channel_id=1, source_target_pairs={{0,480},{32,0},{64,32},{96,64},{128,96},{160,128},{192,160},{224,1... | collective-permute-start | bytes 589832 | tf_op jit(solution)/shard_map/ppermute | solution.py:61
  109.1 0.7 bitcast_dynamic-update-slice_fusion.12
  109.7 0.7 bitcast_dynamic-update-slice_fusion.11
  110.4 2.0 %collective-permute-done.4 = bf16[192,512]{1,0:T(8,128)(2,1)S(1)} collective-permute-done((bf16[192,512]{1,0:T(8,128)(2,1)S(1)}, bf16[192,512]{1,0:T(8,128)(2,1)S(1)}, u32[]{:S(2)}, u32[]{:S(2)}) %collective-permute-start.4) | collective-permute-done | bytes 196640 | tf_op jit(solution)/shard_map/ppermute | solution.py:58
  112.4 3.0 %collective-permute-start.7 = (bf16[192,512]{1,0:T(8,128)(2,1)S(1)}, bf16[192,512]{1,0:T(8,128)(2,1)S(1)}, u32[]{:S(2)}, u32[]{:S(2)}) collective-permute-start(bf16[192,512]{1,0:T(8,128)(2,1)S(1)} %collective-permute-done.5), channel_id=1, source_target_pairs={{0,480},{32,0},{64,32},{96,64},{128,96},{160,128},{192,160},{224,1... | collective-permute-start | bytes 589832 | tf_op jit(solution)/shard_map/ppermute | solution.py:61
  115.4 0.7 bitcast_dynamic-update-slice_fusion.10
  116.0 0.7 bitcast_dynamic-update-slice_fusion.9
  116.7 2.0 %collective-permute-done.6 = bf16[192,512]{1,0:T(8,128)(2,1)S(1)} collective-permute-done((bf16[192,512]{1,0:T(8,128)(2,1)S(1)}, bf16[192,512]{1,0:T(8,128)(2,1)S(1)}, u32[]{:S(2)}, u32[]{:S(2)}) %collective-permute-start.6) | collective-permute-done | bytes 196640 | tf_op jit(solution)/shard_map/ppermute | solution.py:58
  118.7 3.0 %collective-permute-start.9 = (bf16[192,512]{1,0:T(8,128)(2,1)S(1)}, bf16[192,512]{1,0:T(8,128)(2,1)S(1)}, u32[]{:S(2)}, u32[]{:S(2)}) collective-permute-start(bf16[192,512]{1,0:T(8,128)(2,1)S(1)} %collective-permute-done.7), channel_id=1, source_target_pairs={{0,480},{32,0},{64,32},{96,64},{128,96},{160,128},{192,160},{224,1... | collective-permute-start | bytes 589832 | tf_op jit(solution)/shard_map/ppermute | solution.py:61
  121.7 0.7 bitcast_dynamic-update-slice_fusion.8
  122.4 0.7 bitcast_dynamic-update-slice_fusion.7
  123.1 2.0 %collective-permute-done.8 = bf16[192,512]{1,0:T(8,128)(2,1)S(1)} collective-permute-done((bf16[192,512]{1,0:T(8,128)(2,1)S(1)}, bf16[192,512]{1,0:T(8,128)(2,1)S(1)}, u32[]{:S(2)}, u32[]{:S(2)}) %collective-permute-start.8) | collective-permute-done | bytes 196640 | tf_op jit(solution)/shard_map/ppermute | solution.py:58
  125.0 3.4 %collective-permute-start.11 = (bf16[192,512]{1,0:T(8,128)(2,1)S(1)}, bf16[192,512]{1,0:T(8,128)(2,1)S(1)}, u32[]{:S(2)}, u32[]{:S(2)}) collective-permute-start(bf16[192,512]{1,0:T(8,128)(2,1)S(1)} %collective-permute-done.9), channel_id=1, source_target_pairs={{0,480},{32,0},{64,32},{96,64},{128,96},{160,128},{192,160},{224,1... | collective-permute-start | bytes 589832 | tf_op jit(solution)/shard_map/ppermute | solution.py:61
  128.4 0.7 bitcast_dynamic-update-slice_fusion.6
  129.1 0.7 bitcast_dynamic-update-slice_fusion.5
  129.7 1.6 collective-permute-done.10
  131.3 0.2 collective-permute-done.11
  131.6 3.5 %collective-permute-start.13 = (bf16[192,512]{1,0:T(8,128)(2,1)S(1)}, bf16[192,512]{1,0:T(8,128)(2,1)S(1)}, u32[]{:S(2)}, u32[]{:S(2)}) collective-permute-start(bf16[192,512]{1,0:T(8,128)(2,1)S(1)} %collective-permute-done.11), channel_id=1, source_target_pairs={{0,480},{32,0},{64,32},{96,64},{128,96},{160,128},{192,160},{224,1... | collective-permute-start | bytes 589832 | tf_op jit(solution)/shard_map/ppermute | solution.py:61
  135.1 0.7 bitcast_dynamic-update-slice_fusion.4
  135.8 0.7 bitcast_dynamic-update-slice_fusion.3
  136.5 1.2 collective-permute-done.12
  137.6 0.7 bitcast_dynamic-update-slice_fusion.2
  138.3 0.7 bitcast_dynamic-update-slice_fusion.1
  139.0 4.9 %collective-permute-done.14 = bf16[192,512]{1,0:T(8,128)(2,1)S(1)} collective-permute-done((bf16[192,512]{1,0:T(8,128)(2,1)S(1)}, bf16[192,512]{1,0:T(8,128)(2,1)S(1)}, u32[]{:S(2)}, u32[]{:S(2)}) %collective-permute-start.14) | collective-permute-done | bytes 196640 | tf_op jit(solution)/shard_map/ppermute | solution.py:58
  143.9 0.7 bitcast_dynamic-update-slice_fusion
  144.6 14.3 %all-gather.4.cloned.1.call-done = bf16[3072,1024]{1,0:T(8,128)(2,1)} async-done(((bf16[96,1024]{1,0:T(8,128)(2,1)}), bf16[3072,1024]{1,0:T(8,128)(2,1)}) %all-gather.4.cloned.1.call-update) | async-done | bytes 6291472 | tf_op jit(solution)/shard_map/all_gather | solution.py:77
  158.9 8.5 %fusion.17 = f32[512,1024]{1,0:T(8,128)} fusion(bf16[3072,512]{1,0:T(8,128)(2,1)} %bitcast.27, bf16[3072,1024]{1,0:T(8,128)(2,1)} %all-gather.4.cloned.1.call-done), kind=kOutput, calls=%fused_computation.85 | convolution fusion | flops 3221225472 | bytes 11534336 | tf_op jit(solution)/shard_map/dot_general | solution.py:90
  (142 shorter events, 1.8 us)
Async XLA Ops:
  6.5 62.7 %copy-start = (bf16[1024,512]{1,0:T(8,128)(2,1)S(1)}, bf16[1024,512]{1,0:T(8,128)(2,1)}, u32[]{:S(2)}) copy-start(bf16[1024,512]{1,0:T(8,128)(2,1)} %param.12) | copy-start | bytes 3145732
  6.5 15.9 %copy-start.2 = (s32[192,512]{1,0:T(8,128)S(1)}, s32[192,512]{1,0:T(8,128)}, u32[]{:S(2)}) copy-start(s32[192,512]{1,0:T(8,128)} %param.8) | copy-start | bytes 1179652
  6.5 15.9 %copy-start.4 = (f32[512]{0:T(512)S(1)}, f32[512]{0:T(512)}, u32[]{:S(2)}) copy-start(f32[512]{0:T(512)} %param.9) | copy-start | bytes 6148
  8.1 15.2 %copy-start.5 = (s32[192]{0:T(256)S(1)}, s32[192]{0:T(256)}, u32[]{:S(2)}) copy-start(s32[192]{0:T(256)} %param.13) | copy-start | bytes 2308
  8.1 61.1 %copy-start.3 = (bf16[96,1024]{1,0:T(8,128)(2,1)S(1)}, bf16[96,1024]{1,0:T(8,128)(2,1)}, u32[]{:S(2)}) copy-start(bf16[96,1024]{1,0:T(8,128)(2,1)} %param.10) | copy-start | bytes 589828
  9.0 30.2 %all-to-all-start = ((f32[32,6,512]{2,1,0:T(8,128)}), f32[32,6,512]{2,1,0:T(8,128)S(1)}, u32[]{:S(2)}, u32[]{:S(2)}) async-start(f32[32,6,512]{2,1,0:T(8,128)} %all_to_all.6), calls=%async_computation | async-start | bytes 1048576 | tf_op jit(solution)/shard_map/all_to_all | solution.py:24
  22.4 136.5 %all-gather.4.cloned.1.call-start = ((), (), s32[]{:S(2)}) async-start(), calls=%async_computation.1 | async-start | bytes 6488064 | tf_op jit(solution)/shard_map/all_gather | solution.py:77
  22.5 48.3 %copy-start.1 = (f32[192,512]{1,0:T(8,128)}, f32[192,512]{1,0:T(8,128)S(1)}, u32[]{:S(2)}) copy-start(f32[192,512]{1,0:T(8,128)S(1)} %convert_multiply_fusion) | copy-start | bytes 1179652
  39.7 11.0 %collective-permute-start.15 = (bf16[6,512]{1,0:T(8,128)(2,1)S(1)}, bf16[6,512]{1,0:T(8,128)(2,1)S(1)}, u32[]{:S(2)}, u32[]{:S(2)}) collective-permute-start(bf16[6,512]{1,0:T(8,128)(2,1)S(1)} %subtract_convert_fusion), channel_id=1, source_target_pairs={{0,0},{1,32},{2,64},{3,96},{4,128},{5,160},{6,192},{7,224},{8,256}... | collective-permute-start | bytes 18440 | tf_op jit(solution)/shard_map/ppermute | solution.py:44
  71.4 0.7 slice-start
  93.5 6.3 %collective-permute-start = (bf16[192,512]{1,0:T(8,128)(2,1)S(1)}, bf16[192,512]{1,0:T(8,128)(2,1)S(1)}, u32[]{:S(2)}, u32[]{:S(2)}) collective-permute-start(bf16[192,512]{1,0:T(8,128)(2,1)S(1)} %get-tuple-element.129), channel_id=1, source_target_pairs={{0,32},{32,64},{64,96},{96,128},{128,160},{160,192},{192,224},{224... | collective-permute-start | bytes 589832 | tf_op jit(solution)/shard_map/ppermute | solution.py:58
  93.8 6.0 %collective-permute-start.1 = (bf16[192,512]{1,0:T(8,128)(2,1)S(1)}, bf16[192,512]{1,0:T(8,128)(2,1)S(1)}, u32[]{:S(2)}, u32[]{:S(2)}) collective-permute-start(bf16[192,512]{1,0:T(8,128)(2,1)S(1)} %get-tuple-element.129), channel_id=1, source_target_pairs={{0,480},{32,0},{64,32},{96,64},{128,96},{160,128},{192,160},{224,1... | collective-permute-start | bytes 589832 | tf_op jit(solution)/shard_map/ppermute | solution.py:61
  99.8 6.3 %collective-permute-start.2 = (bf16[192,512]{1,0:T(8,128)(2,1)S(1)}, bf16[192,512]{1,0:T(8,128)(2,1)S(1)}, u32[]{:S(2)}, u32[]{:S(2)}) collective-permute-start(bf16[192,512]{1,0:T(8,128)(2,1)S(1)} %collective-permute-done), channel_id=1, source_target_pairs={{0,32},{32,64},{64,96},{96,128},{128,160},{160,192},{192,224},{224... | collective-permute-start | bytes 589832 | tf_op jit(solution)/shard_map/ppermute | solution.py:58
  99.8 6.3 %collective-permute-start.3 = (bf16[192,512]{1,0:T(8,128)(2,1)S(1)}, bf16[192,512]{1,0:T(8,128)(2,1)S(1)}, u32[]{:S(2)}, u32[]{:S(2)}) collective-permute-start(bf16[192,512]{1,0:T(8,128)(2,1)S(1)} %collective-permute-done.1), channel_id=1, source_target_pairs={{0,480},{32,0},{64,32},{96,64},{128,96},{160,128},{192,160},{224,1... | collective-permute-start | bytes 589832 | tf_op jit(solution)/shard_map/ppermute | solution.py:61
  106.1 6.3 %collective-permute-start.4 = (bf16[192,512]{1,0:T(8,128)(2,1)S(1)}, bf16[192,512]{1,0:T(8,128)(2,1)S(1)}, u32[]{:S(2)}, u32[]{:S(2)}) collective-permute-start(bf16[192,512]{1,0:T(8,128)(2,1)S(1)} %collective-permute-done.2), channel_id=1, source_target_pairs={{0,32},{32,64},{64,96},{96,128},{128,160},{160,192},{192,224},{224... | collective-permute-start | bytes 589832 | tf_op jit(solution)/shard_map/ppermute | solution.py:58
  106.1 6.3 %collective-permute-start.5 = (bf16[192,512]{1,0:T(8,128)(2,1)S(1)}, bf16[192,512]{1,0:T(8,128)(2,1)S(1)}, u32[]{:S(2)}, u32[]{:S(2)}) collective-permute-start(bf16[192,512]{1,0:T(8,128)(2,1)S(1)} %collective-permute-done.3), channel_id=1, source_target_pairs={{0,480},{32,0},{64,32},{96,64},{128,96},{160,128},{192,160},{224,1... | collective-permute-start | bytes 589832 | tf_op jit(solution)/shard_map/ppermute | solution.py:61
  112.4 6.3 %collective-permute-start.6 = (bf16[192,512]{1,0:T(8,128)(2,1)S(1)}, bf16[192,512]{1,0:T(8,128)(2,1)S(1)}, u32[]{:S(2)}, u32[]{:S(2)}) collective-permute-start(bf16[192,512]{1,0:T(8,128)(2,1)S(1)} %collective-permute-done.4), channel_id=1, source_target_pairs={{0,32},{32,64},{64,96},{96,128},{128,160},{160,192},{192,224},{224... | collective-permute-start | bytes 589832 | tf_op jit(solution)/shard_map/ppermute | solution.py:58
  112.4 6.3 %collective-permute-start.7 = (bf16[192,512]{1,0:T(8,128)(2,1)S(1)}, bf16[192,512]{1,0:T(8,128)(2,1)S(1)}, u32[]{:S(2)}, u32[]{:S(2)}) collective-permute-start(bf16[192,512]{1,0:T(8,128)(2,1)S(1)} %collective-permute-done.5), channel_id=1, source_target_pairs={{0,480},{32,0},{64,32},{96,64},{128,96},{160,128},{192,160},{224,1... | collective-permute-start | bytes 589832 | tf_op jit(solution)/shard_map/ppermute | solution.py:61
  118.7 6.3 %collective-permute-start.8 = (bf16[192,512]{1,0:T(8,128)(2,1)S(1)}, bf16[192,512]{1,0:T(8,128)(2,1)S(1)}, u32[]{:S(2)}, u32[]{:S(2)}) collective-permute-start(bf16[192,512]{1,0:T(8,128)(2,1)S(1)} %collective-permute-done.6), channel_id=1, source_target_pairs={{0,32},{32,64},{64,96},{96,128},{128,160},{160,192},{192,224},{224... | collective-permute-start | bytes 589832 | tf_op jit(solution)/shard_map/ppermute | solution.py:58
  118.7 6.3 %collective-permute-start.9 = (bf16[192,512]{1,0:T(8,128)(2,1)S(1)}, bf16[192,512]{1,0:T(8,128)(2,1)S(1)}, u32[]{:S(2)}, u32[]{:S(2)}) collective-permute-start(bf16[192,512]{1,0:T(8,128)(2,1)S(1)} %collective-permute-done.7), channel_id=1, source_target_pairs={{0,480},{32,0},{64,32},{96,64},{128,96},{160,128},{192,160},{224,1... | collective-permute-start | bytes 589832 | tf_op jit(solution)/shard_map/ppermute | solution.py:61
  125.0 6.3 %collective-permute-start.10 = (bf16[192,512]{1,0:T(8,128)(2,1)S(1)}, bf16[192,512]{1,0:T(8,128)(2,1)S(1)}, u32[]{:S(2)}, u32[]{:S(2)}) collective-permute-start(bf16[192,512]{1,0:T(8,128)(2,1)S(1)} %collective-permute-done.8), channel_id=1, source_target_pairs={{0,32},{32,64},{64,96},{96,128},{128,160},{160,192},{192,224},{224... | collective-permute-start | bytes 589832 | tf_op jit(solution)/shard_map/ppermute | solution.py:58
  125.0 6.5 %collective-permute-start.11 = (bf16[192,512]{1,0:T(8,128)(2,1)S(1)}, bf16[192,512]{1,0:T(8,128)(2,1)S(1)}, u32[]{:S(2)}, u32[]{:S(2)}) collective-permute-start(bf16[192,512]{1,0:T(8,128)(2,1)S(1)} %collective-permute-done.9), channel_id=1, source_target_pairs={{0,480},{32,0},{64,32},{96,64},{128,96},{160,128},{192,160},{224,1... | collective-permute-start | bytes 589832 | tf_op jit(solution)/shard_map/ppermute | solution.py:61
  131.3 6.3 %collective-permute-start.12 = (bf16[192,512]{1,0:T(8,128)(2,1)S(1)}, bf16[192,512]{1,0:T(8,128)(2,1)S(1)}, u32[]{:S(2)}, u32[]{:S(2)}) collective-permute-start(bf16[192,512]{1,0:T(8,128)(2,1)S(1)} %collective-permute-done.10), channel_id=1, source_target_pairs={{0,32},{32,64},{64,96},{96,128},{128,160},{160,192},{192,224},{224... | collective-permute-start | bytes 589832 | tf_op jit(solution)/shard_map/ppermute | solution.py:58
  131.6 6.8 %collective-permute-start.13 = (bf16[192,512]{1,0:T(8,128)(2,1)S(1)}, bf16[192,512]{1,0:T(8,128)(2,1)S(1)}, u32[]{:S(2)}, u32[]{:S(2)}) collective-permute-start(bf16[192,512]{1,0:T(8,128)(2,1)S(1)} %collective-permute-done.11), channel_id=1, source_target_pairs={{0,480},{32,0},{64,32},{96,64},{128,96},{160,128},{192,160},{224,1... | collective-permute-start | bytes 589832 | tf_op jit(solution)/shard_map/ppermute | solution.py:61
  137.6 6.3 %collective-permute-start.14 = (bf16[192,512]{1,0:T(8,128)(2,1)S(1)}, bf16[192,512]{1,0:T(8,128)(2,1)S(1)}, u32[]{:S(2)}, u32[]{:S(2)}) collective-permute-start(bf16[192,512]{1,0:T(8,128)(2,1)S(1)} %collective-permute-done.12), channel_id=1, source_target_pairs={{0,32},{32,64},{64,96},{96,128},{128,160},{160,192},{192,224},{224... | collective-permute-start | bytes 589832 | tf_op jit(solution)/shard_map/ppermute | solution.py:58
Sparse Core Ops, SparseCore 0:
  70.5 88.3 all-gather.3

commit v2 on v1

--- a/solution.py
+++ b/solution.py
@@ -33,7 +33,6 @@
 def route_errors(errors, ntm, npre, deriv_rows):
     rows = errors.shape[0]
     tstep = rows * npre
-    per = deriv_rows // rows
     perm = []
     for a in range(ntm):
         for b in range(npre):
@@ -42,8 +41,32 @@
             dst_a = (start % deriv_rows) // rows
             perm.append((a * npre + b, dst_a * npre + dst_b))
     moved = lax.ppermute(errors, ("tm", "pre"), perm)
-    assert per == ntm
-    return lax.all_gather(moved, "tm", axis=0, tiled=True)
+    return doubling_gather(moved, "tm", ntm)
+
+
+def doubling_gather(block, axis, count):
+    index = lax.axis_index(axis)
+    have = block
+    span = 1
+    while span < count:
+        pairs = [(i, i ^ span) for i in range(count)]
+        got = lax.ppermute(have, axis, pairs)
+        upper = (index & span) != 0
+        have = jnp.where(upper, jnp.concatenate([got, have], 0), jnp.concatenate([have, got], 0))
+        span *= 2
+    return have
+
+
+def exclusive_carry(end_state, span_power, axis, count):
+    x = lax.ppermute(end_state, axis, [(i, i + 1) for i in range(count - 1)])
+    power = span_power
+    shift = 1
+    while shift < count:
+        got = lax.ppermute(x, axis, [(i, i + shift) for i in range(count - shift)])
+        x = x + power * got
+        power = power * power
+        shift *= 2
+    return x
 
 
 def ring_gather(block, axis, count):
@@ -66,7 +89,6 @@
 def shards(spikes, trace_decay, pseudo_deriv, readout_weight, feedback_weight, targets):
     ntm = lax.axis_size("tm")
     npre = lax.axis_size("pre")
-    a = lax.axis_index("tm")
 
     errors = owned_errors(spikes, readout_weight, targets)
     err_rows = route_errors(errors, ntm, npre, pseudo_deriv.shape[0])
@@ -77,13 +99,7 @@
     weighted_all = lax.all_gather(weighted, "pre", axis=0, tiled=True)
 
     powers, states = local_traces(spikes, trace_decay)
-    ends = lax.all_gather(states[-1], "tm", axis=0)
-    span = powers[-1]
-
-    def step(k, carry):
-        return jnp.where(k < a, span * carry + ends[k], carry)
-
-    incoming = lax.fori_loop(0, ntm, step, jnp.zeros_like(trace_decay))
+    incoming = exclusive_carry(states[-1], powers[-1], "tm", ntm)
     traces = (states + powers * incoming[None, :]).astype(jnp.bfloat16)
     traces_all = ring_gather(traces, "tm", ntm)
 

time: 177 us -> 189 us (1.068)
  starting transfers between devices: 37 us -> 89 us
  blocking collectives: 35.9 us -> 0 us
  waiting for transfers between devices: 58.3 us -> 56.4 us
    ppermute x0 -> x9, starting transfers between devices: none -> 50.2 us  [the longest x4 28.3 us: exclusive_carry(): got = lax.ppermute(x, axis, [(i, i + shift) for i in range(count - shift)])]
    all_gather x2 -> x0, blocking collectives: 35.9 us -> none  [the longest x1 18.5 us: route_errors(): return lax.all_gather(moved, 'tm', axis=0, tiled=True)]
    all_gather x1, waiting for transfers between devices: 14.3 us -> 0.01 us  [shards(): weighted_all = lax.all_gather(weighted, 'pre', axis=0, tiled=True)]
    ppermute x0 -> x9, waiting for transfers between devices: none -> 13.2 us  [the longest x4 7.88 us: doubling_gather(): got = lax.ppermute(have, axis, pairs)]
    ppermute x8, waiting for transfers between devices: 18.9 us -> 13 us  [ring_gather(): f = lax.ppermute(f, axis, fwd)]
    ppermute x7, waiting for transfers between devices: 0.26 us -> 4.47 us  [ring_gather(): b = lax.ppermute(b, axis, bwd)]
    ppermute x7, starting transfers between devices: 21.3 us -> 23.3 us  [ring_gather(): b = lax.ppermute(b, axis, bwd)]
  transfers between devices with their start and end apart: 18 -> 27, of which waited for: 12 -> 23; matrix products, arithmetic and copies ran while one was open for 9% -> 8% of each run, Pallas kernels for 0% -> 0%
where the time goes in v2:
time: 189 us; the launch traced here: 188 us
  starting transfers between devices  89 us (47%)
  waiting for transfers between devices  56.4 us (30%)
  local copies, waits for them, and re-layouts  15 us (8%)
  between operations  14.2 us (8%)
  matrix products  11.2 us (6%)
  other arithmetic  2.03 us (1%)
    ppermute x4, starting transfers between devices, exclusive_carry(): got = lax.ppermute(x, axis, [(i, i + shift) for i in range(count - shift)])  28.3 us
    ppermute x7, starting transfers between devices, ring_gather(): b = lax.ppermute(b, axis, bwd)  23.3 us
    ppermute x4, starting transfers between devices, doubling_gather(): got = lax.ppermute(have, axis, pairs)  20.7 us
    all_to_all x1, waiting for transfers between devices, owned_errors(): pieces = lax.all_to_all(partial_logits, 'pre', 0, 0, tiled=True)  16.7 us
    all_to_all x1, starting transfers between devices, owned_errors(): pieces = lax.all_to_all(partial_logits, 'pre', 0, 0, tiled=True)  13.4 us
    ppermute x8, waiting for transfers between devices, ring_gather(): f = lax.ppermute(f, axis, fwd)  13 us
    ppermute x1, waiting for transfers between devices, route_errors(): moved = lax.ppermute(errors, ('tm', 'pre'), perm)  9.07 us
    dot_general x1, matrix products, shards(): lax.dot_general(traces_all, weighted_all, (((0,), (0,)), ((), ())), prefe...  8.49 us
  transfers between devices with their start and end apart: 27, of which 23 were waited for; matrix products, arithmetic and copies ran while one was open for 8% of the time, Pallas kernels for 0%

profile of v2, /device:TPU:6, one launch (start us, length us, event | category | flops | bytes accessed | tf_op | source)
XLA Modules:
  0.0 187.7 jit_solution(3388498582109953117)
XLA Ops:
  6.5 1.5 fusion.2
  8.1 0.8 all_to_all.6
  8.9 13.4 %all-to-all-start = ((f32[32,6,512]{2,1,0:T(8,128)}), f32[32,6,512]{2,1,0:T(8,128)S(1)}, u32[]{:S(2)}, u32[]{:S(2)}) async-start(f32[32,6,512]{2,1,0:T(8,128)} %all_to_all.6), calls=%async_computation | async-start | bytes 1048576 | tf_op jit(solution)/shard_map/all_to_all | solution.py:24
  22.5 16.7 %all-to-all-done = f32[32,6,512]{2,1,0:T(8,128)S(1)} async-done(((f32[32,6,512]{2,1,0:T(8,128)}), f32[32,6,512]{2,1,0:T(8,128)S(1)}, u32[]{:S(2)}, u32[]{:S(2)}) %all-to-all-start) | async-done | bytes 393248 | tf_op jit(solution)/shard_map/all_to_all | solution.py:24
  39.7 1.9 %collective-permute-start.20 = (bf16[6,512]{1,0:T(8,128)(2,1)S(1)}, bf16[6,512]{1,0:T(8,128)(2,1)S(1)}, u32[]{:S(2)}, u32[]{:S(2)}) collective-permute-start(bf16[6,512]{1,0:T(8,128)(2,1)S(1)} %subtract_convert_fusion), channel_id=1, source_target_pairs={{0,0},{1,32},{2,64},{3,96},{4,128},{5,160},{6,192},{7,224},{8,256}... | collective-permute-start | bytes 18440 | tf_op jit(solution)/shard_map/ppermute | solution.py:43
  41.6 9.1 %collective-permute-done.20 = bf16[6,512]{1,0:T(8,128)(2,1)S(1)} collective-permute-done((bf16[6,512]{1,0:T(8,128)(2,1)S(1)}, bf16[6,512]{1,0:T(8,128)(2,1)S(1)}, u32[]{:S(2)}, u32[]{:S(2)}) %collective-permute-start.20) | collective-permute-done | bytes 6176 | tf_op jit(solution)/shard_map/ppermute | solution.py:43
  50.7 1.9 %collective-permute-start.21 = (bf16[6,512]{1,0:T(8,128)(2,1)S(1)}, bf16[6,512]{1,0:T(8,128)(2,1)S(1)}, u32[]{:S(2)}, u32[]{:S(2)}) collective-permute-start(bf16[6,512]{1,0:T(8,128)(2,1)S(1)} %collective-permute-done.20), channel_id=1, source_target_pairs={{0,32},{32,0},{64,96},{96,64},{128,160},{160,128},{192,224},{224,1... | collective-permute-start | bytes 18440 | tf_op jit(solution)/shard_map/ppermute | solution.py:53
  52.6 1.1 collective-permute-done.21
  53.7 3.2 %collective-permute-start.22 = (bf16[12,512]{1,0:T(8,128)(2,1)S(1)}, bf16[12,512]{1,0:T(8,128)(2,1)S(1)}, u32[]{:S(2)}, u32[]{:S(2)}) collective-permute-start(bf16[12,512]{1,0:T(8,128)(2,1)S(1)} %maximum_select_fusion.4), channel_id=1, source_target_pairs={{0,64},{32,96},{64,0},{96,32},{128,192},{160,224},{192,128},{224,1... | collective-permute-start | bytes 36872 | tf_op jit(solution)/shard_map/ppermute | solution.py:53
  57.0 2.4 %collective-permute-done.22 = bf16[12,512]{1,0:T(8,128)(2,1)S(1)} collective-permute-done((bf16[12,512]{1,0:T(8,128)(2,1)S(1)}, bf16[12,512]{1,0:T(8,128)(2,1)S(1)}, u32[]{:S(2)}, u32[]{:S(2)}) %collective-permute-start.22) | collective-permute-done | bytes 12320 | tf_op jit(solution)/shard_map/ppermute | solution.py:53
  59.4 5.4 %collective-permute-start.23 = (bf16[24,512]{1,0:T(8,128)(2,1)S(1)}, bf16[24,512]{1,0:T(8,128)(2,1)S(1)}, u32[]{:S(2)}, u32[]{:S(2)}) collective-permute-start(bf16[24,512]{1,0:T(8,128)(2,1)S(1)} %maximum_select_fusion.3), channel_id=1, source_target_pairs={{0,128},{32,160},{64,192},{96,224},{128,0},{160,32},{192,64},{224,... | collective-permute-start | bytes 73736 | tf_op jit(solution)/shard_map/ppermute | solution.py:53
  64.8 1.8 collective-permute-done.23
  66.6 10.2 %collective-permute-start.24 = (bf16[48,512]{1,0:T(8,128)(2,1)S(1)}, bf16[48,512]{1,0:T(8,128)(2,1)S(1)}, u32[]{:S(2)}, u32[]{:S(2)}) collective-permute-start(bf16[48,512]{1,0:T(8,128)(2,1)S(1)} %maximum_select_fusion.2), channel_id=1, source_target_pairs={{0,256},{32,288},{64,320},{96,352},{128,384},{160,416},{192,448},{... | collective-permute-start | bytes 147464 | tf_op jit(solution)/shard_map/ppermute | solution.py:53
  76.8 2.6 %collective-permute-done.24 = bf16[48,512]{1,0:T(8,128)(2,1)S(1)} collective-permute-done((bf16[48,512]{1,0:T(8,128)(2,1)S(1)}, bf16[48,512]{1,0:T(8,128)(2,1)S(1)}, u32[]{:S(2)}, u32[]{:S(2)}) %collective-permute-start.24) | collective-permute-done | bytes 49184 | tf_op jit(solution)/shard_map/ppermute | solution.py:53
  79.3 1.1 fusion
  81.4 0.2 slice.190
  82.8 0.2 slice-done
  83.2 1.3 collective-permute-start
  84.7 0.6 collective-permute-done
  85.3 2.2 %collective-permute-start.1 = (f32[512]{0:T(512)S(1)}, f32[512]{0:T(512)S(1)}, u32[]{:S(2)}, u32[]{:S(2)}) collective-permute-start(f32[512]{0:T(512)S(1)} %collective-permute-done), channel_id=1, source_target_pairs={{0,32},{32,64},{64,96},{96,128},{128,160},{160,192},{192,224},{224... | collective-permute-start | bytes 6152 | tf_op jit(solution)/shard_map/ppermute | solution.py:65
  87.5 0.8 collective-permute-done.1
  88.3 6.1 %collective-permute-start.2 = (f32[512]{0:T(512)S(1)}, f32[512]{0:T(512)S(1)}, u32[]{:S(2)}, u32[]{:S(2)}) collective-permute-start(f32[512]{0:T(512)S(1)} %multiply_add_fusion.9), channel_id=1, source_target_pairs={{0,64},{32,96},{64,128},{96,160},{128,192},{160,224},{192,256},{22... | collective-permute-start | bytes 6152 | tf_op jit(solution)/shard_map/ppermute | solution.py:65
  94.4 1.3 collective-permute-done.2
  95.7 4.8 %collective-permute-start.3 = (f32[512]{0:T(512)S(1)}, f32[512]{0:T(512)S(1)}, u32[]{:S(2)}, u32[]{:S(2)}) collective-permute-start(f32[512]{0:T(512)S(1)} %multiply_add_fusion.8), channel_id=1, source_target_pairs={{0,128},{32,160},{64,192},{96,224},{128,256},{160,288},{192,320},{... | collective-permute-start | bytes 6152 | tf_op jit(solution)/shard_map/ppermute | solution.py:65
  100.5 1.3 collective-permute-done.3
  101.8 15.1 %collective-permute-start.4 = (f32[512]{0:T(512)S(1)}, f32[512]{0:T(512)S(1)}, u32[]{:S(2)}, u32[]{:S(2)}) collective-permute-start(f32[512]{0:T(512)S(1)} %multiply_add_fusion.7), channel_id=1, source_target_pairs={{0,256},{32,288},{64,320},{96,352},{128,384},{160,416},{192,448},{... | collective-permute-start | bytes 6152 | tf_op jit(solution)/shard_map/ppermute | solution.py:65
  117.0 1.3 collective-permute-done.4
  118.3 2.0 %broadcast_in_dim.62 = bf16[16,192,512]{2,1,0:T(8,128)(2,1)} broadcast(bf16[]{:T(256)} %constant.95.clone.1), dimensions={} | broadcast | bytes 3145730 | tf_op jit(solution)/shard_map/broadcast_in_dim | solution.py:76
  120.3 0.8 bitcast_dynamic-update-slice_fusion.15
  121.1 3.0 %collective-permute-start.6 = (bf16[192,512]{1,0:T(8,128)(2,1)S(1)}, bf16[192,512]{1,0:T(8,128)(2,1)S(1)}, u32[]{:S(2)}, u32[]{:S(2)}) collective-permute-start(bf16[192,512]{1,0:T(8,128)(2,1)S(1)} %get-tuple-element.6), channel_id=1, source_target_pairs={{0,480},{32,0},{64,32},{96,64},{128,96},{160,128},{192,160},{224,1... | collective-permute-start | bytes 589832 | tf_op jit(solution)/shard_map/ppermute | solution.py:84
  124.1 3.3 %collective-permute-done.5 = bf16[192,512]{1,0:T(8,128)(2,1)S(1)} collective-permute-done((bf16[192,512]{1,0:T(8,128)(2,1)S(1)}, bf16[192,512]{1,0:T(8,128)(2,1)S(1)}, u32[]{:S(2)}, u32[]{:S(2)}) %collective-permute-start.5) | collective-permute-done | bytes 196640 | tf_op jit(solution)/shard_map/ppermute | solution.py:81
  127.4 3.0 %collective-permute-start.8 = (bf16[192,512]{1,0:T(8,128)(2,1)S(1)}, bf16[192,512]{1,0:T(8,128)(2,1)S(1)}, u32[]{:S(2)}, u32[]{:S(2)}) collective-permute-start(bf16[192,512]{1,0:T(8,128)(2,1)S(1)} %collective-permute-done.6), channel_id=1, source_target_pairs={{0,480},{32,0},{64,32},{96,64},{128,96},{160,128},{192,160},{224,1... | collective-permute-start | bytes 589832 | tf_op jit(solution)/shard_map/ppermute | solution.py:84
  130.4 0.7 bitcast_dynamic-update-slice_fusion.14
  131.1 0.7 bitcast_dynamic-update-slice_fusion.13
  131.8 2.0 %collective-permute-done.7 = bf16[192,512]{1,0:T(8,128)(2,1)S(1)} collective-permute-done((bf16[192,512]{1,0:T(8,128)(2,1)S(1)}, bf16[192,512]{1,0:T(8,128)(2,1)S(1)}, u32[]{:S(2)}, u32[]{:S(2)}) %collective-permute-start.7) | collective-permute-done | bytes 196640 | tf_op jit(solution)/shard_map/ppermute | solution.py:81
  133.7 3.4 %collective-permute-start.10 = (bf16[192,512]{1,0:T(8,128)(2,1)S(1)}, bf16[192,512]{1,0:T(8,128)(2,1)S(1)}, u32[]{:S(2)}, u32[]{:S(2)}) collective-permute-start(bf16[192,512]{1,0:T(8,128)(2,1)S(1)} %collective-permute-done.8), channel_id=1, source_target_pairs={{0,480},{32,0},{64,32},{96,64},{128,96},{160,128},{192,160},{224,1... | collective-permute-start | bytes 589832 | tf_op jit(solution)/shard_map/ppermute | solution.py:84
  137.1 0.7 bitcast_dynamic-update-slice_fusion.12
  137.8 0.7 bitcast_dynamic-update-slice_fusion.11
  138.5 1.6 collective-permute-done.9
  140.0 0.2 collective-permute-done.10
  140.3 3.5 %collective-permute-start.12 = (bf16[192,512]{1,0:T(8,128)(2,1)S(1)}, bf16[192,512]{1,0:T(8,128)(2,1)S(1)}, u32[]{:S(2)}, u32[]{:S(2)}) collective-permute-start(bf16[192,512]{1,0:T(8,128)(2,1)S(1)} %collective-permute-done.10), channel_id=1, source_target_pairs={{0,480},{32,0},{64,32},{96,64},{128,96},{160,128},{192,160},{224,1... | collective-permute-start | bytes 589832 | tf_op jit(solution)/shard_map/ppermute | solution.py:84
  143.8 0.7 bitcast_dynamic-update-slice_fusion.10
  144.5 0.7 bitcast_dynamic-update-slice_fusion.9
  145.2 1.2 collective-permute-done.11
  146.4 0.6 collective-permute-done.12
  147.0 3.5 %collective-permute-start.14 = (bf16[192,512]{1,0:T(8,128)(2,1)S(1)}, bf16[192,512]{1,0:T(8,128)(2,1)S(1)}, u32[]{:S(2)}, u32[]{:S(2)}) collective-permute-start(bf16[192,512]{1,0:T(8,128)(2,1)S(1)} %collective-permute-done.12), channel_id=1, source_target_pairs={{0,480},{32,0},{64,32},{96,64},{128,96},{160,128},{192,160},{224,1... | collective-permute-start | bytes 589832 | tf_op jit(solution)/shard_map/ppermute | solution.py:84
  150.5 0.7 bitcast_dynamic-update-slice_fusion.8
  151.2 0.7 bitcast_dynamic-update-slice_fusion.7
  151.9 0.8 collective-permute-done.13
  152.7 1.0 collective-permute-done.14
  153.7 3.5 %collective-permute-start.16 = (bf16[192,512]{1,0:T(8,128)(2,1)S(1)}, bf16[192,512]{1,0:T(8,128)(2,1)S(1)}, u32[]{:S(2)}, u32[]{:S(2)}) collective-permute-start(bf16[192,512]{1,0:T(8,128)(2,1)S(1)} %collective-permute-done.14), channel_id=1, source_target_pairs={{0,480},{32,0},{64,32},{96,64},{128,96},{160,128},{192,160},{224,1... | collective-permute-start | bytes 589832 | tf_op jit(solution)/shard_map/ppermute | solution.py:84
  157.2 0.7 bitcast_dynamic-update-slice_fusion.6
  157.9 0.7 bitcast_dynamic-update-slice_fusion.5
  158.6 0.4 collective-permute-done.15
  159.0 1.4 collective-permute-done.16
  160.4 3.5 %collective-permute-start.18 = (bf16[192,512]{1,0:T(8,128)(2,1)S(1)}, bf16[192,512]{1,0:T(8,128)(2,1)S(1)}, u32[]{:S(2)}, u32[]{:S(2)}) collective-permute-start(bf16[192,512]{1,0:T(8,128)(2,1)S(1)} %collective-permute-done.16), channel_id=1, source_target_pairs={{0,480},{32,0},{64,32},{96,64},{128,96},{160,128},{192,160},{224,1... | collective-permute-start | bytes 589832 | tf_op jit(solution)/shard_map/ppermute | solution.py:84
  163.9 0.7 bitcast_dynamic-update-slice_fusion.4
  164.6 0.7 bitcast_dynamic-update-slice_fusion.3
  165.3 0.7 bitcast_dynamic-update-slice_fusion.2
  166.0 1.1 collective-permute-done.18
  167.1 0.7 bitcast_dynamic-update-slice_fusion.1
  167.8 3.8 %collective-permute-done.19 = bf16[192,512]{1,0:T(8,128)(2,1)S(1)} collective-permute-done((bf16[192,512]{1,0:T(8,128)(2,1)S(1)}, bf16[192,512]{1,0:T(8,128)(2,1)S(1)}, u32[]{:S(2)}, u32[]{:S(2)}) %collective-permute-start.19) | collective-permute-done | bytes 196640 | tf_op jit(solution)/shard_map/ppermute | solution.py:81
  171.6 0.7 bitcast_dynamic-update-slice_fusion
  172.3 8.5 %fusion.24 = f32[512,1024]{1,0:T(8,128)} fusion(bf16[3072,512]{1,0:T(8,128)(2,1)} %bitcast.27, bf16[3072,1024]{1,0:T(8,128)(2,1)} %all-gather.2.cloned.1.call-done), kind=kOutput, calls=%fused_computation.97 | convolution fusion | flops 3221225472 | bytes 11534336 | tf_op jit(solution)/shard_map/dot_general | solution.py:106
  (129 shorter events, 2.5 us)
Async XLA Ops:
  6.5 72.8 %copy-start = (bf16[1024,512]{1,0:T(8,128)(2,1)S(1)}, bf16[1024,512]{1,0:T(8,128)(2,1)}, u32[]{:S(2)}) copy-start(bf16[1024,512]{1,0:T(8,128)(2,1)} %param.10) | copy-start | bytes 3145732
  6.5 74.0 %copy-start.2 = (s32[192,512]{1,0:T(8,128)S(1)}, s32[192,512]{1,0:T(8,128)}, u32[]{:S(2)}) copy-start(s32[192,512]{1,0:T(8,128)} %param.6) | copy-start | bytes 1179652
  6.5 15.9 %copy-start.5 = (s32[192]{0:T(256)S(1)}, s32[192]{0:T(256)}, u32[]{:S(2)}) copy-start(s32[192]{0:T(256)} %param.11) | copy-start | bytes 2308
  6.5 72.8 %copy-start.3 = (bf16[96,1024]{1,0:T(8,128)(2,1)S(1)}, bf16[96,1024]{1,0:T(8,128)(2,1)}, u32[]{:S(2)}) copy-start(bf16[96,1024]{1,0:T(8,128)(2,1)} %param.8) | copy-start | bytes 589828
  6.5 73.9 %copy-start.4 = (f32[512]{0:T(512)S(1)}, f32[512]{0:T(512)}, u32[]{:S(2)}) copy-start(f32[512]{0:T(512)} %param.7) | copy-start | bytes 6148
  8.9 30.2 %all-to-all-start = ((f32[32,6,512]{2,1,0:T(8,128)}), f32[32,6,512]{2,1,0:T(8,128)S(1)}, u32[]{:S(2)}, u32[]{:S(2)}) async-start(f32[32,6,512]{2,1,0:T(8,128)} %all_to_all.6), calls=%async_computation | async-start | bytes 1048576 | tf_op jit(solution)/shard_map/all_to_all | solution.py:24
  22.4 150.0 %all-gather.2.cloned.1.call-start = ((), (), s32[]{:S(2)}) async-start(), calls=%async_computation.1 | async-start | bytes 6488064 | tf_op jit(solution)/shard_map/all_gather | solution.py:99
  39.7 11.0 %collective-permute-start.20 = (bf16[6,512]{1,0:T(8,128)(2,1)S(1)}, bf16[6,512]{1,0:T(8,128)(2,1)S(1)}, u32[]{:S(2)}, u32[]{:S(2)}) collective-permute-start(bf16[6,512]{1,0:T(8,128)(2,1)S(1)} %subtract_convert_fusion), channel_id=1, source_target_pairs={{0,0},{1,32},{2,64},{3,96},{4,128},{5,160},{6,192},{7,224},{8,256}... | collective-permute-start | bytes 18440 | tf_op jit(solution)/shard_map/ppermute | solution.py:43
  50.7 3.1 %collective-permute-start.21 = (bf16[6,512]{1,0:T(8,128)(2,1)S(1)}, bf16[6,512]{1,0:T(8,128)(2,1)S(1)}, u32[]{:S(2)}, u32[]{:S(2)}) collective-permute-start(bf16[6,512]{1,0:T(8,128)(2,1)S(1)} %collective-permute-done.20), channel_id=1, source_target_pairs={{0,32},{32,0},{64,96},{96,64},{128,160},{160,128},{192,224},{224,1... | collective-permute-start | bytes 18440 | tf_op jit(solution)/shard_map/ppermute | solution.py:53
  53.7 5.6 %collective-permute-start.22 = (bf16[12,512]{1,0:T(8,128)(2,1)S(1)}, bf16[12,512]{1,0:T(8,128)(2,1)S(1)}, u32[]{:S(2)}, u32[]{:S(2)}) collective-permute-start(bf16[12,512]{1,0:T(8,128)(2,1)S(1)} %maximum_select_fusion.4), channel_id=1, source_target_pairs={{0,64},{32,96},{64,0},{96,32},{128,192},{160,224},{192,128},{224,1... | collective-permute-start | bytes 36872 | tf_op jit(solution)/shard_map/ppermute | solution.py:53
  59.4 7.2 %collective-permute-start.23 = (bf16[24,512]{1,0:T(8,128)(2,1)S(1)}, bf16[24,512]{1,0:T(8,128)(2,1)S(1)}, u32[]{:S(2)}, u32[]{:S(2)}) collective-permute-start(bf16[24,512]{1,0:T(8,128)(2,1)S(1)} %maximum_select_fusion.3), channel_id=1, source_target_pairs={{0,128},{32,160},{64,192},{96,224},{128,0},{160,32},{192,64},{224,... | collective-permute-start | bytes 73736 | tf_op jit(solution)/shard_map/ppermute | solution.py:53
  66.6 12.7 %collective-permute-start.24 = (bf16[48,512]{1,0:T(8,128)(2,1)S(1)}, bf16[48,512]{1,0:T(8,128)(2,1)S(1)}, u32[]{:S(2)}, u32[]{:S(2)}) collective-permute-start(bf16[48,512]{1,0:T(8,128)(2,1)S(1)} %maximum_select_fusion.2), channel_id=1, source_target_pairs={{0,256},{32,288},{64,320},{96,352},{128,384},{160,416},{192,448},{... | collective-permute-start | bytes 147464 | tf_op jit(solution)/shard_map/ppermute | solution.py:53
  80.6 1.7 copy-start.1
  82.3 0.7 slice-start
  83.2 2.1 %collective-permute-start = (f32[512]{0:T(512)S(1)}, f32[512]{0:T(512)S(1)}, u32[]{:S(2)}, u32[]{:S(2)}) collective-permute-start(f32[512]{0:T(512)S(1)} %bitcast.63), channel_id=1, source_target_pairs={{0,32},{32,64},{64,96},{96,128},{128,160},{160,192},{192,224},{224... | collective-permute-start | bytes 6152 | tf_op jit(solution)/shard_map/ppermute | solution.py:61
  85.3 3.0 %collective-permute-start.1 = (f32[512]{0:T(512)S(1)}, f32[512]{0:T(512)S(1)}, u32[]{:S(2)}, u32[]{:S(2)}) collective-permute-start(f32[512]{0:T(512)S(1)} %collective-permute-done), channel_id=1, source_target_pairs={{0,32},{32,64},{64,96},{96,128},{128,160},{160,192},{192,224},{224... | collective-permute-start | bytes 6152 | tf_op jit(solution)/shard_map/ppermute | solution.py:65
  88.3 7.4 %collective-permute-start.2 = (f32[512]{0:T(512)S(1)}, f32[512]{0:T(512)S(1)}, u32[]{:S(2)}, u32[]{:S(2)}) collective-permute-start(f32[512]{0:T(512)S(1)} %multiply_add_fusion.9), channel_id=1, source_target_pairs={{0,64},{32,96},{64,128},{96,160},{128,192},{160,224},{192,256},{22... | collective-permute-start | bytes 6152 | tf_op jit(solution)/shard_map/ppermute | solution.py:65
  95.7 6.1 %collective-permute-start.3 = (f32[512]{0:T(512)S(1)}, f32[512]{0:T(512)S(1)}, u32[]{:S(2)}, u32[]{:S(2)}) collective-permute-start(f32[512]{0:T(512)S(1)} %multiply_add_fusion.8), channel_id=1, source_target_pairs={{0,128},{32,160},{64,192},{96,224},{128,256},{160,288},{192,320},{... | collective-permute-start | bytes 6152 | tf_op jit(solution)/shard_map/ppermute | solution.py:65
  101.8 16.4 %collective-permute-start.4 = (f32[512]{0:T(512)S(1)}, f32[512]{0:T(512)S(1)}, u32[]{:S(2)}, u32[]{:S(2)}) collective-permute-start(f32[512]{0:T(512)S(1)} %multiply_add_fusion.7), channel_id=1, source_target_pairs={{0,256},{32,288},{64,320},{96,352},{128,384},{160,416},{192,448},{... | collective-permute-start | bytes 6152 | tf_op jit(solution)/shard_map/ppermute | solution.py:65
  121.1 6.3 %collective-permute-start.5 = (bf16[192,512]{1,0:T(8,128)(2,1)S(1)}, bf16[192,512]{1,0:T(8,128)(2,1)S(1)}, u32[]{:S(2)}, u32[]{:S(2)}) collective-permute-start(bf16[192,512]{1,0:T(8,128)(2,1)S(1)} %get-tuple-element.6), channel_id=1, source_target_pairs={{0,32},{32,64},{64,96},{96,128},{128,160},{160,192},{192,224},{224... | collective-permute-start | bytes 589832 | tf_op jit(solution)/shard_map/ppermute | solution.py:81
  121.1 6.3 %collective-permute-start.6 = (bf16[192,512]{1,0:T(8,128)(2,1)S(1)}, bf16[192,512]{1,0:T(8,128)(2,1)S(1)}, u32[]{:S(2)}, u32[]{:S(2)}) collective-permute-start(bf16[192,512]{1,0:T(8,128)(2,1)S(1)} %get-tuple-element.6), channel_id=1, source_target_pairs={{0,480},{32,0},{64,32},{96,64},{128,96},{160,128},{192,160},{224,1... | collective-permute-start | bytes 589832 | tf_op jit(solution)/shard_map/ppermute | solution.py:84
  127.4 6.3 %collective-permute-start.7 = (bf16[192,512]{1,0:T(8,128)(2,1)S(1)}, bf16[192,512]{1,0:T(8,128)(2,1)S(1)}, u32[]{:S(2)}, u32[]{:S(2)}) collective-permute-start(bf16[192,512]{1,0:T(8,128)(2,1)S(1)} %collective-permute-done.5), channel_id=1, source_target_pairs={{0,32},{32,64},{64,96},{96,128},{128,160},{160,192},{192,224},{224... | collective-permute-start | bytes 589832 | tf_op jit(solution)/shard_map/ppermute | solution.py:81
  127.4 6.3 %collective-permute-start.8 = (bf16[192,512]{1,0:T(8,128)(2,1)S(1)}, bf16[192,512]{1,0:T(8,128)(2,1)S(1)}, u32[]{:S(2)}, u32[]{:S(2)}) collective-permute-start(bf16[192,512]{1,0:T(8,128)(2,1)S(1)} %collective-permute-done.6), channel_id=1, source_target_pairs={{0,480},{32,0},{64,32},{96,64},{128,96},{160,128},{192,160},{224,1... | collective-permute-start | bytes 589832 | tf_op jit(solution)/shard_map/ppermute | solution.py:84
  133.7 6.3 %collective-permute-start.9 = (bf16[192,512]{1,0:T(8,128)(2,1)S(1)}, bf16[192,512]{1,0:T(8,128)(2,1)S(1)}, u32[]{:S(2)}, u32[]{:S(2)}) collective-permute-start(bf16[192,512]{1,0:T(8,128)(2,1)S(1)} %collective-permute-done.7), channel_id=1, source_target_pairs={{0,32},{32,64},{64,96},{96,128},{128,160},{160,192},{192,224},{224... | collective-permute-start | bytes 589832 | tf_op jit(solution)/shard_map/ppermute | solution.py:81
  133.7 6.5 %collective-permute-start.10 = (bf16[192,512]{1,0:T(8,128)(2,1)S(1)}, bf16[192,512]{1,0:T(8,128)(2,1)S(1)}, u32[]{:S(2)}, u32[]{:S(2)}) collective-permute-start(bf16[192,512]{1,0:T(8,128)(2,1)S(1)} %collective-permute-done.8), channel_id=1, source_target_pairs={{0,480},{32,0},{64,32},{96,64},{128,96},{160,128},{192,160},{224,1... | collective-permute-start | bytes 589832 | tf_op jit(solution)/shard_map/ppermute | solution.py:84
  140.0 6.3 %collective-permute-start.11 = (bf16[192,512]{1,0:T(8,128)(2,1)S(1)}, bf16[192,512]{1,0:T(8,128)(2,1)S(1)}, u32[]{:S(2)}, u32[]{:S(2)}) collective-permute-start(bf16[192,512]{1,0:T(8,128)(2,1)S(1)} %collective-permute-done.9), channel_id=1, source_target_pairs={{0,32},{32,64},{64,96},{96,128},{128,160},{160,192},{192,224},{224... | collective-permute-start | bytes 589832 | tf_op jit(solution)/shard_map/ppermute | solution.py:81
  140.3 6.7 %collective-permute-start.12 = (bf16[192,512]{1,0:T(8,128)(2,1)S(1)}, bf16[192,512]{1,0:T(8,128)(2,1)S(1)}, u32[]{:S(2)}, u32[]{:S(2)}) collective-permute-start(bf16[192,512]{1,0:T(8,128)(2,1)S(1)} %collective-permute-done.10), channel_id=1, source_target_pairs={{0,480},{32,0},{64,32},{96,64},{128,96},{160,128},{192,160},{224,1... | collective-permute-start | bytes 589832 | tf_op jit(solution)/shard_map/ppermute | solution.py:84
  146.4 6.3 %collective-permute-start.13 = (bf16[192,512]{1,0:T(8,128)(2,1)S(1)}, bf16[192,512]{1,0:T(8,128)(2,1)S(1)}, u32[]{:S(2)}, u32[]{:S(2)}) collective-permute-start(bf16[192,512]{1,0:T(8,128)(2,1)S(1)} %collective-permute-done.11), channel_id=1, source_target_pairs={{0,32},{32,64},{64,96},{96,128},{128,160},{160,192},{192,224},{224... | collective-permute-start | bytes 589832 | tf_op jit(solution)/shard_map/ppermute | solution.py:81
  147.0 6.7 %collective-permute-start.14 = (bf16[192,512]{1,0:T(8,128)(2,1)S(1)}, bf16[192,512]{1,0:T(8,128)(2,1)S(1)}, u32[]{:S(2)}, u32[]{:S(2)}) collective-permute-start(bf16[192,512]{1,0:T(8,128)(2,1)S(1)} %collective-permute-done.12), channel_id=1, source_target_pairs={{0,480},{32,0},{64,32},{96,64},{128,96},{160,128},{192,160},{224,1... | collective-permute-start | bytes 589832 | tf_op jit(solution)/shard_map/ppermute | solution.py:84
  152.7 6.3 %collective-permute-start.15 = (bf16[192,512]{1,0:T(8,128)(2,1)S(1)}, bf16[192,512]{1,0:T(8,128)(2,1)S(1)}, u32[]{:S(2)}, u32[]{:S(2)}) collective-permute-start(bf16[192,512]{1,0:T(8,128)(2,1)S(1)} %collective-permute-done.13), channel_id=1, source_target_pairs={{0,32},{32,64},{64,96},{96,128},{128,160},{160,192},{192,224},{224... | collective-permute-start | bytes 589832 | tf_op jit(solution)/shard_map/ppermute | solution.py:81
  153.7 6.7 %collective-permute-start.16 = (bf16[192,512]{1,0:T(8,128)(2,1)S(1)}, bf16[192,512]{1,0:T(8,128)(2,1)S(1)}, u32[]{:S(2)}, u32[]{:S(2)}) collective-permute-start(bf16[192,512]{1,0:T(8,128)(2,1)S(1)} %collective-permute-done.14), channel_id=1, source_target_pairs={{0,480},{32,0},{64,32},{96,64},{128,96},{160,128},{192,160},{224,1... | collective-permute-start | bytes 589832 | tf_op jit(solution)/shard_map/ppermute | solution.py:84
  159.0 6.4 %collective-permute-start.17 = (bf16[192,512]{1,0:T(8,128)(2,1)S(1)}, bf16[192,512]{1,0:T(8,128)(2,1)S(1)}, u32[]{:S(2)}, u32[]{:S(2)}) collective-permute-start(bf16[192,512]{1,0:T(8,128)(2,1)S(1)} %collective-permute-done.15), channel_id=1, source_target_pairs={{0,32},{32,64},{64,96},{96,128},{128,160},{160,192},{192,224},{224... | collective-permute-start | bytes 589832 | tf_op jit(solution)/shard_map/ppermute | solution.py:81
  160.4 6.7 %collective-permute-start.18 = (bf16[192,512]{1,0:T(8,128)(2,1)S(1)}, bf16[192,512]{1,0:T(8,128)(2,1)S(1)}, u32[]{:S(2)}, u32[]{:S(2)}) collective-permute-start(bf16[192,512]{1,0:T(8,128)(2,1)S(1)} %collective-permute-done.16), channel_id=1, source_target_pairs={{0,480},{32,0},{64,32},{96,64},{128,96},{160,128},{192,160},{224,1... | collective-permute-start | bytes 589832 | tf_op jit(solution)/shard_map/ppermute | solution.py:84
  165.3 6.3 %collective-permute-start.19 = (bf16[192,512]{1,0:T(8,128)(2,1)S(1)}, bf16[192,512]{1,0:T(8,128)(2,1)S(1)}, u32[]{:S(2)}, u32[]{:S(2)}) collective-permute-start(bf16[192,512]{1,0:T(8,128)(2,1)S(1)} %collective-permute-done.17), channel_id=1, source_target_pairs={{0,32},{32,64},{64,96},{96,128},{128,160},{160,192},{192,224},{224... | collective-permute-start | bytes 589832 | tf_op jit(solution)/shard_map/ppermute | solution.py:81
Sparse Core Ops, SparseCore 0:
  80.6 88.3 all-gather.1

commit v3 on v1

--- a/solution.py
+++ b/solution.py
@@ -2,6 +2,8 @@
 import jax.numpy as jnp
 from jax import lax
 from jax.sharding import PartitionSpec as P
+
+NZ = 8
 
 
 def combine_pairs(earlier, later):
@@ -63,6 +65,37 @@
     return out.reshape((count * block.shape[0],) + block.shape[1:])
 
 
+def plane_gather(block, nz, nx):
+    b = lax.axis_index("pre")
+    z = b // nx
+    x = b % nx
+    xf = [(zz * nx + xx, zz * nx + (xx + 1) % nx) for zz in range(nz) for xx in range(nx)]
+    xb = [(zz * nx + xx, zz * nx + (xx - 1) % nx) for zz in range(nz) for xx in range(nx)]
+    zf = [(zz * nx + xx, ((zz + 1) % nz) * nx + xx) for zz in range(nz) for xx in range(nx)]
+    zb = [(zz * nx + xx, ((zz - 1) % nz) * nx + xx) for zz in range(nz) for xx in range(nx)]
+    group = jnp.zeros((nx,) + block.shape, block.dtype)
+    group = lax.dynamic_update_slice_in_dim(group, block[None], x, 0)
+    f = block
+    r = block
+    for s in range(1, nx // 2 + 1):
+        f = lax.ppermute(f, "pre", xf)
+        group = lax.dynamic_update_slice_in_dim(group, f[None], (x - s) % nx, 0)
+        if s < nx - nx // 2:
+            r = lax.ppermute(r, "pre", xb)
+            group = lax.dynamic_update_slice_in_dim(group, r[None], (x + s) % nx, 0)
+    out = jnp.zeros((nz,) + group.shape, block.dtype)
+    out = lax.dynamic_update_slice_in_dim(out, group[None], z, 0)
+    f = group
+    r = group
+    for s in range(1, nz // 2 + 1):
+        f = lax.ppermute(f, "pre", zf)
+        out = lax.dynamic_update_slice_in_dim(out, f[None], (z - s) % nz, 0)
+        if s < nz - nz // 2:
+            r = lax.ppermute(r, "pre", zb)
+            out = lax.dynamic_update_slice_in_dim(out, r[None], (z + s) % nz, 0)
+    return out.reshape((nz * nx * block.shape[0],) + block.shape[1:])
+
+
 def shards(spikes, trace_decay, pseudo_deriv, readout_weight, feedback_weight, targets):
     ntm = lax.axis_size("tm")
     npre = lax.axis_size("pre")
@@ -74,7 +107,9 @@
         err_rows, feedback_weight, (((1,), (1,)), ((), ())), preferred_element_type=jnp.float32
     )
     weighted = (signal * pseudo_deriv.astype(jnp.float32)).astype(jnp.bfloat16)
-    weighted_all = lax.all_gather(weighted, "pre", axis=0, tiled=True)
+    half = weighted.shape[1] // 2
+    left_all = lax.all_gather(weighted[:, :half], "pre", axis=0, tiled=True)
+    right_all = plane_gather(weighted[:, half:], NZ, npre // NZ)
 
     powers, states = local_traces(spikes, trace_decay)
     ends = lax.all_gather(states[-1], "tm", axis=0)
@@ -87,8 +122,14 @@
     traces = (states + powers * incoming[None, :]).astype(jnp.bfloat16)
     traces_all = ring_gather(traces, "tm", ntm)
 
+    left = outer_sum(traces_all, left_all)
+    right = outer_sum(traces_all, right_all)
+    return jnp.concatenate([left, right], 1)
+
+
+def outer_sum(left_rows, right_rows):
     return lax.dot_general(
-        traces_all, weighted_all, (((0,), (0,)), ((), ())), preferred_element_type=jnp.float32
+        left_rows, right_rows, (((0,), (0,)), ((), ())), preferred_element_type=jnp.float32
     )
 
 

time: 177 us -> 205 us (1.16)
  the two profiles are of different devices: /device:TPU:6 before, /device:TPU:25 now
where the time goes in v3:
time: 205 us
  starting transfers between devices  79.8 us (39%)
  waiting for transfers between devices  43.3 us (21%)
  blocking collectives  33 us (16%)
  local copies, waits for them, and re-layouts  18.1 us (9%)
  between operations  14.4 us (7%)
  matrix products  11.5 us (6%)
  other arithmetic  3.96 us (2%)
    ppermute x4, waiting for transfers between devices, plane_gather(): f = lax.ppermute(f, 'pre', zf)  30.9 us
    ppermute x8, starting transfers between devices, ring_gather(): f = lax.ppermute(f, axis, fwd)  25.7 us
    all_gather x1, blocking collectives, shards(): ends = lax.all_gather(states[-1], 'tm', axis=0)  16.6 us
    all_gather x1, blocking collectives, route_errors(): return lax.all_gather(moved, 'tm', axis=0, tiled=True)  16.4 us
    all_to_all x1, starting transfers between devices, owned_errors(): pieces = lax.all_to_all(partial_logits, 'pre', 0, 0, tiled=True)  12.9 us
    ppermute x3, starting transfers between devices, plane_gather(): r = lax.ppermute(r, 'pre', zb)  12.3 us
    ppermute x1, starting transfers between devices, route_errors(): moved = lax.ppermute(errors, ('tm', 'pre'), perm)  10.5 us
    dot_general x2, matrix products, outer_sum(): lax.dot_general(left_rows, right_rows, (((0,), (0,)), ((), ())), preferre...  9.48 us
  transfers between devices with their start and end apart: 28, of which 8 were waited for; matrix products, arithmetic and copies ran while one was open for 12% of the time, Pallas kernels for 0%

profile of v3, /device:TPU:25, one launch (start us, length us, event | category | flops | bytes accessed | tf_op | source)
XLA Modules:
  0.0 204.6 jit_solution(13449306423668807240)
XLA Ops:
  6.5 1.5 fusion.2
  8.1 0.8 all_to_all.6
  8.9 12.9 %all-to-all-start = ((f32[32,6,512]{2,1,0:T(8,128)}), f32[32,6,512]{2,1,0:T(8,128)S(1)}, u32[]{:S(2)}, u32[]{:S(2)}) async-start(f32[32,6,512]{2,1,0:T(8,128)} %all_to_all.6), calls=%async_computation | async-start | bytes 1048576 | tf_op jit(solution)/shard_map/all_to_all | solution.py:26
  22.0 0.1 slice.198
  22.1 0.1 slice.200
  22.8 0.2 slice.196
  24.2 0.8 fusion.1
  25.1 0.9 pad_maximum_fusion.1
  26.2 16.6 %all-gather = f32[16,1,512]{2,1,0:T(1,128)S(1)} all-gather(f32[1,1,512]{2,1,0:T(1,128)S(1)} %add_bitcast_fusion), channel_id=1, replica_groups=mesh['tm'=16,'pre'=32] {'tm'}, dimensions={0}, use_global_device_ids=true | all-gather | bytes 34816 | tf_op jit(solution)/shard_map/all_gather | solution.py:115
  42.8 0.9 while.14
  43.7 2.0 broadcast_in_dim.107
  45.7 0.8 bitcast_dynamic-update-slice_fusion.23
  46.5 1.7 collective-permute-start
  48.3 2.5 %collective-permute-done = bf16[192,512]{1,0:T(8,128)(2,1)S(1)} collective-permute-done((bf16[192,512]{1,0:T(8,128)(2,1)S(1)}, bf16[192,512]{1,0:T(8,128)(2,1)S(1)}, u32[]{:S(2)}, u32[]{:S(2)}) %collective-permute-start) | collective-permute-done | bytes 196640 | tf_op jit(solution)/shard_map/ppermute | solution.py:60
  50.8 3.7 %collective-permute-start.2 = (bf16[192,512]{1,0:T(8,128)(2,1)S(1)}, bf16[192,512]{1,0:T(8,128)(2,1)S(1)}, u32[]{:S(2)}, u32[]{:S(2)}) collective-permute-start(bf16[192,512]{1,0:T(8,128)(2,1)S(1)} %collective-permute-done), channel_id=1, source_target_pairs={{0,32},{32,64},{64,96},{96,128},{128,160},{160,192},{192,224},{224... | collective-permute-start | bytes 589832 | tf_op jit(solution)/shard_map/ppermute | solution.py:60
  54.5 0.7 bitcast_dynamic-update-slice_fusion.22
  55.2 0.7 bitcast_dynamic-update-slice_fusion.21
  55.9 1.2 collective-permute-done.2
  57.1 3.7 %collective-permute-start.4 = (bf16[192,512]{1,0:T(8,128)(2,1)S(1)}, bf16[192,512]{1,0:T(8,128)(2,1)S(1)}, u32[]{:S(2)}, u32[]{:S(2)}) collective-permute-start(bf16[192,512]{1,0:T(8,128)(2,1)S(1)} %collective-permute-done.2), channel_id=1, source_target_pairs={{0,32},{32,64},{64,96},{96,128},{128,160},{160,192},{192,224},{224... | collective-permute-start | bytes 589832 | tf_op jit(solution)/shard_map/ppermute | solution.py:60
  60.9 0.1 reduce_max.9
  61.0 0.2 fusion.8
  61.2 0.1 subtract_convert_fusion
  61.3 10.5 %collective-permute-start.15 = (bf16[6,512]{1,0:T(8,128)(2,1)S(1)}, bf16[6,512]{1,0:T(8,128)(2,1)S(1)}, u32[]{:S(2)}, u32[]{:S(2)}) collective-permute-start(bf16[6,512]{1,0:T(8,128)(2,1)S(1)} %subtract_convert_fusion), channel_id=1, source_target_pairs={{0,0},{1,32},{2,64},{3,96},{4,128},{5,160},{6,192},{7,224},{8,256}... | collective-permute-start | bytes 18440 | tf_op jit(solution)/shard_map/ppermute | solution.py:46
  71.8 0.7 bitcast_dynamic-update-slice_fusion.20
  72.6 16.4 %all-gather.1 = bf16[16,6,512]{2,1,0:T(8,128)(2,1)S(1)} all-gather(bf16[1,6,512]{2,1,0:T(8,128)(2,1)S(1)} %bitcast.98), channel_id=1, replica_groups=mesh['tm'=16,'pre'=32] {'tm'}, dimensions={0}, use_global_device_ids=true | all-gather | bytes 104448 | tf_op jit(solution)/shard_map/all_gather | solution.py:48
  89.1 0.5 fusion
  89.5 0.6 fusion.17
  90.2 0.7 bitcast_dynamic-update-slice_fusion.19
  90.9 2.9 %collective-permute-start.6 = (bf16[192,512]{1,0:T(8,128)(2,1)S(1)}, bf16[192,512]{1,0:T(8,128)(2,1)S(1)}, u32[]{:S(2)}, u32[]{:S(2)}) collective-permute-start(bf16[192,512]{1,0:T(8,128)(2,1)S(1)} %collective-permute-done.4), channel_id=1, source_target_pairs={{0,32},{32,64},{64,96},{96,128},{128,160},{160,192},{192,224},{224... | collective-permute-start | bytes 589832 | tf_op jit(solution)/shard_map/ppermute | solution.py:60
  93.8 0.7 bitcast_dynamic-update-slice_fusion.18
  94.6 0.7 bitcast_dynamic-update-slice_fusion.17
  95.3 3.6 %collective-permute-start.16 = (bf16[96,512]{1,0:T(8,128)(2,1)S(1)}, bf16[96,512]{1,0:T(8,128)(2,1)S(1)}, u32[]{:S(2)}, u32[]{:S(2)}) collective-permute-start(bf16[96,512]{1,0:T(8,128)(2,1)S(1)} %get-tuple-element.133), channel_id=1, source_target_pairs={{0,1},{1,2},{2,3},{3,0},{4,5},{5,6},{6,7},{7,4},{8,9},{9,10},{10,1... | collective-permute-start | bytes 294920 | tf_op jit(solution)/shard_map/ppermute | solution.py:81
  98.8 3.8 %collective-permute-start.17 = (bf16[96,512]{1,0:T(8,128)(2,1)S(1)}, bf16[96,512]{1,0:T(8,128)(2,1)S(1)}, u32[]{:S(2)}, u32[]{:S(2)}) collective-permute-start(bf16[96,512]{1,0:T(8,128)(2,1)S(1)} %get-tuple-element.133), channel_id=1, source_target_pairs={{0,3},{1,0},{2,1},{3,2},{4,7},{5,4},{6,5},{7,6},{8,11},{9,8},{10,9... | collective-permute-start | bytes 294920 | tf_op jit(solution)/shard_map/ppermute | solution.py:84
  102.7 3.2 %collective-permute-start.8 = (bf16[192,512]{1,0:T(8,128)(2,1)S(1)}, bf16[192,512]{1,0:T(8,128)(2,1)S(1)}, u32[]{:S(2)}, u32[]{:S(2)}) collective-permute-start(bf16[192,512]{1,0:T(8,128)(2,1)S(1)} %collective-permute-done.6), channel_id=1, source_target_pairs={{0,32},{32,64},{64,96},{96,128},{128,160},{160,192},{192,224},{224... | collective-permute-start | bytes 589832 | tf_op jit(solution)/shard_map/ppermute | solution.py:60
  105.9 0.7 bitcast_dynamic-update-slice_fusion.16
  106.6 0.7 bitcast_dynamic-update-slice_fusion.15
  107.3 1.9 collective-permute-start.18
  109.3 6.1 %collective-permute-done.18 = bf16[96,512]{1,0:T(8,128)(2,1)S(1)} collective-permute-done((bf16[96,512]{1,0:T(8,128)(2,1)S(1)}, bf16[96,512]{1,0:T(8,128)(2,1)S(1)}, u32[]{:S(2)}, u32[]{:S(2)}) %collective-permute-start.18) | collective-permute-done | bytes 98336 | tf_op jit(solution)/shard_map/ppermute | solution.py:81
  115.4 3.3 %collective-permute-start.19 = (bf16[4,96,512]{2,1,0:T(8,128)(2,1)S(1)}, bf16[4,96,512]{2,1,0:T(8,128)(2,1)S(1)}, u32[]{:S(2)}, u32[]{:S(2)}) collective-permute-start(bf16[4,96,512]{2,1,0:T(8,128)(2,1)S(1)} %bitcast_dynamic-update-slice_fusion.24), channel_id=1, source_target_pairs={{0,4},{1,5},{2,6},{3,7},{4,8},{5,9},{6,10},{7,11},{8,12},{9,13},{1... | collective-permute-start | bytes 1179656 | tf_op jit(solution)/shard_map/ppermute | solution.py:91
  118.6 3.2 %collective-permute-start.20 = (bf16[4,96,512]{2,1,0:T(8,128)(2,1)S(1)}, bf16[4,96,512]{2,1,0:T(8,128)(2,1)S(1)}, u32[]{:S(2)}, u32[]{:S(2)}) collective-permute-start(bf16[4,96,512]{2,1,0:T(8,128)(2,1)S(1)} %bitcast_dynamic-update-slice_fusion.24), channel_id=1, source_target_pairs={{0,28},{1,29},{2,30},{3,31},{4,0},{5,1},{6,2},{7,3},{8,4},{9,5},{1... | collective-permute-start | bytes 1179656 | tf_op jit(solution)/shard_map/ppermute | solution.py:94
  121.9 0.3 broadcast_in_dim.126
  122.3 3.3 %collective-permute-start.10 = (bf16[192,512]{1,0:T(8,128)(2,1)S(1)}, bf16[192,512]{1,0:T(8,128)(2,1)S(1)}, u32[]{:S(2)}, u32[]{:S(2)}) collective-permute-start(bf16[192,512]{1,0:T(8,128)(2,1)S(1)} %collective-permute-done.8), channel_id=1, source_target_pairs={{0,32},{32,64},{64,96},{96,128},{128,160},{160,192},{192,224},{224... | collective-permute-start | bytes 589832 | tf_op jit(solution)/shard_map/ppermute | solution.py:60
  125.6 0.7 bitcast_dynamic-update-slice_fusion.14
  126.2 0.7 bitcast_dynamic-update-slice_fusion.13
  126.9 1.2 collective-permute-done.10
  128.2 3.7 %collective-permute-start.12 = (bf16[192,512]{1,0:T(8,128)(2,1)S(1)}, bf16[192,512]{1,0:T(8,128)(2,1)S(1)}, u32[]{:S(2)}, u32[]{:S(2)}) collective-permute-start(bf16[192,512]{1,0:T(8,128)(2,1)S(1)} %collective-permute-done.10), channel_id=1, source_target_pairs={{0,32},{32,64},{64,96},{96,128},{128,160},{160,192},{192,224},{224... | collective-permute-start | bytes 589832 | tf_op jit(solution)/shard_map/ppermute | solution.py:60
  131.9 0.7 bitcast_dynamic-update-slice_fusion.12
  132.6 0.7 bitcast_dynamic-update-slice_fusion.11
  133.2 2.0 collective-permute-start.21
  135.2 4.5 %collective-permute-start.22 = (bf16[4,96,512]{2,1,0:T(8,128)(2,1)S(1)}, bf16[4,96,512]{2,1,0:T(8,128)(2,1)S(1)}, u32[]{:S(2)}, u32[]{:S(2)}) collective-permute-start(bf16[4,96,512]{2,1,0:T(8,128)(2,1)S(1)} %collective-permute-done.20), channel_id=1, source_target_pairs={{0,28},{1,29},{2,30},{3,31},{4,0},{5,1},{6,2},{7,3},{8,4},{9,5},{1... | collective-permute-start | bytes 1179656 | tf_op jit(solution)/shard_map/ppermute | solution.py:94
  139.8 3.5 %collective-permute-start.14 = (bf16[192,512]{1,0:T(8,128)(2,1)S(1)}, bf16[192,512]{1,0:T(8,128)(2,1)S(1)}, u32[]{:S(2)}, u32[]{:S(2)}) collective-permute-start(bf16[192,512]{1,0:T(8,128)(2,1)S(1)} %collective-permute-done.12), channel_id=1, source_target_pairs={{0,32},{32,64},{64,96},{96,128},{128,160},{160,192},{192,224},{224... | collective-permute-start | bytes 589832 | tf_op jit(solution)/shard_map/ppermute | solution.py:60
  143.4 0.7 bitcast_dynamic-update-slice_fusion.10
  144.1 0.7 bitcast_dynamic-update-slice_fusion.9
  144.8 1.2 collective-permute-done.14
  146.0 0.7 bitcast_dynamic-update-slice_fusion.8
  146.7 1.9 collective-permute-start.23
  148.6 4.6 %collective-permute-start.24 = (bf16[4,96,512]{2,1,0:T(8,128)(2,1)S(1)}, bf16[4,96,512]{2,1,0:T(8,128)(2,1)S(1)}, u32[]{:S(2)}, u32[]{:S(2)}) collective-permute-start(bf16[4,96,512]{2,1,0:T(8,128)(2,1)S(1)} %collective-permute-done.22), channel_id=1, source_target_pairs={{0,28},{1,29},{2,30},{3,31},{4,0},{5,1},{6,2},{7,3},{8,4},{9,5},{1... | collective-permute-start | bytes 1179656 | tf_op jit(solution)/shard_map/ppermute | solution.py:94
  153.3 15.4 %collective-permute-done.23 = bf16[4,96,512]{2,1,0:T(8,128)(2,1)S(1)} collective-permute-done((bf16[4,96,512]{2,1,0:T(8,128)(2,1)S(1)}, bf16[4,96,512]{2,1,0:T(8,128)(2,1)S(1)}, u32[]{:S(2)}, u32[]{:S(2)}) %collective-permute-start.23) | collective-permute-done | bytes 393248 | tf_op jit(solution)/shard_map/ppermute | solution.py:91
  168.7 1.9 collective-permute-start.25
  170.7 15.5 %collective-permute-done.25 = bf16[4,96,512]{2,1,0:T(8,128)(2,1)S(1)} collective-permute-done((bf16[4,96,512]{2,1,0:T(8,128)(2,1)S(1)}, bf16[4,96,512]{2,1,0:T(8,128)(2,1)S(1)}, u32[]{:S(2)}, u32[]{:S(2)}) %collective-permute-start.25) | collective-permute-done | bytes 393248 | tf_op jit(solution)/shard_map/ppermute | solution.py:91
  186.2 4.7 %fusion.19 = f32[512,512]{0,1:T(8,128)} fusion(bf16[3072,512]{1,0:T(8,128)(2,1)} %bitcast.27, bf16[3072,512]{1,0:T(8,128)(2,1)S(1)} %bitcast.84), kind=kOutput, calls=%fused_computation.100 | convolution fusion | flops 1610612736 | bytes 7340032 | tf_op jit(solution)/shard_map/dot_general | solution.py:131
  190.9 4.8 %fusion.18 = f32[512,512]{0,1:T(8,128)S(1)} fusion(bf16[3072,512]{1,0:T(8,128)(2,1)} %bitcast.27, bf16[3072,512]{1,0:T(8,128)(2,1)} %all-gather.4.cloned.1.call-done), kind=kOutput, calls=%fused_computation.99 | convolution fusion | flops 1610612736 | bytes 7340032 | tf_op jit(solution)/shard_map/dot_general | solution.py:131
  195.7 0.2 pad_maximum_fusion
  195.9 1.8 copy.9
  (182 shorter events, 2.6 us)
Async XLA Ops:
  6.5 82.5 %copy-start = (bf16[1024,512]{1,0:T(8,128)(2,1)S(1)}, bf16[1024,512]{1,0:T(8,128)(2,1)}, u32[]{:S(2)}) copy-start(bf16[1024,512]{1,0:T(8,128)(2,1)} %param.12) | copy-start | bytes 3145732
  6.5 15.4 %copy-start.2 = (s32[192,512]{1,0:T(8,128)S(1)}, s32[192,512]{1,0:T(8,128)}, u32[]{:S(2)}) copy-start(s32[192,512]{1,0:T(8,128)} %param.8) | copy-start | bytes 1179652
  6.5 15.4 %copy-start.5 = (f32[512]{0:T(512)S(1)}, f32[512]{0:T(512)}, u32[]{:S(2)}) copy-start(f32[512]{0:T(512)} %param.9) | copy-start | bytes 6148
  8.9 51.9 %all-to-all-start = ((f32[32,6,512]{2,1,0:T(8,128)}), f32[32,6,512]{2,1,0:T(8,128)S(1)}, u32[]{:S(2)}, u32[]{:S(2)}) async-start(f32[32,6,512]{2,1,0:T(8,128)} %all_to_all.6), calls=%async_computation | async-start | bytes 1048576 | tf_op jit(solution)/shard_map/all_to_all | solution.py:26
  21.8 169.1 %all-gather.4.cloned.1.call-start = ((), (), s32[]{:S(2)}) async-start(), calls=%async_computation.1 | async-start | bytes 3244032 | tf_op jit(solution)/shard_map/all_gather | solution.py:111
  22.0 1.7 copy-start.1
  23.9 1.3 slice-start
  26.2 22.1 %copy-start.6 = (s32[192]{0:T(256)S(1)}, s32[192]{0:T(256)}, u32[]{:S(2)}) copy-start(s32[192]{0:T(256)} %param.13) | copy-start | bytes 2308
  45.7 43.4 %copy-start.4 = (bf16[96,1024]{1,0:T(8,128)(2,1)S(1)}, bf16[96,1024]{1,0:T(8,128)(2,1)}, u32[]{:S(2)}) copy-start(bf16[96,1024]{1,0:T(8,128)(2,1)} %param.10) | copy-start | bytes 589828
  46.5 4.3 %collective-permute-start = (bf16[192,512]{1,0:T(8,128)(2,1)S(1)}, bf16[192,512]{1,0:T(8,128)(2,1)S(1)}, u32[]{:S(2)}, u32[]{:S(2)}) collective-permute-start(bf16[192,512]{1,0:T(8,128)(2,1)S(1)} %get-tuple-element.129), channel_id=1, source_target_pairs={{0,32},{32,64},{64,96},{96,128},{128,160},{160,192},{192,224},{224... | collective-permute-start | bytes 589832 | tf_op jit(solution)/shard_map/ppermute | solution.py:60
  48.2 6.3 %collective-permute-start.1 = (bf16[192,512]{1,0:T(8,128)(2,1)S(1)}, bf16[192,512]{1,0:T(8,128)(2,1)S(1)}, u32[]{:S(2)}, u32[]{:S(2)}) collective-permute-start(bf16[192,512]{1,0:T(8,128)(2,1)S(1)} %get-tuple-element.129), channel_id=1, source_target_pairs={{0,480},{32,0},{64,32},{96,64},{128,96},{160,128},{192,160},{224,1... | collective-permute-start | bytes 589832 | tf_op jit(solution)/shard_map/ppermute | solution.py:63
  50.8 6.3 %collective-permute-start.2 = (bf16[192,512]{1,0:T(8,128)(2,1)S(1)}, bf16[192,512]{1,0:T(8,128)(2,1)S(1)}, u32[]{:S(2)}, u32[]{:S(2)}) collective-permute-start(bf16[192,512]{1,0:T(8,128)(2,1)S(1)} %collective-permute-done), channel_id=1, source_target_pairs={{0,32},{32,64},{64,96},{96,128},{128,160},{160,192},{192,224},{224... | collective-permute-start | bytes 589832 | tf_op jit(solution)/shard_map/ppermute | solution.py:60
  54.5 6.3 %collective-permute-start.3 = (bf16[192,512]{1,0:T(8,128)(2,1)S(1)}, bf16[192,512]{1,0:T(8,128)(2,1)S(1)}, u32[]{:S(2)}, u32[]{:S(2)}) collective-permute-start(bf16[192,512]{1,0:T(8,128)(2,1)S(1)} %collective-permute-done.1), channel_id=1, source_target_pairs={{0,480},{32,0},{64,32},{96,64},{128,96},{160,128},{192,160},{224,1... | collective-permute-start | bytes 589832 | tf_op jit(solution)/shard_map/ppermute | solution.py:63
  57.1 33.8 %collective-permute-start.4 = (bf16[192,512]{1,0:T(8,128)(2,1)S(1)}, bf16[192,512]{1,0:T(8,128)(2,1)S(1)}, u32[]{:S(2)}, u32[]{:S(2)}) collective-permute-start(bf16[192,512]{1,0:T(8,128)(2,1)S(1)} %collective-permute-done.2), channel_id=1, source_target_pairs={{0,32},{32,64},{64,96},{96,128},{128,160},{160,192},{192,224},{224... | collective-permute-start | bytes 589832 | tf_op jit(solution)/shard_map/ppermute | solution.py:60
  60.8 33.0 %collective-permute-start.5 = (bf16[192,512]{1,0:T(8,128)(2,1)S(1)}, bf16[192,512]{1,0:T(8,128)(2,1)S(1)}, u32[]{:S(2)}, u32[]{:S(2)}) collective-permute-start(bf16[192,512]{1,0:T(8,128)(2,1)S(1)} %collective-permute-done.3), channel_id=1, source_target_pairs={{0,480},{32,0},{64,32},{96,64},{128,96},{160,128},{192,160},{224,1... | collective-permute-start | bytes 589832 | tf_op jit(solution)/shard_map/ppermute | solution.py:63
  61.3 11.3 %collective-permute-start.15 = (bf16[6,512]{1,0:T(8,128)(2,1)S(1)}, bf16[6,512]{1,0:T(8,128)(2,1)S(1)}, u32[]{:S(2)}, u32[]{:S(2)}) collective-permute-start(bf16[6,512]{1,0:T(8,128)(2,1)S(1)} %subtract_convert_fusion), channel_id=1, source_target_pairs={{0,0},{1,32},{2,64},{3,96},{4,128},{5,160},{6,192},{7,224},{8,256}... | collective-permute-start | bytes 18440 | tf_op jit(solution)/shard_map/ppermute | solution.py:46
  90.9 11.8 %collective-permute-start.6 = (bf16[192,512]{1,0:T(8,128)(2,1)S(1)}, bf16[192,512]{1,0:T(8,128)(2,1)S(1)}, u32[]{:S(2)}, u32[]{:S(2)}) collective-permute-start(bf16[192,512]{1,0:T(8,128)(2,1)S(1)} %collective-permute-done.4), channel_id=1, source_target_pairs={{0,32},{32,64},{64,96},{96,128},{128,160},{160,192},{192,224},{224... | collective-permute-start | bytes 589832 | tf_op jit(solution)/shard_map/ppermute | solution.py:60
  93.8 12.1 %collective-permute-start.7 = (bf16[192,512]{1,0:T(8,128)(2,1)S(1)}, bf16[192,512]{1,0:T(8,128)(2,1)S(1)}, u32[]{:S(2)}, u32[]{:S(2)}) collective-permute-start(bf16[192,512]{1,0:T(8,128)(2,1)S(1)} %collective-permute-done.5), channel_id=1, source_target_pairs={{0,480},{32,0},{64,32},{96,64},{128,96},{160,128},{192,160},{224,1... | collective-permute-start | bytes 589832 | tf_op jit(solution)/shard_map/ppermute | solution.py:63
  95.3 12.1 %collective-permute-start.16 = (bf16[96,512]{1,0:T(8,128)(2,1)S(1)}, bf16[96,512]{1,0:T(8,128)(2,1)S(1)}, u32[]{:S(2)}, u32[]{:S(2)}) collective-permute-start(bf16[96,512]{1,0:T(8,128)(2,1)S(1)} %get-tuple-element.133), channel_id=1, source_target_pairs={{0,1},{1,2},{2,3},{3,0},{4,5},{5,6},{6,7},{7,4},{8,9},{9,10},{10,1... | collective-permute-start | bytes 294920 | tf_op jit(solution)/shard_map/ppermute | solution.py:81
  98.8 10.4 %collective-permute-start.17 = (bf16[96,512]{1,0:T(8,128)(2,1)S(1)}, bf16[96,512]{1,0:T(8,128)(2,1)S(1)}, u32[]{:S(2)}, u32[]{:S(2)}) collective-permute-start(bf16[96,512]{1,0:T(8,128)(2,1)S(1)} %get-tuple-element.133), channel_id=1, source_target_pairs={{0,3},{1,0},{2,1},{3,2},{4,7},{5,4},{6,5},{7,6},{8,11},{9,8},{10,9... | collective-permute-start | bytes 294920 | tf_op jit(solution)/shard_map/ppermute | solution.py:84
  102.7 19.6 %collective-permute-start.8 = (bf16[192,512]{1,0:T(8,128)(2,1)S(1)}, bf16[192,512]{1,0:T(8,128)(2,1)S(1)}, u32[]{:S(2)}, u32[]{:S(2)}) collective-permute-start(bf16[192,512]{1,0:T(8,128)(2,1)S(1)} %collective-permute-done.6), channel_id=1, source_target_pairs={{0,32},{32,64},{64,96},{96,128},{128,160},{160,192},{192,224},{224... | collective-permute-start | bytes 589832 | tf_op jit(solution)/shard_map/ppermute | solution.py:60
  105.9 19.6 %collective-permute-start.9 = (bf16[192,512]{1,0:T(8,128)(2,1)S(1)}, bf16[192,512]{1,0:T(8,128)(2,1)S(1)}, u32[]{:S(2)}, u32[]{:S(2)}) collective-permute-start(bf16[192,512]{1,0:T(8,128)(2,1)S(1)} %collective-permute-done.7), channel_id=1, source_target_pairs={{0,480},{32,0},{64,32},{96,64},{128,96},{160,128},{192,160},{224,1... | collective-permute-start | bytes 589832 | tf_op jit(solution)/shard_map/ppermute | solution.py:63
  107.3 8.0 %collective-permute-start.18 = (bf16[96,512]{1,0:T(8,128)(2,1)S(1)}, bf16[96,512]{1,0:T(8,128)(2,1)S(1)}, u32[]{:S(2)}, u32[]{:S(2)}) collective-permute-start(bf16[96,512]{1,0:T(8,128)(2,1)S(1)} %collective-permute-done.16), channel_id=1, source_target_pairs={{0,1},{1,2},{2,3},{3,0},{4,5},{5,6},{6,7},{7,4},{8,9},{9,10},{10,1... | collective-permute-start | bytes 294920 | tf_op jit(solution)/shard_map/ppermute | solution.py:81
  115.4 17.9 %collective-permute-start.19 = (bf16[4,96,512]{2,1,0:T(8,128)(2,1)S(1)}, bf16[4,96,512]{2,1,0:T(8,128)(2,1)S(1)}, u32[]{:S(2)}, u32[]{:S(2)}) collective-permute-start(bf16[4,96,512]{2,1,0:T(8,128)(2,1)S(1)} %bitcast_dynamic-update-slice_fusion.24), channel_id=1, source_target_pairs={{0,4},{1,5},{2,6},{3,7},{4,8},{5,9},{6,10},{7,11},{8,12},{9,13},{1... | collective-permute-start | bytes 1179656 | tf_op jit(solution)/shard_map/ppermute | solution.py:91
  118.6 16.6 %collective-permute-start.20 = (bf16[4,96,512]{2,1,0:T(8,128)(2,1)S(1)}, bf16[4,96,512]{2,1,0:T(8,128)(2,1)S(1)}, u32[]{:S(2)}, u32[]{:S(2)}) collective-permute-start(bf16[4,96,512]{2,1,0:T(8,128)(2,1)S(1)} %bitcast_dynamic-update-slice_fusion.24), channel_id=1, source_target_pairs={{0,28},{1,29},{2,30},{3,31},{4,0},{5,1},{6,2},{7,3},{8,4},{9,5},{1... | collective-permute-start | bytes 1179656 | tf_op jit(solution)/shard_map/ppermute | solution.py:94
  122.3 5.9 %collective-permute-start.10 = (bf16[192,512]{1,0:T(8,128)(2,1)S(1)}, bf16[192,512]{1,0:T(8,128)(2,1)S(1)}, u32[]{:S(2)}, u32[]{:S(2)}) collective-permute-start(bf16[192,512]{1,0:T(8,128)(2,1)S(1)} %collective-permute-done.8), channel_id=1, source_target_pairs={{0,32},{32,64},{64,96},{96,128},{128,160},{160,192},{192,224},{224... | collective-permute-start | bytes 589832 | tf_op jit(solution)/shard_map/ppermute | solution.py:60
  125.6 6.3 %collective-permute-start.11 = (bf16[192,512]{1,0:T(8,128)(2,1)S(1)}, bf16[192,512]{1,0:T(8,128)(2,1)S(1)}, u32[]{:S(2)}, u32[]{:S(2)}) collective-permute-start(bf16[192,512]{1,0:T(8,128)(2,1)S(1)} %collective-permute-done.9), channel_id=1, source_target_pairs={{0,480},{32,0},{64,32},{96,64},{128,96},{160,128},{192,160},{224,1... | collective-permute-start | bytes 589832 | tf_op jit(solution)/shard_map/ppermute | solution.py:63
  128.2 11.7 %collective-permute-start.12 = (bf16[192,512]{1,0:T(8,128)(2,1)S(1)}, bf16[192,512]{1,0:T(8,128)(2,1)S(1)}, u32[]{:S(2)}, u32[]{:S(2)}) collective-permute-start(bf16[192,512]{1,0:T(8,128)(2,1)S(1)} %collective-permute-done.10), channel_id=1, source_target_pairs={{0,32},{32,64},{64,96},{96,128},{128,160},{160,192},{192,224},{224... | collective-permute-start | bytes 589832 | tf_op jit(solution)/shard_map/ppermute | solution.py:60
  131.9 12.2 %collective-permute-start.13 = (bf16[192,512]{1,0:T(8,128)(2,1)S(1)}, bf16[192,512]{1,0:T(8,128)(2,1)S(1)}, u32[]{:S(2)}, u32[]{:S(2)}) collective-permute-start(bf16[192,512]{1,0:T(8,128)(2,1)S(1)} %collective-permute-done.11), channel_id=1, source_target_pairs={{0,480},{32,0},{64,32},{96,64},{128,96},{160,128},{192,160},{224,1... | collective-permute-start | bytes 589832 | tf_op jit(solution)/shard_map/ppermute | solution.py:63
  133.2 13.4 %collective-permute-start.21 = (bf16[4,96,512]{2,1,0:T(8,128)(2,1)S(1)}, bf16[4,96,512]{2,1,0:T(8,128)(2,1)S(1)}, u32[]{:S(2)}, u32[]{:S(2)}) collective-permute-start(bf16[4,96,512]{2,1,0:T(8,128)(2,1)S(1)} %collective-permute-done.19), channel_id=1, source_target_pairs={{0,4},{1,5},{2,6},{3,7},{4,8},{5,9},{6,10},{7,11},{8,12},{9,13},{1... | collective-permute-start | bytes 1179656 | tf_op jit(solution)/shard_map/ppermute | solution.py:91
  135.2 13.4 %collective-permute-start.22 = (bf16[4,96,512]{2,1,0:T(8,128)(2,1)S(1)}, bf16[4,96,512]{2,1,0:T(8,128)(2,1)S(1)}, u32[]{:S(2)}, u32[]{:S(2)}) collective-permute-start(bf16[4,96,512]{2,1,0:T(8,128)(2,1)S(1)} %collective-permute-done.20), channel_id=1, source_target_pairs={{0,28},{1,29},{2,30},{3,31},{4,0},{5,1},{6,2},{7,3},{8,4},{9,5},{1... | collective-permute-start | bytes 1179656 | tf_op jit(solution)/shard_map/ppermute | solution.py:94
  139.8 6.1 %collective-permute-start.14 = (bf16[192,512]{1,0:T(8,128)(2,1)S(1)}, bf16[192,512]{1,0:T(8,128)(2,1)S(1)}, u32[]{:S(2)}, u32[]{:S(2)}) collective-permute-start(bf16[192,512]{1,0:T(8,128)(2,1)S(1)} %collective-permute-done.12), channel_id=1, source_target_pairs={{0,32},{32,64},{64,96},{96,128},{128,160},{160,192},{192,224},{224... | collective-permute-start | bytes 589832 | tf_op jit(solution)/shard_map/ppermute | solution.py:60
  146.7 22.0 %collective-permute-start.23 = (bf16[4,96,512]{2,1,0:T(8,128)(2,1)S(1)}, bf16[4,96,512]{2,1,0:T(8,128)(2,1)S(1)}, u32[]{:S(2)}, u32[]{:S(2)}) collective-permute-start(bf16[4,96,512]{2,1,0:T(8,128)(2,1)S(1)} %collective-permute-done.21), channel_id=1, source_target_pairs={{0,4},{1,5},{2,6},{3,7},{4,8},{5,9},{6,10},{7,11},{8,12},{9,13},{1... | collective-permute-start | bytes 1179656 | tf_op jit(solution)/shard_map/ppermute | solution.py:91
  148.6 22.0 %collective-permute-start.24 = (bf16[4,96,512]{2,1,0:T(8,128)(2,1)S(1)}, bf16[4,96,512]{2,1,0:T(8,128)(2,1)S(1)}, u32[]{:S(2)}, u32[]{:S(2)}) collective-permute-start(bf16[4,96,512]{2,1,0:T(8,128)(2,1)S(1)} %collective-permute-done.22), channel_id=1, source_target_pairs={{0,28},{1,29},{2,30},{3,31},{4,0},{5,1},{6,2},{7,3},{8,4},{9,5},{1... | collective-permute-start | bytes 1179656 | tf_op jit(solution)/shard_map/ppermute | solution.py:94
  168.7 17.5 %collective-permute-start.25 = (bf16[4,96,512]{2,1,0:T(8,128)(2,1)S(1)}, bf16[4,96,512]{2,1,0:T(8,128)(2,1)S(1)}, u32[]{:S(2)}, u32[]{:S(2)}) collective-permute-start(bf16[4,96,512]{2,1,0:T(8,128)(2,1)S(1)} %collective-permute-done.23), channel_id=1, source_target_pairs={{0,4},{1,5},{2,6},{3,7},{4,8},{5,9},{6,10},{7,11},{8,12},{9,13},{1... | collective-permute-start | bytes 1179656 | tf_op jit(solution)/shard_map/ppermute | solution.py:91
  190.9 4.8 %copy-start.3 = (f32[512,512]{0,1:T(8,128)S(1)}, f32[512,512]{0,1:T(8,128)}, u32[]{:S(2)}) copy-start(f32[512,512]{0,1:T(8,128)} %fusion.19) | copy-start | bytes 3145732
Sparse Core Ops, SparseCore 0:
  90.3 89.9 all-gather.3

commit v4 on v1

--- a/solution.py
+++ b/solution.py
@@ -2,6 +2,8 @@
 import jax.numpy as jnp
 from jax import lax
 from jax.sharding import PartitionSpec as P
+
+NZ = 8
 
 
 def combine_pairs(earlier, later):
@@ -46,21 +48,34 @@
     return lax.all_gather(moved, "tm", axis=0, tiled=True)
 
 
-def ring_gather(block, axis, count):
-    index = lax.axis_index(axis)
-    fwd = [(i, (i + 1) % count) for i in range(count)]
-    bwd = [(i, (i - 1) % count) for i in range(count)]
+def ring_stage(block, coord, count, fwd, bwd):
     out = jnp.zeros((count,) + block.shape, block.dtype)
-    out = lax.dynamic_update_slice_in_dim(out, block[None], index, 0)
+    out = lax.dynamic_update_slice_in_dim(out, block[None], coord, 0)
     f = block
-    b = block
+    r = block
     for s in range(1, count // 2 + 1):
-        f = lax.ppermute(f, axis, fwd)
-        out = lax.dynamic_update_slice_in_dim(out, f[None], (index - s) % count, 0)
+        f = lax.ppermute(f, "pre", fwd)
+        out = lax.dynamic_update_slice_in_dim(out, f[None], (coord - s) % count, 0)
         if s < count - count // 2:
-            b = lax.ppermute(b, axis, bwd)
-            out = lax.dynamic_update_slice_in_dim(out, b[None], (index + s) % count, 0)
-    return out.reshape((count * block.shape[0],) + block.shape[1:])
+            r = lax.ppermute(r, "pre", bwd)
+            out = lax.dynamic_update_slice_in_dim(out, r[None], (coord + s) % count, 0)
+    return out
+
+
+def plane_gather(block, nz, nx):
+    b = lax.axis_index("pre")
+    z = b // nx
+    x = b % nx
+    xf = [(zz * nx + xx, zz * nx + (xx + 1) % nx) for zz in range(nz) for xx in range(nx)]
+    xb = [(zz * nx + xx, zz * nx + (xx - 1) % nx) for zz in range(nz) for xx in range(nx)]
+    zf = [(zz * nx + xx, ((zz + 1) % nz) * nx + xx) for zz in range(nz) for xx in range(nx)]
+    zb = [(zz * nx + xx, ((zz - 1) % nz) * nx + xx) for zz in range(nz) for xx in range(nx)]
+    half = block.shape[1] // 2
+    rows = nz * nx * block.shape[0]
+    first = ring_stage(ring_stage(block[:, :half], x, nx, xf, xb), z, nz, zf, zb)
+    second = ring_stage(ring_stage(block[:, half:], z, nz, zf, zb), x, nx, xf, xb)
+    second = jnp.swapaxes(second, 0, 1)
+    return first.reshape(rows, half), second.reshape(rows, -1)
 
 
 def shards(spikes, trace_decay, pseudo_deriv, readout_weight, feedback_weight, targets):
@@ -74,7 +89,8 @@
         err_rows, feedback_weight, (((1,), (1,)), ((), ())), preferred_element_type=jnp.float32
     )
     weighted = (signal * pseudo_deriv.astype(jnp.float32)).astype(jnp.bfloat16)
-    weighted_all = lax.all_gather(weighted, "pre", axis=0, tiled=True)
+    assert npre % NZ == 0
+    left_all, right_all = plane_gather(weighted, NZ, npre // NZ)
 
     powers, states = local_traces(spikes, trace_decay)
     ends = lax.all_gather(states[-1], "tm", axis=0)
@@ -85,10 +101,15 @@
 
     incoming = lax.fori_loop(0, ntm, step, jnp.zeros_like(trace_decay))
     traces = (states + powers * incoming[None, :]).astype(jnp.bfloat16)
-    traces_all = ring_gather(traces, "tm", ntm)
+    traces_all = lax.all_gather(traces, "tm", axis=0, tiled=True)
+    left = outer_sum(traces_all, left_all)
+    right = outer_sum(traces_all, right_all)
+    return jnp.concatenate([left, right], 1)
 
+
+def outer_sum(left_rows, right_rows):
     return lax.dot_general(
-        traces_all, weighted_all, (((0,), (0,)), ((), ())), preferred_element_type=jnp.float32
+        left_rows, right_rows, (((0,), (0,)), ((), ())), preferred_element_type=jnp.float32
     )
 
 

time: 177 us -> 194 us (1.096)
  starting transfers between devices: 37 us -> 85.2 us
  waiting for transfers between devices: 58.3 us -> 26.3 us
  local copies, waits for them, and re-layouts: 15 us -> 19.3 us
    ppermute x15 -> x20, starting transfers between devices: 21.7 us -> 69.8 us  [the longest x12 40.2 us: ring_stage(): f = lax.ppermute(f, 'pre', fwd)]
    all_to_all x1, waiting for transfers between devices: 15.8 us -> 0.01 us  [owned_errors(): pieces = lax.all_to_all(partial_logits, 'pre', 0, 0, tiled=True)]
    all_gather x1, waiting for transfers between devices: 14.3 us -> 0.01 us  [shards(): traces_all = lax.all_gather(traces, 'tm', axis=0, tiled=True)]
    broadcast_in_dim x1 -> x4, local copies, waits for them, and re-layouts: 2.01 us -> 4.2 us  [ring_stage(): out = jnp.zeros((count,) + block.shape, block.dtype)]
    all_gather x1, blocking collectives: 18.5 us -> 16.4 us  [route_errors(): return lax.all_gather(moved, 'tm', axis=0, tiled=True)]
    ppermute x15 -> x20, waiting for transfers between devices: 19.1 us -> 17.4 us  [the longest x12 17.4 us: ring_stage(): f = lax.ppermute(f, 'pre', fwd)]
    dynamic_update_slice x15 -> x23, local copies, waits for them, and re-layouts: 10.3 us -> 10.6 us  [the longest x12 5.31 us: ring_stage(): out = lax.dynamic_update_slice_in_dim(out, f[None], (coord - s) % count, 0)]
    dot_general x1 -> x2, matrix products: 8.49 us -> 8.56 us  [outer_sum(): lax.dot_general(left_rows, right_rows, (((0,), (0,)), ((), ())), preferre...]
  transfers between devices with their start and end apart: 18 -> 23, of which waited for: 12 -> 5; matrix products, arithmetic and copies ran while one was open for 9% -> 10% of each run, Pallas kernels for 0% -> 0%
where the time goes in v4:
time: 194 us; the launch traced here: 193 us
  starting transfers between devices  85.2 us (44%)
  blocking collectives  34 us (18%)
  waiting for transfers between devices  26.3 us (14%)
  local copies, waits for them, and re-layouts  19.3 us (10%)
  between operations  14.7 us (8%)
  matrix products  10.6 us (5%)
  other arithmetic  2.37 us (1%)
    ppermute x12, starting transfers between devices, ring_stage(): f = lax.ppermute(f, 'pre', fwd)  40.2 us
    ppermute x8, starting transfers between devices, ring_stage(): r = lax.ppermute(r, 'pre', bwd)  29.6 us
    all_gather x1, blocking collectives, shards(): ends = lax.all_gather(states[-1], 'tm', axis=0)  17.7 us
    ppermute x12, waiting for transfers between devices, ring_stage(): f = lax.ppermute(f, 'pre', fwd)  17.4 us
    all_gather x1, blocking collectives, route_errors(): return lax.all_gather(moved, 'tm', axis=0, tiled=True)  16.4 us
    all_to_all x1, starting transfers between devices, owned_errors(): pieces = lax.all_to_all(partial_logits, 'pre', 0, 0, tiled=True)  13.4 us
    ppermute x1, waiting for transfers between devices, route_errors(): moved = lax.ppermute(errors, ('tm', 'pre'), perm)  8.87 us
    dot_general x2, matrix products, outer_sum(): lax.dot_general(left_rows, right_rows, (((0,), (0,)), ((), ())), preferre...  8.56 us
  transfers between devices with their start and end apart: 23, of which 5 were waited for; matrix products, arithmetic and copies ran while one was open for 10% of the time, Pallas kernels for 0%

profile of v4, /device:TPU:6, one launch (start us, length us, event | category | flops | bytes accessed | tf_op | source)
XLA Modules:
  0.0 193.0 jit_solution(17414160645709224798)
XLA Ops:
  6.5 1.6 fusion.2
  8.1 0.8 all_to_all.6
  8.9 13.4 %all-to-all-start = ((f32[32,6,512]{2,1,0:T(8,128)}), f32[32,6,512]{2,1,0:T(8,128)S(1)}, u32[]{:S(2)}, u32[]{:S(2)}) async-start(f32[32,6,512]{2,1,0:T(8,128)} %all_to_all.6), calls=%async_computation | async-start | bytes 1048576 | tf_op jit(solution)/shard_map/all_to_all | solution.py:26
  22.5 0.2 slice.196
  22.7 0.1 slice.198
  22.9 0.1 slice.200
  24.7 0.1 fusion.1
  24.9 0.1 pad.113
  24.9 0.1 slice-done
  25.2 17.7 %all-gather = f32[16,1,512]{2,1,0:T(1,128)S(1)} all-gather(f32[1,1,512]{2,1,0:T(1,128)S(1)} %add_bitcast_fusion), channel_id=1, replica_groups=mesh['tm'=16,'pre'=32] {'tm'}, dimensions={0}, use_global_device_ids=true | all-gather | bytes 34816 | tf_op jit(solution)/shard_map/all_gather | solution.py:96
  42.9 0.9 while.14
  43.8 0.8 add_convert_fusion
  44.8 0.1 dynamic_slice.10
  44.8 0.1 reduce_sum.18
  44.9 0.1 reduce_max.9
  45.0 0.2 fusion.8
  45.2 0.1 subtract_convert_fusion
  45.3 1.9 collective-permute-start
  47.4 8.9 %collective-permute-done = bf16[6,512]{1,0:T(8,128)(2,1)S(1)} collective-permute-done((bf16[6,512]{1,0:T(8,128)(2,1)S(1)}, bf16[6,512]{1,0:T(8,128)(2,1)S(1)}, u32[]{:S(2)}, u32[]{:S(2)}) %collective-permute-start) | collective-permute-done | bytes 6176 | tf_op jit(solution)/shard_map/ppermute | solution.py:46
  56.3 16.4 %all-gather.1 = bf16[16,6,512]{2,1,0:T(8,128)(2,1)S(1)} all-gather(bf16[1,6,512]{2,1,0:T(8,128)(2,1)S(1)} %bitcast.97), channel_id=1, replica_groups=mesh['tm'=16,'pre'=32] {'tm'}, dimensions={0}, use_global_device_ids=true | all-gather | bytes 104448 | tf_op jit(solution)/shard_map/all_gather | solution.py:48
  72.7 0.4 fusion
  73.2 5.3 %collective-permute-start.11 = (bf16[96,512]{1,0:T(8,128)(2,1)S(1)}, bf16[96,512]{1,0:T(8,128)(2,1)S(1)}, u32[]{:S(2)}, u32[]{:S(2)}) collective-permute-start(bf16[96,512]{1,0:T(8,128)(2,1)S(1)} %get-tuple-element.131), channel_id=1, source_target_pairs={{0,4},{1,5},{2,6},{3,7},{4,8},{5,9},{6,10},{7,11},{8,12},{9,13},{1... | collective-permute-start | bytes 294920 | tf_op jit(solution)/shard_map/ppermute | solution.py:57
  78.5 1.9 collective-permute-start.12
  80.4 3.6 %collective-permute-start.1 = (bf16[96,512]{1,0:T(8,128)(2,1)S(1)}, bf16[96,512]{1,0:T(8,128)(2,1)S(1)}, u32[]{:S(2)}, u32[]{:S(2)}) collective-permute-start(bf16[96,512]{1,0:T(8,128)(2,1)S(1)} %get-tuple-element.130), channel_id=1, source_target_pairs={{0,1},{1,2},{2,3},{3,0},{4,5},{5,6},{6,7},{7,4},{8,9},{9,10},{10,1... | collective-permute-start | bytes 294920 | tf_op jit(solution)/shard_map/ppermute | solution.py:57
  84.0 2.3 %collective-permute-start.2 = (bf16[96,512]{1,0:T(8,128)(2,1)S(1)}, bf16[96,512]{1,0:T(8,128)(2,1)S(1)}, u32[]{:S(2)}, u32[]{:S(2)}) collective-permute-start(bf16[96,512]{1,0:T(8,128)(2,1)S(1)} %get-tuple-element.130), channel_id=1, source_target_pairs={{0,3},{1,0},{2,1},{3,2},{4,7},{5,4},{6,5},{7,6},{8,11},{9,8},{10,9... | collective-permute-start | bytes 294920 | tf_op jit(solution)/shard_map/ppermute | solution.py:60
  86.3 0.1 broadcast_in_dim.115
  86.4 3.9 %collective-permute-start.13 = (bf16[96,512]{1,0:T(8,128)(2,1)S(1)}, bf16[96,512]{1,0:T(8,128)(2,1)S(1)}, u32[]{:S(2)}, u32[]{:S(2)}) collective-permute-start(bf16[96,512]{1,0:T(8,128)(2,1)S(1)} %collective-permute-done.11), channel_id=1, source_target_pairs={{0,4},{1,5},{2,6},{3,7},{4,8},{5,9},{6,10},{7,11},{8,12},{9,13},{1... | collective-permute-start | bytes 294920 | tf_op jit(solution)/shard_map/ppermute | solution.py:57
  90.4 3.1 %collective-permute-start.14 = (bf16[96,512]{1,0:T(8,128)(2,1)S(1)}, bf16[96,512]{1,0:T(8,128)(2,1)S(1)}, u32[]{:S(2)}, u32[]{:S(2)}) collective-permute-start(bf16[96,512]{1,0:T(8,128)(2,1)S(1)} %collective-permute-done.12), channel_id=1, source_target_pairs={{0,28},{1,29},{2,30},{3,31},{4,0},{5,1},{6,2},{7,3},{8,4},{9,5},{1... | collective-permute-start | bytes 294920 | tf_op jit(solution)/shard_map/ppermute | solution.py:60
  93.5 4.8 %collective-permute-start.3 = (bf16[96,512]{1,0:T(8,128)(2,1)S(1)}, bf16[96,512]{1,0:T(8,128)(2,1)S(1)}, u32[]{:S(2)}, u32[]{:S(2)}) collective-permute-start(bf16[96,512]{1,0:T(8,128)(2,1)S(1)} %collective-permute-done.1), channel_id=1, source_target_pairs={{0,1},{1,2},{2,3},{3,0},{4,5},{5,6},{6,7},{7,4},{8,9},{9,10},{10,1... | collective-permute-start | bytes 294920 | tf_op jit(solution)/shard_map/ppermute | solution.py:57
  98.4 2.1 %collective-permute-done.3 = bf16[96,512]{1,0:T(8,128)(2,1)S(1)} collective-permute-done((bf16[96,512]{1,0:T(8,128)(2,1)S(1)}, bf16[96,512]{1,0:T(8,128)(2,1)S(1)}, u32[]{:S(2)}, u32[]{:S(2)}) %collective-permute-start.3) | collective-permute-done | bytes 98336 | tf_op jit(solution)/shard_map/ppermute | solution.py:57
  100.5 2.2 %collective-permute-start.4 = (bf16[4,96,512]{2,1,0:T(8,128)(2,1)S(1)}, bf16[4,96,512]{2,1,0:T(8,128)(2,1)S(1)}, u32[]{:S(2)}, u32[]{:S(2)}) collective-permute-start(bf16[4,96,512]{2,1,0:T(8,128)(2,1)S(1)} %bitcast_dynamic-update-slice_fusion.20), channel_id=1, source_target_pairs={{0,4},{1,5},{2,6},{3,7},{4,8},{5,9},{6,10},{7,11},{8,12},{9,13},{1... | collective-permute-start | bytes 1179656 | tf_op jit(solution)/shard_map/ppermute | solution.py:57
  102.7 4.8 %collective-permute-start.5 = (bf16[4,96,512]{2,1,0:T(8,128)(2,1)S(1)}, bf16[4,96,512]{2,1,0:T(8,128)(2,1)S(1)}, u32[]{:S(2)}, u32[]{:S(2)}) collective-permute-start(bf16[4,96,512]{2,1,0:T(8,128)(2,1)S(1)} %bitcast_dynamic-update-slice_fusion.20), channel_id=1, source_target_pairs={{0,28},{1,29},{2,30},{3,31},{4,0},{5,1},{6,2},{7,3},{8,4},{9,5},{1... | collective-permute-start | bytes 1179656 | tf_op jit(solution)/shard_map/ppermute | solution.py:60
  107.6 1.9 collective-permute-start.15
  109.5 5.1 %collective-permute-start.16 = (bf16[96,512]{1,0:T(8,128)(2,1)S(1)}, bf16[96,512]{1,0:T(8,128)(2,1)S(1)}, u32[]{:S(2)}, u32[]{:S(2)}) collective-permute-start(bf16[96,512]{1,0:T(8,128)(2,1)S(1)} %collective-permute-done.14), channel_id=1, source_target_pairs={{0,28},{1,29},{2,30},{3,31},{4,0},{5,1},{6,2},{7,3},{8,4},{9,5},{1... | collective-permute-start | bytes 294920 | tf_op jit(solution)/shard_map/ppermute | solution.py:60
  114.7 2.1 %broadcast_in_dim.100 = bf16[8,4,96,512]{3,2,1,0:T(8,128)(2,1)} broadcast(bf16[]{:T(256)} %constant.138.clone.1), dimensions={} | broadcast | bytes 3145730 | tf_op jit(solution)/shard_map/broadcast_in_dim | solution.py:52
  116.8 0.8 bitcast_dynamic-update-slice_fusion.11
  117.6 1.9 collective-permute-start.17
  119.6 5.7 %collective-permute-done.17 = bf16[96,512]{1,0:T(8,128)(2,1)S(1)} collective-permute-done((bf16[96,512]{1,0:T(8,128)(2,1)S(1)}, bf16[96,512]{1,0:T(8,128)(2,1)S(1)}, u32[]{:S(2)}, u32[]{:S(2)}) %collective-permute-start.17) | collective-permute-done | bytes 98336 | tf_op jit(solution)/shard_map/ppermute | solution.py:57
  125.3 5.5 %collective-permute-start.18 = (bf16[8,96,512]{2,1,0:T(8,128)(2,1)S(1)}, bf16[8,96,512]{2,1,0:T(8,128)(2,1)S(1)}, u32[]{:S(2)}, u32[]{:S(2)}) collective-permute-start(bf16[8,96,512]{2,1,0:T(8,128)(2,1)S(1)} %bitcast_dynamic-update-slice_fusion.12), channel_id=1, source_target_pairs={{0,1},{1,2},{2,3},{3,0},{4,5},{5,6},{6,7},{7,4},{8,9},{9,10},{10,1... | collective-permute-start | bytes 2359304 | tf_op jit(solution)/shard_map/ppermute | solution.py:57
  130.8 1.9 collective-permute-start.19
  132.8 2.0 %broadcast_in_dim.114 = bf16[4,8,96,512]{3,2,0,1:T(8,128)(2,1)} broadcast(bf16[]{:T(256)} %constant.138.clone.1), dimensions={} | broadcast | bytes 3145730 | tf_op jit(solution)/shard_map/broadcast_in_dim | solution.py:52
  134.8 1.0 bitcast_dynamic-update-slice_fusion.2
  135.9 1.9 collective-permute-start.6
  137.8 5.1 %collective-permute-start.7 = (bf16[4,96,512]{2,1,0:T(8,128)(2,1)S(1)}, bf16[4,96,512]{2,1,0:T(8,128)(2,1)S(1)}, u32[]{:S(2)}, u32[]{:S(2)}) collective-permute-start(bf16[4,96,512]{2,1,0:T(8,128)(2,1)S(1)} %collective-permute-done.5), channel_id=1, source_target_pairs={{0,28},{1,29},{2,30},{3,31},{4,0},{5,1},{6,2},{7,3},{8,4},{9,5},{1... | collective-permute-start | bytes 1179656 | tf_op jit(solution)/shard_map/ppermute | solution.py:60
  142.9 0.8 bitcast_dynamic-update-slice_fusion.10
  143.7 0.8 bitcast_dynamic-update-slice_fusion.9
  144.5 2.2 %collective-permute-done.6 = bf16[4,96,512]{2,1,0:T(8,128)(2,1)S(1)} collective-permute-done((bf16[4,96,512]{2,1,0:T(8,128)(2,1)S(1)}, bf16[4,96,512]{2,1,0:T(8,128)(2,1)S(1)}, u32[]{:S(2)}, u32[]{:S(2)}) %collective-permute-start.6) | collective-permute-done | bytes 393248 | tf_op jit(solution)/shard_map/ppermute | solution.py:57
  146.7 1.9 collective-permute-start.8
  148.7 5.3 %collective-permute-start.9 = (bf16[4,96,512]{2,1,0:T(8,128)(2,1)S(1)}, bf16[4,96,512]{2,1,0:T(8,128)(2,1)S(1)}, u32[]{:S(2)}, u32[]{:S(2)}) collective-permute-start(bf16[4,96,512]{2,1,0:T(8,128)(2,1)S(1)} %collective-permute-done.7), channel_id=1, source_target_pairs={{0,28},{1,29},{2,30},{3,31},{4,0},{5,1},{6,2},{7,3},{8,4},{9,5},{1... | collective-permute-start | bytes 1179656 | tf_op jit(solution)/shard_map/ppermute | solution.py:60
  153.9 0.8 bitcast_dynamic-update-slice_fusion.8
  154.7 0.8 bitcast_dynamic-update-slice_fusion.7
  155.5 5.3 %collective-permute-start.20 = (bf16[8,96,512]{2,1,0:T(8,128)(2,1)S(1)}, bf16[8,96,512]{2,1,0:T(8,128)(2,1)S(1)}, u32[]{:S(2)}, u32[]{:S(2)}) collective-permute-start(bf16[8,96,512]{2,1,0:T(8,128)(2,1)S(1)} %collective-permute-done.18), channel_id=1, source_target_pairs={{0,1},{1,2},{2,3},{3,0},{4,5},{5,6},{6,7},{7,4},{8,9},{9,10},{10,1... | collective-permute-start | bytes 2359304 | tf_op jit(solution)/shard_map/ppermute | solution.py:57
  160.9 1.0 bitcast_dynamic-update-slice_fusion.1
  161.9 1.0 bitcast_dynamic-update-slice_fusion
  162.9 1.9 collective-permute-start.10
  164.8 0.8 bitcast_dynamic-update-slice_fusion.6
  165.6 0.8 bitcast_dynamic-update-slice_fusion.5
  166.5 7.3 %collective-permute-done.10 = bf16[4,96,512]{2,1,0:T(8,128)(2,1)S(1)} collective-permute-done((bf16[4,96,512]{2,1,0:T(8,128)(2,1)S(1)}, bf16[4,96,512]{2,1,0:T(8,128)(2,1)S(1)}, u32[]{:S(2)}, u32[]{:S(2)}) %collective-permute-start.10) | collective-permute-done | bytes 393248 | tf_op jit(solution)/shard_map/ppermute | solution.py:57
  173.8 0.8 bitcast_dynamic-update-slice_fusion.4
  174.6 1.0 bitcast_dynamic-update-slice_fusion.3
  175.5 4.8 %fusion.19 = f32[512,512]{0,1:T(8,128)S(1)} fusion(bf16[3072,512]{1,0:T(8,128)(2,1)} %all-gather.4.cloned.1.call-done, bf16[3072,512]{1,0:T(8,128)(2,1)} %bitcast.41), kind=kOutput, calls=%fused_computation.96 | convolution fusion | flops 1610612736 | bytes 7340032 | tf_op jit(solution)/shard_map/dot_general | solution.py:111
  180.4 3.7 %fusion.18 = f32[512,512]{0,1:T(8,128)S(1)} fusion(bf16[3072,512]{1,0:T(8,128)(2,1)S(1)} %copy-done.5, bf16[3072,512]{1,0:T(8,128)(2,1)} %bitcast.24), kind=kOutput, calls=%fused_computation.95 | convolution fusion | flops 1610612736 | bytes 7340032 | tf_op jit(solution)/shard_map/dot_general | solution.py:111
  184.1 0.2 pad_maximum_fusion
  184.3 1.8 copy.15
  (169 shorter events, 2.2 us)
Async XLA Ops:
  6.5 66.2 %copy-start = (bf16[1024,512]{1,0:T(8,128)(2,1)S(1)}, bf16[1024,512]{1,0:T(8,128)(2,1)}, u32[]{:S(2)}) copy-start(bf16[1024,512]{1,0:T(8,128)(2,1)} %param.12) | copy-start | bytes 3145732
  6.5 15.9 %copy-start.2 = (s32[192,512]{1,0:T(8,128)S(1)}, s32[192,512]{1,0:T(8,128)}, u32[]{:S(2)}) copy-start(s32[192,512]{1,0:T(8,128)} %param.8) | copy-start | bytes 1179652
  6.5 15.9 %copy-start.4 = (f32[512]{0:T(512)S(1)}, f32[512]{0:T(512)}, u32[]{:S(2)}) copy-start(f32[512]{0:T(512)} %param.9) | copy-start | bytes 6148
  8.9 35.9 %all-to-all-start = ((f32[32,6,512]{2,1,0:T(8,128)}), f32[32,6,512]{2,1,0:T(8,128)S(1)}, u32[]{:S(2)}, u32[]{:S(2)}) async-start(f32[32,6,512]{2,1,0:T(8,128)} %all_to_all.6), calls=%async_computation | async-start | bytes 1048576 | tf_op jit(solution)/shard_map/all_to_all | solution.py:26
  22.4 153.2 %all-gather.4.cloned.1.call-start = ((), (), s32[]{:S(2)}) async-start(), calls=%async_computation.1 | async-start | bytes 3342336 | tf_op jit(solution)/shard_map/all_gather | solution.py:104
  22.5 1.7 copy-start.1
  24.4 0.7 slice-start
  24.8 20.0 %copy-start.6 = (s32[192]{0:T(256)S(1)}, s32[192]{0:T(256)}, u32[]{:S(2)}) copy-start(s32[192]{0:T(256)} %param.13) | copy-start | bytes 2308
  24.8 47.9 %copy-start.3 = (bf16[96,1024]{1,0:T(8,128)(2,1)S(1)}, bf16[96,1024]{1,0:T(8,128)(2,1)}, u32[]{:S(2)}) copy-start(bf16[96,1024]{1,0:T(8,128)(2,1)} %param.10) | copy-start | bytes 589828
  45.3 11.0 %collective-permute-start = (bf16[6,512]{1,0:T(8,128)(2,1)S(1)}, bf16[6,512]{1,0:T(8,128)(2,1)S(1)}, u32[]{:S(2)}, u32[]{:S(2)}) collective-permute-start(bf16[6,512]{1,0:T(8,128)(2,1)S(1)} %subtract_convert_fusion), channel_id=1, source_target_pairs={{0,0},{1,32},{2,64},{3,96},{4,128},{5,160},{6,192},{7,224},{8,256}... | collective-permute-start | bytes 18440 | tf_op jit(solution)/shard_map/ppermute | solution.py:46
  73.2 13.2 %collective-permute-start.11 = (bf16[96,512]{1,0:T(8,128)(2,1)S(1)}, bf16[96,512]{1,0:T(8,128)(2,1)S(1)}, u32[]{:S(2)}, u32[]{:S(2)}) collective-permute-start(bf16[96,512]{1,0:T(8,128)(2,1)S(1)} %get-tuple-element.131), channel_id=1, source_target_pairs={{0,4},{1,5},{2,6},{3,7},{4,8},{5,9},{6,10},{7,11},{8,12},{9,13},{1... | collective-permute-start | bytes 294920 | tf_op jit(solution)/shard_map/ppermute | solution.py:57
  78.5 11.9 %collective-permute-start.12 = (bf16[96,512]{1,0:T(8,128)(2,1)S(1)}, bf16[96,512]{1,0:T(8,128)(2,1)S(1)}, u32[]{:S(2)}, u32[]{:S(2)}) collective-permute-start(bf16[96,512]{1,0:T(8,128)(2,1)S(1)} %get-tuple-element.131), channel_id=1, source_target_pairs={{0,28},{1,29},{2,30},{3,31},{4,0},{5,1},{6,2},{7,3},{8,4},{9,5},{1... | collective-permute-start | bytes 294920 | tf_op jit(solution)/shard_map/ppermute | solution.py:60
  80.4 13.1 %collective-permute-start.1 = (bf16[96,512]{1,0:T(8,128)(2,1)S(1)}, bf16[96,512]{1,0:T(8,128)(2,1)S(1)}, u32[]{:S(2)}, u32[]{:S(2)}) collective-permute-start(bf16[96,512]{1,0:T(8,128)(2,1)S(1)} %get-tuple-element.130), channel_id=1, source_target_pairs={{0,1},{1,2},{2,3},{3,0},{4,5},{5,6},{6,7},{7,4},{8,9},{9,10},{10,1... | collective-permute-start | bytes 294920 | tf_op jit(solution)/shard_map/ppermute | solution.py:57
  84.0 14.4 %collective-permute-start.2 = (bf16[96,512]{1,0:T(8,128)(2,1)S(1)}, bf16[96,512]{1,0:T(8,128)(2,1)S(1)}, u32[]{:S(2)}, u32[]{:S(2)}) collective-permute-start(bf16[96,512]{1,0:T(8,128)(2,1)S(1)} %get-tuple-element.130), channel_id=1, source_target_pairs={{0,3},{1,0},{2,1},{3,2},{4,7},{5,4},{6,5},{7,6},{8,11},{9,8},{10,9... | collective-permute-start | bytes 294920 | tf_op jit(solution)/shard_map/ppermute | solution.py:60
  86.4 21.2 %collective-permute-start.13 = (bf16[96,512]{1,0:T(8,128)(2,1)S(1)}, bf16[96,512]{1,0:T(8,128)(2,1)S(1)}, u32[]{:S(2)}, u32[]{:S(2)}) collective-permute-start(bf16[96,512]{1,0:T(8,128)(2,1)S(1)} %collective-permute-done.11), channel_id=1, source_target_pairs={{0,4},{1,5},{2,6},{3,7},{4,8},{5,9},{6,10},{7,11},{8,12},{9,13},{1... | collective-permute-start | bytes 294920 | tf_op jit(solution)/shard_map/ppermute | solution.py:57
  90.4 19.2 %collective-permute-start.14 = (bf16[96,512]{1,0:T(8,128)(2,1)S(1)}, bf16[96,512]{1,0:T(8,128)(2,1)S(1)}, u32[]{:S(2)}, u32[]{:S(2)}) collective-permute-start(bf16[96,512]{1,0:T(8,128)(2,1)S(1)} %collective-permute-done.12), channel_id=1, source_target_pairs={{0,28},{1,29},{2,30},{3,31},{4,0},{5,1},{6,2},{7,3},{8,4},{9,5},{1... | collective-permute-start | bytes 294920 | tf_op jit(solution)/shard_map/ppermute | solution.py:60
  93.5 7.0 %collective-permute-start.3 = (bf16[96,512]{1,0:T(8,128)(2,1)S(1)}, bf16[96,512]{1,0:T(8,128)(2,1)S(1)}, u32[]{:S(2)}, u32[]{:S(2)}) collective-permute-start(bf16[96,512]{1,0:T(8,128)(2,1)S(1)} %collective-permute-done.1), channel_id=1, source_target_pairs={{0,1},{1,2},{2,3},{3,0},{4,5},{5,6},{6,7},{7,4},{8,9},{9,10},{10,1... | collective-permute-start | bytes 294920 | tf_op jit(solution)/shard_map/ppermute | solution.py:57
  100.5 35.3 %collective-permute-start.4 = (bf16[4,96,512]{2,1,0:T(8,128)(2,1)S(1)}, bf16[4,96,512]{2,1,0:T(8,128)(2,1)S(1)}, u32[]{:S(2)}, u32[]{:S(2)}) collective-permute-start(bf16[4,96,512]{2,1,0:T(8,128)(2,1)S(1)} %bitcast_dynamic-update-slice_fusion.20), channel_id=1, source_target_pairs={{0,4},{1,5},{2,6},{3,7},{4,8},{5,9},{6,10},{7,11},{8,12},{9,13},{1... | collective-permute-start | bytes 1179656 | tf_op jit(solution)/shard_map/ppermute | solution.py:57
  102.7 35.0 %collective-permute-start.5 = (bf16[4,96,512]{2,1,0:T(8,128)(2,1)S(1)}, bf16[4,96,512]{2,1,0:T(8,128)(2,1)S(1)}, u32[]{:S(2)}, u32[]{:S(2)}) collective-permute-start(bf16[4,96,512]{2,1,0:T(8,128)(2,1)S(1)} %bitcast_dynamic-update-slice_fusion.20), channel_id=1, source_target_pairs={{0,28},{1,29},{2,30},{3,31},{4,0},{5,1},{6,2},{7,3},{8,4},{9,5},{1... | collective-permute-start | bytes 1179656 | tf_op jit(solution)/shard_map/ppermute | solution.py:60
  107.6 10.0 %collective-permute-start.15 = (bf16[96,512]{1,0:T(8,128)(2,1)S(1)}, bf16[96,512]{1,0:T(8,128)(2,1)S(1)}, u32[]{:S(2)}, u32[]{:S(2)}) collective-permute-start(bf16[96,512]{1,0:T(8,128)(2,1)S(1)} %collective-permute-done.13), channel_id=1, source_target_pairs={{0,4},{1,5},{2,6},{3,7},{4,8},{5,9},{6,10},{7,11},{8,12},{9,13},{1... | collective-permute-start | bytes 294920 | tf_op jit(solution)/shard_map/ppermute | solution.py:57
  109.5 10.0 %collective-permute-start.16 = (bf16[96,512]{1,0:T(8,128)(2,1)S(1)}, bf16[96,512]{1,0:T(8,128)(2,1)S(1)}, u32[]{:S(2)}, u32[]{:S(2)}) collective-permute-start(bf16[96,512]{1,0:T(8,128)(2,1)S(1)} %collective-permute-done.14), channel_id=1, source_target_pairs={{0,28},{1,29},{2,30},{3,31},{4,0},{5,1},{6,2},{7,3},{8,4},{9,5},{1... | collective-permute-start | bytes 294920 | tf_op jit(solution)/shard_map/ppermute | solution.py:60
  117.6 7.7 %collective-permute-start.17 = (bf16[96,512]{1,0:T(8,128)(2,1)S(1)}, bf16[96,512]{1,0:T(8,128)(2,1)S(1)}, u32[]{:S(2)}, u32[]{:S(2)}) collective-permute-start(bf16[96,512]{1,0:T(8,128)(2,1)S(1)} %collective-permute-done.15), channel_id=1, source_target_pairs={{0,4},{1,5},{2,6},{3,7},{4,8},{5,9},{6,10},{7,11},{8,12},{9,13},{1... | collective-permute-start | bytes 294920 | tf_op jit(solution)/shard_map/ppermute | solution.py:57
  125.3 30.2 %collective-permute-start.18 = (bf16[8,96,512]{2,1,0:T(8,128)(2,1)S(1)}, bf16[8,96,512]{2,1,0:T(8,128)(2,1)S(1)}, u32[]{:S(2)}, u32[]{:S(2)}) collective-permute-start(bf16[8,96,512]{2,1,0:T(8,128)(2,1)S(1)} %bitcast_dynamic-update-slice_fusion.12), channel_id=1, source_target_pairs={{0,1},{1,2},{2,3},{3,0},{4,5},{5,6},{6,7},{7,4},{8,9},{9,10},{10,1... | collective-permute-start | bytes 2359304 | tf_op jit(solution)/shard_map/ppermute | solution.py:57
  130.8 31.1 %collective-permute-start.19 = (bf16[8,96,512]{2,1,0:T(8,128)(2,1)S(1)}, bf16[8,96,512]{2,1,0:T(8,128)(2,1)S(1)}, u32[]{:S(2)}, u32[]{:S(2)}) collective-permute-start(bf16[8,96,512]{2,1,0:T(8,128)(2,1)S(1)} %bitcast_dynamic-update-slice_fusion.12), channel_id=1, source_target_pairs={{0,3},{1,0},{2,1},{3,2},{4,7},{5,4},{6,5},{7,6},{8,11},{9,8},{10,9... | collective-permute-start | bytes 2359304 | tf_op jit(solution)/shard_map/ppermute | solution.py:60
  135.9 10.9 %collective-permute-start.6 = (bf16[4,96,512]{2,1,0:T(8,128)(2,1)S(1)}, bf16[4,96,512]{2,1,0:T(8,128)(2,1)S(1)}, u32[]{:S(2)}, u32[]{:S(2)}) collective-permute-start(bf16[4,96,512]{2,1,0:T(8,128)(2,1)S(1)} %collective-permute-done.4), channel_id=1, source_target_pairs={{0,4},{1,5},{2,6},{3,7},{4,8},{5,9},{6,10},{7,11},{8,12},{9,13},{1... | collective-permute-start | bytes 1179656 | tf_op jit(solution)/shard_map/ppermute | solution.py:57
  137.8 10.9 %collective-permute-start.7 = (bf16[4,96,512]{2,1,0:T(8,128)(2,1)S(1)}, bf16[4,96,512]{2,1,0:T(8,128)(2,1)S(1)}, u32[]{:S(2)}, u32[]{:S(2)}) collective-permute-start(bf16[4,96,512]{2,1,0:T(8,128)(2,1)S(1)} %collective-permute-done.5), channel_id=1, source_target_pairs={{0,28},{1,29},{2,30},{3,31},{4,0},{5,1},{6,2},{7,3},{8,4},{9,5},{1... | collective-permute-start | bytes 1179656 | tf_op jit(solution)/shard_map/ppermute | solution.py:60
  146.7 16.2 %collective-permute-start.8 = (bf16[4,96,512]{2,1,0:T(8,128)(2,1)S(1)}, bf16[4,96,512]{2,1,0:T(8,128)(2,1)S(1)}, u32[]{:S(2)}, u32[]{:S(2)}) collective-permute-start(bf16[4,96,512]{2,1,0:T(8,128)(2,1)S(1)} %collective-permute-done.6), channel_id=1, source_target_pairs={{0,4},{1,5},{2,6},{3,7},{4,8},{5,9},{6,10},{7,11},{8,12},{9,13},{1... | collective-permute-start | bytes 1179656 | tf_op jit(solution)/shard_map/ppermute | solution.py:57
  148.7 17.0 %collective-permute-start.9 = (bf16[4,96,512]{2,1,0:T(8,128)(2,1)S(1)}, bf16[4,96,512]{2,1,0:T(8,128)(2,1)S(1)}, u32[]{:S(2)}, u32[]{:S(2)}) collective-permute-start(bf16[4,96,512]{2,1,0:T(8,128)(2,1)S(1)} %collective-permute-done.7), channel_id=1, source_target_pairs={{0,28},{1,29},{2,30},{3,31},{4,0},{5,1},{6,2},{7,3},{8,4},{9,5},{1... | collective-permute-start | bytes 1179656 | tf_op jit(solution)/shard_map/ppermute | solution.py:60
  155.5 19.1 %collective-permute-start.20 = (bf16[8,96,512]{2,1,0:T(8,128)(2,1)S(1)}, bf16[8,96,512]{2,1,0:T(8,128)(2,1)S(1)}, u32[]{:S(2)}, u32[]{:S(2)}) collective-permute-start(bf16[8,96,512]{2,1,0:T(8,128)(2,1)S(1)} %collective-permute-done.18), channel_id=1, source_target_pairs={{0,1},{1,2},{2,3},{3,0},{4,5},{5,6},{6,7},{7,4},{8,9},{9,10},{10,1... | collective-permute-start | bytes 2359304 | tf_op jit(solution)/shard_map/ppermute | solution.py:57
  162.9 10.9 %collective-permute-start.10 = (bf16[4,96,512]{2,1,0:T(8,128)(2,1)S(1)}, bf16[4,96,512]{2,1,0:T(8,128)(2,1)S(1)}, u32[]{:S(2)}, u32[]{:S(2)}) collective-permute-start(bf16[4,96,512]{2,1,0:T(8,128)(2,1)S(1)} %collective-permute-done.8), channel_id=1, source_target_pairs={{0,4},{1,5},{2,6},{3,7},{4,8},{5,9},{6,10},{7,11},{8,12},{9,13},{1... | collective-permute-start | bytes 1179656 | tf_op jit(solution)/shard_map/ppermute | solution.py:57
  175.5 4.8 %copy-start.5 = (bf16[3072,512]{1,0:T(8,128)(2,1)S(1)}, bf16[3072,512]{1,0:T(8,128)(2,1)}, u32[]{:S(2)}) copy-start(bf16[3072,512]{1,0:T(8,128)(2,1)} %all-gather.4.cloned.1.call-done) | copy-start | bytes 9437188
Sparse Core Ops, SparseCore 0:
  44.8 41.3 all-gather.3

commit v5 on v1

--- a/solution.py
+++ b/solution.py
@@ -1,7 +1,10 @@
 import jax
 import jax.numpy as jnp
 from jax import lax
-from jax.sharding import PartitionSpec as P
+from jax.sharding import Mesh, PartitionSpec as P
+
+NZ = 8
+PRE = ("z", "x")
 
 
 def combine_pairs(earlier, later):
@@ -14,14 +17,22 @@
     return lax.associative_scan(combine_pairs, (factor, source), axis=0)
 
 
+def pre_size():
+    return lax.axis_size("z") * lax.axis_size("x")
+
+
+def pre_index():
+    return lax.axis_index("z") * lax.axis_size("x") + lax.axis_index("x")
+
+
 def owned_errors(spikes, readout_weight, targets):
-    npre = lax.axis_size("pre")
-    b = lax.axis_index("pre")
+    npre = pre_size()
+    b = pre_index()
     partial_logits = jnp.dot(
         spikes.astype(jnp.bfloat16), readout_weight, preferred_element_type=jnp.float32
     )
     rows = partial_logits.shape[0] // npre
-    pieces = lax.all_to_all(partial_logits, "pre", 0, 0, tiled=True)
+    pieces = lax.all_to_all(partial_logits, PRE, 0, 0, tiled=True)
     logits = pieces.reshape(npre, rows, -1).sum(0)
     class_prob = jax.nn.softmax(logits, axis=-1)
     classes = lax.broadcasted_iota(jnp.int32, logits.shape, 1)
@@ -41,7 +52,7 @@
             dst_b = start // deriv_rows
             dst_a = (start % deriv_rows) // rows
             perm.append((a * npre + b, dst_a * npre + dst_b))
-    moved = lax.ppermute(errors, ("tm", "pre"), perm)
+    moved = lax.ppermute(errors, ("tm",) + PRE, perm)
     assert per == ntm
     return lax.all_gather(moved, "tm", axis=0, tiled=True)
 
@@ -63,9 +74,41 @@
     return out.reshape((count * block.shape[0],) + block.shape[1:])
 
 
+def ring_stage(block, axis, count, fwd, bwd):
+    coord = lax.axis_index(axis)
+    pieces = [None] * count
+    pieces[0] = block
+    f = block
+    r = block
+    for s in range(1, count // 2 + 1):
+        f = lax.ppermute(f, axis, fwd)
+        pieces[count - s] = f
+        if s < count - count // 2:
+            r = lax.ppermute(r, axis, bwd)
+            pieces[s] = r
+    stacked = jnp.stack(pieces + pieces, 0)
+    return lax.dynamic_slice_in_dim(stacked, (count - coord) % count, count, 0)
+
+
+def weighted_gather(weighted):
+    nz = lax.axis_size("z")
+    nx = lax.axis_size("x")
+    half = weighted.shape[1] // 2
+    rows = nz * nx * weighted.shape[0]
+    first = lax.all_gather(weighted[:, :half], "x", axis=0, tiled=True)
+    first = lax.all_gather(first, "z", axis=0, tiled=True)
+    zf = [(i, (i + 1) % nz) for i in range(nz)]
+    zb = [(i, (i - 1) % nz) for i in range(nz)]
+    xf = [(i, (i + 1) % nx) for i in range(nx)]
+    xb = [(i, (i - 1) % nx) for i in range(nx)]
+    second = ring_stage(ring_stage(weighted[:, half:], "z", nz, zf, zb), "x", nx, xf, xb)
+    second = jnp.swapaxes(second, 0, 1)
+    return first, second.reshape(rows, -1)
+
+
 def shards(spikes, trace_decay, pseudo_deriv, readout_weight, feedback_weight, targets):
     ntm = lax.axis_size("tm")
-    npre = lax.axis_size("pre")
+    npre = pre_size()
     a = lax.axis_index("tm")
 
     errors = owned_errors(spikes, readout_weight, targets)
@@ -74,7 +117,7 @@
         err_rows, feedback_weight, (((1,), (1,)), ((), ())), preferred_element_type=jnp.float32
     )
     weighted = (signal * pseudo_deriv.astype(jnp.float32)).astype(jnp.bfloat16)
-    weighted_all = lax.all_gather(weighted, "pre", axis=0, tiled=True)
+    left_all, right_all = weighted_gather(weighted)
 
     powers, states = local_traces(spikes, trace_decay)
     ends = lax.all_gather(states[-1], "tm", axis=0)
@@ -87,13 +130,22 @@
     traces = (states + powers * incoming[None, :]).astype(jnp.bfloat16)
     traces_all = ring_gather(traces, "tm", ntm)
 
+    left = outer_sum(traces_all, left_all)
+    right = outer_sum(traces_all, right_all)
+    return jnp.concatenate([left, right], 1)
+
+
+def outer_sum(left_rows, right_rows):
     return lax.dot_general(
-        traces_all, weighted_all, (((0,), (0,)), ((), ())), preferred_element_type=jnp.float32
+        left_rows, right_rows, (((0,), (0,)), ((), ())), preferred_element_type=jnp.float32
     )
 
 
 def solution(mesh):
-    placed = (P("tm", "pre"), P("pre"), P("pre", "tm"), P("pre", None), P("tm", None), P("tm"))
+    ntm, npre = mesh.devices.shape
+    assert npre % NZ == 0
+    plane = Mesh(mesh.devices.reshape(ntm, NZ, npre // NZ), ("tm",) + PRE)
+    placed = (P("tm", PRE), P(PRE), P(PRE, "tm"), P(PRE, None), P("tm", None), P("tm"))
     return jax.shard_map(
-        shards, mesh=mesh, in_specs=placed, out_specs=P("pre", "tm"), check_vma=False
+        shards, mesh=plane, in_specs=placed, out_specs=P(PRE, "tm"), check_vma=False
     )

time: 177 us -> 227 us (1.28)
  the two profiles are of different devices: /device:TPU:6 before, /device:TPU:16 now
where the time goes in v5:
time: 227 us; the launch traced here: 225 us
  starting transfers between devices  63.5 us (28%)
  waiting for transfers between devices  50.7 us (22%)
  blocking collectives  50.3 us (22%)
  local copies, waits for them, and re-layouts  30.4 us (13%)
  between operations  14.8 us (7%)
  matrix products  10.2 us (4%)
  other arithmetic  4.88 us (2%)
    ppermute x6, waiting for transfers between devices, ring_stage(): f = lax.ppermute(f, axis, fwd)  38.1 us
    ppermute x4, starting transfers between devices, ring_stage(): r = lax.ppermute(r, axis, bwd)  21.2 us
    all_gather x1, blocking collectives, route_errors(): return lax.all_gather(moved, 'tm', axis=0, tiled=True)  18.8 us
    all_gather x1, blocking collectives, shards(): ends = lax.all_gather(states[-1], 'tm', axis=0)  17.3 us
    all_gather x1, blocking collectives, weighted_gather(): first = lax.all_gather(weighted[:, :half], 'x', axis=0, tiled=True)  14.1 us
    ppermute x7, starting transfers between devices, ring_gather(): b = lax.ppermute(b, axis, bwd)  13.4 us
    dynamic_slice x16, local copies, waits for them, and re-layouts, step(): return jnp.where(k < a, span * carry + ends[k], carry)  11.7 us
    ppermute x6, starting transfers between devices, ring_stage(): f = lax.ppermute(f, axis, fwd)  11.5 us
  transfers between devices with their start and end apart: 28, of which 10 were waited for; matrix products, arithmetic and copies ran while one was open for 8% of the time, Pallas kernels for 0%

profile of v5, /device:TPU:16, one launch (start us, length us, event | category | flops | bytes accessed | tf_op | source)
XLA Modules:
  0.0 224.9 jit_solution(6964825766229947155)
XLA Ops:
  6.5 0.8 broadcast_subtract_fusion
  7.3 1.0 convert_multiply_fusion
  8.6 0.7 multiply_add_fusion
  11.6 17.3 %all-gather = f32[16,1,512]{2,1,0:T(1,128)S(1)} all-gather(f32[1,1,512]{2,1,0:T(1,128)S(1)} %add_bitcast_fusion), channel_id=1, replica_groups=mesh['tm'=16,'z'=8,'x'=4] {'tm'}, dimensions={0}, use_global_device_ids=true | all-gather | bytes 34816 | tf_op jit(solution)/shard_map/all_gather | solution.py:123
  29.7 12.1 %while.14 = (s32[]{:T(128)}, f32[512]{0:T(512)S(1)}, s32[]{:T(128)}, f32[512]{0:T(512)S(1)}, f32[16,512]{1,0:T(8,128)}, /*index=5*/s32[]{:T(128)}, s32[]{:T(128)}) while((s32[]{:T(128)}, f32[512]{0:T(512)S(1)}, s32[]{:T(128)}, f32[512]{0:T(512)S(1)}, f32[16,512]{1,0:T(8,128)}, /*index=5*/s32[]{:T(128)}, s32[]{:T(128)}) %tuple.58), condition=%wide.region_1.0_spmd.clone, body=%wide.region_0.0_spmd.clone.sunk | while | flops 2052 | bytes 12389 | solution.py:129
  29.7 0.8 constant_dynamic-slice_fusion.4
  30.5 0.7 constant_dynamic-slice_fusion.4
  31.3 0.7 constant_dynamic-slice_fusion.4
  32.0 0.7 constant_dynamic-slice_fusion.4
  32.8 0.7 constant_dynamic-slice_fusion.4
  33.5 0.7 constant_dynamic-slice_fusion.4
  34.3 0.7 constant_dynamic-slice_fusion.4
  35.0 0.7 constant_dynamic-slice_fusion.4
  35.8 0.7 constant_dynamic-slice_fusion.4
  36.5 0.7 constant_dynamic-slice_fusion.4
  37.3 0.7 constant_dynamic-slice_fusion.4
  38.0 0.7 constant_dynamic-slice_fusion.4
  38.8 0.7 constant_dynamic-slice_fusion.4
  39.5 0.7 constant_dynamic-slice_fusion.4
  40.3 0.7 constant_dynamic-slice_fusion.4
  41.0 0.7 constant_dynamic-slice_fusion.4
  41.8 2.0 broadcast_in_dim.65
  43.8 0.9 bitcast_dynamic-update-slice_fusion.23
  45.0 2.8 %collective-permute-start.1 = (bf16[192,512]{1,0:T(8,128)(2,1)}, bf16[192,512]{1,0:T(8,128)(2,1)S(1)}, u32[]{:S(2)}, u32[]{:S(2)}) collective-permute-start(bf16[192,512]{1,0:T(8,128)(2,1)} %get-tuple-element.131), channel_id=1, source_target_pairs={{0,480},{32,0},{64,32},{96,64},{128,96},{160,128},{192,160},{224,1... | collective-permute-start | bytes 589832 | tf_op jit(solution)/shard_map/ppermute | solution.py:72
  48.1 0.8 all_to_all.6
  49.0 9.8 %all-to-all-start = ((f32[32,6,512]{2,1,0:T(8,128)}), f32[32,6,512]{2,1,0:T(8,128)S(1)}, u32[]{:S(2)}, u32[]{:S(2)}) async-start(f32[32,6,512]{2,1,0:T(8,128)} %all_to_all.6), calls=%async_computation | async-start | bytes 1048576 | tf_op jit(solution)/shard_map/all_to_all | solution.py:35
  59.4 1.7 collective-permute-start.3
  61.7 0.7 bitcast_dynamic-update-slice_fusion.21
  62.4 2.0 collective-permute-done.2
  64.4 1.7 collective-permute-start.5
  67.5 2.0 collective-permute-done.4
  69.5 2.0 collective-permute-start.7
  72.2 4.8 %all-to-all-done = f32[32,6,512]{2,1,0:T(8,128)S(1)} async-done(((f32[32,6,512]{2,1,0:T(8,128)}), f32[32,6,512]{2,1,0:T(8,128)S(1)}, u32[]{:S(2)}, u32[]{:S(2)}) %all-to-all-start) | async-done | bytes 393248 | tf_op jit(solution)/shard_map/all_to_all | solution.py:35
  77.5 7.0 %collective-permute-start.15 = (bf16[6,512]{1,0:T(8,128)(2,1)S(1)}, bf16[6,512]{1,0:T(8,128)(2,1)S(1)}, u32[]{:S(2)}, u32[]{:S(2)}) collective-permute-start(bf16[6,512]{1,0:T(8,128)(2,1)S(1)} %subtract_convert_fusion), channel_id=1, source_target_pairs={{0,0},{1,32},{2,64},{3,96},{4,128},{5,160},{6,192},{7,224},{8,256}... | collective-permute-start | bytes 18440 | tf_op jit(solution)/shard_map/ppermute | solution.py:55
  85.8 18.8 %all-gather.1 = bf16[16,6,512]{2,1,0:T(8,128)(2,1)S(1)} all-gather(bf16[1,6,512]{2,1,0:T(8,128)(2,1)S(1)} %bitcast.112), channel_id=1, replica_groups=mesh['tm'=16,'z'=8,'x'=4] {'tm'}, dimensions={0}, use_global_device_ids=true | all-gather | bytes 104448 | tf_op jit(solution)/shard_map/all_gather | solution.py:57
  105.2 4.9 %collective-permute-start.16 = (bf16[96,512]{1,0:T(8,128)(2,1)S(1)}, bf16[96,512]{1,0:T(8,128)(2,1)S(1)}, u32[]{:S(2)}, u32[]{:S(2)}) collective-permute-start(bf16[96,512]{1,0:T(8,128)(2,1)S(1)} %get-tuple-element.135), channel_id=1, source_target_pairs={{0,28},{4,0},{8,4},{12,8},{16,12},{20,16},{24,20},{28,24},{1,29},{... | collective-permute-start | bytes 294920 | tf_op jit(solution)/shard_map/ppermute | solution.py:87
  110.1 1.9 collective-permute-start.19
  112.0 14.1 %all_gather.14 = bf16[384,512]{1,0:T(8,128)(2,1)} all-gather(bf16[96,512]{1,0:T(8,128)(2,1)S(1)} %get-tuple-element.134), channel_id=1, replica_groups=mesh['tm'=16,'z'=8,'x'=4] {'x'}, dimensions={0}, use_global_device_ids=true | all-gather | bytes 491520 | tf_op jit(solution)/shard_map/all_gather | solution.py:98
  126.3 1.7 collective-permute-start.9
  128.0 0.7 bitcast_dynamic-update-slice_fusion.16
  128.7 0.7 bitcast_dynamic-update-slice_fusion.15
  129.4 5.6 %collective-permute-start.17 = (bf16[96,512]{1,0:T(8,128)(2,1)S(1)}, bf16[96,512]{1,0:T(8,128)(2,1)S(1)}, u32[]{:S(2)}, u32[]{:S(2)}) collective-permute-start(bf16[96,512]{1,0:T(8,128)(2,1)S(1)} %collective-permute-done.16), channel_id=1, source_target_pairs={{0,28},{4,0},{8,4},{12,8},{16,12},{20,16},{24,20},{28,24},{1,29},{... | collective-permute-start | bytes 294920 | tf_op jit(solution)/shard_map/ppermute | solution.py:87
  135.0 1.9 collective-permute-start.20
  137.0 1.2 collective-permute-done.17
  138.1 5.6 %collective-permute-start.18 = (bf16[96,512]{1,0:T(8,128)(2,1)S(1)}, bf16[96,512]{1,0:T(8,128)(2,1)S(1)}, u32[]{:S(2)}, u32[]{:S(2)}) collective-permute-start(bf16[96,512]{1,0:T(8,128)(2,1)S(1)} %collective-permute-done.17), channel_id=1, source_target_pairs={{0,28},{4,0},{8,4},{12,8},{16,12},{20,16},{24,20},{28,24},{1,29},{... | collective-permute-start | bytes 294920 | tf_op jit(solution)/shard_map/ppermute | solution.py:87
  143.7 1.9 collective-permute-start.21
  145.7 1.7 collective-permute-start.11
  147.4 6.7 %collective-permute-done.21 = bf16[96,512]{1,0:T(8,128)(2,1)S(1)} collective-permute-done((bf16[96,512]{1,0:T(8,128)(2,1)S(1)}, bf16[96,512]{1,0:T(8,128)(2,1)S(1)}, u32[]{:S(2)}, u32[]{:S(2)}) %collective-permute-start.21) | collective-permute-done | bytes 98336 | tf_op jit(solution)/shard_map/ppermute | solution.py:84
  154.2 1.9 collective-permute-start.22
  156.1 8.2 %collective-permute-done.22 = bf16[96,512]{1,0:T(8,128)(2,1)S(1)} collective-permute-done((bf16[96,512]{1,0:T(8,128)(2,1)S(1)}, bf16[96,512]{1,0:T(8,128)(2,1)S(1)}, u32[]{:S(2)}, u32[]{:S(2)}) %collective-permute-start.22) | collective-permute-done | bytes 98336 | tf_op jit(solution)/shard_map/ppermute | solution.py:84
  164.7 1.9 collective-permute-start.24
  166.6 0.7 bitcast_dynamic-update-slice_fusion.14
  168.0 5.1 %collective-permute-start.23 = (bf16[8,96,512]{2,1,0:T(8,128)(2,1)S(1)}, bf16[8,96,512]{2,1,0:T(8,128)(2,1)S(1)}, u32[]{:S(2)}, u32[]{:S(2)}) collective-permute-start(bf16[8,96,512]{2,1,0:T(8,128)(2,1)S(1)} %get-tuple-element.129), channel_id=1, source_target_pairs={{0,3},{1,0},{2,1},{3,2},{4,7},{5,4},{6,5},{7,6},{8,11},{9,8},{10,9... | collective-permute-start | bytes 2359304 | tf_op jit(solution)/shard_map/ppermute | solution.py:87
  173.2 1.7 collective-permute-start.13
  175.6 0.7 bitcast_dynamic-update-slice_fusion.11
  176.3 2.0 collective-permute-done.12
  178.3 7.3 %collective-permute-done.24 = bf16[8,96,512]{2,1,0:T(8,128)(2,1)S(1)} collective-permute-done((bf16[8,96,512]{2,1,0:T(8,128)(2,1)S(1)}, bf16[8,96,512]{2,1,0:T(8,128)(2,1)S(1)}, u32[]{:S(2)}, u32[]{:S(2)}) %collective-permute-start.24) | collective-permute-done | bytes 786464 | tf_op jit(solution)/shard_map/ppermute | solution.py:84
  185.6 1.9 collective-permute-start.25
  188.2 0.7 bitcast_dynamic-update-slice_fusion.9
  188.9 0.7 bitcast_dynamic-update-slice_fusion.8
  189.6 15.8 %collective-permute-done.25 = bf16[8,96,512]{2,1,0:T(8,128)(2,1)S(1)} collective-permute-done((bf16[8,96,512]{2,1,0:T(8,128)(2,1)S(1)}, bf16[8,96,512]{2,1,0:T(8,128)(2,1)S(1)}, u32[]{:S(2)}, u32[]{:S(2)}) %collective-permute-start.25) | collective-permute-done | bytes 786464 | tf_op jit(solution)/shard_map/ppermute | solution.py:84
  206.6 4.7 %fusion.19 = f32[512,512]{0,1:T(8,128)} fusion(bf16[3072,512]{1,0:T(8,128)(2,1)} %bitcast.27, bf16[3072,512]{1,0:T(8,128)(2,1)S(1)} %bitcast.98), kind=kOutput, calls=%fused_computation.114 | convolution fusion | flops 1610612736 | bytes 7340032 | tf_op jit(solution)/shard_map/dot_general | solution.py:139
  211.3 4.8 %fusion.18 = f32[512,512]{0,1:T(8,128)S(1)} fusion(bf16[3072,512]{1,0:T(8,128)(2,1)} %bitcast.27, bf16[3072,512]{1,0:T(8,128)(2,1)} %all-gather.4.cloned.1.call-done), kind=kOutput, calls=%fused_computation.113 | convolution fusion | flops 1610612736 | bytes 7340032 | tf_op jit(solution)/shard_map/dot_general | solution.py:139
  216.2 1.8 copy.11
  (197 shorter events, 12.6 us)
Async XLA Ops:
  6.5 98.2 %copy-start = (bf16[1024,512]{1,0:T(8,128)(2,1)S(1)}, bf16[1024,512]{1,0:T(8,128)(2,1)}, u32[]{:S(2)}) copy-start(bf16[1024,512]{1,0:T(8,128)(2,1)} %param.12) | copy-start | bytes 3145732
  8.4 2.4 %copy-start.1 = (f32[192,512]{1,0:T(8,128)}, f32[192,512]{1,0:T(8,128)S(1)}, u32[]{:S(2)}) copy-start(f32[192,512]{1,0:T(8,128)S(1)} %convert_multiply_fusion) | copy-start | bytes 1179652
  10.6 0.7 copy-start.6
  10.8 0.7 slice-start
  29.5 18.3 %copy-start.2 = (s32[192,512]{1,0:T(8,128)S(1)}, s32[192,512]{1,0:T(8,128)}, u32[]{:S(2)}) copy-start(s32[192,512]{1,0:T(8,128)} %param.8) | copy-start | bytes 1179652
  29.7 18.2 %copy-start.4 = (bf16[512,512]{1,0:T(8,128)(2,1)S(1)}, bf16[512,512]{1,0:T(8,128)(2,1)}, u32[]{:S(2)}) copy-start(bf16[512,512]{1,0:T(8,128)(2,1)} %param.11) | copy-start | bytes 1572868
  43.8 15.4 %copy-start.7 = (s32[192]{0:T(256)S(1)}, s32[192]{0:T(256)}, u32[]{:S(2)}) copy-start(s32[192]{0:T(256)} %param.13) | copy-start | bytes 2308
  44.7 14.6 %collective-permute-start = (bf16[192,512]{1,0:T(8,128)(2,1)}, bf16[192,512]{1,0:T(8,128)(2,1)S(1)}, u32[]{:S(2)}, u32[]{:S(2)}) collective-permute-start(bf16[192,512]{1,0:T(8,128)(2,1)} %get-tuple-element.131), channel_id=1, source_target_pairs={{0,32},{32,64},{64,96},{96,128},{128,160},{160,192},{192,224},{224... | collective-permute-start | bytes 589832 | tf_op jit(solution)/shard_map/ppermute | solution.py:69
  45.0 14.3 %collective-permute-start.1 = (bf16[192,512]{1,0:T(8,128)(2,1)}, bf16[192,512]{1,0:T(8,128)(2,1)S(1)}, u32[]{:S(2)}, u32[]{:S(2)}) collective-permute-start(bf16[192,512]{1,0:T(8,128)(2,1)} %get-tuple-element.131), channel_id=1, source_target_pairs={{0,480},{32,0},{64,32},{96,64},{128,96},{160,128},{192,160},{224,1... | collective-permute-start | bytes 589832 | tf_op jit(solution)/shard_map/ppermute | solution.py:72
  48.1 56.6 %copy-start.5 = (bf16[96,1024]{1,0:T(8,128)(2,1)S(1)}, bf16[96,1024]{1,0:T(8,128)(2,1)}, u32[]{:S(2)}) copy-start(bf16[96,1024]{1,0:T(8,128)(2,1)} %param.10) | copy-start | bytes 589828
  49.0 28.1 %all-to-all-start = ((f32[32,6,512]{2,1,0:T(8,128)}), f32[32,6,512]{2,1,0:T(8,128)S(1)}, u32[]{:S(2)}, u32[]{:S(2)}) async-start(f32[32,6,512]{2,1,0:T(8,128)} %all_to_all.6), calls=%async_computation | async-start | bytes 1048576 | tf_op jit(solution)/shard_map/all_to_all | solution.py:35
  58.8 152.5 %all-gather.4.cloned.1.call-start = ((), (), s32[]{:S(2)}) async-start(), calls=%async_computation.1 | async-start | bytes 3538944 | tf_op jit(solution)/shard_map/all_gather | solution.py:99
  59.3 5.1 %collective-permute-start.2 = (bf16[192,512]{1,0:T(8,128)(2,1)S(1)}, bf16[192,512]{1,0:T(8,128)(2,1)S(1)}, u32[]{:S(2)}, u32[]{:S(2)}) collective-permute-start(bf16[192,512]{1,0:T(8,128)(2,1)S(1)} %collective-permute-done), channel_id=1, source_target_pairs={{0,32},{32,64},{64,96},{96,128},{128,160},{160,192},{192,224},{224... | collective-permute-start | bytes 589832 | tf_op jit(solution)/shard_map/ppermute | solution.py:69
  59.4 5.0 %collective-permute-start.3 = (bf16[192,512]{1,0:T(8,128)(2,1)S(1)}, bf16[192,512]{1,0:T(8,128)(2,1)S(1)}, u32[]{:S(2)}, u32[]{:S(2)}) collective-permute-start(bf16[192,512]{1,0:T(8,128)(2,1)S(1)} %collective-permute-done.1), channel_id=1, source_target_pairs={{0,480},{32,0},{64,32},{96,64},{128,96},{160,128},{192,160},{224,1... | collective-permute-start | bytes 589832 | tf_op jit(solution)/shard_map/ppermute | solution.py:72
  64.4 5.1 %collective-permute-start.4 = (bf16[192,512]{1,0:T(8,128)(2,1)S(1)}, bf16[192,512]{1,0:T(8,128)(2,1)S(1)}, u32[]{:S(2)}, u32[]{:S(2)}) collective-permute-start(bf16[192,512]{1,0:T(8,128)(2,1)S(1)} %collective-permute-done.2), channel_id=1, source_target_pairs={{0,32},{32,64},{64,96},{96,128},{128,160},{160,192},{192,224},{224... | collective-permute-start | bytes 589832 | tf_op jit(solution)/shard_map/ppermute | solution.py:69
  64.4 5.1 %collective-permute-start.5 = (bf16[192,512]{1,0:T(8,128)(2,1)S(1)}, bf16[192,512]{1,0:T(8,128)(2,1)S(1)}, u32[]{:S(2)}, u32[]{:S(2)}) collective-permute-start(bf16[192,512]{1,0:T(8,128)(2,1)S(1)} %collective-permute-done.3), channel_id=1, source_target_pairs={{0,480},{32,0},{64,32},{96,64},{128,96},{160,128},{192,160},{224,1... | collective-permute-start | bytes 589832 | tf_op jit(solution)/shard_map/ppermute | solution.py:72
  69.5 56.8 %collective-permute-start.6 = (bf16[192,512]{1,0:T(8,128)(2,1)S(1)}, bf16[192,512]{1,0:T(8,128)(2,1)S(1)}, u32[]{:S(2)}, u32[]{:S(2)}) collective-permute-start(bf16[192,512]{1,0:T(8,128)(2,1)S(1)} %collective-permute-done.4), channel_id=1, source_target_pairs={{0,32},{32,64},{64,96},{96,128},{128,160},{160,192},{192,224},{224... | collective-permute-start | bytes 589832 | tf_op jit(solution)/shard_map/ppermute | solution.py:69
  69.5 56.8 %collective-permute-start.7 = (bf16[192,512]{1,0:T(8,128)(2,1)S(1)}, bf16[192,512]{1,0:T(8,128)(2,1)S(1)}, u32[]{:S(2)}, u32[]{:S(2)}) collective-permute-start(bf16[192,512]{1,0:T(8,128)(2,1)S(1)} %collective-permute-done.5), channel_id=1, source_target_pairs={{0,480},{32,0},{64,32},{96,64},{128,96},{160,128},{192,160},{224,1... | collective-permute-start | bytes 589832 | tf_op jit(solution)/shard_map/ppermute | solution.py:72
  77.5 8.3 %collective-permute-start.15 = (bf16[6,512]{1,0:T(8,128)(2,1)S(1)}, bf16[6,512]{1,0:T(8,128)(2,1)S(1)}, u32[]{:S(2)}, u32[]{:S(2)}) collective-permute-start(bf16[6,512]{1,0:T(8,128)(2,1)S(1)} %subtract_convert_fusion), channel_id=1, source_target_pairs={{0,0},{1,32},{2,64},{3,96},{4,128},{5,160},{6,192},{7,224},{8,256}... | collective-permute-start | bytes 18440 | tf_op jit(solution)/shard_map/ppermute | solution.py:55
  105.2 24.2 %collective-permute-start.16 = (bf16[96,512]{1,0:T(8,128)(2,1)S(1)}, bf16[96,512]{1,0:T(8,128)(2,1)S(1)}, u32[]{:S(2)}, u32[]{:S(2)}) collective-permute-start(bf16[96,512]{1,0:T(8,128)(2,1)S(1)} %get-tuple-element.135), channel_id=1, source_target_pairs={{0,28},{4,0},{8,4},{12,8},{16,12},{20,16},{24,20},{28,24},{1,29},{... | collective-permute-start | bytes 294920 | tf_op jit(solution)/shard_map/ppermute | solution.py:87
  110.1 24.9 %collective-permute-start.19 = (bf16[96,512]{1,0:T(8,128)(2,1)S(1)}, bf16[96,512]{1,0:T(8,128)(2,1)S(1)}, u32[]{:S(2)}, u32[]{:S(2)}) collective-permute-start(bf16[96,512]{1,0:T(8,128)(2,1)S(1)} %get-tuple-element.135), channel_id=1, source_target_pairs={{0,4},{4,8},{8,12},{12,16},{16,20},{20,24},{24,28},{28,0},{1,5},{5... | collective-permute-start | bytes 294920 | tf_op jit(solution)/shard_map/ppermute | solution.py:84
  126.2 19.4 %collective-permute-start.8 = (bf16[192,512]{1,0:T(8,128)(2,1)S(1)}, bf16[192,512]{1,0:T(8,128)(2,1)S(1)}, u32[]{:S(2)}, u32[]{:S(2)}) collective-permute-start(bf16[192,512]{1,0:T(8,128)(2,1)S(1)} %collective-permute-done.6), channel_id=1, source_target_pairs={{0,32},{32,64},{64,96},{96,128},{128,160},{160,192},{192,224},{224... | collective-permute-start | bytes 589832 | tf_op jit(solution)/shard_map/ppermute | solution.py:69
  126.3 19.4 %collective-permute-start.9 = (bf16[192,512]{1,0:T(8,128)(2,1)S(1)}, bf16[192,512]{1,0:T(8,128)(2,1)S(1)}, u32[]{:S(2)}, u32[]{:S(2)}) collective-permute-start(bf16[192,512]{1,0:T(8,128)(2,1)S(1)} %collective-permute-done.7), channel_id=1, source_target_pairs={{0,480},{32,0},{64,32},{96,64},{128,96},{160,128},{192,160},{224,1... | collective-permute-start | bytes 589832 | tf_op jit(solution)/shard_map/ppermute | solution.py:72
  129.4 8.7 %collective-permute-start.17 = (bf16[96,512]{1,0:T(8,128)(2,1)S(1)}, bf16[96,512]{1,0:T(8,128)(2,1)S(1)}, u32[]{:S(2)}, u32[]{:S(2)}) collective-permute-start(bf16[96,512]{1,0:T(8,128)(2,1)S(1)} %collective-permute-done.16), channel_id=1, source_target_pairs={{0,28},{4,0},{8,4},{12,8},{16,12},{20,16},{24,20},{28,24},{1,29},{... | collective-permute-start | bytes 294920 | tf_op jit(solution)/shard_map/ppermute | solution.py:87
  135.0 8.7 %collective-permute-start.20 = (bf16[96,512]{1,0:T(8,128)(2,1)S(1)}, bf16[96,512]{1,0:T(8,128)(2,1)S(1)}, u32[]{:S(2)}, u32[]{:S(2)}) collective-permute-start(bf16[96,512]{1,0:T(8,128)(2,1)S(1)} %collective-permute-done.19), channel_id=1, source_target_pairs={{0,4},{4,8},{8,12},{12,16},{16,20},{20,24},{24,28},{28,0},{1,5},{5... | collective-permute-start | bytes 294920 | tf_op jit(solution)/shard_map/ppermute | solution.py:84
  138.1 18.0 %collective-permute-start.18 = (bf16[96,512]{1,0:T(8,128)(2,1)S(1)}, bf16[96,512]{1,0:T(8,128)(2,1)S(1)}, u32[]{:S(2)}, u32[]{:S(2)}) collective-permute-start(bf16[96,512]{1,0:T(8,128)(2,1)S(1)} %collective-permute-done.17), channel_id=1, source_target_pairs={{0,28},{4,0},{8,4},{12,8},{16,12},{20,16},{24,20},{28,24},{1,29},{... | collective-permute-start | bytes 294920 | tf_op jit(solution)/shard_map/ppermute | solution.py:87
  143.7 10.4 %collective-permute-start.21 = (bf16[96,512]{1,0:T(8,128)(2,1)S(1)}, bf16[96,512]{1,0:T(8,128)(2,1)S(1)}, u32[]{:S(2)}, u32[]{:S(2)}) collective-permute-start(bf16[96,512]{1,0:T(8,128)(2,1)S(1)} %collective-permute-done.20), channel_id=1, source_target_pairs={{0,4},{4,8},{8,12},{12,16},{16,20},{20,24},{24,28},{28,0},{1,5},{5... | collective-permute-start | bytes 294920 | tf_op jit(solution)/shard_map/ppermute | solution.py:84
  145.7 27.5 %collective-permute-start.10 = (bf16[192,512]{1,0:T(8,128)(2,1)S(1)}, bf16[192,512]{1,0:T(8,128)(2,1)S(1)}, u32[]{:S(2)}, u32[]{:S(2)}) collective-permute-start(bf16[192,512]{1,0:T(8,128)(2,1)S(1)} %collective-permute-done.8), channel_id=1, source_target_pairs={{0,32},{32,64},{64,96},{96,128},{128,160},{160,192},{192,224},{224... | collective-permute-start | bytes 589832 | tf_op jit(solution)/shard_map/ppermute | solution.py:69
  145.7 27.5 %collective-permute-start.11 = (bf16[192,512]{1,0:T(8,128)(2,1)S(1)}, bf16[192,512]{1,0:T(8,128)(2,1)S(1)}, u32[]{:S(2)}, u32[]{:S(2)}) collective-permute-start(bf16[192,512]{1,0:T(8,128)(2,1)S(1)} %collective-permute-done.9), channel_id=1, source_target_pairs={{0,480},{32,0},{64,32},{96,64},{128,96},{160,128},{192,160},{224,1... | collective-permute-start | bytes 589832 | tf_op jit(solution)/shard_map/ppermute | solution.py:72
  154.2 10.2 %collective-permute-start.22 = (bf16[96,512]{1,0:T(8,128)(2,1)S(1)}, bf16[96,512]{1,0:T(8,128)(2,1)S(1)}, u32[]{:S(2)}, u32[]{:S(2)}) collective-permute-start(bf16[96,512]{1,0:T(8,128)(2,1)S(1)} %collective-permute-done.21), channel_id=1, source_target_pairs={{0,4},{4,8},{8,12},{12,16},{16,20},{20,24},{24,28},{28,0},{1,5},{5... | collective-permute-start | bytes 294920 | tf_op jit(solution)/shard_map/ppermute | solution.py:84
  164.7 20.9 %collective-permute-start.24 = (bf16[8,96,512]{2,1,0:T(8,128)(2,1)S(1)}, bf16[8,96,512]{2,1,0:T(8,128)(2,1)S(1)}, u32[]{:S(2)}, u32[]{:S(2)}) collective-permute-start(bf16[8,96,512]{2,1,0:T(8,128)(2,1)S(1)} %get-tuple-element.129), channel_id=1, source_target_pairs={{0,1},{1,2},{2,3},{3,0},{4,5},{5,6},{6,7},{7,4},{8,9},{9,10},{10,1... | collective-permute-start | bytes 2359304 | tf_op jit(solution)/shard_map/ppermute | solution.py:84
  168.0 21.5 %collective-permute-start.23 = (bf16[8,96,512]{2,1,0:T(8,128)(2,1)S(1)}, bf16[8,96,512]{2,1,0:T(8,128)(2,1)S(1)}, u32[]{:S(2)}, u32[]{:S(2)}) collective-permute-start(bf16[8,96,512]{2,1,0:T(8,128)(2,1)S(1)} %get-tuple-element.129), channel_id=1, source_target_pairs={{0,3},{1,0},{2,1},{3,2},{4,7},{5,4},{6,5},{7,6},{8,11},{9,8},{10,9... | collective-permute-start | bytes 2359304 | tf_op jit(solution)/shard_map/ppermute | solution.py:87
  173.2 5.1 %collective-permute-start.12 = (bf16[192,512]{1,0:T(8,128)(2,1)S(1)}, bf16[192,512]{1,0:T(8,128)(2,1)S(1)}, u32[]{:S(2)}, u32[]{:S(2)}) collective-permute-start(bf16[192,512]{1,0:T(8,128)(2,1)S(1)} %collective-permute-done.10), channel_id=1, source_target_pairs={{0,32},{32,64},{64,96},{96,128},{128,160},{160,192},{192,224},{224... | collective-permute-start | bytes 589832 | tf_op jit(solution)/shard_map/ppermute | solution.py:69
  173.2 15.0 %collective-permute-start.13 = (bf16[192,512]{1,0:T(8,128)(2,1)S(1)}, bf16[192,512]{1,0:T(8,128)(2,1)S(1)}, u32[]{:S(2)}, u32[]{:S(2)}) collective-permute-start(bf16[192,512]{1,0:T(8,128)(2,1)S(1)} %collective-permute-done.11), channel_id=1, source_target_pairs={{0,480},{32,0},{64,32},{96,64},{128,96},{160,128},{192,160},{224,1... | collective-permute-start | bytes 589832 | tf_op jit(solution)/shard_map/ppermute | solution.py:72
  178.3 10.6 %collective-permute-start.14 = (bf16[192,512]{1,0:T(8,128)(2,1)S(1)}, bf16[192,512]{1,0:T(8,128)(2,1)S(1)}, u32[]{:S(2)}, u32[]{:S(2)}) collective-permute-start(bf16[192,512]{1,0:T(8,128)(2,1)S(1)} %collective-permute-done.12), channel_id=1, source_target_pairs={{0,32},{32,64},{64,96},{96,128},{128,160},{160,192},{192,224},{224... | collective-permute-start | bytes 589832 | tf_op jit(solution)/shard_map/ppermute | solution.py:69
  185.6 19.9 %collective-permute-start.25 = (bf16[8,96,512]{2,1,0:T(8,128)(2,1)S(1)}, bf16[8,96,512]{2,1,0:T(8,128)(2,1)S(1)}, u32[]{:S(2)}, u32[]{:S(2)}) collective-permute-start(bf16[8,96,512]{2,1,0:T(8,128)(2,1)S(1)} %collective-permute-done.24), channel_id=1, source_target_pairs={{0,1},{1,2},{2,3},{3,0},{4,5},{5,6},{6,7},{7,4},{8,9},{9,10},{10,1... | collective-permute-start | bytes 2359304 | tf_op jit(solution)/shard_map/ppermute | solution.py:84
  211.3 4.8 %copy-start.3 = (f32[512,512]{0,1:T(8,128)S(1)}, f32[512,512]{0,1:T(8,128)}, u32[]{:S(2)}) copy-start(f32[512,512]{0,1:T(8,128)} %fusion.19) | copy-start | bytes 3145732
Sparse Core Ops, SparseCore 0:
  126.3 52.9 all-gather.3

commit v6 on v5

--- a/solution.py
+++ b/solution.py
@@ -57,23 +57,6 @@
     return lax.all_gather(moved, "tm", axis=0, tiled=True)
 
 
-def ring_gather(block, axis, count):
-    index = lax.axis_index(axis)
-    fwd = [(i, (i + 1) % count) for i in range(count)]
-    bwd = [(i, (i - 1) % count) for i in range(count)]
-    out = jnp.zeros((count,) + block.shape, block.dtype)
-    out = lax.dynamic_update_slice_in_dim(out, block[None], index, 0)
-    f = block
-    b = block
-    for s in range(1, count // 2 + 1):
-        f = lax.ppermute(f, axis, fwd)
-        out = lax.dynamic_update_slice_in_dim(out, f[None], (index - s) % count, 0)
-        if s < count - count // 2:
-            b = lax.ppermute(b, axis, bwd)
-            out = lax.dynamic_update_slice_in_dim(out, b[None], (index + s) % count, 0)
-    return out.reshape((count * block.shape[0],) + block.shape[1:])
-
-
 def ring_stage(block, axis, count, fwd, bwd):
     coord = lax.axis_index(axis)
     pieces = [None] * count
@@ -95,12 +78,12 @@
     nx = lax.axis_size("x")
     half = weighted.shape[1] // 2
     rows = nz * nx * weighted.shape[0]
-    first = lax.all_gather(weighted[:, :half], "x", axis=0, tiled=True)
-    first = lax.all_gather(first, "z", axis=0, tiled=True)
     zf = [(i, (i + 1) % nz) for i in range(nz)]
     zb = [(i, (i - 1) % nz) for i in range(nz)]
     xf = [(i, (i + 1) % nx) for i in range(nx)]
     xb = [(i, (i - 1) % nx) for i in range(nx)]
+    first = ring_stage(weighted[:, :half], "x", nx, xf, xb)
+    first = lax.all_gather(first.reshape(-1, half), "z", axis=0, tiled=True)
     second = ring_stage(ring_stage(weighted[:, half:], "z", nz, zf, zb), "x", nx, xf, xb)
     second = jnp.swapaxes(second, 0, 1)
     return first, second.reshape(rows, -1)
@@ -128,7 +111,7 @@
 
     incoming = lax.fori_loop(0, ntm, step, jnp.zeros_like(trace_decay))
     traces = (states + powers * incoming[None, :]).astype(jnp.bfloat16)
-    traces_all = ring_gather(traces, "tm", ntm)
+    traces_all = lax.all_gather(traces, "tm", axis=0, tiled=True)
 
     left = outer_sum(traces_all, left_all)
     right = outer_sum(traces_all, right_all)

time: 227 us -> 208 us (0.916)
  the two profiles are of different devices: /device:TPU:16 before, /device:TPU:6 now
where the time goes in v6:
time: 208 us; the launch traced here: 205 us
  waiting for transfers between devices  65.5 us (31%)
  starting transfers between devices  54.6 us (26%)
  blocking collectives  33.7 us (16%)
  local copies, waits for them, and re-layouts  21.1 us (10%)
  between operations  14.6 us (7%)
  matrix products  11.2 us (5%)
  other arithmetic  4.14 us (2%)
    ppermute x8, waiting for transfers between devices, ring_stage(): f = lax.ppermute(f, axis, fwd)  36.8 us
    ppermute x8, starting transfers between devices, ring_stage(): f = lax.ppermute(f, axis, fwd)  23.7 us
    all_gather x1, blocking collectives, shards(): ends = lax.all_gather(states[-1], 'tm', axis=0)  17.7 us
    all_to_all x1, waiting for transfers between devices, owned_errors(): pieces = lax.all_to_all(partial_logits, PRE, 0, 0, tiled=True)  17.2 us
    all_gather x1, blocking collectives, route_errors(): return lax.all_gather(moved, 'tm', axis=0, tiled=True)  16 us
    ppermute x5, starting transfers between devices, ring_stage(): r = lax.ppermute(r, axis, bwd)  15.6 us
    all_to_all x1, starting transfers between devices, owned_errors(): pieces = lax.all_to_all(partial_logits, PRE, 0, 0, tiled=True)  13.4 us
    dynamic_slice x16, local copies, waits for them, and re-layouts, step(): return jnp.where(k < a, span * carry + ends[k], carry)  11.7 us
  transfers between devices with their start and end apart: 17, of which 7 were waited for; matrix products, arithmetic and copies ran while one was open for 5% of the time, Pallas kernels for 0%

profile of v6, /device:TPU:6, one launch (start us, length us, event | category | flops | bytes accessed | tf_op | source)
XLA Modules:
  0.0 205.0 jit_solution(2100665058981949287)
XLA Ops:
  6.5 0.8 broadcast_subtract_fusion
  7.3 1.0 convert_multiply_fusion
  8.4 0.1 slice.198
  8.5 0.1 slice.200
  9.2 0.2 slice.196
  10.3 0.3 slice-done.1
  10.9 0.1 fusion.1
  11.0 0.4 slice-done
  11.5 17.7 %all-gather = f32[16,1,512]{2,1,0:T(1,128)S(1)} all-gather(f32[1,1,512]{2,1,0:T(1,128)S(1)} %add_bitcast_fusion), channel_id=1, replica_groups=mesh['tm'=16,'z'=8,'x'=4] {'tm'}, dimensions={0}, use_global_device_ids=true | all-gather | bytes 34816 | tf_op jit(solution)/shard_map/all_gather | solution.py:106
  29.2 0.6 copy.14
  30.0 12.1 %while.14 = (s32[]{:T(128)}, f32[512]{0:T(512)S(1)}, s32[]{:T(128)}, f32[512]{0:T(512)S(1)}, f32[16,512]{1,0:T(8,128)}, /*index=5*/s32[]{:T(128)}, s32[]{:T(128)}) while((s32[]{:T(128)}, f32[512]{0:T(512)S(1)}, s32[]{:T(128)}, f32[512]{0:T(512)S(1)}, f32[16,512]{1,0:T(8,128)}, /*index=5*/s32[]{:T(128)}, s32[]{:T(128)}) %tuple.62), condition=%wide.region_1.0_spmd.clone, body=%wide.region_0.0_spmd.clone.sunk | while | flops 2052 | bytes 12389 | solution.py:112
  30.0 0.8 constant_dynamic-slice_fusion.5
  30.8 0.7 constant_dynamic-slice_fusion.5
  31.5 0.7 constant_dynamic-slice_fusion.5
  32.3 0.7 constant_dynamic-slice_fusion.5
  33.0 0.7 constant_dynamic-slice_fusion.5
  33.8 0.7 constant_dynamic-slice_fusion.5
  34.5 0.7 constant_dynamic-slice_fusion.5
  35.3 0.7 constant_dynamic-slice_fusion.5
  36.0 0.7 constant_dynamic-slice_fusion.5
  36.8 0.7 constant_dynamic-slice_fusion.5
  37.5 0.7 constant_dynamic-slice_fusion.5
  38.3 0.7 constant_dynamic-slice_fusion.5
  39.1 0.7 constant_dynamic-slice_fusion.5
  39.8 0.7 constant_dynamic-slice_fusion.5
  40.6 0.7 constant_dynamic-slice_fusion.5
  41.3 0.7 constant_dynamic-slice_fusion.5
  42.0 0.9 add_convert_fusion
  43.0 0.3 fusion.2
  43.3 0.8 all_to_all.6
  44.1 13.4 %all-to-all-start = ((f32[32,6,512]{2,1,0:T(8,128)}), f32[32,6,512]{2,1,0:T(8,128)S(1)}, u32[]{:S(2)}, u32[]{:S(2)}) async-start(f32[32,6,512]{2,1,0:T(8,128)} %all_to_all.6), calls=%async_computation | async-start | bytes 1048576 | tf_op jit(solution)/shard_map/all_to_all | solution.py:35
  57.7 17.2 %all-to-all-done = f32[32,6,512]{2,1,0:T(8,128)S(1)} async-done(((f32[32,6,512]{2,1,0:T(8,128)}), f32[32,6,512]{2,1,0:T(8,128)S(1)}, u32[]{:S(2)}, u32[]{:S(2)}) %all-to-all-start) | async-done | bytes 393248 | tf_op jit(solution)/shard_map/all_to_all | solution.py:35
  74.9 0.1 reduce_max.9
  75.0 0.2 fusion.8
  75.3 1.9 collective-permute-start
  77.3 9.3 %collective-permute-done = bf16[6,512]{1,0:T(8,128)(2,1)S(1)} collective-permute-done((bf16[6,512]{1,0:T(8,128)(2,1)S(1)}, bf16[6,512]{1,0:T(8,128)(2,1)S(1)}, u32[]{:S(2)}, u32[]{:S(2)}) %collective-permute-start) | collective-permute-done | bytes 6176 | tf_op jit(solution)/shard_map/ppermute | solution.py:55
  86.5 16.0 %all-gather.1 = bf16[16,6,512]{2,1,0:T(8,128)(2,1)S(1)} all-gather(bf16[1,6,512]{2,1,0:T(8,128)(2,1)S(1)} %bitcast.93), channel_id=1, replica_groups=mesh['tm'=16,'z'=8,'x'=4] {'tm'}, dimensions={0}, use_global_device_ids=true | all-gather | bytes 104448 | tf_op jit(solution)/shard_map/all_gather | solution.py:57
  102.6 0.5 fusion
  103.1 1.9 collective-permute-start.4
  105.0 4.4 %collective-permute-start.7 = (bf16[96,512]{1,0:T(8,128)(2,1)S(1)}, bf16[96,512]{1,0:T(8,128)(2,1)S(1)}, u32[]{:S(2)}, u32[]{:S(2)}) collective-permute-start(bf16[96,512]{1,0:T(8,128)(2,1)S(1)} %get-tuple-element.135), channel_id=1, source_target_pairs={{0,4},{4,8},{8,12},{12,16},{16,20},{20,24},{24,28},{28,0},{1,5},{5... | collective-permute-start | bytes 294920 | tf_op jit(solution)/shard_map/ppermute | solution.py:67
  109.4 1.9 collective-permute-start.1
  111.3 5.1 %collective-permute-start.2 = (bf16[96,512]{1,0:T(8,128)(2,1)S(1)}, bf16[96,512]{1,0:T(8,128)(2,1)S(1)}, u32[]{:S(2)}, u32[]{:S(2)}) collective-permute-start(bf16[96,512]{1,0:T(8,128)(2,1)S(1)} %get-tuple-element.134), channel_id=1, source_target_pairs={{0,1},{1,2},{2,3},{3,0},{4,5},{5,6},{6,7},{7,4},{8,9},{9,10},{10,1... | collective-permute-start | bytes 294920 | tf_op jit(solution)/shard_map/ppermute | solution.py:67
  116.5 2.7 %collective-permute-start.5 = (bf16[96,512]{1,0:T(8,128)(2,1)S(1)}, bf16[96,512]{1,0:T(8,128)(2,1)S(1)}, u32[]{:S(2)}, u32[]{:S(2)}) collective-permute-start(bf16[96,512]{1,0:T(8,128)(2,1)S(1)} %collective-permute-done.4), channel_id=1, source_target_pairs={{0,28},{4,0},{8,4},{12,8},{16,12},{20,16},{24,20},{28,24},{1,29},{... | collective-permute-start | bytes 294920 | tf_op jit(solution)/shard_map/ppermute | solution.py:70
  119.2 3.2 %collective-permute-start.8 = (bf16[96,512]{1,0:T(8,128)(2,1)S(1)}, bf16[96,512]{1,0:T(8,128)(2,1)S(1)}, u32[]{:S(2)}, u32[]{:S(2)}) collective-permute-start(bf16[96,512]{1,0:T(8,128)(2,1)S(1)} %collective-permute-done.7), channel_id=1, source_target_pairs={{0,4},{4,8},{8,12},{12,16},{16,20},{20,24},{24,28},{28,0},{1,5},{5... | collective-permute-start | bytes 294920 | tf_op jit(solution)/shard_map/ppermute | solution.py:67
  122.4 2.4 %collective-permute-start.3 = (bf16[96,512]{1,0:T(8,128)(2,1)S(1)}, bf16[96,512]{1,0:T(8,128)(2,1)S(1)}, u32[]{:S(2)}, u32[]{:S(2)}) collective-permute-start(bf16[96,512]{1,0:T(8,128)(2,1)S(1)} %collective-permute-done.2), channel_id=1, source_target_pairs={{0,1},{1,2},{2,3},{3,0},{4,5},{5,6},{6,7},{7,4},{8,9},{9,10},{10,1... | collective-permute-start | bytes 294920 | tf_op jit(solution)/shard_map/ppermute | solution.py:67
  124.9 5.1 %collective-permute-start.6 = (bf16[96,512]{1,0:T(8,128)(2,1)S(1)}, bf16[96,512]{1,0:T(8,128)(2,1)S(1)}, u32[]{:S(2)}, u32[]{:S(2)}) collective-permute-start(bf16[96,512]{1,0:T(8,128)(2,1)S(1)} %collective-permute-done.5), channel_id=1, source_target_pairs={{0,28},{4,0},{8,4},{12,8},{16,12},{20,16},{24,20},{28,24},{1,29},{... | collective-permute-start | bytes 294920 | tf_op jit(solution)/shard_map/ppermute | solution.py:70
  130.0 1.9 collective-permute-start.9
  132.0 5.7 %collective-permute-done.9 = bf16[96,512]{1,0:T(8,128)(2,1)S(1)} collective-permute-done((bf16[96,512]{1,0:T(8,128)(2,1)S(1)}, bf16[96,512]{1,0:T(8,128)(2,1)S(1)}, u32[]{:S(2)}, u32[]{:S(2)}) %collective-permute-start.9) | collective-permute-done | bytes 98336 | tf_op jit(solution)/shard_map/ppermute | solution.py:67
  137.8 1.9 collective-permute-start.10
  139.7 5.8 %collective-permute-done.10 = bf16[96,512]{1,0:T(8,128)(2,1)S(1)} collective-permute-done((bf16[96,512]{1,0:T(8,128)(2,1)S(1)}, bf16[96,512]{1,0:T(8,128)(2,1)S(1)}, u32[]{:S(2)}, u32[]{:S(2)}) %collective-permute-start.10) | collective-permute-done | bytes 98336 | tf_op jit(solution)/shard_map/ppermute | solution.py:67
  145.6 0.8 constant_dynamic-slice_fusion.2
  146.5 0.2 bitcast_dynamic-update-slice_fusion.6
  146.7 1.9 collective-permute-start.12
  148.6 3.9 %collective-permute-start.11 = (bf16[8,96,512]{2,1,0:T(8,128)(2,1)S(1)}, bf16[8,96,512]{2,1,0:T(8,128)(2,1)S(1)}, u32[]{:S(2)}, u32[]{:S(2)}) collective-permute-start(bf16[8,96,512]{2,1,0:T(8,128)(2,1)S(1)} %get-tuple-element.129), channel_id=1, source_target_pairs={{0,3},{1,0},{2,1},{3,2},{4,7},{5,4},{6,5},{7,6},{8,11},{9,8},{10,9... | collective-permute-start | bytes 2359304 | tf_op jit(solution)/shard_map/ppermute | solution.py:70
  152.6 11.9 %collective-permute-done.12 = bf16[8,96,512]{2,1,0:T(8,128)(2,1)S(1)} collective-permute-done((bf16[8,96,512]{2,1,0:T(8,128)(2,1)S(1)}, bf16[8,96,512]{2,1,0:T(8,128)(2,1)S(1)}, u32[]{:S(2)}, u32[]{:S(2)}) %collective-permute-start.12) | collective-permute-done | bytes 786464 | tf_op jit(solution)/shard_map/ppermute | solution.py:67
  164.4 2.8 %collective-permute-start.13 = (bf16[8,96,512]{2,1,0:T(8,128)(2,1)S(1)}, bf16[8,96,512]{2,1,0:T(8,128)(2,1)S(1)}, u32[]{:S(2)}, u32[]{:S(2)}) collective-permute-start(bf16[8,96,512]{2,1,0:T(8,128)(2,1)S(1)} %collective-permute-done.12), channel_id=1, source_target_pairs={{0,1},{1,2},{2,3},{3,0},{4,5},{5,6},{6,7},{7,4},{8,9},{9,10},{10,1... | collective-permute-start | bytes 2359304 | tf_op jit(solution)/shard_map/ppermute | solution.py:67
  167.3 13.4 %collective-permute-done.13 = bf16[8,96,512]{2,1,0:T(8,128)(2,1)S(1)} collective-permute-done((bf16[8,96,512]{2,1,0:T(8,128)(2,1)S(1)}, bf16[8,96,512]{2,1,0:T(8,128)(2,1)S(1)}, u32[]{:S(2)}, u32[]{:S(2)}) %collective-permute-start.13) | collective-permute-done | bytes 786464 | tf_op jit(solution)/shard_map/ppermute | solution.py:67
  181.1 0.3 dynamic-slice_bitcast_fusion
  181.5 2.0 copy.10
  183.5 5.7 %fusion.19 = f32[512,512]{0,1:T(8,128)} fusion(bf16[3072,512]{1,0:T(8,128)(2,1)} %all-gather.5.cloned.1.call-done, bf16[3072,512]{1,0:T(8,128)(2,1)} %bitcast.78), kind=kOutput, calls=%fused_computation.107 | convolution fusion | flops 1610612736 | bytes 7340032 | tf_op jit(solution)/shard_map/dot_general | solution.py:122
  189.2 2.2 %all-gather.7.cloned.1.call-done = bf16[3072,512]{1,0:T(8,128)(2,1)} async-done(((bf16[384,512]{1,0:T(8,128)(2,1)}), bf16[3072,512]{1,0:T(8,128)(2,1)}) %all-gather.7.cloned.1.call-update) | async-done | bytes 3145744 | tf_op jit(solution)/shard_map/all_gather | solution.py:86
  191.4 4.8 %fusion.18 = f32[512,512]{0,1:T(8,128)S(1)} fusion(bf16[3072,512]{1,0:T(8,128)(2,1)} %all-gather.5.cloned.1.call-done, bf16[3072,512]{1,0:T(8,128)(2,1)} %all-gather.7.cloned.1.call-done), kind=kOutput, calls=%fused_computation.106 | convolution fusion | flops 1610612736 | bytes 7340032 | tf_op jit(solution)/shard_map/dot_general | solution.py:122
  196.2 0.2 pad_maximum_fusion
  196.4 1.8 copy.11
  (168 shorter events, 2.7 us)
Async XLA Ops:
  6.5 96.0 %copy-start = (bf16[1024,512]{1,0:T(8,128)(2,1)S(1)}, bf16[1024,512]{1,0:T(8,128)(2,1)}, u32[]{:S(2)}) copy-start(bf16[1024,512]{1,0:T(8,128)(2,1)} %param.12) | copy-start | bytes 3145732
  6.5 2.1 %copy-start.7 = (f32[512]{0:T(512)S(1)}, f32[512]{0:T(512)}, u32[]{:S(2)}) copy-start(f32[512]{0:T(512)} %param.9) | copy-start | bytes 6148
  6.5 177.0 %all-gather.5.cloned.1.call-start = ((), (), s32[]{:S(2)}) async-start(), calls=%async_computation.1 | async-start | bytes 3342336 | tf_op jit(solution)/shard_map/all_gather | solution.py:114
  8.4 1.1 copy-start.1
  8.7 1.2 copy-start.3
  9.9 0.7 slice-start.1
  10.7 0.7 slice-start
  29.8 13.1 %copy-start.2 = (s32[192,512]{1,0:T(8,128)S(1)}, s32[192,512]{1,0:T(8,128)}, u32[]{:S(2)}) copy-start(s32[192,512]{1,0:T(8,128)} %param.8) | copy-start | bytes 1179652
  29.9 13.0 %copy-start.5 = (bf16[512,512]{1,0:T(8,128)(2,1)S(1)}, bf16[512,512]{1,0:T(8,128)(2,1)}, u32[]{:S(2)}) copy-start(bf16[512,512]{1,0:T(8,128)(2,1)} %param.11) | copy-start | bytes 1572868
  43.0 14.6 %copy-start.8 = (s32[192]{0:T(256)S(1)}, s32[192]{0:T(256)}, u32[]{:S(2)}) copy-start(s32[192]{0:T(256)} %param.13) | copy-start | bytes 2308
  43.2 59.3 %copy-start.6 = (bf16[96,1024]{1,0:T(8,128)(2,1)S(1)}, bf16[96,1024]{1,0:T(8,128)(2,1)}, u32[]{:S(2)}) copy-start(bf16[96,1024]{1,0:T(8,128)(2,1)} %param.10) | copy-start | bytes 589828
  44.1 30.7 %all-to-all-start = ((f32[32,6,512]{2,1,0:T(8,128)}), f32[32,6,512]{2,1,0:T(8,128)S(1)}, u32[]{:S(2)}, u32[]{:S(2)}) async-start(f32[32,6,512]{2,1,0:T(8,128)} %all_to_all.6), calls=%async_computation | async-start | bytes 1048576 | tf_op jit(solution)/shard_map/all_to_all | solution.py:35
  57.5 133.9 %all-gather.7.cloned.1.call-start = ((), (), s32[]{:S(2)}) async-start(), calls=%async_computation.2 | async-start | bytes 3538944 | tf_op jit(solution)/shard_map/all_gather | solution.py:86
  75.3 11.2 %collective-permute-start = (bf16[6,512]{1,0:T(8,128)(2,1)S(1)}, bf16[6,512]{1,0:T(8,128)(2,1)S(1)}, u32[]{:S(2)}, u32[]{:S(2)}) collective-permute-start(bf16[6,512]{1,0:T(8,128)(2,1)S(1)} %subtract_convert_fusion), channel_id=1, source_target_pairs={{0,0},{1,32},{2,64},{3,96},{4,128},{5,160},{6,192},{7,224},{8,256}... | collective-permute-start | bytes 18440 | tf_op jit(solution)/shard_map/ppermute | solution.py:55
  103.1 13.4 %collective-permute-start.4 = (bf16[96,512]{1,0:T(8,128)(2,1)S(1)}, bf16[96,512]{1,0:T(8,128)(2,1)S(1)}, u32[]{:S(2)}, u32[]{:S(2)}) collective-permute-start(bf16[96,512]{1,0:T(8,128)(2,1)S(1)} %get-tuple-element.135), channel_id=1, source_target_pairs={{0,28},{4,0},{8,4},{12,8},{16,12},{20,16},{24,20},{28,24},{1,29},{... | collective-permute-start | bytes 294920 | tf_op jit(solution)/shard_map/ppermute | solution.py:70
  105.0 14.2 %collective-permute-start.7 = (bf16[96,512]{1,0:T(8,128)(2,1)S(1)}, bf16[96,512]{1,0:T(8,128)(2,1)S(1)}, u32[]{:S(2)}, u32[]{:S(2)}) collective-permute-start(bf16[96,512]{1,0:T(8,128)(2,1)S(1)} %get-tuple-element.135), channel_id=1, source_target_pairs={{0,4},{4,8},{8,12},{12,16},{16,20},{20,24},{24,28},{28,0},{1,5},{5... | collective-permute-start | bytes 294920 | tf_op jit(solution)/shard_map/ppermute | solution.py:67
  109.4 15.4 %collective-permute-start.1 = (bf16[96,512]{1,0:T(8,128)(2,1)S(1)}, bf16[96,512]{1,0:T(8,128)(2,1)S(1)}, u32[]{:S(2)}, u32[]{:S(2)}) collective-permute-start(bf16[96,512]{1,0:T(8,128)(2,1)S(1)} %get-tuple-element.134), channel_id=1, source_target_pairs={{0,3},{1,0},{2,1},{3,2},{4,7},{5,4},{6,5},{7,6},{8,11},{9,8},{10,9... | collective-permute-start | bytes 294920 | tf_op jit(solution)/shard_map/ppermute | solution.py:70
  111.3 11.0 %collective-permute-start.2 = (bf16[96,512]{1,0:T(8,128)(2,1)S(1)}, bf16[96,512]{1,0:T(8,128)(2,1)S(1)}, u32[]{:S(2)}, u32[]{:S(2)}) collective-permute-start(bf16[96,512]{1,0:T(8,128)(2,1)S(1)} %get-tuple-element.134), channel_id=1, source_target_pairs={{0,1},{1,2},{2,3},{3,0},{4,5},{5,6},{6,7},{7,4},{8,9},{9,10},{10,1... | collective-permute-start | bytes 294920 | tf_op jit(solution)/shard_map/ppermute | solution.py:67
  116.5 8.4 %collective-permute-start.5 = (bf16[96,512]{1,0:T(8,128)(2,1)S(1)}, bf16[96,512]{1,0:T(8,128)(2,1)S(1)}, u32[]{:S(2)}, u32[]{:S(2)}) collective-permute-start(bf16[96,512]{1,0:T(8,128)(2,1)S(1)} %collective-permute-done.4), channel_id=1, source_target_pairs={{0,28},{4,0},{8,4},{12,8},{16,12},{20,16},{24,20},{28,24},{1,29},{... | collective-permute-start | bytes 294920 | tf_op jit(solution)/shard_map/ppermute | solution.py:70
  119.2 10.8 %collective-permute-start.8 = (bf16[96,512]{1,0:T(8,128)(2,1)S(1)}, bf16[96,512]{1,0:T(8,128)(2,1)S(1)}, u32[]{:S(2)}, u32[]{:S(2)}) collective-permute-start(bf16[96,512]{1,0:T(8,128)(2,1)S(1)} %collective-permute-done.7), channel_id=1, source_target_pairs={{0,4},{4,8},{8,12},{12,16},{16,20},{20,24},{24,28},{28,0},{1,5},{5... | collective-permute-start | bytes 294920 | tf_op jit(solution)/shard_map/ppermute | solution.py:67
  122.4 9.6 %collective-permute-start.3 = (bf16[96,512]{1,0:T(8,128)(2,1)S(1)}, bf16[96,512]{1,0:T(8,128)(2,1)S(1)}, u32[]{:S(2)}, u32[]{:S(2)}) collective-permute-start(bf16[96,512]{1,0:T(8,128)(2,1)S(1)} %collective-permute-done.2), channel_id=1, source_target_pairs={{0,1},{1,2},{2,3},{3,0},{4,5},{5,6},{6,7},{7,4},{8,9},{9,10},{10,1... | collective-permute-start | bytes 294920 | tf_op jit(solution)/shard_map/ppermute | solution.py:67
  124.9 14.8 %collective-permute-start.6 = (bf16[96,512]{1,0:T(8,128)(2,1)S(1)}, bf16[96,512]{1,0:T(8,128)(2,1)S(1)}, u32[]{:S(2)}, u32[]{:S(2)}) collective-permute-start(bf16[96,512]{1,0:T(8,128)(2,1)S(1)} %collective-permute-done.5), channel_id=1, source_target_pairs={{0,28},{4,0},{8,4},{12,8},{16,12},{20,16},{24,20},{28,24},{1,29},{... | collective-permute-start | bytes 294920 | tf_op jit(solution)/shard_map/ppermute | solution.py:70
  130.0 7.7 %collective-permute-start.9 = (bf16[96,512]{1,0:T(8,128)(2,1)S(1)}, bf16[96,512]{1,0:T(8,128)(2,1)S(1)}, u32[]{:S(2)}, u32[]{:S(2)}) collective-permute-start(bf16[96,512]{1,0:T(8,128)(2,1)S(1)} %collective-permute-done.8), channel_id=1, source_target_pairs={{0,4},{4,8},{8,12},{12,16},{16,20},{20,24},{24,28},{28,0},{1,5},{5... | collective-permute-start | bytes 294920 | tf_op jit(solution)/shard_map/ppermute | solution.py:67
  137.8 7.7 %collective-permute-start.10 = (bf16[96,512]{1,0:T(8,128)(2,1)S(1)}, bf16[96,512]{1,0:T(8,128)(2,1)S(1)}, u32[]{:S(2)}, u32[]{:S(2)}) collective-permute-start(bf16[96,512]{1,0:T(8,128)(2,1)S(1)} %collective-permute-done.9), channel_id=1, source_target_pairs={{0,4},{4,8},{8,12},{12,16},{16,20},{20,24},{24,28},{28,0},{1,5},{5... | collective-permute-start | bytes 294920 | tf_op jit(solution)/shard_map/ppermute | solution.py:67
  146.7 17.7 %collective-permute-start.12 = (bf16[8,96,512]{2,1,0:T(8,128)(2,1)S(1)}, bf16[8,96,512]{2,1,0:T(8,128)(2,1)S(1)}, u32[]{:S(2)}, u32[]{:S(2)}) collective-permute-start(bf16[8,96,512]{2,1,0:T(8,128)(2,1)S(1)} %get-tuple-element.129), channel_id=1, source_target_pairs={{0,1},{1,2},{2,3},{3,0},{4,5},{5,6},{6,7},{7,4},{8,9},{9,10},{10,1... | collective-permute-start | bytes 2359304 | tf_op jit(solution)/shard_map/ppermute | solution.py:67
  148.6 18.6 %collective-permute-start.11 = (bf16[8,96,512]{2,1,0:T(8,128)(2,1)S(1)}, bf16[8,96,512]{2,1,0:T(8,128)(2,1)S(1)}, u32[]{:S(2)}, u32[]{:S(2)}) collective-permute-start(bf16[8,96,512]{2,1,0:T(8,128)(2,1)S(1)} %get-tuple-element.129), channel_id=1, source_target_pairs={{0,3},{1,0},{2,1},{3,2},{4,7},{5,4},{6,5},{7,6},{8,11},{9,8},{10,9... | collective-permute-start | bytes 2359304 | tf_op jit(solution)/shard_map/ppermute | solution.py:70
  164.4 16.3 %collective-permute-start.13 = (bf16[8,96,512]{2,1,0:T(8,128)(2,1)S(1)}, bf16[8,96,512]{2,1,0:T(8,128)(2,1)S(1)}, u32[]{:S(2)}, u32[]{:S(2)}) collective-permute-start(bf16[8,96,512]{2,1,0:T(8,128)(2,1)S(1)} %collective-permute-done.12), channel_id=1, source_target_pairs={{0,1},{1,2},{2,3},{3,0},{4,5},{5,6},{6,7},{7,4},{8,9},{9,10},{10,1... | collective-permute-start | bytes 2359304 | tf_op jit(solution)/shard_map/ppermute | solution.py:67
  191.4 4.8 %copy-start.4 = (f32[512,512]{0,1:T(8,128)S(1)}, f32[512,512]{0,1:T(8,128)}, u32[]{:S(2)}) copy-start(f32[512,512]{0,1:T(8,128)} %fusion.19) | copy-start | bytes 3145732
Sparse Core Ops, SparseCore 0:
  43.1 45.3 all-gather.4
  146.5 44.8 all-gather.6

commit v7 on v6

--- a/solution.py
+++ b/solution.py
@@ -25,12 +25,9 @@
     return lax.axis_index("z") * lax.axis_size("x") + lax.axis_index("x")
 
 
-def owned_errors(spikes, readout_weight, targets):
+def owned_errors(partial_logits, targets, spikes):
     npre = pre_size()
     b = pre_index()
-    partial_logits = jnp.dot(
-        spikes.astype(jnp.bfloat16), readout_weight, preferred_element_type=jnp.float32
-    )
     rows = partial_logits.shape[0] // npre
     pieces = lax.all_to_all(partial_logits, PRE, 0, 0, tiled=True)
     logits = pieces.reshape(npre, rows, -1).sum(0)
@@ -38,7 +35,7 @@
     classes = lax.broadcasted_iota(jnp.int32, logits.shape, 1)
     mine = lax.dynamic_slice_in_dim(targets, b * rows, rows, 0)
     onehot = (mine[:, None] == classes).astype(jnp.float32)
-    return (class_prob - onehot).astype(jnp.bfloat16)
+    return (class_prob - onehot).astype(jnp.bfloat16), spikes
 
 
 def route_errors(errors, ntm, npre, deriv_rows):
@@ -77,16 +74,14 @@
     nz = lax.axis_size("z")
     nx = lax.axis_size("x")
     half = weighted.shape[1] // 2
-    rows = nz * nx * weighted.shape[0]
     zf = [(i, (i + 1) % nz) for i in range(nz)]
     zb = [(i, (i - 1) % nz) for i in range(nz)]
     xf = [(i, (i + 1) % nx) for i in range(nx)]
     xb = [(i, (i - 1) % nx) for i in range(nx)]
-    first = ring_stage(weighted[:, :half], "x", nx, xf, xb)
-    first = lax.all_gather(first.reshape(-1, half), "z", axis=0, tiled=True)
-    second = ring_stage(ring_stage(weighted[:, half:], "z", nz, zf, zb), "x", nx, xf, xb)
-    second = jnp.swapaxes(second, 0, 1)
-    return first, second.reshape(rows, -1)
+    group = ring_stage(weighted, "x", nx, xf, xb)
+    first = lax.all_gather(group[..., :half].reshape(-1, half), "z", axis=0, tiled=True)
+    second = ring_stage(group[..., half:], "z", nz, zf, zb)
+    return first, second.reshape(first.shape[0], -1)
 
 
 def shards(spikes, trace_decay, pseudo_deriv, readout_weight, feedback_weight, targets):
@@ -94,7 +89,10 @@
     npre = pre_size()
     a = lax.axis_index("tm")
 
-    errors = owned_errors(spikes, readout_weight, targets)
+    partial_logits = jnp.dot(
+        spikes.astype(jnp.bfloat16), readout_weight, preferred_element_type=jnp.float32
+    )
+    errors, spikes = owned_errors(partial_logits, targets, spikes)
     err_rows = route_errors(errors, ntm, npre, pseudo_deriv.shape[0])
     signal = lax.dot_general(
         err_rows, feedback_weight, (((1,), (1,)), ((), ())), preferred_element_type=jnp.float32
@@ -106,10 +104,9 @@
     ends = lax.all_gather(states[-1], "tm", axis=0)
     span = powers[-1]
 
-    def step(k, carry):
-        return jnp.where(k < a, span * carry + ends[k], carry)
-
-    incoming = lax.fori_loop(0, ntm, step, jnp.zeros_like(trace_decay))
+    incoming = jnp.zeros_like(trace_decay)
+    for k in range(ntm - 1):
+        incoming = jnp.where(k < a, span * incoming + ends[k], incoming)
     traces = (states + powers * incoming[None, :]).astype(jnp.bfloat16)
     traces_all = lax.all_gather(traces, "tm", axis=0, tiled=True)
 

time: 208 us -> 218 us (1.048)
  waiting for transfers between devices: 65.5 us -> 72.3 us
    unnamed x46 -> x36, local copies, waits for them, and re-layouts: 1.44 us -> 13.4 us
    dynamic_slice x16 -> x0, local copies, waits for them, and re-layouts: 11.7 us -> none  [step(): return jnp.where(k < a, span * carry + ends[k], carry)]
    ppermute x5 -> x4, waiting for transfers between devices: 0.01 us -> 9.98 us  [ring_stage(): r = lax.ppermute(r, axis, bwd)]
    dynamic_slice x1, local copies, waits for them, and re-layouts: 0.78 us -> 3.86 us  [ring_stage(): return lax.dynamic_slice_in_dim(stacked, (count - coord) % count, count, 0)]
    ppermute x8 -> x6, starting transfers between devices: 23.7 us -> 21.1 us  [ring_stage(): f = lax.ppermute(f, axis, fwd)]
    transpose x2 -> x0, local copies, waits for them, and re-layouts: 2.35 us -> none  [weighted_gather(): second = jnp.swapaxes(second, 0, 1)]
    all_gather x1, waiting for transfers between devices: 2.23 us -> 0.01 us  [weighted_gather(): lax.all_gather(group[..., :half].reshape(-1, half), 'z', axis=0, tiled=True)]
    ppermute x5 -> x4, starting transfers between devices: 15.6 us -> 16.7 us  [ring_stage(): r = lax.ppermute(r, axis, bwd)]
  transfers between devices with their start and end apart: 17 -> 14, of which waited for: 7 -> 11; matrix products, arithmetic and copies ran while one was open for 5% -> 12% of each run, Pallas kernels for 0% -> 0%
where the time goes in v7:
time: 218 us; the launch traced here: 214 us
  waiting for transfers between devices  72.3 us (33%)
  starting transfers between devices  53.2 us (24%)
  blocking collectives  34 us (16%)
  local copies, waits for them, and re-layouts  23 us (11%)
  between operations  14.3 us (7%)
  matrix products  12.2 us (6%)
  other arithmetic  4.65 us (2%)
    ppermute x6, waiting for transfers between devices, ring_stage(): f = lax.ppermute(f, axis, fwd)  36.1 us
    ppermute x6, starting transfers between devices, ring_stage(): f = lax.ppermute(f, axis, fwd)  21.1 us
    all_gather x1, blocking collectives, shards(): ends = lax.all_gather(states[-1], 'tm', axis=0)  17.7 us
    all_to_all x1, waiting for transfers between devices, owned_errors(): pieces = lax.all_to_all(partial_logits, PRE, 0, 0, tiled=True)  17.2 us
    ppermute x4, starting transfers between devices, ring_stage(): r = lax.ppermute(r, axis, bwd)  16.7 us
    all_gather x1, blocking collectives, route_errors(): return lax.all_gather(moved, 'tm', axis=0, tiled=True)  16.3 us
    all_to_all x1, starting transfers between devices, owned_errors(): pieces = lax.all_to_all(partial_logits, PRE, 0, 0, tiled=True)  13.4 us
    unnamed x36, local copies, waits for them, and re-layouts  13.4 us
  transfers between devices with their start and end apart: 14, of which 11 were waited for; matrix products, arithmetic and copies ran while one was open for 12% of the time, Pallas kernels for 0%

profile of v7, /device:TPU:6, one launch (start us, length us, event | category | flops | bytes accessed | tf_op | source)
XLA Modules:
  0.0 213.7 jit_solution(12846239994933670181)
XLA Ops:
  6.5 0.8 broadcast_subtract_fusion
  7.3 1.0 convert_multiply_fusion
  8.4 0.1 slice.243
  8.5 0.1 slice.245
  8.6 0.7 multiply_add_fusion
  9.9 0.2 slice.241
  11.3 0.1 fusion.1
  11.5 17.7 %all-gather = f32[16,1,512]{2,1,0:T(1,128)S(1)} all-gather(f32[1,1,512]{2,1,0:T(1,128)S(1)} %add_bitcast_fusion), channel_id=1, replica_groups=mesh['tm'=16,'z'=8,'x'=4] {'tm'}, dimensions={0}, use_global_device_ids=true | all-gather | bytes 34816 | tf_op jit(solution)/shard_map/all_gather | solution.py:104
  29.4 0.9 add_convert_fusion
  30.3 1.3 fusion.2
  31.6 0.8 all_to_all.6
  32.5 13.4 %all-to-all-start = ((f32[32,6,512]{2,1,0:T(8,128)}), f32[32,6,512]{2,1,0:T(8,128)S(1)}, u32[]{:S(2)}, u32[]{:S(2)}) async-start(f32[32,6,512]{2,1,0:T(8,128)} %all_to_all.6), calls=%async_computation | async-start | bytes 1048576 | tf_op jit(solution)/shard_map/all_to_all | solution.py:32
  45.9 0.1 dynamic_slice.9
  46.0 17.2 %all-to-all-done = f32[32,6,512]{2,1,0:T(8,128)S(1)} async-done(((f32[32,6,512]{2,1,0:T(8,128)}), f32[32,6,512]{2,1,0:T(8,128)S(1)}, u32[]{:S(2)}, u32[]{:S(2)}) %all-to-all-start) | async-done | bytes 393248 | tf_op jit(solution)/shard_map/all_to_all | solution.py:32
  63.2 0.1 reduce_sum.18
  63.3 0.1 reduce_max.9
  63.4 0.2 fusion.8
  63.6 0.1 subtract_convert_fusion
  63.7 1.9 collective-permute-start
  65.6 9.1 %collective-permute-done = bf16[6,512]{1,0:T(8,128)(2,1)S(1)} collective-permute-done((bf16[6,512]{1,0:T(8,128)(2,1)S(1)}, bf16[6,512]{1,0:T(8,128)(2,1)S(1)}, u32[]{:S(2)}, u32[]{:S(2)}) %collective-permute-start) | collective-permute-done | bytes 6176 | tf_op jit(solution)/shard_map/ppermute | solution.py:52
  74.7 16.3 %all-gather.1 = bf16[16,6,512]{2,1,0:T(8,128)(2,1)S(1)} all-gather(bf16[1,6,512]{2,1,0:T(8,128)(2,1)S(1)} %bitcast.188), channel_id=1, replica_groups=mesh['tm'=16,'z'=8,'x'=4] {'tm'}, dimensions={0}, use_global_device_ids=true | all-gather | bytes 104448 | tf_op jit(solution)/shard_map/all_gather | solution.py:54
  91.1 0.4 bitcast_dynamic-update-slice_fusion.22
  91.5 3.8 %collective-permute-start.2 = (bf16[96,1024]{1,0:T(8,128)(2,1)S(1)}, bf16[96,1024]{1,0:T(8,128)(2,1)S(1)}, u32[]{:S(2)}, u32[]{:S(2)}) collective-permute-start(bf16[96,1024]{1,0:T(8,128)(2,1)S(1)} %get-tuple-element.32), channel_id=1, source_target_pairs={{0,1},{1,2},{2,3},{3,0},{4,5},{5,6},{6,7},{7,4},{8,9},{9,10},{10,1... | collective-permute-start | bytes 589832 | tf_op jit(solution)/shard_map/ppermute | solution.py:64
  95.4 2.0 collective-permute-start.1
  97.4 3.2 %collective-permute-done.2 = bf16[96,1024]{1,0:T(8,128)(2,1)S(1)} collective-permute-done((bf16[96,1024]{1,0:T(8,128)(2,1)S(1)}, bf16[96,1024]{1,0:T(8,128)(2,1)S(1)}, u32[]{:S(2)}, u32[]{:S(2)}) %collective-permute-start.2) | collective-permute-done | bytes 196640 | tf_op jit(solution)/shard_map/ppermute | solution.py:64
  100.6 5.0 %collective-permute-start.3 = (bf16[96,1024]{1,0:T(8,128)(2,1)S(1)}, bf16[96,1024]{1,0:T(8,128)(2,1)S(1)}, u32[]{:S(2)}, u32[]{:S(2)}) collective-permute-start(bf16[96,1024]{1,0:T(8,128)(2,1)S(1)} %collective-permute-done.2), channel_id=1, source_target_pairs={{0,1},{1,2},{2,3},{3,0},{4,5},{5,6},{6,7},{7,4},{8,9},{9,10},{10,1... | collective-permute-start | bytes 589832 | tf_op jit(solution)/shard_map/ppermute | solution.py:64
  105.6 3.8 %collective-permute-done.3 = bf16[96,1024]{1,0:T(8,128)(2,1)S(1)} collective-permute-done((bf16[96,1024]{1,0:T(8,128)(2,1)S(1)}, bf16[96,1024]{1,0:T(8,128)(2,1)S(1)}, u32[]{:S(2)}, u32[]{:S(2)}) %collective-permute-start.3) | collective-permute-done | bytes 196640 | tf_op jit(solution)/shard_map/ppermute | solution.py:64
  109.6 0.9 constant_dynamic-slice_fusion
  110.5 0.4 copy-done.3
  110.8 1.8 bitcast_dynamic-update-slice_fusion.14
  112.7 3.5 %collective-permute-start.7 = (bf16[4,96,512]{2,1,0:T(8,128)(2,1)S(1)}, bf16[4,96,512]{2,1,0:T(8,128)(2,1)S(1)}, u32[]{:S(2)}, u32[]{:S(2)}) collective-permute-start(bf16[4,96,512]{2,1,0:T(8,128)(2,1)S(1)} %get-tuple-element.6), channel_id=1, source_target_pairs={{0,4},{4,8},{8,12},{12,16},{16,20},{20,24},{24,28},{28,0},{1,5},{5... | collective-permute-start | bytes 1179656 | tf_op jit(solution)/shard_map/ppermute | solution.py:64
  116.2 3.5 %collective-permute-start.4 = (bf16[4,96,512]{2,1,0:T(8,128)(2,1)S(1)}, bf16[4,96,512]{2,1,0:T(8,128)(2,1)S(1)}, u32[]{:S(2)}, u32[]{:S(2)}) collective-permute-start(bf16[4,96,512]{2,1,0:T(8,128)(2,1)S(1)} %get-tuple-element.6), channel_id=1, source_target_pairs={{0,28},{4,0},{8,4},{12,8},{16,12},{20,16},{24,20},{28,24},{1,29},{... | collective-permute-start | bytes 1179656 | tf_op jit(solution)/shard_map/ppermute | solution.py:67
  119.7 6.6 %collective-permute-done.7 = bf16[4,96,512]{2,1,0:T(8,128)(2,1)S(1)} collective-permute-done((bf16[4,96,512]{2,1,0:T(8,128)(2,1)S(1)}, bf16[4,96,512]{2,1,0:T(8,128)(2,1)S(1)}, u32[]{:S(2)}, u32[]{:S(2)}) %collective-permute-start.7) | collective-permute-done | bytes 393248 | tf_op jit(solution)/shard_map/ppermute | solution.py:64
  126.3 4.4 %collective-permute-start.8 = (bf16[4,96,512]{2,1,0:T(8,128)(2,1)S(1)}, bf16[4,96,512]{2,1,0:T(8,128)(2,1)S(1)}, u32[]{:S(2)}, u32[]{:S(2)}) collective-permute-start(bf16[4,96,512]{2,1,0:T(8,128)(2,1)S(1)} %collective-permute-done.7), channel_id=1, source_target_pairs={{0,4},{4,8},{8,12},{12,16},{16,20},{20,24},{24,28},{28,0},{1,5},{5... | collective-permute-start | bytes 1179656 | tf_op jit(solution)/shard_map/ppermute | solution.py:64
  130.7 4.0 %collective-permute-done.4 = bf16[4,96,512]{2,1,0:T(8,128)(2,1)S(1)} collective-permute-done((bf16[4,96,512]{2,1,0:T(8,128)(2,1)S(1)}, bf16[4,96,512]{2,1,0:T(8,128)(2,1)S(1)}, u32[]{:S(2)}, u32[]{:S(2)}) %collective-permute-start.4) | collective-permute-done | bytes 393248 | tf_op jit(solution)/shard_map/ppermute | solution.py:67
  134.7 5.6 %collective-permute-start.5 = (bf16[4,96,512]{2,1,0:T(8,128)(2,1)S(1)}, bf16[4,96,512]{2,1,0:T(8,128)(2,1)S(1)}, u32[]{:S(2)}, u32[]{:S(2)}) collective-permute-start(bf16[4,96,512]{2,1,0:T(8,128)(2,1)S(1)} %collective-permute-done.4), channel_id=1, source_target_pairs={{0,28},{4,0},{8,4},{12,8},{16,12},{20,16},{24,20},{28,24},{1,29},{... | collective-permute-start | bytes 1179656 | tf_op jit(solution)/shard_map/ppermute | solution.py:67
  140.3 8.1 %collective-permute-done.8 = bf16[4,96,512]{2,1,0:T(8,128)(2,1)S(1)} collective-permute-done((bf16[4,96,512]{2,1,0:T(8,128)(2,1)S(1)}, bf16[4,96,512]{2,1,0:T(8,128)(2,1)S(1)}, u32[]{:S(2)}, u32[]{:S(2)}) %collective-permute-start.8) | collective-permute-done | bytes 393248 | tf_op jit(solution)/shard_map/ppermute | solution.py:64
  148.4 2.4 %collective-permute-start.9 = (bf16[4,96,512]{2,1,0:T(8,128)(2,1)S(1)}, bf16[4,96,512]{2,1,0:T(8,128)(2,1)S(1)}, u32[]{:S(2)}, u32[]{:S(2)}) collective-permute-start(bf16[4,96,512]{2,1,0:T(8,128)(2,1)S(1)} %collective-permute-done.8), channel_id=1, source_target_pairs={{0,4},{4,8},{8,12},{12,16},{16,20},{20,24},{24,28},{28,0},{1,5},{5... | collective-permute-start | bytes 1179656 | tf_op jit(solution)/shard_map/ppermute | solution.py:64
  150.9 5.1 %collective-permute-done.5 = bf16[4,96,512]{2,1,0:T(8,128)(2,1)S(1)} collective-permute-done((bf16[4,96,512]{2,1,0:T(8,128)(2,1)S(1)}, bf16[4,96,512]{2,1,0:T(8,128)(2,1)S(1)}, u32[]{:S(2)}, u32[]{:S(2)}) %collective-permute-start.5) | collective-permute-done | bytes 393248 | tf_op jit(solution)/shard_map/ppermute | solution.py:67
  156.0 5.6 %collective-permute-start.6 = (bf16[4,96,512]{2,1,0:T(8,128)(2,1)S(1)}, bf16[4,96,512]{2,1,0:T(8,128)(2,1)S(1)}, u32[]{:S(2)}, u32[]{:S(2)}) collective-permute-start(bf16[4,96,512]{2,1,0:T(8,128)(2,1)S(1)} %collective-permute-done.5), channel_id=1, source_target_pairs={{0,28},{4,0},{8,4},{12,8},{16,12},{20,16},{24,20},{28,24},{1,29},{... | collective-permute-start | bytes 1179656 | tf_op jit(solution)/shard_map/ppermute | solution.py:67
  161.6 0.8 bitcast_dynamic-update-slice_fusion.12
  162.4 7.8 %collective-permute-done.9 = bf16[4,96,512]{2,1,0:T(8,128)(2,1)S(1)} collective-permute-done((bf16[4,96,512]{2,1,0:T(8,128)(2,1)S(1)}, bf16[4,96,512]{2,1,0:T(8,128)(2,1)S(1)}, u32[]{:S(2)}, u32[]{:S(2)}) %collective-permute-start.9) | collective-permute-done | bytes 393248 | tf_op jit(solution)/shard_map/ppermute | solution.py:64
  170.2 1.9 collective-permute-start.10
  172.1 0.8 bitcast_dynamic-update-slice_fusion.10
  172.9 0.9 collective-permute-done.6
  173.8 0.8 bitcast_dynamic-update-slice_fusion.8
  174.6 6.5 %collective-permute-done.10 = bf16[4,96,512]{2,1,0:T(8,128)(2,1)S(1)} collective-permute-done((bf16[4,96,512]{2,1,0:T(8,128)(2,1)S(1)}, bf16[4,96,512]{2,1,0:T(8,128)(2,1)S(1)}, u32[]{:S(2)}, u32[]{:S(2)}) %collective-permute-start.10) | collective-permute-done | bytes 393248 | tf_op jit(solution)/shard_map/ppermute | solution.py:64
  181.1 0.8 bitcast_dynamic-update-slice_fusion.6
  181.9 0.8 bitcast_dynamic-update-slice_fusion.4
  182.7 0.8 bitcast_dynamic-update-slice_fusion.2
  183.5 0.8 bitcast_dynamic-update-slice_fusion
  184.3 0.8 bitcast_dynamic-update-slice_fusion.15
  185.0 0.8 bitcast_dynamic-update-slice_fusion.13
  185.8 0.8 bitcast_dynamic-update-slice_fusion.11
  186.6 0.8 bitcast_dynamic-update-slice_fusion.9
  187.4 0.8 bitcast_dynamic-update-slice_fusion.7
  188.2 0.8 bitcast_dynamic-update-slice_fusion.5
  189.0 0.8 bitcast_dynamic-update-slice_fusion.3
  189.8 0.8 bitcast_dynamic-update-slice_fusion.1
  190.6 3.9 %constant_dynamic-slice_fusion.1 = bf16[8,4,96,512]{3,2,1,0:T(8,128)(2,1)} fusion(bf16[16,4,96,512]{3,2,1,0:T(8,128)(2,1)} %bitcast_dynamic-update-slice_fusion.1, s32[]{:T(128)S(6)} %select_n.161), kind=kLoop, calls=%fused_computation.131 | loop fusion | bytes 6291460 | tf_op jit(solution)/shard_map/dynamic_slice | solution.py:70
  194.4 5.6 %fusion.33 = f32[512,512]{0,1:T(8,128)} fusion(bf16[3072,512]{1,0:T(8,128)(2,1)} %all-gather.5.cloned.1.call-done, bf16[3072,512]{1,0:T(8,128)(2,1)} %bitcast.176), kind=kOutput, calls=%fused_computation.140 | convolution fusion | flops 1610612736 | bytes 7340032 | tf_op jit(solution)/shard_map/dot_general | solution.py:119
  200.1 4.8 %fusion.32 = f32[512,512]{0,1:T(8,128)S(1)} fusion(bf16[3072,512]{1,0:T(8,128)(2,1)} %all-gather.5.cloned.1.call-done, bf16[3072,512]{1,0:T(8,128)(2,1)} %all-gather.7.cloned.1.call-done), kind=kOutput, calls=%fused_computation.139 | convolution fusion | flops 1610612736 | bytes 7340032 | tf_op jit(solution)/shard_map/dot_general | solution.py:119
  204.8 0.2 pad_maximum_fusion
  205.0 1.8 copy.9
  (113 shorter events, 1.7 us)
Async XLA Ops:
  6.5 84.5 %copy-start = (bf16[1024,512]{1,0:T(8,128)(2,1)S(1)}, bf16[1024,512]{1,0:T(8,128)(2,1)}, u32[]{:S(2)}) copy-start(bf16[1024,512]{1,0:T(8,128)(2,1)} %param.10) | copy-start | bytes 3145732
  6.5 4.8 %copy-start.5 = (f32[512]{0:T(512)S(1)}, f32[512]{0:T(512)}, u32[]{:S(2)}) copy-start(f32[512]{0:T(512)} %param.7) | copy-start | bytes 6148
  6.5 187.9 %all-gather.5.cloned.1.call-start = ((), (), s32[]{:S(2)}) async-start(), calls=%async_computation.1 | async-start | bytes 3342336 | tf_op jit(solution)/shard_map/all_gather | solution.py:111
  10.6 19.7 %copy-start.1 = (s32[192,512]{1,0:T(8,128)S(1)}, s32[192,512]{1,0:T(8,128)}, u32[]{:S(2)}) copy-start(s32[192,512]{1,0:T(8,128)} %param.6) | copy-start | bytes 1179652
  11.0 35.0 %copy-start.6 = (s32[192]{0:T(256)S(1)}, s32[192]{0:T(256)}, u32[]{:S(2)}) copy-start(s32[192]{0:T(256)} %param.11) | copy-start | bytes 2308
  11.1 80.0 %copy-start.4 = (bf16[96,1024]{1,0:T(8,128)(2,1)S(1)}, bf16[96,1024]{1,0:T(8,128)(2,1)}, u32[]{:S(2)}) copy-start(bf16[96,1024]{1,0:T(8,128)(2,1)} %param.8) | copy-start | bytes 589828
  32.5 30.7 %all-to-all-start = ((f32[32,6,512]{2,1,0:T(8,128)}), f32[32,6,512]{2,1,0:T(8,128)S(1)}, u32[]{:S(2)}, u32[]{:S(2)}) async-start(f32[32,6,512]{2,1,0:T(8,128)} %all_to_all.6), calls=%async_computation | async-start | bytes 1048576 | tf_op jit(solution)/shard_map/all_to_all | solution.py:32
  45.9 154.2 %all-gather.7.cloned.1.call-start = ((), (), s32[]{:S(2)}) async-start(), calls=%async_computation.2 | async-start | bytes 3538944 | tf_op jit(solution)/shard_map/all_gather | solution.py:82
  63.7 11.0 %collective-permute-start = (bf16[6,512]{1,0:T(8,128)(2,1)S(1)}, bf16[6,512]{1,0:T(8,128)(2,1)S(1)}, u32[]{:S(2)}, u32[]{:S(2)}) collective-permute-start(bf16[6,512]{1,0:T(8,128)(2,1)S(1)} %subtract_convert_fusion), channel_id=1, source_target_pairs={{0,0},{1,32},{2,64},{3,96},{4,128},{5,160},{6,192},{7,224},{8,256}... | collective-permute-start | bytes 18440 | tf_op jit(solution)/shard_map/ppermute | solution.py:52
  91.5 9.0 %collective-permute-start.2 = (bf16[96,1024]{1,0:T(8,128)(2,1)S(1)}, bf16[96,1024]{1,0:T(8,128)(2,1)S(1)}, u32[]{:S(2)}, u32[]{:S(2)}) collective-permute-start(bf16[96,1024]{1,0:T(8,128)(2,1)S(1)} %get-tuple-element.32), channel_id=1, source_target_pairs={{0,1},{1,2},{2,3},{3,0},{4,5},{5,6},{6,7},{7,4},{8,9},{9,10},{10,1... | collective-permute-start | bytes 589832 | tf_op jit(solution)/shard_map/ppermute | solution.py:64
  95.4 10.2 %collective-permute-start.1 = (bf16[96,1024]{1,0:T(8,128)(2,1)S(1)}, bf16[96,1024]{1,0:T(8,128)(2,1)S(1)}, u32[]{:S(2)}, u32[]{:S(2)}) collective-permute-start(bf16[96,1024]{1,0:T(8,128)(2,1)S(1)} %get-tuple-element.32), channel_id=1, source_target_pairs={{0,3},{1,0},{2,1},{3,2},{4,7},{5,4},{6,5},{7,6},{8,11},{9,8},{10,9... | collective-permute-start | bytes 589832 | tf_op jit(solution)/shard_map/ppermute | solution.py:67
  100.6 8.9 %collective-permute-start.3 = (bf16[96,1024]{1,0:T(8,128)(2,1)S(1)}, bf16[96,1024]{1,0:T(8,128)(2,1)S(1)}, u32[]{:S(2)}, u32[]{:S(2)}) collective-permute-start(bf16[96,1024]{1,0:T(8,128)(2,1)S(1)} %collective-permute-done.2), channel_id=1, source_target_pairs={{0,1},{1,2},{2,3},{3,0},{4,5},{5,6},{6,7},{7,4},{8,9},{9,10},{10,1... | collective-permute-start | bytes 589832 | tf_op jit(solution)/shard_map/ppermute | solution.py:64
  109.6 1.3 copy-start.3
  112.7 13.7 %collective-permute-start.7 = (bf16[4,96,512]{2,1,0:T(8,128)(2,1)S(1)}, bf16[4,96,512]{2,1,0:T(8,128)(2,1)S(1)}, u32[]{:S(2)}, u32[]{:S(2)}) collective-permute-start(bf16[4,96,512]{2,1,0:T(8,128)(2,1)S(1)} %get-tuple-element.6), channel_id=1, source_target_pairs={{0,4},{4,8},{8,12},{12,16},{16,20},{20,24},{24,28},{28,0},{1,5},{5... | collective-permute-start | bytes 1179656 | tf_op jit(solution)/shard_map/ppermute | solution.py:64
  116.2 18.5 %collective-permute-start.4 = (bf16[4,96,512]{2,1,0:T(8,128)(2,1)S(1)}, bf16[4,96,512]{2,1,0:T(8,128)(2,1)S(1)}, u32[]{:S(2)}, u32[]{:S(2)}) collective-permute-start(bf16[4,96,512]{2,1,0:T(8,128)(2,1)S(1)} %get-tuple-element.6), channel_id=1, source_target_pairs={{0,28},{4,0},{8,4},{12,8},{16,12},{20,16},{24,20},{28,24},{1,29},{... | collective-permute-start | bytes 1179656 | tf_op jit(solution)/shard_map/ppermute | solution.py:67
  126.3 22.1 %collective-permute-start.8 = (bf16[4,96,512]{2,1,0:T(8,128)(2,1)S(1)}, bf16[4,96,512]{2,1,0:T(8,128)(2,1)S(1)}, u32[]{:S(2)}, u32[]{:S(2)}) collective-permute-start(bf16[4,96,512]{2,1,0:T(8,128)(2,1)S(1)} %collective-permute-done.7), channel_id=1, source_target_pairs={{0,4},{4,8},{8,12},{12,16},{16,20},{20,24},{24,28},{28,0},{1,5},{5... | collective-permute-start | bytes 1179656 | tf_op jit(solution)/shard_map/ppermute | solution.py:64
  134.7 21.3 %collective-permute-start.5 = (bf16[4,96,512]{2,1,0:T(8,128)(2,1)S(1)}, bf16[4,96,512]{2,1,0:T(8,128)(2,1)S(1)}, u32[]{:S(2)}, u32[]{:S(2)}) collective-permute-start(bf16[4,96,512]{2,1,0:T(8,128)(2,1)S(1)} %collective-permute-done.4), channel_id=1, source_target_pairs={{0,28},{4,0},{8,4},{12,8},{16,12},{20,16},{24,20},{28,24},{1,29},{... | collective-permute-start | bytes 1179656 | tf_op jit(solution)/shard_map/ppermute | solution.py:67
  148.4 21.8 %collective-permute-start.9 = (bf16[4,96,512]{2,1,0:T(8,128)(2,1)S(1)}, bf16[4,96,512]{2,1,0:T(8,128)(2,1)S(1)}, u32[]{:S(2)}, u32[]{:S(2)}) collective-permute-start(bf16[4,96,512]{2,1,0:T(8,128)(2,1)S(1)} %collective-permute-done.8), channel_id=1, source_target_pairs={{0,4},{4,8},{8,12},{12,16},{16,20},{20,24},{24,28},{28,0},{1,5},{5... | collective-permute-start | bytes 1179656 | tf_op jit(solution)/shard_map/ppermute | solution.py:64
  156.0 17.8 %collective-permute-start.6 = (bf16[4,96,512]{2,1,0:T(8,128)(2,1)S(1)}, bf16[4,96,512]{2,1,0:T(8,128)(2,1)S(1)}, u32[]{:S(2)}, u32[]{:S(2)}) collective-permute-start(bf16[4,96,512]{2,1,0:T(8,128)(2,1)S(1)} %collective-permute-done.5), channel_id=1, source_target_pairs={{0,28},{4,0},{8,4},{12,8},{16,12},{20,16},{24,20},{28,24},{1,29},{... | collective-permute-start | bytes 1179656 | tf_op jit(solution)/shard_map/ppermute | solution.py:67
  170.2 10.9 %collective-permute-start.10 = (bf16[4,96,512]{2,1,0:T(8,128)(2,1)S(1)}, bf16[4,96,512]{2,1,0:T(8,128)(2,1)S(1)}, u32[]{:S(2)}, u32[]{:S(2)}) collective-permute-start(bf16[4,96,512]{2,1,0:T(8,128)(2,1)S(1)} %collective-permute-done.9), channel_id=1, source_target_pairs={{0,4},{4,8},{8,12},{12,16},{16,20},{20,24},{24,28},{28,0},{1,5},{5... | collective-permute-start | bytes 1179656 | tf_op jit(solution)/shard_map/ppermute | solution.py:64
  200.1 4.8 %copy-start.2 = (f32[512,512]{0,1:T(8,128)S(1)}, f32[512,512]{0,1:T(8,128)}, u32[]{:S(2)}) copy-start(f32[512,512]{0,1:T(8,128)} %fusion.33) | copy-start | bytes 3145732
Sparse Core Ops, SparseCore 0:
  30.4 45.3 all-gather.4
  110.6 63.4 all-gather.6

commit v8 on v1

--- a/solution.py
+++ b/solution.py
@@ -30,22 +30,6 @@
     return (class_prob - onehot).astype(jnp.bfloat16)
 
 
-def route_errors(errors, ntm, npre, deriv_rows):
-    rows = errors.shape[0]
-    tstep = rows * npre
-    per = deriv_rows // rows
-    perm = []
-    for a in range(ntm):
-        for b in range(npre):
-            start = tstep * a + rows * b
-            dst_b = start // deriv_rows
-            dst_a = (start % deriv_rows) // rows
-            perm.append((a * npre + b, dst_a * npre + dst_b))
-    moved = lax.ppermute(errors, ("tm", "pre"), perm)
-    assert per == ntm
-    return lax.all_gather(moved, "tm", axis=0, tiled=True)
-
-
 def ring_gather(block, axis, count):
     index = lax.axis_index(axis)
     fwd = [(i, (i + 1) % count) for i in range(count)]
@@ -65,27 +49,27 @@
 
 def shards(spikes, trace_decay, pseudo_deriv, readout_weight, feedback_weight, targets):
     ntm = lax.axis_size("tm")
-    npre = lax.axis_size("pre")
     a = lax.axis_index("tm")
 
+    derivs_all = lax.all_gather(pseudo_deriv, "pre", axis=0, tiled=True)
+
     errors = owned_errors(spikes, readout_weight, targets)
-    err_rows = route_errors(errors, ntm, npre, pseudo_deriv.shape[0])
-    signal = lax.dot_general(
-        err_rows, feedback_weight, (((1,), (1,)), ((), ())), preferred_element_type=jnp.float32
-    )
-    weighted = (signal * pseudo_deriv.astype(jnp.float32)).astype(jnp.bfloat16)
-    weighted_all = lax.all_gather(weighted, "pre", axis=0, tiled=True)
+    errors_block = lax.all_gather(errors, "pre", axis=0, tiled=True)
 
     powers, states = local_traces(spikes, trace_decay)
     ends = lax.all_gather(states[-1], "tm", axis=0)
     span = powers[-1]
+    incoming = jnp.zeros_like(trace_decay)
+    for k in range(ntm - 1):
+        incoming = jnp.where(k < a, span * incoming + ends[k], incoming)
+    traces = (states + powers * incoming[None, :]).astype(jnp.bfloat16)
+    traces_all = lax.all_gather(traces, "tm", axis=0, tiled=True)
 
-    def step(k, carry):
-        return jnp.where(k < a, span * carry + ends[k], carry)
-
-    incoming = lax.fori_loop(0, ntm, step, jnp.zeros_like(trace_decay))
-    traces = (states + powers * incoming[None, :]).astype(jnp.bfloat16)
-    traces_all = ring_gather(traces, "tm", ntm)
+    errors_all = ring_gather(errors_block, "tm", ntm)
+    signal = lax.dot_general(
+        errors_all, feedback_weight, (((1,), (1,)), ((), ())), preferred_element_type=jnp.float32
+    )
+    weighted_all = (signal * derivs_all.astype(jnp.float32)).astype(jnp.bfloat16)
 
     return lax.dot_general(
         traces_all, weighted_all, (((0,), (0,)), ((), ())), preferred_element_type=jnp.float32

time: 177 us -> 193 us (1.090)
  blocking collectives: 35.9 us -> 64.7 us
  waiting for transfers between devices: 58.3 us -> 41.8 us
  matrix products: 11.2 us -> 14 us
  other arithmetic: 2.2 us -> 4.46 us
    all_gather x1, blocking collectives: 18.5 us -> 47 us  [shards(): errors_block = lax.all_gather(errors, 'pre', axis=0, tiled=True)]
    ppermute x1 -> x0, waiting for transfers between devices: 9.04 us -> none  [route_errors(): moved = lax.ppermute(errors, ('tm', 'pre'), perm)]
    all_gather x1 -> x2, waiting for transfers between devices: 14.3 us -> 8.09 us  [the longest x1 8.08 us: shards(): derivs_all = lax.all_gather(pseudo_deriv, 'pre', axis=0, tiled=True)]
    ppermute x8, waiting for transfers between devices: 18.9 us -> 14.5 us  [ring_gather(): f = lax.ppermute(f, axis, fwd)]
    dot_general x1, matrix products: 8.49 us -> 12.7 us  [shards(): lax.dot_general(traces_all, weighted_all, (((0,), (0,)), ((), ())), prefe...]
  transfers between devices with their start and end apart: 18 -> 18, of which waited for: 12 -> 13; matrix products, arithmetic and copies ran while one was open for 9% -> 8% of each run, Pallas kernels for 0% -> 0%
where the time goes in v8:
time: 193 us; the launch traced here: 190 us
  blocking collectives  64.7 us (34%)
  waiting for transfers between devices  41.8 us (22%)
  starting transfers between devices  35.7 us (18%)
  local copies, waits for them, and re-layouts  15.6 us (8%)
  between operations  14.1 us (7%)
  matrix products  14 us (7%)
  other arithmetic  4.46 us (2%)
    all_gather x1, blocking collectives, shards(): errors_block = lax.all_gather(errors, 'pre', axis=0, tiled=True)  47 us
    ppermute x7, starting transfers between devices, ring_gather(): b = lax.ppermute(b, axis, bwd)  22.2 us
    all_gather x1, blocking collectives, shards(): ends = lax.all_gather(states[-1], 'tm', axis=0)  17.7 us
    all_to_all x1, waiting for transfers between devices, owned_errors(): pieces = lax.all_to_all(partial_logits, 'pre', 0, 0, tiled=True)  17.2 us
    ppermute x8, waiting for transfers between devices, ring_gather(): f = lax.ppermute(f, axis, fwd)  14.5 us
    all_to_all x1, starting transfers between devices, owned_errors(): pieces = lax.all_to_all(partial_logits, 'pre', 0, 0, tiled=True)  13.4 us
    dot_general x1, matrix products, shards(): lax.dot_general(traces_all, weighted_all, (((0,), (0,)), ((), ())), prefe...  12.7 us
    all_gather x1, waiting for transfers between devices, shards(): derivs_all = lax.all_gather(pseudo_deriv, 'pre', axis=0, tiled=True)  8.08 us
  transfers between devices with their start and end apart: 18, of which 13 were waited for; matrix products, arithmetic and copies ran while one was open for 8% of the time, Pallas kernels for 0%

profile of v8, /device:TPU:6, one launch (start us, length us, event | category | flops | bytes accessed | tf_op | source)
XLA Modules:
  0.0 190.3 jit_solution(12329392079901022787)
XLA Ops:
  6.5 0.8 broadcast_subtract_fusion
  7.3 1.0 convert_multiply_fusion
  8.4 0.1 slice.237
  8.5 0.1 slice.239
  8.6 0.7 multiply_add_fusion
  9.9 0.2 slice.235
  11.1 0.1 pad.99
  11.3 0.1 fusion.1
  11.4 0.1 slice-done
  11.5 0.1 pad.98
  11.6 17.7 %all-gather = f32[16,1,512]{2,1,0:T(1,128)S(1)} all-gather(f32[1,1,512]{2,1,0:T(1,128)S(1)} %add_bitcast_fusion), channel_id=1, replica_groups=mesh['tm'=16,'pre'=32] {'tm'}, dimensions={0}, use_global_device_ids=true | all-gather | bytes 34816 | tf_op jit(solution)/shard_map/all_gather | solution.py:60
  29.3 0.1 pad.113
  29.4 0.1 pad.112
  29.5 0.9 add_convert_fusion
  30.4 0.7 all-gather.7.cloned.1.call-update
  31.2 1.3 fusion.2
  32.5 0.8 all_to_all.6
  33.3 13.4 %all-to-all-start = ((f32[32,6,512]{2,1,0:T(8,128)}), f32[32,6,512]{2,1,0:T(8,128)S(1)}, u32[]{:S(2)}, u32[]{:S(2)}) async-start(f32[32,6,512]{2,1,0:T(8,128)} %all_to_all.6), calls=%async_computation | async-start | bytes 1048576 | tf_op jit(solution)/shard_map/all_to_all | solution.py:24
  46.7 0.1 dynamic_slice.3
  46.8 17.2 %all-to-all-done = f32[32,6,512]{2,1,0:T(8,128)S(1)} async-done(((f32[32,6,512]{2,1,0:T(8,128)}), f32[32,6,512]{2,1,0:T(8,128)S(1)}, u32[]{:S(2)}, u32[]{:S(2)}) %all-to-all-start) | async-done | bytes 393248 | tf_op jit(solution)/shard_map/all_to_all | solution.py:24
  64.1 0.1 reduce_sum.18
  64.1 0.1 reduce_max.9
  64.2 0.2 fusion.8
  64.4 0.1 fusion.9
  64.5 47.0 %all-gather.1 = bf16[32,6,512]{2,1,0:T(8,128)(2,1)S(1)} all-gather(bf16[1,6,512]{2,1,0:T(8,128)(2,1)S(1)} %fusion.9), channel_id=1, replica_groups=mesh['tm'=16,'pre'=32] {'pre'}, dimensions={0}, use_global_device_ids=true | all-gather | bytes 202752 | tf_op jit(solution)/shard_map/all_gather | solution.py:57
  111.5 0.1 reshape.37
  111.6 2.9 %collective-permute-start.1 = (bf16[192,512]{1,0:T(8,128)(2,1)S(1)}, bf16[192,512]{1,0:T(8,128)(2,1)S(1)}, u32[]{:S(2)}, u32[]{:S(2)}) collective-permute-start(bf16[192,512]{1,0:T(8,128)(2,1)S(1)} %reshape.37), channel_id=1, source_target_pairs={{0,480},{32,0},{64,32},{96,64},{128,96},{160,128},{192,160},{224,1... | collective-permute-start | bytes 589832 | tf_op jit(solution)/shard_map/ppermute | solution.py:45
  114.6 0.1 broadcast_in_dim.68
  114.6 2.0 %broadcast_in_dim.67 = bf16[16,192,512]{2,1,0:T(8,128)(2,1)} broadcast(bf16[]{:T(256)} %constant.121.clone.1), dimensions={} | broadcast | bytes 3145730 | tf_op jit(solution)/shard_map/broadcast_in_dim | solution.py:37
  116.6 0.7 constant_dynamic-update-slice_fusion
  117.3 0.6 collective-permute-done
  117.9 3.0 %collective-permute-start.3 = (bf16[192,512]{1,0:T(8,128)(2,1)S(1)}, bf16[192,512]{1,0:T(8,128)(2,1)S(1)}, u32[]{:S(2)}, u32[]{:S(2)}) collective-permute-start(bf16[192,512]{1,0:T(8,128)(2,1)S(1)} %collective-permute-done.1), channel_id=1, source_target_pairs={{0,480},{32,0},{64,32},{96,64},{128,96},{160,128},{192,160},{224,1... | collective-permute-start | bytes 589832 | tf_op jit(solution)/shard_map/ppermute | solution.py:45
  120.9 0.7 bitcast_dynamic-update-slice_fusion.14
  121.6 0.7 bitcast_dynamic-update-slice_fusion.13
  122.3 2.0 %collective-permute-done.2 = bf16[192,512]{1,0:T(8,128)(2,1)S(1)} collective-permute-done((bf16[192,512]{1,0:T(8,128)(2,1)S(1)}, bf16[192,512]{1,0:T(8,128)(2,1)S(1)}, u32[]{:S(2)}, u32[]{:S(2)}) %collective-permute-start.2) | collective-permute-done | bytes 196640 | tf_op jit(solution)/shard_map/ppermute | solution.py:42
  124.2 3.0 %collective-permute-start.5 = (bf16[192,512]{1,0:T(8,128)(2,1)S(1)}, bf16[192,512]{1,0:T(8,128)(2,1)S(1)}, u32[]{:S(2)}, u32[]{:S(2)}) collective-permute-start(bf16[192,512]{1,0:T(8,128)(2,1)S(1)} %collective-permute-done.3), channel_id=1, source_target_pairs={{0,480},{32,0},{64,32},{96,64},{128,96},{160,128},{192,160},{224,1... | collective-permute-start | bytes 589832 | tf_op jit(solution)/shard_map/ppermute | solution.py:45
  127.2 0.7 bitcast_dynamic-update-slice_fusion.12
  127.9 0.7 bitcast_dynamic-update-slice_fusion.11
  128.5 2.0 %collective-permute-done.4 = bf16[192,512]{1,0:T(8,128)(2,1)S(1)} collective-permute-done((bf16[192,512]{1,0:T(8,128)(2,1)S(1)}, bf16[192,512]{1,0:T(8,128)(2,1)S(1)}, u32[]{:S(2)}, u32[]{:S(2)}) %collective-permute-start.4) | collective-permute-done | bytes 196640 | tf_op jit(solution)/shard_map/ppermute | solution.py:42
  130.5 3.0 %collective-permute-start.7 = (bf16[192,512]{1,0:T(8,128)(2,1)S(1)}, bf16[192,512]{1,0:T(8,128)(2,1)S(1)}, u32[]{:S(2)}, u32[]{:S(2)}) collective-permute-start(bf16[192,512]{1,0:T(8,128)(2,1)S(1)} %collective-permute-done.5), channel_id=1, source_target_pairs={{0,480},{32,0},{64,32},{96,64},{128,96},{160,128},{192,160},{224,1... | collective-permute-start | bytes 589832 | tf_op jit(solution)/shard_map/ppermute | solution.py:45
  133.5 0.7 bitcast_dynamic-update-slice_fusion.10
  134.2 0.7 bitcast_dynamic-update-slice_fusion.9
  134.9 1.9 %collective-permute-done.6 = bf16[192,512]{1,0:T(8,128)(2,1)S(1)} collective-permute-done((bf16[192,512]{1,0:T(8,128)(2,1)S(1)}, bf16[192,512]{1,0:T(8,128)(2,1)S(1)}, u32[]{:S(2)}, u32[]{:S(2)}) %collective-permute-start.6) | collective-permute-done | bytes 196640 | tf_op jit(solution)/shard_map/ppermute | solution.py:42
  136.8 3.4 %collective-permute-start.9 = (bf16[192,512]{1,0:T(8,128)(2,1)S(1)}, bf16[192,512]{1,0:T(8,128)(2,1)S(1)}, u32[]{:S(2)}, u32[]{:S(2)}) collective-permute-start(bf16[192,512]{1,0:T(8,128)(2,1)S(1)} %collective-permute-done.7), channel_id=1, source_target_pairs={{0,480},{32,0},{64,32},{96,64},{128,96},{160,128},{192,160},{224,1... | collective-permute-start | bytes 589832 | tf_op jit(solution)/shard_map/ppermute | solution.py:45
  140.2 0.7 bitcast_dynamic-update-slice_fusion.8
  140.9 0.7 bitcast_dynamic-update-slice_fusion.7
  141.6 1.5 collective-permute-done.8
  143.1 0.2 collective-permute-done.9
  143.4 3.5 %collective-permute-start.11 = (bf16[192,512]{1,0:T(8,128)(2,1)S(1)}, bf16[192,512]{1,0:T(8,128)(2,1)S(1)}, u32[]{:S(2)}, u32[]{:S(2)}) collective-permute-start(bf16[192,512]{1,0:T(8,128)(2,1)S(1)} %collective-permute-done.9), channel_id=1, source_target_pairs={{0,480},{32,0},{64,32},{96,64},{128,96},{160,128},{192,160},{224,1... | collective-permute-start | bytes 589832 | tf_op jit(solution)/shard_map/ppermute | solution.py:45
  146.9 0.7 bitcast_dynamic-update-slice_fusion.6
  147.6 0.7 bitcast_dynamic-update-slice_fusion.5
  148.3 1.2 collective-permute-done.10
  149.4 0.6 collective-permute-done.11
  150.1 3.5 %collective-permute-start.13 = (bf16[192,512]{1,0:T(8,128)(2,1)S(1)}, bf16[192,512]{1,0:T(8,128)(2,1)S(1)}, u32[]{:S(2)}, u32[]{:S(2)}) collective-permute-start(bf16[192,512]{1,0:T(8,128)(2,1)S(1)} %collective-permute-done.11), channel_id=1, source_target_pairs={{0,480},{32,0},{64,32},{96,64},{128,96},{160,128},{192,160},{224,1... | collective-permute-start | bytes 589832 | tf_op jit(solution)/shard_map/ppermute | solution.py:45
  153.6 0.7 bitcast_dynamic-update-slice_fusion.4
  154.3 0.7 bitcast_dynamic-update-slice_fusion.3
  155.0 0.7 collective-permute-done.12
  155.8 0.7 bitcast_dynamic-update-slice_fusion.2
  156.4 0.4 collective-permute-done.13
  156.8 0.7 bitcast_dynamic-update-slice_fusion.1
  157.5 4.6 %collective-permute-done.14 = bf16[192,512]{1,0:T(8,128)(2,1)S(1)} collective-permute-done((bf16[192,512]{1,0:T(8,128)(2,1)S(1)}, bf16[192,512]{1,0:T(8,128)(2,1)S(1)}, u32[]{:S(2)}, u32[]{:S(2)}) %collective-permute-start.14) | collective-permute-done | bytes 196640 | tf_op jit(solution)/shard_map/ppermute | solution.py:42
  162.1 0.7 bitcast_dynamic-update-slice_fusion
  162.7 8.1 %all-gather.7.cloned.1.call-done = bf16[3072,1024]{1,0:T(8,128)(2,1)} async-done(((bf16[96,1024]{1,0:T(8,128)(2,1)}), bf16[3072,1024]{1,0:T(8,128)(2,1)}) %all-gather.7.cloned.1.call-update) | async-done | bytes 6291472 | tf_op jit(solution)/shard_map/all_gather | solution.py:54
  170.8 12.7 %fusion = f32[512,1024]{1,0:T(8,128)} fusion(bf16[3072,512]{1,0:T(8,128)(2,1)} %all-gather.5.cloned.1.call-done, bf16[3072,1024]{1,0:T(8,128)(2,1)} %all-gather.7.cloned.1.call-done, bf16[3072,512]{1,0:T(8,128)(2,1)} %bitcast.42, bf16[1024,512]{1,0:T(8,128)(2,1)S(1)} %copy-done), kind=kOutput, calls=%fused_computation.1 | convolution fusion | flops 6451888128 | bytes 15728640 | tf_op jit(solution)/shard_map/dot_general | solution.py:74
  (107 shorter events, 1.4 us)
Async XLA Ops:
  6.5 164.3 %copy-start = (bf16[1024,512]{1,0:T(8,128)(2,1)S(1)}, bf16[1024,512]{1,0:T(8,128)(2,1)}, u32[]{:S(2)}) copy-start(bf16[1024,512]{1,0:T(8,128)(2,1)} %param.10) | copy-start | bytes 3145732
  6.5 156.2 %all-gather.5.cloned.1.call-start = ((), (), s32[]{:S(2)}) async-start(), calls=%async_computation.1 | async-start | bytes 3342336 | tf_op jit(solution)/shard_map/all_gather | solution.py:66
  8.4 2.4 %copy-start.1 = (f32[192,512]{1,0:T(8,128)}, f32[192,512]{1,0:T(8,128)S(1)}, u32[]{:S(2)}) copy-start(f32[192,512]{1,0:T(8,128)S(1)} %convert_multiply_fusion) | copy-start | bytes 1179652
  10.6 0.7 copy-start.3
  10.8 0.7 slice-start
  11.3 19.9 %copy-start.2 = (s32[192,512]{1,0:T(8,128)S(1)}, s32[192,512]{1,0:T(8,128)}, u32[]{:S(2)}) copy-start(s32[192,512]{1,0:T(8,128)} %param.6) | copy-start | bytes 1179652
  29.4 17.4 %copy-start.4 = (s32[192]{0:T(256)S(1)}, s32[192]{0:T(256)}, u32[]{:S(2)}) copy-start(s32[192]{0:T(256)} %param.11) | copy-start | bytes 2308
  30.4 140.4 %all-gather.7.cloned.1.call-start = ((), (), s32[]{:S(2)}) async-start(), calls=%async_computation.2 | async-start | bytes 6488064 | tf_op jit(solution)/shard_map/all_gather | solution.py:54
  33.3 30.7 %all-to-all-start = ((f32[32,6,512]{2,1,0:T(8,128)}), f32[32,6,512]{2,1,0:T(8,128)S(1)}, u32[]{:S(2)}, u32[]{:S(2)}) async-start(f32[32,6,512]{2,1,0:T(8,128)} %all_to_all.6), calls=%async_computation | async-start | bytes 1048576 | tf_op jit(solution)/shard_map/all_to_all | solution.py:24
  111.6 6.3 %collective-permute-start = (bf16[192,512]{1,0:T(8,128)(2,1)S(1)}, bf16[192,512]{1,0:T(8,128)(2,1)S(1)}, u32[]{:S(2)}, u32[]{:S(2)}) collective-permute-start(bf16[192,512]{1,0:T(8,128)(2,1)S(1)} %reshape.37), channel_id=1, source_target_pairs={{0,32},{32,64},{64,96},{96,128},{128,160},{160,192},{192,224},{224... | collective-permute-start | bytes 589832 | tf_op jit(solution)/shard_map/ppermute | solution.py:42
  111.6 6.3 %collective-permute-start.1 = (bf16[192,512]{1,0:T(8,128)(2,1)S(1)}, bf16[192,512]{1,0:T(8,128)(2,1)S(1)}, u32[]{:S(2)}, u32[]{:S(2)}) collective-permute-start(bf16[192,512]{1,0:T(8,128)(2,1)S(1)} %reshape.37), channel_id=1, source_target_pairs={{0,480},{32,0},{64,32},{96,64},{128,96},{160,128},{192,160},{224,1... | collective-permute-start | bytes 589832 | tf_op jit(solution)/shard_map/ppermute | solution.py:45
  117.9 6.3 %collective-permute-start.2 = (bf16[192,512]{1,0:T(8,128)(2,1)S(1)}, bf16[192,512]{1,0:T(8,128)(2,1)S(1)}, u32[]{:S(2)}, u32[]{:S(2)}) collective-permute-start(bf16[192,512]{1,0:T(8,128)(2,1)S(1)} %collective-permute-done), channel_id=1, source_target_pairs={{0,32},{32,64},{64,96},{96,128},{128,160},{160,192},{192,224},{224... | collective-permute-start | bytes 589832 | tf_op jit(solution)/shard_map/ppermute | solution.py:42
  117.9 6.3 %collective-permute-start.3 = (bf16[192,512]{1,0:T(8,128)(2,1)S(1)}, bf16[192,512]{1,0:T(8,128)(2,1)S(1)}, u32[]{:S(2)}, u32[]{:S(2)}) collective-permute-start(bf16[192,512]{1,0:T(8,128)(2,1)S(1)} %collective-permute-done.1), channel_id=1, source_target_pairs={{0,480},{32,0},{64,32},{96,64},{128,96},{160,128},{192,160},{224,1... | collective-permute-start | bytes 589832 | tf_op jit(solution)/shard_map/ppermute | solution.py:45
  124.2 6.3 %collective-permute-start.4 = (bf16[192,512]{1,0:T(8,128)(2,1)S(1)}, bf16[192,512]{1,0:T(8,128)(2,1)S(1)}, u32[]{:S(2)}, u32[]{:S(2)}) collective-permute-start(bf16[192,512]{1,0:T(8,128)(2,1)S(1)} %collective-permute-done.2), channel_id=1, source_target_pairs={{0,32},{32,64},{64,96},{96,128},{128,160},{160,192},{192,224},{224... | collective-permute-start | bytes 589832 | tf_op jit(solution)/shard_map/ppermute | solution.py:42
  124.2 6.3 %collective-permute-start.5 = (bf16[192,512]{1,0:T(8,128)(2,1)S(1)}, bf16[192,512]{1,0:T(8,128)(2,1)S(1)}, u32[]{:S(2)}, u32[]{:S(2)}) collective-permute-start(bf16[192,512]{1,0:T(8,128)(2,1)S(1)} %collective-permute-done.3), channel_id=1, source_target_pairs={{0,480},{32,0},{64,32},{96,64},{128,96},{160,128},{192,160},{224,1... | collective-permute-start | bytes 589832 | tf_op jit(solution)/shard_map/ppermute | solution.py:45
  130.5 6.3 %collective-permute-start.6 = (bf16[192,512]{1,0:T(8,128)(2,1)S(1)}, bf16[192,512]{1,0:T(8,128)(2,1)S(1)}, u32[]{:S(2)}, u32[]{:S(2)}) collective-permute-start(bf16[192,512]{1,0:T(8,128)(2,1)S(1)} %collective-permute-done.4), channel_id=1, source_target_pairs={{0,32},{32,64},{64,96},{96,128},{128,160},{160,192},{192,224},{224... | collective-permute-start | bytes 589832 | tf_op jit(solution)/shard_map/ppermute | solution.py:42
  130.5 6.3 %collective-permute-start.7 = (bf16[192,512]{1,0:T(8,128)(2,1)S(1)}, bf16[192,512]{1,0:T(8,128)(2,1)S(1)}, u32[]{:S(2)}, u32[]{:S(2)}) collective-permute-start(bf16[192,512]{1,0:T(8,128)(2,1)S(1)} %collective-permute-done.5), channel_id=1, source_target_pairs={{0,480},{32,0},{64,32},{96,64},{128,96},{160,128},{192,160},{224,1... | collective-permute-start | bytes 589832 | tf_op jit(solution)/shard_map/ppermute | solution.py:45
  136.8 6.3 %collective-permute-start.8 = (bf16[192,512]{1,0:T(8,128)(2,1)S(1)}, bf16[192,512]{1,0:T(8,128)(2,1)S(1)}, u32[]{:S(2)}, u32[]{:S(2)}) collective-permute-start(bf16[192,512]{1,0:T(8,128)(2,1)S(1)} %collective-permute-done.6), channel_id=1, source_target_pairs={{0,32},{32,64},{64,96},{96,128},{128,160},{160,192},{192,224},{224... | collective-permute-start | bytes 589832 | tf_op jit(solution)/shard_map/ppermute | solution.py:42
  136.8 6.5 %collective-permute-start.9 = (bf16[192,512]{1,0:T(8,128)(2,1)S(1)}, bf16[192,512]{1,0:T(8,128)(2,1)S(1)}, u32[]{:S(2)}, u32[]{:S(2)}) collective-permute-start(bf16[192,512]{1,0:T(8,128)(2,1)S(1)} %collective-permute-done.7), channel_id=1, source_target_pairs={{0,480},{32,0},{64,32},{96,64},{128,96},{160,128},{192,160},{224,1... | collective-permute-start | bytes 589832 | tf_op jit(solution)/shard_map/ppermute | solution.py:45
  143.1 6.3 %collective-permute-start.10 = (bf16[192,512]{1,0:T(8,128)(2,1)S(1)}, bf16[192,512]{1,0:T(8,128)(2,1)S(1)}, u32[]{:S(2)}, u32[]{:S(2)}) collective-permute-start(bf16[192,512]{1,0:T(8,128)(2,1)S(1)} %collective-permute-done.8), channel_id=1, source_target_pairs={{0,32},{32,64},{64,96},{96,128},{128,160},{160,192},{192,224},{224... | collective-permute-start | bytes 589832 | tf_op jit(solution)/shard_map/ppermute | solution.py:42
  143.4 6.7 %collective-permute-start.11 = (bf16[192,512]{1,0:T(8,128)(2,1)S(1)}, bf16[192,512]{1,0:T(8,128)(2,1)S(1)}, u32[]{:S(2)}, u32[]{:S(2)}) collective-permute-start(bf16[192,512]{1,0:T(8,128)(2,1)S(1)} %collective-permute-done.9), channel_id=1, source_target_pairs={{0,480},{32,0},{64,32},{96,64},{128,96},{160,128},{192,160},{224,1... | collective-permute-start | bytes 589832 | tf_op jit(solution)/shard_map/ppermute | solution.py:45
  149.4 6.3 %collective-permute-start.12 = (bf16[192,512]{1,0:T(8,128)(2,1)S(1)}, bf16[192,512]{1,0:T(8,128)(2,1)S(1)}, u32[]{:S(2)}, u32[]{:S(2)}) collective-permute-start(bf16[192,512]{1,0:T(8,128)(2,1)S(1)} %collective-permute-done.10), channel_id=1, source_target_pairs={{0,32},{32,64},{64,96},{96,128},{128,160},{160,192},{192,224},{224... | collective-permute-start | bytes 589832 | tf_op jit(solution)/shard_map/ppermute | solution.py:42
  150.1 6.7 %collective-permute-start.13 = (bf16[192,512]{1,0:T(8,128)(2,1)S(1)}, bf16[192,512]{1,0:T(8,128)(2,1)S(1)}, u32[]{:S(2)}, u32[]{:S(2)}) collective-permute-start(bf16[192,512]{1,0:T(8,128)(2,1)S(1)} %collective-permute-done.11), channel_id=1, source_target_pairs={{0,480},{32,0},{64,32},{96,64},{128,96},{160,128},{192,160},{224,1... | collective-permute-start | bytes 589832 | tf_op jit(solution)/shard_map/ppermute | solution.py:45
  155.8 6.3 %collective-permute-start.14 = (bf16[192,512]{1,0:T(8,128)(2,1)S(1)}, bf16[192,512]{1,0:T(8,128)(2,1)S(1)}, u32[]{:S(2)}, u32[]{:S(2)}) collective-permute-start(bf16[192,512]{1,0:T(8,128)(2,1)S(1)} %collective-permute-done.12), channel_id=1, source_target_pairs={{0,32},{32,64},{64,96},{96,128},{128,160},{160,192},{192,224},{224... | collective-permute-start | bytes 589832 | tf_op jit(solution)/shard_map/ppermute | solution.py:42
Sparse Core Ops, SparseCore 0:
  30.5 45.3 all-gather.4
  79.0 91.7 all-gather.6

commit v9 on v1

--- a/solution.py
+++ b/solution.py
@@ -2,6 +2,8 @@
 import jax.numpy as jnp
 from jax import lax
 from jax.sharding import PartitionSpec as P
+
+NZ = 8
 
 
 def combine_pairs(earlier, later):
@@ -46,6 +48,33 @@
     return lax.all_gather(moved, "tm", axis=0, tiled=True)
 
 
+def ring_stage(block, coord, count, fwd, bwd):
+    out = jnp.zeros((count,) + block.shape, block.dtype)
+    out = lax.dynamic_update_slice_in_dim(out, block[None], coord, 0)
+    f = block
+    r = block
+    for s in range(1, count // 2 + 1):
+        f = lax.ppermute(f, "pre", fwd)
+        out = lax.dynamic_update_slice_in_dim(out, f[None], (coord - s) % count, 0)
+        if s < count - count // 2:
+            r = lax.ppermute(r, "pre", bwd)
+            out = lax.dynamic_update_slice_in_dim(out, r[None], (coord + s) % count, 0)
+    return out
+
+
+def plane_gather(block, nz, nx):
+    b = lax.axis_index("pre")
+    z = b // nx
+    x = b % nx
+    xf = [(zz * nx + xx, zz * nx + (xx + 1) % nx) for zz in range(nz) for xx in range(nx)]
+    xb = [(zz * nx + xx, zz * nx + (xx - 1) % nx) for zz in range(nz) for xx in range(nx)]
+    zf = [(zz * nx + xx, ((zz + 1) % nz) * nx + xx) for zz in range(nz) for xx in range(nx)]
+    zb = [(zz * nx + xx, ((zz - 1) % nz) * nx + xx) for zz in range(nz) for xx in range(nx)]
+    group = ring_stage(block, x, nx, xf, xb)
+    full = ring_stage(group, z, nz, zf, zb)
+    return full.reshape((nz * nx * block.shape[0],) + block.shape[1:])
+
+
 def ring_gather(block, axis, count):
     index = lax.axis_index(axis)
     fwd = [(i, (i + 1) % count) for i in range(count)]
@@ -65,27 +94,29 @@
 
 def shards(spikes, trace_decay, pseudo_deriv, readout_weight, feedback_weight, targets):
     ntm = lax.axis_size("tm")
-    npre = lax.axis_size("pre")
     a = lax.axis_index("tm")
 
+    derivs_all = lax.all_gather(pseudo_deriv, "pre", axis=0, tiled=True)
+
     errors = owned_errors(spikes, readout_weight, targets)
+    npre = lax.axis_size("pre")
+    assert npre % NZ == 0
     err_rows = route_errors(errors, ntm, npre, pseudo_deriv.shape[0])
-    signal = lax.dot_general(
-        err_rows, feedback_weight, (((1,), (1,)), ((), ())), preferred_element_type=jnp.float32
-    )
-    weighted = (signal * pseudo_deriv.astype(jnp.float32)).astype(jnp.bfloat16)
-    weighted_all = lax.all_gather(weighted, "pre", axis=0, tiled=True)
 
     powers, states = local_traces(spikes, trace_decay)
     ends = lax.all_gather(states[-1], "tm", axis=0)
     span = powers[-1]
-
-    def step(k, carry):
-        return jnp.where(k < a, span * carry + ends[k], carry)
-
-    incoming = lax.fori_loop(0, ntm, step, jnp.zeros_like(trace_decay))
+    incoming = jnp.zeros_like(trace_decay)
+    for k in range(ntm - 1):
+        incoming = jnp.where(k < a, span * incoming + ends[k], incoming)
     traces = (states + powers * incoming[None, :]).astype(jnp.bfloat16)
     traces_all = ring_gather(traces, "tm", ntm)
+
+    errors_all = plane_gather(err_rows, NZ, npre // NZ)
+    signal = lax.dot_general(
+        errors_all, feedback_weight, (((1,), (1,)), ((), ())), preferred_element_type=jnp.float32
+    )
+    weighted_all = (signal * derivs_all.astype(jnp.float32)).astype(jnp.bfloat16)
 
     return lax.dot_general(
         traces_all, weighted_all, (((0,), (0,)), ((), ())), preferred_element_type=jnp.float32

time: 177 us -> 196 us (1.11)
  the two profiles are of different devices: /device:TPU:6 before, /device:TPU:25 now
where the time goes in v9:
time: 196 us; the launch traced here: 195 us
  starting transfers between devices  78.2 us (40%)
  blocking collectives  35.8 us (18%)
  waiting for transfers between devices  25.7 us (13%)
  local copies, waits for them, and re-layouts  23.4 us (12%)
  between operations  14.8 us (8%)
  matrix products  12.9 us (7%)
  other arithmetic  4.47 us (2%)
    ppermute x8, starting transfers between devices, ring_gather(): f = lax.ppermute(f, axis, fwd)  23.7 us
    ppermute x6, waiting for transfers between devices, ring_stage(): f = lax.ppermute(f, 'pre', fwd)  18.7 us
    all_gather x1, blocking collectives, shards(): ends = lax.all_gather(states[-1], 'tm', axis=0)  18.3 us
    all_gather x1, blocking collectives, route_errors(): return lax.all_gather(moved, 'tm', axis=0, tiled=True)  17.4 us
    ppermute x4, starting transfers between devices, ring_stage(): r = lax.ppermute(r, 'pre', bwd)  16.3 us
    ppermute x6, starting transfers between devices, ring_stage(): f = lax.ppermute(f, 'pre', fwd)  16 us
    dot_general x1, matrix products, shards(): lax.dot_general(traces_all, weighted_all, (((0,), (0,)), ((), ())), prefe...  12.7 us
    all_to_all x1, starting transfers between devices, owned_errors(): pieces = lax.all_to_all(partial_logits, 'pre', 0, 0, tiled=True)  12.1 us
  transfers between devices with their start and end apart: 28, of which 10 were waited for; matrix products, arithmetic and copies ran while one was open for 14% of the time, Pallas kernels for 0%

profile of v9, /device:TPU:25, one launch (start us, length us, event | category | flops | bytes accessed | tf_op | source)
XLA Modules:
  0.0 195.3 jit_solution(14548015936983914718)
XLA Ops:
  6.5 0.7 all-gather.4.cloned.1.call-update
  7.3 0.7 multiply_multiply_fusion
  8.0 1.0 convert_multiply_fusion
  9.3 0.7 multiply_add_fusion
  12.5 18.3 %all-gather = f32[16,1,512]{2,1,0:T(1,128)S(1)} all-gather(f32[1,1,512]{2,1,0:T(1,128)S(1)} %add_bitcast_fusion), channel_id=1, replica_groups=mesh['tm'=16,'pre'=32] {'tm'}, dimensions={0}, use_global_device_ids=true | all-gather | bytes 34816 | tf_op jit(solution)/shard_map/all_gather | solution.py:107
  30.8 2.0 %broadcast_in_dim.107 = bf16[16,192,512]{2,1,0:T(8,128)(2,1)} broadcast(bf16[]{:T(256)} %constant.170.clone.1), dimensions={} | broadcast | bytes 3145730 | tf_op jit(solution)/shard_map/broadcast_in_dim | solution.py:82
  32.8 0.9 bitcast_dynamic-update-slice_fusion.23
  33.8 0.5 collective-permute-start.1
  34.6 0.8 all_to_all.6
  35.4 12.1 %all-to-all-start = ((f32[32,6,512]{2,1,0:T(8,128)}), f32[32,6,512]{2,1,0:T(8,128)S(1)}, u32[]{:S(2)}, u32[]{:S(2)}) async-start(f32[32,6,512]{2,1,0:T(8,128)} %all_to_all.6), calls=%async_computation | async-start | bytes 1048576 | tf_op jit(solution)/shard_map/all_to_all | solution.py:26
  48.2 3.2 %collective-permute-start.2 = (bf16[192,512]{1,0:T(8,128)(2,1)S(1)}, bf16[192,512]{1,0:T(8,128)(2,1)S(1)}, u32[]{:S(2)}, u32[]{:S(2)}) collective-permute-start(bf16[192,512]{1,0:T(8,128)(2,1)S(1)} %collective-permute-done), channel_id=1, source_target_pairs={{0,32},{32,64},{64,96},{96,128},{128,160},{160,192},{192,224},{224... | collective-permute-start | bytes 589832 | tf_op jit(solution)/shard_map/ppermute | solution.py:87
  51.4 0.7 bitcast_dynamic-update-slice_fusion.22
  52.1 0.7 bitcast_dynamic-update-slice_fusion.21
  52.8 1.2 collective-permute-done.2
  54.0 3.7 %collective-permute-start.4 = (bf16[192,512]{1,0:T(8,128)(2,1)S(1)}, bf16[192,512]{1,0:T(8,128)(2,1)S(1)}, u32[]{:S(2)}, u32[]{:S(2)}) collective-permute-start(bf16[192,512]{1,0:T(8,128)(2,1)S(1)} %collective-permute-done.2), channel_id=1, source_target_pairs={{0,32},{32,64},{64,96},{96,128},{128,160},{160,192},{192,224},{224... | collective-permute-start | bytes 589832 | tf_op jit(solution)/shard_map/ppermute | solution.py:87
  57.7 0.4 collective-permute-done.3
  58.1 0.7 bitcast_dynamic-update-slice_fusion.20
  58.8 0.7 bitcast_dynamic-update-slice_fusion.19
  59.5 0.8 collective-permute-done.4
  60.3 3.7 %collective-permute-start.6 = (bf16[192,512]{1,0:T(8,128)(2,1)S(1)}, bf16[192,512]{1,0:T(8,128)(2,1)S(1)}, u32[]{:S(2)}, u32[]{:S(2)}) collective-permute-start(bf16[192,512]{1,0:T(8,128)(2,1)S(1)} %collective-permute-done.4), channel_id=1, source_target_pairs={{0,32},{32,64},{64,96},{96,128},{128,160},{160,192},{192,224},{224... | collective-permute-start | bytes 589832 | tf_op jit(solution)/shard_map/ppermute | solution.py:87
  64.0 0.7 collective-permute-done.5
  64.7 0.7 bitcast_dynamic-update-slice_fusion.18
  65.4 0.6 all-to-all-done
  66.4 9.7 %collective-permute-start.15 = (bf16[6,512]{1,0:T(8,128)(2,1)S(1)}, bf16[6,512]{1,0:T(8,128)(2,1)S(1)}, u32[]{:S(2)}, u32[]{:S(2)}) collective-permute-start(bf16[6,512]{1,0:T(8,128)(2,1)S(1)} %subtract_convert_fusion), channel_id=1, source_target_pairs={{0,0},{1,32},{2,64},{3,96},{4,128},{5,160},{6,192},{7,224},{8,256}... | collective-permute-start | bytes 18440 | tf_op jit(solution)/shard_map/ppermute | solution.py:46
  76.1 0.7 bitcast_dynamic-update-slice_fusion.17
  76.9 17.4 %all-gather.1 = bf16[16,6,512]{2,1,0:T(8,128)(2,1)S(1)} all-gather(bf16[1,6,512]{2,1,0:T(8,128)(2,1)S(1)} %bitcast.202), channel_id=1, replica_groups=mesh['tm'=16,'pre'=32] {'tm'}, dimensions={0}, use_global_device_ids=true | all-gather | bytes 104448 | tf_op jit(solution)/shard_map/all_gather | solution.py:48
  94.4 4.7 %collective-permute-start.16 = (bf16[96,512]{1,0:T(8,128)(2,1)S(1)}, bf16[96,512]{1,0:T(8,128)(2,1)S(1)}, u32[]{:S(2)}, u32[]{:S(2)}) collective-permute-start(bf16[96,512]{1,0:T(8,128)(2,1)S(1)} %reshape.41), channel_id=1, source_target_pairs={{0,1},{1,2},{2,3},{3,0},{4,5},{5,6},{6,7},{7,4},{8,9},{9,10},{10,1... | collective-permute-start | bytes 294920 | tf_op jit(solution)/shard_map/ppermute | solution.py:57
  99.1 4.1 %collective-permute-start.17 = (bf16[96,512]{1,0:T(8,128)(2,1)S(1)}, bf16[96,512]{1,0:T(8,128)(2,1)S(1)}, u32[]{:S(2)}, u32[]{:S(2)}) collective-permute-start(bf16[96,512]{1,0:T(8,128)(2,1)S(1)} %reshape.41), channel_id=1, source_target_pairs={{0,3},{1,0},{2,1},{3,2},{4,7},{5,4},{6,5},{7,6},{8,11},{9,8},{10,9... | collective-permute-start | bytes 294920 | tf_op jit(solution)/shard_map/ppermute | solution.py:60
  103.3 1.8 collective-permute-start.8
  105.0 0.7 bitcast_dynamic-update-slice_fusion.16
  105.7 0.7 bitcast_dynamic-update-slice_fusion.15
  106.4 1.9 collective-permute-start.18
  108.4 5.1 %collective-permute-done.18 = bf16[96,512]{1,0:T(8,128)(2,1)S(1)} collective-permute-done((bf16[96,512]{1,0:T(8,128)(2,1)S(1)}, bf16[96,512]{1,0:T(8,128)(2,1)S(1)}, u32[]{:S(2)}, u32[]{:S(2)}) %collective-permute-start.18) | collective-permute-done | bytes 98336 | tf_op jit(solution)/shard_map/ppermute | solution.py:57
  113.6 3.4 %collective-permute-start.19 = (bf16[4,96,512]{2,1,0:T(8,128)(2,1)S(1)}, bf16[4,96,512]{2,1,0:T(8,128)(2,1)S(1)}, u32[]{:S(2)}, u32[]{:S(2)}) collective-permute-start(bf16[4,96,512]{2,1,0:T(8,128)(2,1)S(1)} %bitcast_dynamic-update-slice_fusion.24), channel_id=1, source_target_pairs={{0,4},{1,5},{2,6},{3,7},{4,8},{5,9},{6,10},{7,11},{8,12},{9,13},{1... | collective-permute-start | bytes 1179656 | tf_op jit(solution)/shard_map/ppermute | solution.py:57
  117.0 3.1 %collective-permute-start.20 = (bf16[4,96,512]{2,1,0:T(8,128)(2,1)S(1)}, bf16[4,96,512]{2,1,0:T(8,128)(2,1)S(1)}, u32[]{:S(2)}, u32[]{:S(2)}) collective-permute-start(bf16[4,96,512]{2,1,0:T(8,128)(2,1)S(1)} %bitcast_dynamic-update-slice_fusion.24), channel_id=1, source_target_pairs={{0,28},{1,29},{2,30},{3,31},{4,0},{5,1},{6,2},{7,3},{8,4},{9,5},{1... | collective-permute-start | bytes 1179656 | tf_op jit(solution)/shard_map/ppermute | solution.py:60
  120.1 2.1 %broadcast_in_dim.126 = bf16[8,4,96,512]{3,2,1,0:T(8,128)(2,1)} broadcast(bf16[]{:T(256)} %constant.170.clone.1), dimensions={} | broadcast | bytes 3145730 | tf_op jit(solution)/shard_map/broadcast_in_dim | solution.py:52
  122.1 0.8 bitcast_dynamic-update-slice_fusion.7
  122.9 4.1 %collective-permute-start.10 = (bf16[192,512]{1,0:T(8,128)(2,1)S(1)}, bf16[192,512]{1,0:T(8,128)(2,1)S(1)}, u32[]{:S(2)}, u32[]{:S(2)}) collective-permute-start(bf16[192,512]{1,0:T(8,128)(2,1)S(1)} %collective-permute-done.8), channel_id=1, source_target_pairs={{0,32},{32,64},{64,96},{96,128},{128,160},{160,192},{192,224},{224... | collective-permute-start | bytes 589832 | tf_op jit(solution)/shard_map/ppermute | solution.py:87
  127.0 0.7 bitcast_dynamic-update-slice_fusion.14
  127.7 0.7 bitcast_dynamic-update-slice_fusion.13
  128.4 1.2 collective-permute-done.10
  129.6 3.7 %collective-permute-start.12 = (bf16[192,512]{1,0:T(8,128)(2,1)S(1)}, bf16[192,512]{1,0:T(8,128)(2,1)S(1)}, u32[]{:S(2)}, u32[]{:S(2)}) collective-permute-start(bf16[192,512]{1,0:T(8,128)(2,1)S(1)} %collective-permute-done.10), channel_id=1, source_target_pairs={{0,32},{32,64},{64,96},{96,128},{128,160},{160,192},{192,224},{224... | collective-permute-start | bytes 589832 | tf_op jit(solution)/shard_map/ppermute | solution.py:87
  133.3 0.7 bitcast_dynamic-update-slice_fusion.12
  134.0 0.7 bitcast_dynamic-update-slice_fusion.11
  134.7 2.0 %collective-permute-start.21 = (bf16[4,96,512]{2,1,0:T(8,128)(2,1)S(1)}, bf16[4,96,512]{2,1,0:T(8,128)(2,1)S(1)}, u32[]{:S(2)}, u32[]{:S(2)}) collective-permute-start(bf16[4,96,512]{2,1,0:T(8,128)(2,1)S(1)} %collective-permute-done.19), channel_id=1, source_target_pairs={{0,4},{1,5},{2,6},{3,7},{4,8},{5,9},{6,10},{7,11},{8,12},{9,13},{1... | collective-permute-start | bytes 1179656 | tf_op jit(solution)/shard_map/ppermute | solution.py:57
  136.7 4.5 %collective-permute-start.22 = (bf16[4,96,512]{2,1,0:T(8,128)(2,1)S(1)}, bf16[4,96,512]{2,1,0:T(8,128)(2,1)S(1)}, u32[]{:S(2)}, u32[]{:S(2)}) collective-permute-start(bf16[4,96,512]{2,1,0:T(8,128)(2,1)S(1)} %collective-permute-done.20), channel_id=1, source_target_pairs={{0,28},{1,29},{2,30},{3,31},{4,0},{5,1},{6,2},{7,3},{8,4},{9,5},{1... | collective-permute-start | bytes 1179656 | tf_op jit(solution)/shard_map/ppermute | solution.py:60
  141.2 0.8 bitcast_dynamic-update-slice_fusion.6
  142.0 0.8 bitcast_dynamic-update-slice_fusion.5
  142.8 3.5 %collective-permute-start.14 = (bf16[192,512]{1,0:T(8,128)(2,1)S(1)}, bf16[192,512]{1,0:T(8,128)(2,1)S(1)}, u32[]{:S(2)}, u32[]{:S(2)}) collective-permute-start(bf16[192,512]{1,0:T(8,128)(2,1)S(1)} %collective-permute-done.12), channel_id=1, source_target_pairs={{0,32},{32,64},{64,96},{96,128},{128,160},{160,192},{192,224},{224... | collective-permute-start | bytes 589832 | tf_op jit(solution)/shard_map/ppermute | solution.py:87
  146.3 0.7 bitcast_dynamic-update-slice_fusion.10
  147.0 0.7 bitcast_dynamic-update-slice_fusion.9
  147.7 1.2 collective-permute-done.14
  148.9 0.7 bitcast_dynamic-update-slice_fusion.8
  149.6 1.9 collective-permute-start.23
  151.6 4.6 %collective-permute-start.24 = (bf16[4,96,512]{2,1,0:T(8,128)(2,1)S(1)}, bf16[4,96,512]{2,1,0:T(8,128)(2,1)S(1)}, u32[]{:S(2)}, u32[]{:S(2)}) collective-permute-start(bf16[4,96,512]{2,1,0:T(8,128)(2,1)S(1)} %collective-permute-done.22), channel_id=1, source_target_pairs={{0,28},{1,29},{2,30},{3,31},{4,0},{5,1},{6,2},{7,3},{8,4},{9,5},{1... | collective-permute-start | bytes 1179656 | tf_op jit(solution)/shard_map/ppermute | solution.py:60
  156.2 0.8 bitcast_dynamic-update-slice_fusion.4
  156.9 0.8 bitcast_dynamic-update-slice_fusion.3
  157.7 4.0 %collective-permute-done.23 = bf16[4,96,512]{2,1,0:T(8,128)(2,1)S(1)} collective-permute-done((bf16[4,96,512]{2,1,0:T(8,128)(2,1)S(1)}, bf16[4,96,512]{2,1,0:T(8,128)(2,1)S(1)}, u32[]{:S(2)}, u32[]{:S(2)}) %collective-permute-start.23) | collective-permute-done | bytes 393248 | tf_op jit(solution)/shard_map/ppermute | solution.py:57
  161.8 2.1 %collective-permute-start.25 = (bf16[4,96,512]{2,1,0:T(8,128)(2,1)S(1)}, bf16[4,96,512]{2,1,0:T(8,128)(2,1)S(1)}, u32[]{:S(2)}, u32[]{:S(2)}) collective-permute-start(bf16[4,96,512]{2,1,0:T(8,128)(2,1)S(1)} %collective-permute-done.23), channel_id=1, source_target_pairs={{0,4},{1,5},{2,6},{3,7},{4,8},{5,9},{6,10},{7,11},{8,12},{9,13},{1... | collective-permute-start | bytes 1179656 | tf_op jit(solution)/shard_map/ppermute | solution.py:57
  163.9 0.8 bitcast_dynamic-update-slice_fusion.2
  164.6 0.8 bitcast_dynamic-update-slice_fusion.1
  165.4 9.5 %collective-permute-done.25 = bf16[4,96,512]{2,1,0:T(8,128)(2,1)S(1)} collective-permute-done((bf16[4,96,512]{2,1,0:T(8,128)(2,1)S(1)}, bf16[4,96,512]{2,1,0:T(8,128)(2,1)S(1)}, u32[]{:S(2)}, u32[]{:S(2)}) %collective-permute-start.25) | collective-permute-done | bytes 393248 | tf_op jit(solution)/shard_map/ppermute | solution.py:57
  174.9 0.8 bitcast_dynamic-update-slice_fusion
  175.7 12.7 %fusion = f32[512,1024]{1,0:T(8,128)} fusion(bf16[3072,512]{1,0:T(8,128)(2,1)} %bitcast.42, bf16[3072,1024]{1,0:T(8,128)(2,1)} %all-gather.4.cloned.1.call-done, bf16[3072,512]{1,0:T(8,128)(2,1)} %bitcast.55, bf16[1024,512]{1,0:T(8,128)(2,1)S(1)} %copy-done), kind=kOutput, calls=%fused_computation.1 | convolution fusion | flops 6451888128 | bytes 15728640 | tf_op jit(solution)/shard_map/dot_general | solution.py:121
  (141 shorter events, 3.2 us)
Async XLA Ops:
  6.5 169.2 %copy-start = (bf16[1024,512]{1,0:T(8,128)(2,1)S(1)}, bf16[1024,512]{1,0:T(8,128)(2,1)}, u32[]{:S(2)}) copy-start(bf16[1024,512]{1,0:T(8,128)(2,1)} %param.10) | copy-start | bytes 3145732
  6.5 169.2 %all-gather.4.cloned.1.call-start = ((), (), s32[]{:S(2)}) async-start(), calls=%async_computation.1 | async-start | bytes 6488064 | tf_op jit(solution)/shard_map/all_gather | solution.py:99
  9.0 2.4 %copy-start.1 = (f32[192,512]{1,0:T(8,128)}, f32[192,512]{1,0:T(8,128)S(1)}, u32[]{:S(2)}) copy-start(f32[192,512]{1,0:T(8,128)S(1)} %convert_multiply_fusion) | copy-start | bytes 1179652
  11.2 0.7 copy-start.4
  11.5 0.7 slice-start
  12.3 22.0 %copy-start.2 = (s32[192,512]{1,0:T(8,128)S(1)}, s32[192,512]{1,0:T(8,128)}, u32[]{:S(2)}) copy-start(s32[192,512]{1,0:T(8,128)} %param.6) | copy-start | bytes 1179652
  12.4 21.9 %copy-start.3 = (bf16[512,512]{1,0:T(8,128)(2,1)S(1)}, bf16[512,512]{1,0:T(8,128)(2,1)}, u32[]{:S(2)}) copy-start(bf16[512,512]{1,0:T(8,128)(2,1)} %param.9) | copy-start | bytes 1572868
  32.8 15.2 %copy-start.5 = (s32[192]{0:T(256)S(1)}, s32[192]{0:T(256)}, u32[]{:S(2)}) copy-start(s32[192]{0:T(256)} %param.11) | copy-start | bytes 2308
  33.8 14.4 %collective-permute-start = (bf16[192,512]{1,0:T(8,128)(2,1)}, bf16[192,512]{1,0:T(8,128)(2,1)S(1)}, u32[]{:S(2)}, u32[]{:S(2)}) collective-permute-start(bf16[192,512]{1,0:T(8,128)(2,1)} %get-tuple-element.6), channel_id=1, source_target_pairs={{0,32},{32,64},{64,96},{96,128},{128,160},{160,192},{192,224},{224... | collective-permute-start | bytes 589832 | tf_op jit(solution)/shard_map/ppermute | solution.py:87
  33.8 17.6 %collective-permute-start.1 = (bf16[192,512]{1,0:T(8,128)(2,1)}, bf16[192,512]{1,0:T(8,128)(2,1)S(1)}, u32[]{:S(2)}, u32[]{:S(2)}) collective-permute-start(bf16[192,512]{1,0:T(8,128)(2,1)} %get-tuple-element.6), channel_id=1, source_target_pairs={{0,480},{32,0},{64,32},{96,64},{128,96},{160,128},{192,160},{224,1... | collective-permute-start | bytes 589832 | tf_op jit(solution)/shard_map/ppermute | solution.py:90
  35.4 30.6 %all-to-all-start = ((f32[32,6,512]{2,1,0:T(8,128)}), f32[32,6,512]{2,1,0:T(8,128)S(1)}, u32[]{:S(2)}, u32[]{:S(2)}) async-start(f32[32,6,512]{2,1,0:T(8,128)} %all_to_all.6), calls=%async_computation | async-start | bytes 1048576 | tf_op jit(solution)/shard_map/all_to_all | solution.py:26
  48.2 5.9 %collective-permute-start.2 = (bf16[192,512]{1,0:T(8,128)(2,1)S(1)}, bf16[192,512]{1,0:T(8,128)(2,1)S(1)}, u32[]{:S(2)}, u32[]{:S(2)}) collective-permute-start(bf16[192,512]{1,0:T(8,128)(2,1)S(1)} %collective-permute-done), channel_id=1, source_target_pairs={{0,32},{32,64},{64,96},{96,128},{128,160},{160,192},{192,224},{224... | collective-permute-start | bytes 589832 | tf_op jit(solution)/shard_map/ppermute | solution.py:87
  51.4 6.7 %collective-permute-start.3 = (bf16[192,512]{1,0:T(8,128)(2,1)S(1)}, bf16[192,512]{1,0:T(8,128)(2,1)S(1)}, u32[]{:S(2)}, u32[]{:S(2)}) collective-permute-start(bf16[192,512]{1,0:T(8,128)(2,1)S(1)} %collective-permute-done.1), channel_id=1, source_target_pairs={{0,480},{32,0},{64,32},{96,64},{128,96},{160,128},{192,160},{224,1... | collective-permute-start | bytes 589832 | tf_op jit(solution)/shard_map/ppermute | solution.py:90
  54.0 6.3 %collective-permute-start.4 = (bf16[192,512]{1,0:T(8,128)(2,1)S(1)}, bf16[192,512]{1,0:T(8,128)(2,1)S(1)}, u32[]{:S(2)}, u32[]{:S(2)}) collective-permute-start(bf16[192,512]{1,0:T(8,128)(2,1)S(1)} %collective-permute-done.2), channel_id=1, source_target_pairs={{0,32},{32,64},{64,96},{96,128},{128,160},{160,192},{192,224},{224... | collective-permute-start | bytes 589832 | tf_op jit(solution)/shard_map/ppermute | solution.py:87
  58.1 6.6 %collective-permute-start.5 = (bf16[192,512]{1,0:T(8,128)(2,1)S(1)}, bf16[192,512]{1,0:T(8,128)(2,1)S(1)}, u32[]{:S(2)}, u32[]{:S(2)}) collective-permute-start(bf16[192,512]{1,0:T(8,128)(2,1)S(1)} %collective-permute-done.3), channel_id=1, source_target_pairs={{0,480},{32,0},{64,32},{96,64},{128,96},{160,128},{192,160},{224,1... | collective-permute-start | bytes 589832 | tf_op jit(solution)/shard_map/ppermute | solution.py:90
  60.3 42.9 %collective-permute-start.6 = (bf16[192,512]{1,0:T(8,128)(2,1)S(1)}, bf16[192,512]{1,0:T(8,128)(2,1)S(1)}, u32[]{:S(2)}, u32[]{:S(2)}) collective-permute-start(bf16[192,512]{1,0:T(8,128)(2,1)S(1)} %collective-permute-done.4), channel_id=1, source_target_pairs={{0,32},{32,64},{64,96},{96,128},{128,160},{160,192},{192,224},{224... | collective-permute-start | bytes 589832 | tf_op jit(solution)/shard_map/ppermute | solution.py:87
  64.7 40.3 %collective-permute-start.7 = (bf16[192,512]{1,0:T(8,128)(2,1)S(1)}, bf16[192,512]{1,0:T(8,128)(2,1)S(1)}, u32[]{:S(2)}, u32[]{:S(2)}) collective-permute-start(bf16[192,512]{1,0:T(8,128)(2,1)S(1)} %collective-permute-done.5), channel_id=1, source_target_pairs={{0,480},{32,0},{64,32},{96,64},{128,96},{160,128},{192,160},{224,1... | collective-permute-start | bytes 589832 | tf_op jit(solution)/shard_map/ppermute | solution.py:90
  66.4 10.4 %collective-permute-start.15 = (bf16[6,512]{1,0:T(8,128)(2,1)S(1)}, bf16[6,512]{1,0:T(8,128)(2,1)S(1)}, u32[]{:S(2)}, u32[]{:S(2)}) collective-permute-start(bf16[6,512]{1,0:T(8,128)(2,1)S(1)} %subtract_convert_fusion), channel_id=1, source_target_pairs={{0,0},{1,32},{2,64},{3,96},{4,128},{5,160},{6,192},{7,224},{8,256}... | collective-permute-start | bytes 18440 | tf_op jit(solution)/shard_map/ppermute | solution.py:46
  94.4 12.0 %collective-permute-start.16 = (bf16[96,512]{1,0:T(8,128)(2,1)S(1)}, bf16[96,512]{1,0:T(8,128)(2,1)S(1)}, u32[]{:S(2)}, u32[]{:S(2)}) collective-permute-start(bf16[96,512]{1,0:T(8,128)(2,1)S(1)} %reshape.41), channel_id=1, source_target_pairs={{0,1},{1,2},{2,3},{3,0},{4,5},{5,6},{6,7},{7,4},{8,9},{9,10},{10,1... | collective-permute-start | bytes 294920 | tf_op jit(solution)/shard_map/ppermute | solution.py:57
  99.1 9.3 %collective-permute-start.17 = (bf16[96,512]{1,0:T(8,128)(2,1)S(1)}, bf16[96,512]{1,0:T(8,128)(2,1)S(1)}, u32[]{:S(2)}, u32[]{:S(2)}) collective-permute-start(bf16[96,512]{1,0:T(8,128)(2,1)S(1)} %reshape.41), channel_id=1, source_target_pairs={{0,3},{1,0},{2,1},{3,2},{4,7},{5,4},{6,5},{7,6},{8,11},{9,8},{10,9... | collective-permute-start | bytes 294920 | tf_op jit(solution)/shard_map/ppermute | solution.py:60
  103.3 19.7 %collective-permute-start.8 = (bf16[192,512]{1,0:T(8,128)(2,1)S(1)}, bf16[192,512]{1,0:T(8,128)(2,1)S(1)}, u32[]{:S(2)}, u32[]{:S(2)}) collective-permute-start(bf16[192,512]{1,0:T(8,128)(2,1)S(1)} %collective-permute-done.6), channel_id=1, source_target_pairs={{0,32},{32,64},{64,96},{96,128},{128,160},{160,192},{192,224},{224... | collective-permute-start | bytes 589832 | tf_op jit(solution)/shard_map/ppermute | solution.py:87
  105.0 22.0 %collective-permute-start.9 = (bf16[192,512]{1,0:T(8,128)(2,1)S(1)}, bf16[192,512]{1,0:T(8,128)(2,1)S(1)}, u32[]{:S(2)}, u32[]{:S(2)}) collective-permute-start(bf16[192,512]{1,0:T(8,128)(2,1)S(1)} %collective-permute-done.7), channel_id=1, source_target_pairs={{0,480},{32,0},{64,32},{96,64},{128,96},{160,128},{192,160},{224,1... | collective-permute-start | bytes 589832 | tf_op jit(solution)/shard_map/ppermute | solution.py:90
  106.4 7.1 %collective-permute-start.18 = (bf16[96,512]{1,0:T(8,128)(2,1)S(1)}, bf16[96,512]{1,0:T(8,128)(2,1)S(1)}, u32[]{:S(2)}, u32[]{:S(2)}) collective-permute-start(bf16[96,512]{1,0:T(8,128)(2,1)S(1)} %collective-permute-done.16), channel_id=1, source_target_pairs={{0,1},{1,2},{2,3},{3,0},{4,5},{5,6},{6,7},{7,4},{8,9},{9,10},{10,1... | collective-permute-start | bytes 294920 | tf_op jit(solution)/shard_map/ppermute | solution.py:57
  113.6 21.1 %collective-permute-start.19 = (bf16[4,96,512]{2,1,0:T(8,128)(2,1)S(1)}, bf16[4,96,512]{2,1,0:T(8,128)(2,1)S(1)}, u32[]{:S(2)}, u32[]{:S(2)}) collective-permute-start(bf16[4,96,512]{2,1,0:T(8,128)(2,1)S(1)} %bitcast_dynamic-update-slice_fusion.24), channel_id=1, source_target_pairs={{0,4},{1,5},{2,6},{3,7},{4,8},{5,9},{6,10},{7,11},{8,12},{9,13},{1... | collective-permute-start | bytes 1179656 | tf_op jit(solution)/shard_map/ppermute | solution.py:57
  117.0 19.7 %collective-permute-start.20 = (bf16[4,96,512]{2,1,0:T(8,128)(2,1)S(1)}, bf16[4,96,512]{2,1,0:T(8,128)(2,1)S(1)}, u32[]{:S(2)}, u32[]{:S(2)}) collective-permute-start(bf16[4,96,512]{2,1,0:T(8,128)(2,1)S(1)} %bitcast_dynamic-update-slice_fusion.24), channel_id=1, source_target_pairs={{0,28},{1,29},{2,30},{3,31},{4,0},{5,1},{6,2},{7,3},{8,4},{9,5},{1... | collective-permute-start | bytes 1179656 | tf_op jit(solution)/shard_map/ppermute | solution.py:60
  122.9 6.7 %collective-permute-start.10 = (bf16[192,512]{1,0:T(8,128)(2,1)S(1)}, bf16[192,512]{1,0:T(8,128)(2,1)S(1)}, u32[]{:S(2)}, u32[]{:S(2)}) collective-permute-start(bf16[192,512]{1,0:T(8,128)(2,1)S(1)} %collective-permute-done.8), channel_id=1, source_target_pairs={{0,32},{32,64},{64,96},{96,128},{128,160},{160,192},{192,224},{224... | collective-permute-start | bytes 589832 | tf_op jit(solution)/shard_map/ppermute | solution.py:87
  127.0 6.3 %collective-permute-start.11 = (bf16[192,512]{1,0:T(8,128)(2,1)S(1)}, bf16[192,512]{1,0:T(8,128)(2,1)S(1)}, u32[]{:S(2)}, u32[]{:S(2)}) collective-permute-start(bf16[192,512]{1,0:T(8,128)(2,1)S(1)} %collective-permute-done.9), channel_id=1, source_target_pairs={{0,480},{32,0},{64,32},{96,64},{128,96},{160,128},{192,160},{224,1... | collective-permute-start | bytes 589832 | tf_op jit(solution)/shard_map/ppermute | solution.py:90
  129.6 13.2 %collective-permute-start.12 = (bf16[192,512]{1,0:T(8,128)(2,1)S(1)}, bf16[192,512]{1,0:T(8,128)(2,1)S(1)}, u32[]{:S(2)}, u32[]{:S(2)}) collective-permute-start(bf16[192,512]{1,0:T(8,128)(2,1)S(1)} %collective-permute-done.10), channel_id=1, source_target_pairs={{0,32},{32,64},{64,96},{96,128},{128,160},{160,192},{192,224},{224... | collective-permute-start | bytes 589832 | tf_op jit(solution)/shard_map/ppermute | solution.py:87
  133.3 13.7 %collective-permute-start.13 = (bf16[192,512]{1,0:T(8,128)(2,1)S(1)}, bf16[192,512]{1,0:T(8,128)(2,1)S(1)}, u32[]{:S(2)}, u32[]{:S(2)}) collective-permute-start(bf16[192,512]{1,0:T(8,128)(2,1)S(1)} %collective-permute-done.11), channel_id=1, source_target_pairs={{0,480},{32,0},{64,32},{96,64},{128,96},{160,128},{192,160},{224,1... | collective-permute-start | bytes 589832 | tf_op jit(solution)/shard_map/ppermute | solution.py:90
  134.7 15.0 %collective-permute-start.21 = (bf16[4,96,512]{2,1,0:T(8,128)(2,1)S(1)}, bf16[4,96,512]{2,1,0:T(8,128)(2,1)S(1)}, u32[]{:S(2)}, u32[]{:S(2)}) collective-permute-start(bf16[4,96,512]{2,1,0:T(8,128)(2,1)S(1)} %collective-permute-done.19), channel_id=1, source_target_pairs={{0,4},{1,5},{2,6},{3,7},{4,8},{5,9},{6,10},{7,11},{8,12},{9,13},{1... | collective-permute-start | bytes 1179656 | tf_op jit(solution)/shard_map/ppermute | solution.py:57
  136.7 14.9 %collective-permute-start.22 = (bf16[4,96,512]{2,1,0:T(8,128)(2,1)S(1)}, bf16[4,96,512]{2,1,0:T(8,128)(2,1)S(1)}, u32[]{:S(2)}, u32[]{:S(2)}) collective-permute-start(bf16[4,96,512]{2,1,0:T(8,128)(2,1)S(1)} %collective-permute-done.20), channel_id=1, source_target_pairs={{0,28},{1,29},{2,30},{3,31},{4,0},{5,1},{6,2},{7,3},{8,4},{9,5},{1... | collective-permute-start | bytes 1179656 | tf_op jit(solution)/shard_map/ppermute | solution.py:60
  142.8 6.1 %collective-permute-start.14 = (bf16[192,512]{1,0:T(8,128)(2,1)S(1)}, bf16[192,512]{1,0:T(8,128)(2,1)S(1)}, u32[]{:S(2)}, u32[]{:S(2)}) collective-permute-start(bf16[192,512]{1,0:T(8,128)(2,1)S(1)} %collective-permute-done.12), channel_id=1, source_target_pairs={{0,32},{32,64},{64,96},{96,128},{128,160},{160,192},{192,224},{224... | collective-permute-start | bytes 589832 | tf_op jit(solution)/shard_map/ppermute | solution.py:87
  149.6 12.1 %collective-permute-start.23 = (bf16[4,96,512]{2,1,0:T(8,128)(2,1)S(1)}, bf16[4,96,512]{2,1,0:T(8,128)(2,1)S(1)}, u32[]{:S(2)}, u32[]{:S(2)}) collective-permute-start(bf16[4,96,512]{2,1,0:T(8,128)(2,1)S(1)} %collective-permute-done.21), channel_id=1, source_target_pairs={{0,4},{1,5},{2,6},{3,7},{4,8},{5,9},{6,10},{7,11},{8,12},{9,13},{1... | collective-permute-start | bytes 1179656 | tf_op jit(solution)/shard_map/ppermute | solution.py:57
  151.6 13.1 %collective-permute-start.24 = (bf16[4,96,512]{2,1,0:T(8,128)(2,1)S(1)}, bf16[4,96,512]{2,1,0:T(8,128)(2,1)S(1)}, u32[]{:S(2)}, u32[]{:S(2)}) collective-permute-start(bf16[4,96,512]{2,1,0:T(8,128)(2,1)S(1)} %collective-permute-done.22), channel_id=1, source_target_pairs={{0,28},{1,29},{2,30},{3,31},{4,0},{5,1},{6,2},{7,3},{8,4},{9,5},{1... | collective-permute-start | bytes 1179656 | tf_op jit(solution)/shard_map/ppermute | solution.py:60
  161.8 13.2 %collective-permute-start.25 = (bf16[4,96,512]{2,1,0:T(8,128)(2,1)S(1)}, bf16[4,96,512]{2,1,0:T(8,128)(2,1)S(1)}, u32[]{:S(2)}, u32[]{:S(2)}) collective-permute-start(bf16[4,96,512]{2,1,0:T(8,128)(2,1)S(1)} %collective-permute-done.23), channel_id=1, source_target_pairs={{0,4},{1,5},{2,6},{3,7},{4,8},{5,9},{6,10},{7,11},{8,12},{9,13},{1... | collective-permute-start | bytes 1179656 | tf_op jit(solution)/shard_map/ppermute | solution.py:57
Sparse Core Ops, SparseCore 0:
  10.5 103.0 all-gather.3

commit v10 on v6

--- a/solution.py
+++ b/solution.py
@@ -83,8 +83,9 @@
     xf = [(i, (i + 1) % nx) for i in range(nx)]
     xb = [(i, (i - 1) % nx) for i in range(nx)]
     first = ring_stage(weighted[:, :half], "x", nx, xf, xb)
+    first, rest = lax.optimization_barrier((first, weighted[:, half:]))
     first = lax.all_gather(first.reshape(-1, half), "z", axis=0, tiled=True)
-    second = ring_stage(ring_stage(weighted[:, half:], "z", nz, zf, zb), "x", nx, xf, xb)
+    second = ring_stage(ring_stage(rest, "z", nz, zf, zb), "x", nx, xf, xb)
     second = jnp.swapaxes(second, 0, 1)
     return first, second.reshape(rows, -1)
 
@@ -95,23 +96,27 @@
     a = lax.axis_index("tm")
 
     errors = owned_errors(spikes, readout_weight, targets)
+
+    powers, states = local_traces(spikes, trace_decay)
+    spikes_all = lax.all_gather(spikes.astype(jnp.bfloat16), "tm", axis=0, tiled=True)
+    spikes_all, errors = lax.optimization_barrier((spikes_all, errors))
     err_rows = route_errors(errors, ntm, npre, pseudo_deriv.shape[0])
+    steps = spikes.shape[0]
+    weights = jnp.concatenate([powers[steps - 2::-1], jnp.ones_like(powers[:1])], 0)
+    weights = weights * (1.0 - trace_decay)[None, :]
+    blocks = spikes_all.reshape(ntm, steps, -1).astype(jnp.float32)
+    ends = jnp.sum(blocks * weights[None], axis=1)
+    span = powers[-1]
+    incoming = jnp.zeros_like(trace_decay)
+    for k in range(ntm - 1):
+        incoming = jnp.where(k < a, span * incoming + ends[k], incoming)
+    traces = (states + powers * incoming[None, :]).astype(jnp.bfloat16)
+    traces_all = lax.all_gather(traces, "tm", axis=0, tiled=True)
     signal = lax.dot_general(
         err_rows, feedback_weight, (((1,), (1,)), ((), ())), preferred_element_type=jnp.float32
     )
     weighted = (signal * pseudo_deriv.astype(jnp.float32)).astype(jnp.bfloat16)
     left_all, right_all = weighted_gather(weighted)
-
-    powers, states = local_traces(spikes, trace_decay)
-    ends = lax.all_gather(states[-1], "tm", axis=0)
-    span = powers[-1]
-
-    def step(k, carry):
-        return jnp.where(k < a, span * carry + ends[k], carry)
-
-    incoming = lax.fori_loop(0, ntm, step, jnp.zeros_like(trace_decay))
-    traces = (states + powers * incoming[None, :]).astype(jnp.bfloat16)
-    traces_all = lax.all_gather(traces, "tm", axis=0, tiled=True)
 
     left = outer_sum(traces_all, left_all)
     right = outer_sum(traces_all, right_all)

time: 208 us -> 211 us (1.014)
  the two profiles are of different devices: /device:TPU:6 before, /device:TPU:256 now
where the time goes in v10:
time: 211 us; the launch traced here: 209 us
  waiting for transfers between devices  64 us (30%)
  starting transfers between devices  54.6 us (26%)
  local copies, waits for them, and re-layouts  23.7 us (11%)
  other arithmetic  23.1 us (11%)
  blocking collectives  17.7 us (8%)
  between operations  14.2 us (7%)
  matrix products  12.3 us (6%)
    ppermute x8, waiting for transfers between devices, ring_stage(): f = lax.ppermute(f, axis, fwd)  52.6 us
    ppermute x5, starting transfers between devices, ring_stage(): r = lax.ppermute(r, axis, bwd)  23.5 us
    ppermute x8, starting transfers between devices, ring_stage(): f = lax.ppermute(f, axis, fwd)  17.8 us
    all_gather x1, blocking collectives, route_errors(): return lax.all_gather(moved, 'tm', axis=0, tiled=True)  17.7 us
    ppermute x1, waiting for transfers between devices, route_errors(): moved = lax.ppermute(errors, ('tm',) + PRE, perm)  10.9 us
    dot_general x2, matrix products, outer_sum(): lax.dot_general(left_rows, right_rows, (((0,), (0,)), ((), ())), preferre...  10.4 us
    all_to_all x1, starting transfers between devices, owned_errors(): pieces = lax.all_to_all(partial_logits, PRE, 0, 0, tiled=True)  9.86 us
    add x13, other arithmetic, combine_pairs(): return (earlier[0] * later[0], later[1] + later[0] * earlier[1])  9.47 us
  transfers between devices with their start and end apart: 18, of which 10 were waited for; matrix products, arithmetic and copies ran while one was open for 22% of the time, Pallas kernels for 0%

profile of v10, /device:TPU:256, one launch (start us, length us, event | category | flops | bytes accessed | tf_op | source)
XLA Modules:
  0.0 209.4 jit_solution(6513726225123053514)
XLA Ops:
  6.5 1.8 convert_element_type.29
  8.4 1.4 fusion.17
  9.8 0.8 all_to_all.6
  10.6 9.9 %all-to-all-start = ((f32[32,6,512]{2,1,0:T(8,128)}), f32[32,6,512]{2,1,0:T(8,128)S(1)}, u32[]{:S(2)}, u32[]{:S(2)}) async-start(f32[32,6,512]{2,1,0:T(8,128)} %all_to_all.6), calls=%async_computation | async-start | bytes 1048576 | tf_op jit(solution)/shard_map/all_to_all | solution.py:35
  22.0 2.8 %rev.3 = f32[191,512]{1,0:T(8,128)} reverse(f32[191,512]{1,0:T(8,128)S(1)} %slice_add_fusion), dimensions={0} | reverse | bytes 782336 | tf_op jit(solution)/shard_map/rev | solution.py:105
  24.7 1.1 pad_multiply_fusion
  26.0 0.7 slice.245
  26.7 1.0 multiply_add_fusion
  27.7 0.6 slice.251
  28.4 0.9 multiply_add_fusion.1
  29.3 0.6 slice.253
  30.0 0.6 slice.257
  30.6 0.8 multiply_add_fusion.2
  32.0 0.8 multiply_add_fusion.3
  34.0 0.7 multiply_add_fusion.4
  38.4 0.7 multiply_add_fusion.5
  39.1 0.7 slice_add_fusion.18
  39.9 0.7 fusion.10
  40.6 0.7 pad_maximum_fusion.11
  41.3 0.7 fusion.6
  42.0 0.7 pad_maximum_fusion.9
  42.7 0.7 fusion.5
  43.4 0.7 pad_maximum_fusion.7
  44.1 0.8 fusion.4
  45.0 1.3 pad_maximum_fusion.5
  46.5 1.4 add.240
  48.0 0.7 slice.247
  48.6 0.8 pad.95
  49.5 0.8 pad.96
  50.3 0.9 fusion.3
  51.3 0.7 add.244
  52.2 1.0 pad.100
  53.2 1.3 dynamic_slice.12
  54.9 0.8 subtract_convert_fusion
  55.7 2.6 %fusion = f32[16,512]{1,0:T(8,128)S(1)} fusion(bf16[16,192,512]{2,1,0:T(8,128)(2,1)} %bitcast.73, f32[192,512]{1,0:T(8,128)S(1)} %get-tuple-element.22), kind=kLoop, calls=%fused_computation.1 | loop fusion | flops 4710400 | bytes 3571712 | tf_op jit(solution)/shard_map/reduce_sum | solution.py:108
  58.4 0.8 add_convert_fusion
  59.3 3.3 %collective-permute-start = (bf16[6,512]{1,0:T(8,128)(2,1)S(1)}, bf16[6,512]{1,0:T(8,128)(2,1)S(1)}, u32[]{:S(2)}, u32[]{:S(2)}) collective-permute-start(bf16[6,512]{1,0:T(8,128)(2,1)S(1)} %subtract_convert_fusion), channel_id=1, source_target_pairs={{0,0},{1,32},{2,64},{3,96},{4,128},{5,160},{6,192},{7,224},{8,256}... | collective-permute-start | bytes 18440 | tf_op jit(solution)/shard_map/ppermute | solution.py:55
  62.7 10.9 %collective-permute-done = bf16[6,512]{1,0:T(8,128)(2,1)S(1)} collective-permute-done((bf16[6,512]{1,0:T(8,128)(2,1)S(1)}, bf16[6,512]{1,0:T(8,128)(2,1)S(1)}, u32[]{:S(2)}, u32[]{:S(2)}) %collective-permute-start) | collective-permute-done | bytes 6176 | tf_op jit(solution)/shard_map/ppermute | solution.py:55
  73.5 17.7 %all-gather = bf16[16,6,512]{2,1,0:T(8,128)(2,1)S(1)} all-gather(bf16[1,6,512]{2,1,0:T(8,128)(2,1)S(1)} %bitcast.86), channel_id=1, replica_groups=mesh['tm'=16,'z'=8,'x'=4] {'tm'}, dimensions={0}, use_global_device_ids=true | all-gather | bytes 104448 | tf_op jit(solution)/shard_map/all_gather | solution.py:57
  91.8 1.9 collective-permute-start.1
  93.7 3.9 %collective-permute-start.2 = (bf16[96,512]{1,0:T(8,128)(2,1)S(1)}, bf16[96,512]{1,0:T(8,128)(2,1)S(1)}, u32[]{:S(2)}, u32[]{:S(2)}) collective-permute-start(bf16[96,512]{1,0:T(8,128)(2,1)S(1)} %get-tuple-element.18), channel_id=1, source_target_pairs={{0,1},{1,2},{2,3},{3,0},{4,5},{5,6},{6,7},{7,4},{8,9},{9,10},{10,1... | collective-permute-start | bytes 294920 | tf_op jit(solution)/shard_map/ppermute | solution.py:67
  97.6 4.2 %collective-permute-done.2 = bf16[96,512]{1,0:T(8,128)(2,1)S(1)} collective-permute-done((bf16[96,512]{1,0:T(8,128)(2,1)S(1)}, bf16[96,512]{1,0:T(8,128)(2,1)S(1)}, u32[]{:S(2)}, u32[]{:S(2)}) %collective-permute-start.2) | collective-permute-done | bytes 98336 | tf_op jit(solution)/shard_map/ppermute | solution.py:67
  101.8 2.4 %collective-permute-start.3 = (bf16[96,512]{1,0:T(8,128)(2,1)S(1)}, bf16[96,512]{1,0:T(8,128)(2,1)S(1)}, u32[]{:S(2)}, u32[]{:S(2)}) collective-permute-start(bf16[96,512]{1,0:T(8,128)(2,1)S(1)} %collective-permute-done.2), channel_id=1, source_target_pairs={{0,1},{1,2},{2,3},{3,0},{4,5},{5,6},{6,7},{7,4},{8,9},{9,10},{10,1... | collective-permute-start | bytes 294920 | tf_op jit(solution)/shard_map/ppermute | solution.py:67
  104.3 5.3 %collective-permute-done.3 = bf16[96,512]{1,0:T(8,128)(2,1)S(1)} collective-permute-done((bf16[96,512]{1,0:T(8,128)(2,1)S(1)}, bf16[96,512]{1,0:T(8,128)(2,1)S(1)}, u32[]{:S(2)}, u32[]{:S(2)}) %collective-permute-start.3) | collective-permute-done | bytes 98336 | tf_op jit(solution)/shard_map/ppermute | solution.py:67
  109.6 0.8 constant_dynamic-slice_fusion.1
  110.4 5.4 %collective-permute-start.4 = (bf16[96,512]{1,0:T(8,128)(2,1)S(1)}, bf16[96,512]{1,0:T(8,128)(2,1)S(1)}, u32[]{:S(2)}, u32[]{:S(2)}) collective-permute-start(bf16[96,512]{1,0:T(8,128)(2,1)S(1)} %get-tuple-element.12), channel_id=1, source_target_pairs={{0,28},{4,0},{8,4},{12,8},{16,12},{20,16},{24,20},{28,24},{1,29},{... | collective-permute-start | bytes 294920 | tf_op jit(solution)/shard_map/ppermute | solution.py:70
  115.9 1.9 collective-permute-start.7
  118.0 5.5 %collective-permute-start.5 = (bf16[96,512]{1,0:T(8,128)(2,1)S(1)}, bf16[96,512]{1,0:T(8,128)(2,1)S(1)}, u32[]{:S(2)}, u32[]{:S(2)}) collective-permute-start(bf16[96,512]{1,0:T(8,128)(2,1)S(1)} %collective-permute-done.4), channel_id=1, source_target_pairs={{0,28},{4,0},{8,4},{12,8},{16,12},{20,16},{24,20},{28,24},{1,29},{... | collective-permute-start | bytes 294920 | tf_op jit(solution)/shard_map/ppermute | solution.py:70
  123.6 1.9 collective-permute-start.8
  125.8 5.5 %collective-permute-start.6 = (bf16[96,512]{1,0:T(8,128)(2,1)S(1)}, bf16[96,512]{1,0:T(8,128)(2,1)S(1)}, u32[]{:S(2)}, u32[]{:S(2)}) collective-permute-start(bf16[96,512]{1,0:T(8,128)(2,1)S(1)} %collective-permute-done.5), channel_id=1, source_target_pairs={{0,28},{4,0},{8,4},{12,8},{16,12},{20,16},{24,20},{28,24},{1,29},{... | collective-permute-start | bytes 294920 | tf_op jit(solution)/shard_map/ppermute | solution.py:70
  131.3 2.4 %collective-permute-done.8 = bf16[96,512]{1,0:T(8,128)(2,1)S(1)} collective-permute-done((bf16[96,512]{1,0:T(8,128)(2,1)S(1)}, bf16[96,512]{1,0:T(8,128)(2,1)S(1)}, u32[]{:S(2)}, u32[]{:S(2)}) %collective-permute-start.8) | collective-permute-done | bytes 98336 | tf_op jit(solution)/shard_map/ppermute | solution.py:67
  133.7 1.9 collective-permute-start.9
  135.6 8.5 %collective-permute-done.9 = bf16[96,512]{1,0:T(8,128)(2,1)S(1)} collective-permute-done((bf16[96,512]{1,0:T(8,128)(2,1)S(1)}, bf16[96,512]{1,0:T(8,128)(2,1)S(1)}, u32[]{:S(2)}, u32[]{:S(2)}) %collective-permute-start.9) | collective-permute-done | bytes 98336 | tf_op jit(solution)/shard_map/ppermute | solution.py:67
  144.1 1.9 collective-permute-start.10
  146.0 7.8 %collective-permute-done.10 = bf16[96,512]{1,0:T(8,128)(2,1)S(1)} collective-permute-done((bf16[96,512]{1,0:T(8,128)(2,1)S(1)}, bf16[96,512]{1,0:T(8,128)(2,1)S(1)}, u32[]{:S(2)}, u32[]{:S(2)}) %collective-permute-start.10) | collective-permute-done | bytes 98336 | tf_op jit(solution)/shard_map/ppermute | solution.py:67
  154.2 1.9 collective-permute-start.12
  156.2 5.1 %collective-permute-start.11 = (bf16[8,96,512]{2,1,0:T(8,128)(2,1)S(1)}, bf16[8,96,512]{2,1,0:T(8,128)(2,1)S(1)}, u32[]{:S(2)}, u32[]{:S(2)}) collective-permute-start(bf16[8,96,512]{2,1,0:T(8,128)(2,1)S(1)} %get-tuple-element.14), channel_id=1, source_target_pairs={{0,3},{1,0},{2,1},{3,2},{4,7},{5,4},{6,5},{7,6},{8,11},{9,8},{10,9... | collective-permute-start | bytes 2359304 | tf_op jit(solution)/shard_map/ppermute | solution.py:70
  161.3 11.3 %collective-permute-done.12 = bf16[8,96,512]{2,1,0:T(8,128)(2,1)S(1)} collective-permute-done((bf16[8,96,512]{2,1,0:T(8,128)(2,1)S(1)}, bf16[8,96,512]{2,1,0:T(8,128)(2,1)S(1)}, u32[]{:S(2)}, u32[]{:S(2)}) %collective-permute-start.12) | collective-permute-done | bytes 786464 | tf_op jit(solution)/shard_map/ppermute | solution.py:67
  172.6 1.9 collective-permute-start.13
  174.6 13.1 %collective-permute-done.13 = bf16[8,96,512]{2,1,0:T(8,128)(2,1)S(1)} collective-permute-done((bf16[8,96,512]{2,1,0:T(8,128)(2,1)S(1)}, bf16[8,96,512]{2,1,0:T(8,128)(2,1)S(1)}, u32[]{:S(2)}, u32[]{:S(2)}) %collective-permute-start.13) | collective-permute-done | bytes 786464 | tf_op jit(solution)/shard_map/ppermute | solution.py:67
  188.4 2.0 copy.10
  190.5 5.6 %fusion.19 = f32[512,512]{0,1:T(8,128)} fusion(bf16[3072,512]{1,0:T(8,128)(2,1)} %all-gather.7.cloned.1.call-done, bf16[3072,512]{1,0:T(8,128)(2,1)} %bitcast.74), kind=kOutput, calls=%fused_computation.136 | convolution fusion | flops 1610612736 | bytes 7340032 | tf_op jit(solution)/shard_map/dot_general | solution.py:127
  196.1 4.8 %fusion.18 = f32[512,512]{0,1:T(8,128)S(1)} fusion(bf16[3072,512]{1,0:T(8,128)(2,1)} %all-gather.7.cloned.1.call-done, bf16[3072,512]{1,0:T(8,128)(2,1)} %all-gather.9.cloned.1.call-done), kind=kOutput, calls=%fused_computation.135 | convolution fusion | flops 1610612736 | bytes 7340032 | tf_op jit(solution)/shard_map/dot_general | solution.py:127
  201.1 1.8 copy.11
  (158 shorter events, 10.2 us)
Async XLA Ops:
  6.5 84.7 %copy-start = (bf16[1024,512]{1,0:T(8,128)(2,1)S(1)}, bf16[1024,512]{1,0:T(8,128)(2,1)}, u32[]{:S(2)}) copy-start(bf16[1024,512]{1,0:T(8,128)(2,1)} %param.10) | copy-start | bytes 3145732
  6.5 14.0 %copy-start.6 = (f32[512]{0:T(512)S(1)}, f32[512]{0:T(512)}, u32[]{:S(2)}) copy-start(f32[512]{0:T(512)} %param.7) | copy-start | bytes 6148
  6.5 49.2 %all-gather.5.cloned.1.call-start = ((), (), s32[]{:S(2)}) async-start(), calls=%async_computation.1 | async-start | bytes 3342336 | tf_op jit(solution)/shard_map/all_gather | solution.py:101
  10.6 43.9 %all-to-all-start = ((f32[32,6,512]{2,1,0:T(8,128)}), f32[32,6,512]{2,1,0:T(8,128)S(1)}, u32[]{:S(2)}, u32[]{:S(2)}) async-start(f32[32,6,512]{2,1,0:T(8,128)} %all_to_all.6), calls=%async_computation | async-start | bytes 1048576 | tf_op jit(solution)/shard_map/all_to_all | solution.py:35
  20.5 170.0 %all-gather.7.cloned.1.call-start = ((), (), s32[]{:S(2)}) async-start(), calls=%async_computation.2 | async-start | bytes 3342336 | tf_op jit(solution)/shard_map/all_gather | solution.py:114
  20.6 0.6 copy-start.14
  20.6 0.6 copy-start.13
  20.6 0.7 copy-start.12
  20.6 0.9 copy-start.11
  20.6 7.8 %copy-start.8 = (f32[512]{0:T(512)}, f32[512]{0:T(512)S(1)}, u32[]{:S(2)}) copy-start(f32[512]{0:T(512)S(1)} %get-tuple-element.21) | copy-start | bytes 6148
  20.6 10.0 %copy-start.10 = (f32[512]{0:T(512)}, f32[512]{0:T(512)S(1)}, u32[]{:S(2)}) copy-start(f32[512]{0:T(512)S(1)} %get-tuple-element.30) | copy-start | bytes 6148
  21.7 3.0 %copy-start.1 = (s32[192,512]{1,0:T(8,128)S(1)}, s32[192,512]{1,0:T(8,128)}, u32[]{:S(2)}) copy-start(s32[192,512]{1,0:T(8,128)} %param.6) | copy-start | bytes 1179652
  34.8 15.6 %copy-start.9 = (f32[512]{0:T(512)S(1)}, f32[512]{0:T(512)}, u32[]{:S(2)}) copy-start(f32[512]{0:T(512)} %copy-done.8) | copy-start | bytes 6148
  39.8 12.2 %copy-start.7 = (f32[512]{0:T(512)S(1)}, f32[512]{0:T(512)}, u32[]{:S(2)}) copy-start(f32[512]{0:T(512)} %param.7) | copy-start | bytes 6148
  42.7 2.2 %copy-start.3 = (f32[24,512]{1,0:T(8,128)}, f32[24,512]{1,0:T(8,128)S(1)}, u32[]{:S(2)}) copy-start(f32[24,512]{1,0:T(8,128)S(1)} %pad.94) | copy-start | bytes 147460
  44.1 0.9 copy-start.4
  58.3 33.0 %copy-start.5 = (bf16[96,1024]{1,0:T(8,128)(2,1)S(1)}, bf16[96,1024]{1,0:T(8,128)(2,1)}, u32[]{:S(2)}) copy-start(bf16[96,1024]{1,0:T(8,128)(2,1)} %param.8) | copy-start | bytes 589828
  59.2 136.9 %all-gather.9.cloned.1.call-start = ((), (), s32[]{:S(2)}) async-start(), calls=%async_computation.3 | async-start | bytes 3538944 | tf_op jit(solution)/shard_map/all_gather | solution.py:87
  59.3 14.3 %collective-permute-start = (bf16[6,512]{1,0:T(8,128)(2,1)S(1)}, bf16[6,512]{1,0:T(8,128)(2,1)S(1)}, u32[]{:S(2)}, u32[]{:S(2)}) collective-permute-start(bf16[6,512]{1,0:T(8,128)(2,1)S(1)} %subtract_convert_fusion), channel_id=1, source_target_pairs={{0,0},{1,32},{2,64},{3,96},{4,128},{5,160},{6,192},{7,224},{8,256}... | collective-permute-start | bytes 18440 | tf_op jit(solution)/shard_map/ppermute | solution.py:55
  91.8 12.5 %collective-permute-start.1 = (bf16[96,512]{1,0:T(8,128)(2,1)S(1)}, bf16[96,512]{1,0:T(8,128)(2,1)S(1)}, u32[]{:S(2)}, u32[]{:S(2)}) collective-permute-start(bf16[96,512]{1,0:T(8,128)(2,1)S(1)} %get-tuple-element.18), channel_id=1, source_target_pairs={{0,3},{1,0},{2,1},{3,2},{4,7},{5,4},{6,5},{7,6},{8,11},{9,8},{10,9... | collective-permute-start | bytes 294920 | tf_op jit(solution)/shard_map/ppermute | solution.py:70
  93.7 8.1 %collective-permute-start.2 = (bf16[96,512]{1,0:T(8,128)(2,1)S(1)}, bf16[96,512]{1,0:T(8,128)(2,1)S(1)}, u32[]{:S(2)}, u32[]{:S(2)}) collective-permute-start(bf16[96,512]{1,0:T(8,128)(2,1)S(1)} %get-tuple-element.18), channel_id=1, source_target_pairs={{0,1},{1,2},{2,3},{3,0},{4,5},{5,6},{6,7},{7,4},{8,9},{9,10},{10,1... | collective-permute-start | bytes 294920 | tf_op jit(solution)/shard_map/ppermute | solution.py:67
  101.8 7.7 %collective-permute-start.3 = (bf16[96,512]{1,0:T(8,128)(2,1)S(1)}, bf16[96,512]{1,0:T(8,128)(2,1)S(1)}, u32[]{:S(2)}, u32[]{:S(2)}) collective-permute-start(bf16[96,512]{1,0:T(8,128)(2,1)S(1)} %collective-permute-done.2), channel_id=1, source_target_pairs={{0,1},{1,2},{2,3},{3,0},{4,5},{5,6},{6,7},{7,4},{8,9},{9,10},{10,1... | collective-permute-start | bytes 294920 | tf_op jit(solution)/shard_map/ppermute | solution.py:67
  110.4 7.6 %collective-permute-start.4 = (bf16[96,512]{1,0:T(8,128)(2,1)S(1)}, bf16[96,512]{1,0:T(8,128)(2,1)S(1)}, u32[]{:S(2)}, u32[]{:S(2)}) collective-permute-start(bf16[96,512]{1,0:T(8,128)(2,1)S(1)} %get-tuple-element.12), channel_id=1, source_target_pairs={{0,28},{4,0},{8,4},{12,8},{16,12},{20,16},{24,20},{28,24},{1,29},{... | collective-permute-start | bytes 294920 | tf_op jit(solution)/shard_map/ppermute | solution.py:70
  115.9 7.7 %collective-permute-start.7 = (bf16[96,512]{1,0:T(8,128)(2,1)S(1)}, bf16[96,512]{1,0:T(8,128)(2,1)S(1)}, u32[]{:S(2)}, u32[]{:S(2)}) collective-permute-start(bf16[96,512]{1,0:T(8,128)(2,1)S(1)} %get-tuple-element.12), channel_id=1, source_target_pairs={{0,4},{4,8},{8,12},{12,16},{16,20},{20,24},{24,28},{28,0},{1,5},{5... | collective-permute-start | bytes 294920 | tf_op jit(solution)/shard_map/ppermute | solution.py:67
  118.0 7.7 %collective-permute-start.5 = (bf16[96,512]{1,0:T(8,128)(2,1)S(1)}, bf16[96,512]{1,0:T(8,128)(2,1)S(1)}, u32[]{:S(2)}, u32[]{:S(2)}) collective-permute-start(bf16[96,512]{1,0:T(8,128)(2,1)S(1)} %collective-permute-done.4), channel_id=1, source_target_pairs={{0,28},{4,0},{8,4},{12,8},{16,12},{20,16},{24,20},{28,24},{1,29},{... | collective-permute-start | bytes 294920 | tf_op jit(solution)/shard_map/ppermute | solution.py:70
  123.6 10.1 %collective-permute-start.8 = (bf16[96,512]{1,0:T(8,128)(2,1)S(1)}, bf16[96,512]{1,0:T(8,128)(2,1)S(1)}, u32[]{:S(2)}, u32[]{:S(2)}) collective-permute-start(bf16[96,512]{1,0:T(8,128)(2,1)S(1)} %collective-permute-done.7), channel_id=1, source_target_pairs={{0,4},{4,8},{8,12},{12,16},{16,20},{20,24},{24,28},{28,0},{1,5},{5... | collective-permute-start | bytes 294920 | tf_op jit(solution)/shard_map/ppermute | solution.py:67
  125.8 20.2 %collective-permute-start.6 = (bf16[96,512]{1,0:T(8,128)(2,1)S(1)}, bf16[96,512]{1,0:T(8,128)(2,1)S(1)}, u32[]{:S(2)}, u32[]{:S(2)}) collective-permute-start(bf16[96,512]{1,0:T(8,128)(2,1)S(1)} %collective-permute-done.5), channel_id=1, source_target_pairs={{0,28},{4,0},{8,4},{12,8},{16,12},{20,16},{24,20},{28,24},{1,29},{... | collective-permute-start | bytes 294920 | tf_op jit(solution)/shard_map/ppermute | solution.py:70
  133.7 10.4 %collective-permute-start.9 = (bf16[96,512]{1,0:T(8,128)(2,1)S(1)}, bf16[96,512]{1,0:T(8,128)(2,1)S(1)}, u32[]{:S(2)}, u32[]{:S(2)}) collective-permute-start(bf16[96,512]{1,0:T(8,128)(2,1)S(1)} %collective-permute-done.8), channel_id=1, source_target_pairs={{0,4},{4,8},{8,12},{12,16},{16,20},{20,24},{24,28},{28,0},{1,5},{5... | collective-permute-start | bytes 294920 | tf_op jit(solution)/shard_map/ppermute | solution.py:67
  144.1 9.8 %collective-permute-start.10 = (bf16[96,512]{1,0:T(8,128)(2,1)S(1)}, bf16[96,512]{1,0:T(8,128)(2,1)S(1)}, u32[]{:S(2)}, u32[]{:S(2)}) collective-permute-start(bf16[96,512]{1,0:T(8,128)(2,1)S(1)} %collective-permute-done.9), channel_id=1, source_target_pairs={{0,4},{4,8},{8,12},{12,16},{16,20},{20,24},{24,28},{28,0},{1,5},{5... | collective-permute-start | bytes 294920 | tf_op jit(solution)/shard_map/ppermute | solution.py:67
  154.2 18.4 %collective-permute-start.12 = (bf16[8,96,512]{2,1,0:T(8,128)(2,1)S(1)}, bf16[8,96,512]{2,1,0:T(8,128)(2,1)S(1)}, u32[]{:S(2)}, u32[]{:S(2)}) collective-permute-start(bf16[8,96,512]{2,1,0:T(8,128)(2,1)S(1)} %get-tuple-element.14), channel_id=1, source_target_pairs={{0,1},{1,2},{2,3},{3,0},{4,5},{5,6},{6,7},{7,4},{8,9},{9,10},{10,1... | collective-permute-start | bytes 2359304 | tf_op jit(solution)/shard_map/ppermute | solution.py:67
  156.2 18.3 %collective-permute-start.11 = (bf16[8,96,512]{2,1,0:T(8,128)(2,1)S(1)}, bf16[8,96,512]{2,1,0:T(8,128)(2,1)S(1)}, u32[]{:S(2)}, u32[]{:S(2)}) collective-permute-start(bf16[8,96,512]{2,1,0:T(8,128)(2,1)S(1)} %get-tuple-element.14), channel_id=1, source_target_pairs={{0,3},{1,0},{2,1},{3,2},{4,7},{5,4},{6,5},{7,6},{8,11},{9,8},{10,9... | collective-permute-start | bytes 2359304 | tf_op jit(solution)/shard_map/ppermute | solution.py:70
  172.6 15.1 %collective-permute-start.13 = (bf16[8,96,512]{2,1,0:T(8,128)(2,1)S(1)}, bf16[8,96,512]{2,1,0:T(8,128)(2,1)S(1)}, u32[]{:S(2)}, u32[]{:S(2)}) collective-permute-start(bf16[8,96,512]{2,1,0:T(8,128)(2,1)S(1)} %collective-permute-done.12), channel_id=1, source_target_pairs={{0,1},{1,2},{2,3},{3,0},{4,5},{5,6},{6,7},{7,4},{8,9},{9,10},{10,1... | collective-permute-start | bytes 2359304 | tf_op jit(solution)/shard_map/ppermute | solution.py:67
  196.1 4.8 %copy-start.2 = (f32[512,512]{0,1:T(8,128)S(1)}, f32[512,512]{0,1:T(8,128)}, u32[]{:S(2)}) copy-start(f32[512,512]{0,1:T(8,128)} %fusion.19) | copy-start | bytes 3145732
Sparse Core Ops, SparseCore 0:
  9.5 45.2 all-gather.4
  59.4 44.6 all-gather.6
  117.9 45.4 all-gather.8

commit v11 on v1

--- a/solution.py
+++ b/solution.py
@@ -1,7 +1,17 @@
 import jax
 import jax.numpy as jnp
 from jax import lax
-from jax.sharding import PartitionSpec as P
+from jax.sharding import Mesh, PartitionSpec as P
+
+TM = ("y", "core")
+
+
+def tm_size():
+    return lax.axis_size("y") * lax.axis_size("core")
+
+
+def tm_index():
+    return lax.axis_index("y") * lax.axis_size("core") + lax.axis_index("core")
 
 
 def combine_pairs(earlier, later):
@@ -41,13 +51,14 @@
             dst_b = start // deriv_rows
             dst_a = (start % deriv_rows) // rows
             perm.append((a * npre + b, dst_a * npre + dst_b))
-    moved = lax.ppermute(errors, ("tm", "pre"), perm)
+    moved = lax.ppermute(errors, TM + ("pre",), perm)
     assert per == ntm
-    return lax.all_gather(moved, "tm", axis=0, tiled=True)
+    pair = lax.all_gather(moved, "core", axis=0, tiled=True)
+    return lax.all_gather(pair, "y", axis=0, tiled=True)
 
 
 def ring_gather(block, axis, count):
-    index = lax.axis_index(axis)
+    index = tm_index()
     fwd = [(i, (i + 1) % count) for i in range(count)]
     bwd = [(i, (i - 1) % count) for i in range(count)]
     out = jnp.zeros((count,) + block.shape, block.dtype)
@@ -64,20 +75,15 @@
 
 
 def shards(spikes, trace_decay, pseudo_deriv, readout_weight, feedback_weight, targets):
-    ntm = lax.axis_size("tm")
+    ntm = tm_size()
     npre = lax.axis_size("pre")
-    a = lax.axis_index("tm")
+    a = tm_index()
 
     errors = owned_errors(spikes, readout_weight, targets)
     err_rows = route_errors(errors, ntm, npre, pseudo_deriv.shape[0])
-    signal = lax.dot_general(
-        err_rows, feedback_weight, (((1,), (1,)), ((), ())), preferred_element_type=jnp.float32
-    )
-    weighted = (signal * pseudo_deriv.astype(jnp.float32)).astype(jnp.bfloat16)
-    weighted_all = lax.all_gather(weighted, "pre", axis=0, tiled=True)
-
     powers, states = local_traces(spikes, trace_decay)
-    ends = lax.all_gather(states[-1], "tm", axis=0)
+    end_state, err_rows = lax.optimization_barrier((states[-1], err_rows))
+    ends = lax.all_gather(end_state, TM, axis=0)
     span = powers[-1]
 
     def step(k, carry):
@@ -85,7 +91,12 @@
 
     incoming = lax.fori_loop(0, ntm, step, jnp.zeros_like(trace_decay))
     traces = (states + powers * incoming[None, :]).astype(jnp.bfloat16)
-    traces_all = ring_gather(traces, "tm", ntm)
+    traces_all = ring_gather(traces, TM, ntm)
+    signal = lax.dot_general(
+        err_rows, feedback_weight, (((1,), (1,)), ((), ())), preferred_element_type=jnp.float32
+    )
+    weighted = (signal * pseudo_deriv.astype(jnp.float32)).astype(jnp.bfloat16)
+    weighted_all = lax.all_gather(weighted, "pre", axis=0, tiled=True)
 
     return lax.dot_general(
         traces_all, weighted_all, (((0,), (0,)), ((), ())), preferred_element_type=jnp.float32
@@ -93,7 +104,9 @@
 
 
 def solution(mesh):
-    placed = (P("tm", "pre"), P("pre"), P("pre", "tm"), P("pre", None), P("tm", None), P("tm"))
+    ntm, npre = mesh.devices.shape
+    split = Mesh(mesh.devices.reshape(ntm // 2, 2, npre), TM + ("pre",))
+    placed = (P(TM, "pre"), P("pre"), P("pre", TM), P("pre", None), P(TM, None), P(TM))
     return jax.shard_map(
-        shards, mesh=mesh, in_specs=placed, out_specs=P("pre", "tm"), check_vma=False
+        shards, mesh=split, in_specs=placed, out_specs=P("pre", TM), check_vma=False
     )

time: 177 us -> 188 us (1.062)
  blocking collectives: 35.9 us -> 44.7 us
  waiting for transfers between devices: 58.3 us -> 60.4 us
    all_gather x2 -> x3, blocking collectives: 35.9 us -> 44.7 us  [the longest x1 28.6 us: route_errors(): return lax.all_gather(pair, 'y', axis=0, tiled=True)]
    all_gather x1, waiting for transfers between devices: 14.3 us -> 18.1 us  [shards(): weighted_all = lax.all_gather(weighted, 'pre', axis=0, tiled=True)]
  transfers between devices with their start and end apart: 18 -> 18, of which waited for: 12 -> 11; matrix products, arithmetic and copies ran while one was open for 9% -> 8% of each run, Pallas kernels for 0% -> 0%
where the time goes in v11:
time: 188 us; the launch traced here: 185 us
  waiting for transfers between devices  60.4 us (32%)
  blocking collectives  44.7 us (24%)
  starting transfers between devices  37.2 us (20%)
  local copies, waits for them, and re-layouts  15 us (8%)
  between operations  14.1 us (8%)
  matrix products  11.2 us (6%)
  other arithmetic  2.2 us (1%)
    all_gather x1, blocking collectives, route_errors(): return lax.all_gather(pair, 'y', axis=0, tiled=True)  28.6 us
    ppermute x7, starting transfers between devices, ring_gather(): b = lax.ppermute(b, axis, bwd)  21.5 us
    ppermute x8, waiting for transfers between devices, ring_gather(): f = lax.ppermute(f, axis, fwd)  19.1 us
    all_gather x1, waiting for transfers between devices, shards(): weighted_all = lax.all_gather(weighted, 'pre', axis=0, tiled=True)  18.1 us
    all_gather x1, blocking collectives, shards(): ends = lax.all_gather(end_state, TM, axis=0)  14.2 us
    all_to_all x1, waiting for transfers between devices, owned_errors(): pieces = lax.all_to_all(partial_logits, 'pre', 0, 0, tiled=True)  14.1 us
    all_to_all x1, starting transfers between devices, owned_errors(): pieces = lax.all_to_all(partial_logits, 'pre', 0, 0, tiled=True)  13.4 us
    ppermute x1, waiting for transfers between devices, route_errors(): moved = lax.ppermute(errors, TM + ('pre',), perm)  9.05 us
  transfers between devices with their start and end apart: 18, of which 11 were waited for; matrix products, arithmetic and copies ran while one was open for 8% of the time, Pallas kernels for 0%

profile of v11, /device:TPU:6, one launch (start us, length us, event | category | flops | bytes accessed | tf_op | source)
XLA Modules:
  0.0 185.3 jit_solution(1740136917280000693)
XLA Ops:
  6.5 1.6 fusion.2
  8.1 0.8 all_to_all.6
  8.9 13.4 %all-to-all-start = ((f32[32,6,512]{2,1,0:T(8,128)}), f32[32,6,512]{2,1,0:T(8,128)S(1)}, u32[]{:S(2)}, u32[]{:S(2)}) async-start(f32[32,6,512]{2,1,0:T(8,128)} %all_to_all.6), calls=%async_computation | async-start | bytes 1048576 | tf_op jit(solution)/shard_map/all_to_all | solution.py:34
  22.4 0.0 all-gather.6.cloned.1.call-start
  22.5 0.1 slice.192
  22.6 0.1 slice.194
  23.3 0.2 slice.190
  24.3 0.0 copy-start.5
  24.4 0.0 copy-start.3
  24.6 0.1 pad.99
  24.7 0.1 fusion.1
  24.8 0.1 slice-done
  24.9 0.1 pad.98
  25.0 0.1 dynamic_slice.10
  25.1 14.1 %all-to-all-done = f32[32,6,512]{2,1,0:T(8,128)S(1)} async-done(((f32[32,6,512]{2,1,0:T(8,128)}), f32[32,6,512]{2,1,0:T(8,128)S(1)}, u32[]{:S(2)}, u32[]{:S(2)}) %all-to-all-start) | async-done | bytes 393248 | tf_op jit(solution)/shard_map/all_to_all | solution.py:34
  39.2 0.1 reduce_sum.18
  39.2 0.1 reduce_max.9
  39.4 0.2 fusion.8
  39.6 0.1 subtract_convert_fusion
  39.6 1.9 %collective-permute-start = (bf16[6,512]{1,0:T(8,128)(2,1)S(1)}, bf16[6,512]{1,0:T(8,128)(2,1)S(1)}, u32[]{:S(2)}, u32[]{:S(2)}) collective-permute-start(bf16[6,512]{1,0:T(8,128)(2,1)S(1)} %subtract_convert_fusion), channel_id=1, source_target_pairs={{0,0},{1,32},{2,64},{3,96},{4,128},{5,160},{6,192},{7,224},{8,256}... | collective-permute-start | bytes 18440 | tf_op jit(solution)/shard_map/ppermute | solution.py:54
  41.6 9.1 %collective-permute-done = bf16[6,512]{1,0:T(8,128)(2,1)S(1)} collective-permute-done((bf16[6,512]{1,0:T(8,128)(2,1)S(1)}, bf16[6,512]{1,0:T(8,128)(2,1)S(1)}, u32[]{:S(2)}, u32[]{:S(2)}) %collective-permute-start) | collective-permute-done | bytes 6176 | tf_op jit(solution)/shard_map/ppermute | solution.py:54
  50.6 1.8 all-gather.1
  52.5 28.6 %all-gather.2 = bf16[8,12,512]{2,1,0:T(8,128)(2,1)S(1)} all-gather(bf16[1,12,512]{2,1,0:T(8,128)(2,1)S(1)} %reshape.38), channel_id=1, replica_groups=mesh['y'=8,'core'=2,'pre'=32] {'y'}, dimensions={0}, use_global_device_ids=true | all-gather | bytes 110592 | tf_op jit(solution)/shard_map/all_gather | solution.py:57
  81.1 1.1 fusion
  82.3 0.0 all-gather.6.cloned.1.call-update
  82.4 0.1 pad.112
  82.4 0.1 pad.113
  82.5 14.2 %all-gather.3 = f32[16,1,512]{2,1,0:T(1,128)S(1)} all-gather(f32[1,1,512]{2,1,0:T(1,128)S(1)} %bitcast.71), channel_id=2, replica_groups=mesh['y'=8,'core'=2,'pre'=32] {'y','core'}, dimensions={0}, use_global_device_ids=true | all-gather | bytes 34816 | tf_op jit(solution)/shard_map/all_gather | solution.py:86
  96.8 0.9 while.14
  97.6 2.0 %broadcast_in_dim.65 = bf16[16,192,512]{2,1,0:T(8,128)(2,1)} broadcast(bf16[]{:T(256)} %constant.122.clone.1), dimensions={} | broadcast | bytes 3145730 | tf_op jit(solution)/shard_map/broadcast_in_dim | solution.py:64
  99.6 0.8 bitcast_dynamic-update-slice_fusion.15
  100.5 0.3 collective-permute-start.1
  100.8 2.8 %collective-permute-start.2 = (bf16[192,512]{1,0:T(8,128)(2,1)S(1)}, bf16[192,512]{1,0:T(8,128)(2,1)S(1)}, u32[]{:S(2)}, u32[]{:S(2)}) collective-permute-start(bf16[192,512]{1,0:T(8,128)(2,1)S(1)} %get-tuple-element.133), channel_id=1, source_target_pairs={{0,480},{32,0},{64,32},{96,64},{128,96},{160,128},{192,160},{224,1... | collective-permute-start | bytes 589832 | tf_op jit(solution)/shard_map/ppermute | solution.py:72
  103.6 3.3 %collective-permute-done.1 = bf16[192,512]{1,0:T(8,128)(2,1)S(1)} collective-permute-done((bf16[192,512]{1,0:T(8,128)(2,1)S(1)}, bf16[192,512]{1,0:T(8,128)(2,1)S(1)}, u32[]{:S(2)}, u32[]{:S(2)}) %collective-permute-start.1) | collective-permute-done | bytes 196640 | tf_op jit(solution)/shard_map/ppermute | solution.py:69
  107.0 3.0 %collective-permute-start.4 = (bf16[192,512]{1,0:T(8,128)(2,1)S(1)}, bf16[192,512]{1,0:T(8,128)(2,1)S(1)}, u32[]{:S(2)}, u32[]{:S(2)}) collective-permute-start(bf16[192,512]{1,0:T(8,128)(2,1)S(1)} %collective-permute-done.2), channel_id=1, source_target_pairs={{0,480},{32,0},{64,32},{96,64},{128,96},{160,128},{192,160},{224,1... | collective-permute-start | bytes 589832 | tf_op jit(solution)/shard_map/ppermute | solution.py:72
  109.9 0.7 bitcast_dynamic-update-slice_fusion.14
  110.6 0.7 bitcast_dynamic-update-slice_fusion.13
  111.3 2.0 %collective-permute-done.3 = bf16[192,512]{1,0:T(8,128)(2,1)S(1)} collective-permute-done((bf16[192,512]{1,0:T(8,128)(2,1)S(1)}, bf16[192,512]{1,0:T(8,128)(2,1)S(1)}, u32[]{:S(2)}, u32[]{:S(2)}) %collective-permute-start.3) | collective-permute-done | bytes 196640 | tf_op jit(solution)/shard_map/ppermute | solution.py:69
  113.3 3.1 %collective-permute-start.6 = (bf16[192,512]{1,0:T(8,128)(2,1)S(1)}, bf16[192,512]{1,0:T(8,128)(2,1)S(1)}, u32[]{:S(2)}, u32[]{:S(2)}) collective-permute-start(bf16[192,512]{1,0:T(8,128)(2,1)S(1)} %collective-permute-done.4), channel_id=1, source_target_pairs={{0,480},{32,0},{64,32},{96,64},{128,96},{160,128},{192,160},{224,1... | collective-permute-start | bytes 589832 | tf_op jit(solution)/shard_map/ppermute | solution.py:72
  116.4 0.7 bitcast_dynamic-update-slice_fusion.12
  117.0 0.7 bitcast_dynamic-update-slice_fusion.11
  117.7 1.8 collective-permute-done.5
  119.6 3.1 %collective-permute-start.8 = (bf16[192,512]{1,0:T(8,128)(2,1)S(1)}, bf16[192,512]{1,0:T(8,128)(2,1)S(1)}, u32[]{:S(2)}, u32[]{:S(2)}) collective-permute-start(bf16[192,512]{1,0:T(8,128)(2,1)S(1)} %collective-permute-done.6), channel_id=1, source_target_pairs={{0,480},{32,0},{64,32},{96,64},{128,96},{160,128},{192,160},{224,1... | collective-permute-start | bytes 589832 | tf_op jit(solution)/shard_map/ppermute | solution.py:72
  122.7 0.7 bitcast_dynamic-update-slice_fusion.10
  123.4 0.7 bitcast_dynamic-update-slice_fusion.9
  124.0 1.9 %collective-permute-done.7 = bf16[192,512]{1,0:T(8,128)(2,1)S(1)} collective-permute-done((bf16[192,512]{1,0:T(8,128)(2,1)S(1)}, bf16[192,512]{1,0:T(8,128)(2,1)S(1)}, u32[]{:S(2)}, u32[]{:S(2)}) %collective-permute-start.7) | collective-permute-done | bytes 196640 | tf_op jit(solution)/shard_map/ppermute | solution.py:69
  125.9 3.1 %collective-permute-start.10 = (bf16[192,512]{1,0:T(8,128)(2,1)S(1)}, bf16[192,512]{1,0:T(8,128)(2,1)S(1)}, u32[]{:S(2)}, u32[]{:S(2)}) collective-permute-start(bf16[192,512]{1,0:T(8,128)(2,1)S(1)} %collective-permute-done.8), channel_id=1, source_target_pairs={{0,480},{32,0},{64,32},{96,64},{128,96},{160,128},{192,160},{224,1... | collective-permute-start | bytes 589832 | tf_op jit(solution)/shard_map/ppermute | solution.py:72
  129.0 0.7 bitcast_dynamic-update-slice_fusion.8
  129.7 0.7 bitcast_dynamic-update-slice_fusion.7
  130.4 1.8 collective-permute-done.9
  132.2 3.1 %collective-permute-start.12 = (bf16[192,512]{1,0:T(8,128)(2,1)S(1)}, bf16[192,512]{1,0:T(8,128)(2,1)S(1)}, u32[]{:S(2)}, u32[]{:S(2)}) collective-permute-start(bf16[192,512]{1,0:T(8,128)(2,1)S(1)} %collective-permute-done.10), channel_id=1, source_target_pairs={{0,480},{32,0},{64,32},{96,64},{128,96},{160,128},{192,160},{224,1... | collective-permute-start | bytes 589832 | tf_op jit(solution)/shard_map/ppermute | solution.py:72
  135.3 0.7 bitcast_dynamic-update-slice_fusion.6
  136.0 0.7 bitcast_dynamic-update-slice_fusion.5
  136.7 1.9 collective-permute-done.11
  138.5 3.5 %collective-permute-start.14 = (bf16[192,512]{1,0:T(8,128)(2,1)S(1)}, bf16[192,512]{1,0:T(8,128)(2,1)S(1)}, u32[]{:S(2)}, u32[]{:S(2)}) collective-permute-start(bf16[192,512]{1,0:T(8,128)(2,1)S(1)} %collective-permute-done.12), channel_id=1, source_target_pairs={{0,480},{32,0},{64,32},{96,64},{128,96},{160,128},{192,160},{224,1... | collective-permute-start | bytes 589832 | tf_op jit(solution)/shard_map/ppermute | solution.py:72
  142.0 0.7 bitcast_dynamic-update-slice_fusion.4
  142.7 0.7 bitcast_dynamic-update-slice_fusion.3
  143.4 1.4 collective-permute-done.13
  144.8 0.7 bitcast_dynamic-update-slice_fusion.2
  145.5 0.7 bitcast_dynamic-update-slice_fusion.1
  146.2 4.9 %collective-permute-done.15 = bf16[192,512]{1,0:T(8,128)(2,1)S(1)} collective-permute-done((bf16[192,512]{1,0:T(8,128)(2,1)S(1)}, bf16[192,512]{1,0:T(8,128)(2,1)S(1)}, u32[]{:S(2)}, u32[]{:S(2)}) %collective-permute-start.15) | collective-permute-done | bytes 196640 | tf_op jit(solution)/shard_map/ppermute | solution.py:69
  151.1 0.7 bitcast_dynamic-update-slice_fusion
  151.8 18.1 %all-gather.6.cloned.1.call-done = bf16[3072,1024]{1,0:T(8,128)(2,1)} async-done(((bf16[96,1024]{1,0:T(8,128)(2,1)}), bf16[3072,1024]{1,0:T(8,128)(2,1)}) %all-gather.6.cloned.1.call-update) | async-done | bytes 6291472 | tf_op jit(solution)/shard_map/all_gather | solution.py:99
  169.9 8.5 %fusion.17 = f32[512,1024]{1,0:T(8,128)} fusion(bf16[3072,512]{1,0:T(8,128)(2,1)} %bitcast.29, bf16[3072,1024]{1,0:T(8,128)(2,1)} %all-gather.6.cloned.1.call-done), kind=kOutput, calls=%fused_computation.85 | convolution fusion | flops 3221225472 | bytes 11534336 | tf_op jit(solution)/shard_map/dot_general | solution.py:101
  (144 shorter events, 1.8 us)
Async XLA Ops:
  6.5 74.6 %copy-start = (bf16[1024,512]{1,0:T(8,128)(2,1)S(1)}, bf16[1024,512]{1,0:T(8,128)(2,1)}, u32[]{:S(2)}) copy-start(bf16[1024,512]{1,0:T(8,128)(2,1)} %param.12) | copy-start | bytes 3145732
  6.5 15.9 %copy-start.2 = (s32[192,512]{1,0:T(8,128)S(1)}, s32[192,512]{1,0:T(8,128)}, u32[]{:S(2)}) copy-start(s32[192,512]{1,0:T(8,128)} %param.8) | copy-start | bytes 1179652
  6.5 15.9 %copy-start.4 = (f32[512]{0:T(512)S(1)}, f32[512]{0:T(512)}, u32[]{:S(2)}) copy-start(f32[512]{0:T(512)} %param.9) | copy-start | bytes 6148
  8.9 30.2 %all-to-all-start = ((f32[32,6,512]{2,1,0:T(8,128)}), f32[32,6,512]{2,1,0:T(8,128)S(1)}, u32[]{:S(2)}, u32[]{:S(2)}) async-start(f32[32,6,512]{2,1,0:T(8,128)} %all_to_all.6), calls=%async_computation | async-start | bytes 1048576 | tf_op jit(solution)/shard_map/all_to_all | solution.py:34
  22.4 147.6 %all-gather.6.cloned.1.call-start = ((), (), s32[]{:S(2)}) async-start(), calls=%async_computation.1 | async-start | bytes 6488064 | tf_op jit(solution)/shard_map/all_gather | solution.py:99
  22.5 1.7 copy-start.1
  24.2 0.7 slice-start
  24.3 0.7 copy-start.5
  24.4 56.7 %copy-start.3 = (bf16[96,1024]{1,0:T(8,128)(2,1)S(1)}, bf16[96,1024]{1,0:T(8,128)(2,1)}, u32[]{:S(2)}) copy-start(bf16[96,1024]{1,0:T(8,128)(2,1)} %param.10) | copy-start | bytes 589828
  39.6 11.0 %collective-permute-start = (bf16[6,512]{1,0:T(8,128)(2,1)S(1)}, bf16[6,512]{1,0:T(8,128)(2,1)S(1)}, u32[]{:S(2)}, u32[]{:S(2)}) collective-permute-start(bf16[6,512]{1,0:T(8,128)(2,1)S(1)} %subtract_convert_fusion), channel_id=1, source_target_pairs={{0,0},{1,32},{2,64},{3,96},{4,128},{5,160},{6,192},{7,224},{8,256}... | collective-permute-start | bytes 18440 | tf_op jit(solution)/shard_map/ppermute | solution.py:54
  100.5 6.5 %collective-permute-start.1 = (bf16[192,512]{1,0:T(8,128)(2,1)S(1)}, bf16[192,512]{1,0:T(8,128)(2,1)S(1)}, u32[]{:S(2)}, u32[]{:S(2)}) collective-permute-start(bf16[192,512]{1,0:T(8,128)(2,1)S(1)} %get-tuple-element.133), channel_id=1, source_target_pairs={{0,32},{32,64},{64,96},{96,128},{128,160},{160,192},{192,224},{224... | collective-permute-start | bytes 589832 | tf_op jit(solution)/shard_map/ppermute | solution.py:69
  100.8 6.2 %collective-permute-start.2 = (bf16[192,512]{1,0:T(8,128)(2,1)S(1)}, bf16[192,512]{1,0:T(8,128)(2,1)S(1)}, u32[]{:S(2)}, u32[]{:S(2)}) collective-permute-start(bf16[192,512]{1,0:T(8,128)(2,1)S(1)} %get-tuple-element.133), channel_id=1, source_target_pairs={{0,480},{32,0},{64,32},{96,64},{128,96},{160,128},{192,160},{224,1... | collective-permute-start | bytes 589832 | tf_op jit(solution)/shard_map/ppermute | solution.py:72
  107.0 6.3 %collective-permute-start.3 = (bf16[192,512]{1,0:T(8,128)(2,1)S(1)}, bf16[192,512]{1,0:T(8,128)(2,1)S(1)}, u32[]{:S(2)}, u32[]{:S(2)}) collective-permute-start(bf16[192,512]{1,0:T(8,128)(2,1)S(1)} %collective-permute-done.1), channel_id=1, source_target_pairs={{0,32},{32,64},{64,96},{96,128},{128,160},{160,192},{192,224},{224... | collective-permute-start | bytes 589832 | tf_op jit(solution)/shard_map/ppermute | solution.py:69
  107.0 6.3 %collective-permute-start.4 = (bf16[192,512]{1,0:T(8,128)(2,1)S(1)}, bf16[192,512]{1,0:T(8,128)(2,1)S(1)}, u32[]{:S(2)}, u32[]{:S(2)}) collective-permute-start(bf16[192,512]{1,0:T(8,128)(2,1)S(1)} %collective-permute-done.2), channel_id=1, source_target_pairs={{0,480},{32,0},{64,32},{96,64},{128,96},{160,128},{192,160},{224,1... | collective-permute-start | bytes 589832 | tf_op jit(solution)/shard_map/ppermute | solution.py:72
  113.3 6.3 %collective-permute-start.5 = (bf16[192,512]{1,0:T(8,128)(2,1)S(1)}, bf16[192,512]{1,0:T(8,128)(2,1)S(1)}, u32[]{:S(2)}, u32[]{:S(2)}) collective-permute-start(bf16[192,512]{1,0:T(8,128)(2,1)S(1)} %collective-permute-done.3), channel_id=1, source_target_pairs={{0,32},{32,64},{64,96},{96,128},{128,160},{160,192},{192,224},{224... | collective-permute-start | bytes 589832 | tf_op jit(solution)/shard_map/ppermute | solution.py:69
  113.3 6.3 %collective-permute-start.6 = (bf16[192,512]{1,0:T(8,128)(2,1)S(1)}, bf16[192,512]{1,0:T(8,128)(2,1)S(1)}, u32[]{:S(2)}, u32[]{:S(2)}) collective-permute-start(bf16[192,512]{1,0:T(8,128)(2,1)S(1)} %collective-permute-done.4), channel_id=1, source_target_pairs={{0,480},{32,0},{64,32},{96,64},{128,96},{160,128},{192,160},{224,1... | collective-permute-start | bytes 589832 | tf_op jit(solution)/shard_map/ppermute | solution.py:72
  119.6 6.3 %collective-permute-start.7 = (bf16[192,512]{1,0:T(8,128)(2,1)S(1)}, bf16[192,512]{1,0:T(8,128)(2,1)S(1)}, u32[]{:S(2)}, u32[]{:S(2)}) collective-permute-start(bf16[192,512]{1,0:T(8,128)(2,1)S(1)} %collective-permute-done.5), channel_id=1, source_target_pairs={{0,32},{32,64},{64,96},{96,128},{128,160},{160,192},{192,224},{224... | collective-permute-start | bytes 589832 | tf_op jit(solution)/shard_map/ppermute | solution.py:69
  119.6 6.3 %collective-permute-start.8 = (bf16[192,512]{1,0:T(8,128)(2,1)S(1)}, bf16[192,512]{1,0:T(8,128)(2,1)S(1)}, u32[]{:S(2)}, u32[]{:S(2)}) collective-permute-start(bf16[192,512]{1,0:T(8,128)(2,1)S(1)} %collective-permute-done.6), channel_id=1, source_target_pairs={{0,480},{32,0},{64,32},{96,64},{128,96},{160,128},{192,160},{224,1... | collective-permute-start | bytes 589832 | tf_op jit(solution)/shard_map/ppermute | solution.py:72
  125.9 6.3 %collective-permute-start.9 = (bf16[192,512]{1,0:T(8,128)(2,1)S(1)}, bf16[192,512]{1,0:T(8,128)(2,1)S(1)}, u32[]{:S(2)}, u32[]{:S(2)}) collective-permute-start(bf16[192,512]{1,0:T(8,128)(2,1)S(1)} %collective-permute-done.7), channel_id=1, source_target_pairs={{0,32},{32,64},{64,96},{96,128},{128,160},{160,192},{192,224},{224... | collective-permute-start | bytes 589832 | tf_op jit(solution)/shard_map/ppermute | solution.py:69
  125.9 6.3 %collective-permute-start.10 = (bf16[192,512]{1,0:T(8,128)(2,1)S(1)}, bf16[192,512]{1,0:T(8,128)(2,1)S(1)}, u32[]{:S(2)}, u32[]{:S(2)}) collective-permute-start(bf16[192,512]{1,0:T(8,128)(2,1)S(1)} %collective-permute-done.8), channel_id=1, source_target_pairs={{0,480},{32,0},{64,32},{96,64},{128,96},{160,128},{192,160},{224,1... | collective-permute-start | bytes 589832 | tf_op jit(solution)/shard_map/ppermute | solution.py:72
  132.2 6.3 %collective-permute-start.11 = (bf16[192,512]{1,0:T(8,128)(2,1)S(1)}, bf16[192,512]{1,0:T(8,128)(2,1)S(1)}, u32[]{:S(2)}, u32[]{:S(2)}) collective-permute-start(bf16[192,512]{1,0:T(8,128)(2,1)S(1)} %collective-permute-done.9), channel_id=1, source_target_pairs={{0,32},{32,64},{64,96},{96,128},{128,160},{160,192},{192,224},{224... | collective-permute-start | bytes 589832 | tf_op jit(solution)/shard_map/ppermute | solution.py:69
  132.2 6.3 %collective-permute-start.12 = (bf16[192,512]{1,0:T(8,128)(2,1)S(1)}, bf16[192,512]{1,0:T(8,128)(2,1)S(1)}, u32[]{:S(2)}, u32[]{:S(2)}) collective-permute-start(bf16[192,512]{1,0:T(8,128)(2,1)S(1)} %collective-permute-done.10), channel_id=1, source_target_pairs={{0,480},{32,0},{64,32},{96,64},{128,96},{160,128},{192,160},{224,1... | collective-permute-start | bytes 589832 | tf_op jit(solution)/shard_map/ppermute | solution.py:72
  138.5 6.3 %collective-permute-start.13 = (bf16[192,512]{1,0:T(8,128)(2,1)S(1)}, bf16[192,512]{1,0:T(8,128)(2,1)S(1)}, u32[]{:S(2)}, u32[]{:S(2)}) collective-permute-start(bf16[192,512]{1,0:T(8,128)(2,1)S(1)} %collective-permute-done.11), channel_id=1, source_target_pairs={{0,32},{32,64},{64,96},{96,128},{128,160},{160,192},{192,224},{224... | collective-permute-start | bytes 589832 | tf_op jit(solution)/shard_map/ppermute | solution.py:69
  138.5 7.0 %collective-permute-start.14 = (bf16[192,512]{1,0:T(8,128)(2,1)S(1)}, bf16[192,512]{1,0:T(8,128)(2,1)S(1)}, u32[]{:S(2)}, u32[]{:S(2)}) collective-permute-start(bf16[192,512]{1,0:T(8,128)(2,1)S(1)} %collective-permute-done.12), channel_id=1, source_target_pairs={{0,480},{32,0},{64,32},{96,64},{128,96},{160,128},{192,160},{224,1... | collective-permute-start | bytes 589832 | tf_op jit(solution)/shard_map/ppermute | solution.py:72
  144.8 6.3 %collective-permute-start.15 = (bf16[192,512]{1,0:T(8,128)(2,1)S(1)}, bf16[192,512]{1,0:T(8,128)(2,1)S(1)}, u32[]{:S(2)}, u32[]{:S(2)}) collective-permute-start(bf16[192,512]{1,0:T(8,128)(2,1)S(1)} %collective-permute-done.13), channel_id=1, source_target_pairs={{0,32},{32,64},{64,96},{96,128},{128,160},{160,192},{192,224},{224... | collective-permute-start | bytes 589832 | tf_op jit(solution)/shard_map/ppermute | solution.py:69
Sparse Core Ops, SparseCore 0:
  82.4 87.4 all-gather.5

commit v12 on v1

--- a/solution.py
+++ b/solution.py
@@ -21,8 +21,10 @@
         spikes.astype(jnp.bfloat16), readout_weight, preferred_element_type=jnp.float32
     )
     rows = partial_logits.shape[0] // npre
-    pieces = lax.all_to_all(partial_logits, "pre", 0, 0, tiled=True)
-    logits = pieces.reshape(npre, rows, -1).sum(0)
+    tile = -(-rows // 8) * 8
+    padded = jnp.pad(partial_logits.reshape(npre, rows, -1), ((0, 0), (0, tile - rows), (0, 0)))
+    pieces = lax.all_to_all(padded, "pre", 0, 0, tiled=True)
+    logits = pieces[:, :rows].sum(0)
     class_prob = jax.nn.softmax(logits, axis=-1)
     classes = lax.broadcasted_iota(jnp.int32, logits.shape, 1)
     mine = lax.dynamic_slice_in_dim(targets, b * rows, rows, 0)

time: 177 us -> 177 us (level)
  no operation moved by 1% of the time
where the time goes in v12:
time: 177 us; the launch traced here: 174 us
  waiting for transfers between devices  58.3 us (33%)
  starting transfers between devices  37.2 us (21%)
  blocking collectives  35.9 us (20%)
  local copies, waits for them, and re-layouts  15.1 us (9%)
  between operations  14.1 us (8%)
  matrix products  11.2 us (6%)
  other arithmetic  2.18 us (1%)
    ppermute x7, starting transfers between devices, ring_gather(): b = lax.ppermute(b, axis, bwd)  21.3 us
    ppermute x8, waiting for transfers between devices, ring_gather(): f = lax.ppermute(f, axis, fwd)  18.9 us
    all_gather x1, blocking collectives, route_errors(): return lax.all_gather(moved, 'tm', axis=0, tiled=True)  18.5 us
    all_gather x1, blocking collectives, shards(): ends = lax.all_gather(states[-1], 'tm', axis=0)  17.4 us
    all_to_all x1, waiting for transfers between devices, owned_errors(): pieces = lax.all_to_all(padded, 'pre', 0, 0, tiled=True)  15.8 us
    all_gather x1, waiting for transfers between devices, shards(): weighted_all = lax.all_gather(weighted, 'pre', axis=0, tiled=True)  14.3 us
    all_to_all x1, starting transfers between devices, owned_errors(): pieces = lax.all_to_all(padded, 'pre', 0, 0, tiled=True)  13.5 us
    ppermute x1, waiting for transfers between devices, route_errors(): moved = lax.ppermute(errors, ('tm', 'pre'), perm)  9.04 us
  transfers between devices with their start and end apart: 18, of which 12 were waited for; matrix products, arithmetic and copies ran while one was open for 9% of the time, Pallas kernels for 0%

profile of v12, /device:TPU:6, one launch (start us, length us, event | category | flops | bytes accessed | tf_op | source)
XLA Modules:
  0.0 174.4 jit_solution(17329712180107560851)
XLA Ops:
  6.5 1.6 fusion.2
  8.1 0.0 copy-start.5
  8.1 0.1 reshape.34
  8.2 0.8 pad.118
  9.0 13.5 %all-to-all-start = ((f32[32,8,512]{2,1,0:T(8,128)}), f32[32,8,512]{2,1,0:T(8,128)S(1)}, u32[]{:S(2)}, u32[]{:S(2)}) async-start(f32[32,8,512]{2,1,0:T(8,128)} %pad.118), calls=%async_computation | async-start | bytes 1048576 | tf_op jit(solution)/shard_map/all_to_all | solution.py:26
  22.6 0.0 all-gather.4.cloned.1.call-start
  22.7 0.1 slice.195
  22.8 0.1 slice.197
  23.5 0.1 dynamic_slice.10
  23.6 15.8 %all-to-all-done = f32[32,8,512]{2,1,0:T(8,128)S(1)} async-done(((f32[32,8,512]{2,1,0:T(8,128)}), f32[32,8,512]{2,1,0:T(8,128)S(1)}, u32[]{:S(2)}, u32[]{:S(2)}) %all-to-all-start) | async-done | bytes 524320 | tf_op jit(solution)/shard_map/all_to_all | solution.py:26
  39.4 0.1 reduce_max.9
  39.6 0.2 fusion.8
  39.7 0.1 subtract_convert_fusion
  39.8 1.9 %collective-permute-start.15 = (bf16[6,512]{1,0:T(8,128)(2,1)S(1)}, bf16[6,512]{1,0:T(8,128)(2,1)S(1)}, u32[]{:S(2)}, u32[]{:S(2)}) collective-permute-start(bf16[6,512]{1,0:T(8,128)(2,1)S(1)} %subtract_convert_fusion), channel_id=1, source_target_pairs={{0,0},{1,32},{2,64},{3,96},{4,128},{5,160},{6,192},{7,224},{8,256}... | collective-permute-start | bytes 18440 | tf_op jit(solution)/shard_map/ppermute | solution.py:46
  41.8 9.0 %collective-permute-done.15 = bf16[6,512]{1,0:T(8,128)(2,1)S(1)} collective-permute-done((bf16[6,512]{1,0:T(8,128)(2,1)S(1)}, bf16[6,512]{1,0:T(8,128)(2,1)S(1)}, u32[]{:S(2)}, u32[]{:S(2)}) %collective-permute-start.15) | collective-permute-done | bytes 6176 | tf_op jit(solution)/shard_map/ppermute | solution.py:46
  50.8 18.5 %all-gather.1 = bf16[16,6,512]{2,1,0:T(8,128)(2,1)S(1)} all-gather(bf16[1,6,512]{2,1,0:T(8,128)(2,1)S(1)} %bitcast.70), channel_id=1, replica_groups=mesh['tm'=16,'pre'=32] {'tm'}, dimensions={0}, use_global_device_ids=true | all-gather | bytes 104448 | tf_op jit(solution)/shard_map/all_gather | solution.py:48
  69.4 1.1 fusion
  70.5 0.0 all-gather.4.cloned.1.call-update
  70.8 0.2 slice.193
  71.5 0.0 slice-start
  71.8 0.1 pad.103
  72.0 0.1 fusion.1
  72.1 0.1 slice-done
  72.2 0.1 pad.102
  72.3 17.4 %all-gather = f32[16,1,512]{2,1,0:T(1,128)S(1)} all-gather(f32[1,1,512]{2,1,0:T(1,128)S(1)} %add_bitcast_fusion), channel_id=1, replica_groups=mesh['tm'=16,'pre'=32] {'tm'}, dimensions={0}, use_global_device_ids=true | all-gather | bytes 34816 | tf_op jit(solution)/shard_map/all_gather | solution.py:82
  89.7 0.1 pad.116
  89.8 0.1 pad.117
  89.9 0.9 while.14
  90.8 2.0 %broadcast_in_dim.65 = bf16[16,192,512]{2,1,0:T(8,128)(2,1)} broadcast(bf16[]{:T(256)} %constant.119.clone.1), dimensions={} | broadcast | bytes 3145730 | tf_op jit(solution)/shard_map/broadcast_in_dim | solution.py:55
  92.8 0.9 bitcast_dynamic-update-slice_fusion.15
  93.6 0.3 collective-permute-start
  94.0 2.6 %collective-permute-start.1 = (bf16[192,512]{1,0:T(8,128)(2,1)S(1)}, bf16[192,512]{1,0:T(8,128)(2,1)S(1)}, u32[]{:S(2)}, u32[]{:S(2)}) collective-permute-start(bf16[192,512]{1,0:T(8,128)(2,1)S(1)} %get-tuple-element.129), channel_id=1, source_target_pairs={{0,480},{32,0},{64,32},{96,64},{128,96},{160,128},{192,160},{224,1... | collective-permute-start | bytes 589832 | tf_op jit(solution)/shard_map/ppermute | solution.py:63
  96.6 3.3 %collective-permute-done = bf16[192,512]{1,0:T(8,128)(2,1)S(1)} collective-permute-done((bf16[192,512]{1,0:T(8,128)(2,1)S(1)}, bf16[192,512]{1,0:T(8,128)(2,1)S(1)}, u32[]{:S(2)}, u32[]{:S(2)}) %collective-permute-start) | collective-permute-done | bytes 196640 | tf_op jit(solution)/shard_map/ppermute | solution.py:60
  100.0 3.0 %collective-permute-start.3 = (bf16[192,512]{1,0:T(8,128)(2,1)S(1)}, bf16[192,512]{1,0:T(8,128)(2,1)S(1)}, u32[]{:S(2)}, u32[]{:S(2)}) collective-permute-start(bf16[192,512]{1,0:T(8,128)(2,1)S(1)} %collective-permute-done.1), channel_id=1, source_target_pairs={{0,480},{32,0},{64,32},{96,64},{128,96},{160,128},{192,160},{224,1... | collective-permute-start | bytes 589832 | tf_op jit(solution)/shard_map/ppermute | solution.py:63
  102.9 0.7 bitcast_dynamic-update-slice_fusion.14
  103.6 0.7 bitcast_dynamic-update-slice_fusion.13
  104.3 2.0 %collective-permute-done.2 = bf16[192,512]{1,0:T(8,128)(2,1)S(1)} collective-permute-done((bf16[192,512]{1,0:T(8,128)(2,1)S(1)}, bf16[192,512]{1,0:T(8,128)(2,1)S(1)}, u32[]{:S(2)}, u32[]{:S(2)}) %collective-permute-start.2) | collective-permute-done | bytes 196640 | tf_op jit(solution)/shard_map/ppermute | solution.py:60
  106.3 3.0 %collective-permute-start.5 = (bf16[192,512]{1,0:T(8,128)(2,1)S(1)}, bf16[192,512]{1,0:T(8,128)(2,1)S(1)}, u32[]{:S(2)}, u32[]{:S(2)}) collective-permute-start(bf16[192,512]{1,0:T(8,128)(2,1)S(1)} %collective-permute-done.3), channel_id=1, source_target_pairs={{0,480},{32,0},{64,32},{96,64},{128,96},{160,128},{192,160},{224,1... | collective-permute-start | bytes 589832 | tf_op jit(solution)/shard_map/ppermute | solution.py:63
  109.2 0.7 bitcast_dynamic-update-slice_fusion.12
  109.9 0.7 bitcast_dynamic-update-slice_fusion.11
  110.6 2.0 %collective-permute-done.4 = bf16[192,512]{1,0:T(8,128)(2,1)S(1)} collective-permute-done((bf16[192,512]{1,0:T(8,128)(2,1)S(1)}, bf16[192,512]{1,0:T(8,128)(2,1)S(1)}, u32[]{:S(2)}, u32[]{:S(2)}) %collective-permute-start.4) | collective-permute-done | bytes 196640 | tf_op jit(solution)/shard_map/ppermute | solution.py:60
  112.6 3.0 %collective-permute-start.7 = (bf16[192,512]{1,0:T(8,128)(2,1)S(1)}, bf16[192,512]{1,0:T(8,128)(2,1)S(1)}, u32[]{:S(2)}, u32[]{:S(2)}) collective-permute-start(bf16[192,512]{1,0:T(8,128)(2,1)S(1)} %collective-permute-done.5), channel_id=1, source_target_pairs={{0,480},{32,0},{64,32},{96,64},{128,96},{160,128},{192,160},{224,1... | collective-permute-start | bytes 589832 | tf_op jit(solution)/shard_map/ppermute | solution.py:63
  115.5 0.7 bitcast_dynamic-update-slice_fusion.10
  116.2 0.7 bitcast_dynamic-update-slice_fusion.9
  116.9 2.0 %collective-permute-done.6 = bf16[192,512]{1,0:T(8,128)(2,1)S(1)} collective-permute-done((bf16[192,512]{1,0:T(8,128)(2,1)S(1)}, bf16[192,512]{1,0:T(8,128)(2,1)S(1)}, u32[]{:S(2)}, u32[]{:S(2)}) %collective-permute-start.6) | collective-permute-done | bytes 196640 | tf_op jit(solution)/shard_map/ppermute | solution.py:60
  118.9 3.0 %collective-permute-start.9 = (bf16[192,512]{1,0:T(8,128)(2,1)S(1)}, bf16[192,512]{1,0:T(8,128)(2,1)S(1)}, u32[]{:S(2)}, u32[]{:S(2)}) collective-permute-start(bf16[192,512]{1,0:T(8,128)(2,1)S(1)} %collective-permute-done.7), channel_id=1, source_target_pairs={{0,480},{32,0},{64,32},{96,64},{128,96},{160,128},{192,160},{224,1... | collective-permute-start | bytes 589832 | tf_op jit(solution)/shard_map/ppermute | solution.py:63
  121.8 0.7 bitcast_dynamic-update-slice_fusion.8
  122.5 0.7 bitcast_dynamic-update-slice_fusion.7
  123.2 2.0 %collective-permute-done.8 = bf16[192,512]{1,0:T(8,128)(2,1)S(1)} collective-permute-done((bf16[192,512]{1,0:T(8,128)(2,1)S(1)}, bf16[192,512]{1,0:T(8,128)(2,1)S(1)}, u32[]{:S(2)}, u32[]{:S(2)}) %collective-permute-start.8) | collective-permute-done | bytes 196640 | tf_op jit(solution)/shard_map/ppermute | solution.py:60
  125.2 3.4 %collective-permute-start.11 = (bf16[192,512]{1,0:T(8,128)(2,1)S(1)}, bf16[192,512]{1,0:T(8,128)(2,1)S(1)}, u32[]{:S(2)}, u32[]{:S(2)}) collective-permute-start(bf16[192,512]{1,0:T(8,128)(2,1)S(1)} %collective-permute-done.9), channel_id=1, source_target_pairs={{0,480},{32,0},{64,32},{96,64},{128,96},{160,128},{192,160},{224,1... | collective-permute-start | bytes 589832 | tf_op jit(solution)/shard_map/ppermute | solution.py:63
  128.5 0.7 bitcast_dynamic-update-slice_fusion.6
  129.2 0.7 bitcast_dynamic-update-slice_fusion.5
  129.9 1.6 collective-permute-done.10
  131.5 0.2 collective-permute-done.11
  131.7 3.5 %collective-permute-start.13 = (bf16[192,512]{1,0:T(8,128)(2,1)S(1)}, bf16[192,512]{1,0:T(8,128)(2,1)S(1)}, u32[]{:S(2)}, u32[]{:S(2)}) collective-permute-start(bf16[192,512]{1,0:T(8,128)(2,1)S(1)} %collective-permute-done.11), channel_id=1, source_target_pairs={{0,480},{32,0},{64,32},{96,64},{128,96},{160,128},{192,160},{224,1... | collective-permute-start | bytes 589832 | tf_op jit(solution)/shard_map/ppermute | solution.py:63
  135.2 0.7 bitcast_dynamic-update-slice_fusion.4
  135.9 0.7 bitcast_dynamic-update-slice_fusion.3
  136.6 1.2 collective-permute-done.12
  137.8 0.7 bitcast_dynamic-update-slice_fusion.2
  138.5 0.7 bitcast_dynamic-update-slice_fusion.1
  139.2 4.9 %collective-permute-done.14 = bf16[192,512]{1,0:T(8,128)(2,1)S(1)} collective-permute-done((bf16[192,512]{1,0:T(8,128)(2,1)S(1)}, bf16[192,512]{1,0:T(8,128)(2,1)S(1)}, u32[]{:S(2)}, u32[]{:S(2)}) %collective-permute-start.14) | collective-permute-done | bytes 196640 | tf_op jit(solution)/shard_map/ppermute | solution.py:60
  144.1 0.7 bitcast_dynamic-update-slice_fusion
  144.8 14.3 %all-gather.4.cloned.1.call-done = bf16[3072,1024]{1,0:T(8,128)(2,1)} async-done(((bf16[96,1024]{1,0:T(8,128)(2,1)}), bf16[3072,1024]{1,0:T(8,128)(2,1)}) %all-gather.4.cloned.1.call-update) | async-done | bytes 6291472 | tf_op jit(solution)/shard_map/all_gather | solution.py:79
  159.1 8.5 %fusion.17 = f32[512,1024]{1,0:T(8,128)} fusion(bf16[3072,512]{1,0:T(8,128)(2,1)} %bitcast.27, bf16[3072,1024]{1,0:T(8,128)(2,1)} %all-gather.4.cloned.1.call-done), kind=kOutput, calls=%fused_computation.86 | convolution fusion | flops 3221225472 | bytes 11534336 | tf_op jit(solution)/shard_map/dot_general | solution.py:92
  (143 shorter events, 1.8 us)
Async XLA Ops:
  6.5 62.9 %copy-start = (bf16[1024,512]{1,0:T(8,128)(2,1)S(1)}, bf16[1024,512]{1,0:T(8,128)(2,1)}, u32[]{:S(2)}) copy-start(bf16[1024,512]{1,0:T(8,128)(2,1)} %param.12) | copy-start | bytes 3145732
  6.5 16.1 %copy-start.2 = (s32[192,512]{1,0:T(8,128)S(1)}, s32[192,512]{1,0:T(8,128)}, u32[]{:S(2)}) copy-start(s32[192,512]{1,0:T(8,128)} %param.8) | copy-start | bytes 1179652
  6.5 16.1 %copy-start.4 = (f32[512]{0:T(512)S(1)}, f32[512]{0:T(512)}, u32[]{:S(2)}) copy-start(f32[512]{0:T(512)} %param.9) | copy-start | bytes 6148
  8.1 15.3 %copy-start.5 = (s32[192]{0:T(256)S(1)}, s32[192]{0:T(256)}, u32[]{:S(2)}) copy-start(s32[192]{0:T(256)} %param.13) | copy-start | bytes 2308
  9.0 60.4 %copy-start.3 = (bf16[96,1024]{1,0:T(8,128)(2,1)S(1)}, bf16[96,1024]{1,0:T(8,128)(2,1)}, u32[]{:S(2)}) copy-start(bf16[96,1024]{1,0:T(8,128)(2,1)} %param.10) | copy-start | bytes 589828
  9.0 30.4 %all-to-all-start = ((f32[32,8,512]{2,1,0:T(8,128)}), f32[32,8,512]{2,1,0:T(8,128)S(1)}, u32[]{:S(2)}, u32[]{:S(2)}) async-start(f32[32,8,512]{2,1,0:T(8,128)} %pad.118), calls=%async_computation | async-start | bytes 1048576 | tf_op jit(solution)/shard_map/all_to_all | solution.py:26
  22.6 136.5 %all-gather.4.cloned.1.call-start = ((), (), s32[]{:S(2)}) async-start(), calls=%async_computation.1 | async-start | bytes 6488064 | tf_op jit(solution)/shard_map/all_gather | solution.py:79
  22.7 48.3 %copy-start.1 = (f32[192,512]{1,0:T(8,128)}, f32[192,512]{1,0:T(8,128)S(1)}, u32[]{:S(2)}) copy-start(f32[192,512]{1,0:T(8,128)S(1)} %convert_multiply_fusion) | copy-start | bytes 1179652
  39.8 11.0 %collective-permute-start.15 = (bf16[6,512]{1,0:T(8,128)(2,1)S(1)}, bf16[6,512]{1,0:T(8,128)(2,1)S(1)}, u32[]{:S(2)}, u32[]{:S(2)}) collective-permute-start(bf16[6,512]{1,0:T(8,128)(2,1)S(1)} %subtract_convert_fusion), channel_id=1, source_target_pairs={{0,0},{1,32},{2,64},{3,96},{4,128},{5,160},{6,192},{7,224},{8,256}... | collective-permute-start | bytes 18440 | tf_op jit(solution)/shard_map/ppermute | solution.py:46
  71.5 0.7 slice-start
  93.6 6.3 %collective-permute-start = (bf16[192,512]{1,0:T(8,128)(2,1)S(1)}, bf16[192,512]{1,0:T(8,128)(2,1)S(1)}, u32[]{:S(2)}, u32[]{:S(2)}) collective-permute-start(bf16[192,512]{1,0:T(8,128)(2,1)S(1)} %get-tuple-element.129), channel_id=1, source_target_pairs={{0,32},{32,64},{64,96},{96,128},{128,160},{160,192},{192,224},{224... | collective-permute-start | bytes 589832 | tf_op jit(solution)/shard_map/ppermute | solution.py:60
  94.0 6.0 %collective-permute-start.1 = (bf16[192,512]{1,0:T(8,128)(2,1)S(1)}, bf16[192,512]{1,0:T(8,128)(2,1)S(1)}, u32[]{:S(2)}, u32[]{:S(2)}) collective-permute-start(bf16[192,512]{1,0:T(8,128)(2,1)S(1)} %get-tuple-element.129), channel_id=1, source_target_pairs={{0,480},{32,0},{64,32},{96,64},{128,96},{160,128},{192,160},{224,1... | collective-permute-start | bytes 589832 | tf_op jit(solution)/shard_map/ppermute | solution.py:63
  100.0 6.3 %collective-permute-start.2 = (bf16[192,512]{1,0:T(8,128)(2,1)S(1)}, bf16[192,512]{1,0:T(8,128)(2,1)S(1)}, u32[]{:S(2)}, u32[]{:S(2)}) collective-permute-start(bf16[192,512]{1,0:T(8,128)(2,1)S(1)} %collective-permute-done), channel_id=1, source_target_pairs={{0,32},{32,64},{64,96},{96,128},{128,160},{160,192},{192,224},{224... | collective-permute-start | bytes 589832 | tf_op jit(solution)/shard_map/ppermute | solution.py:60
  100.0 6.3 %collective-permute-start.3 = (bf16[192,512]{1,0:T(8,128)(2,1)S(1)}, bf16[192,512]{1,0:T(8,128)(2,1)S(1)}, u32[]{:S(2)}, u32[]{:S(2)}) collective-permute-start(bf16[192,512]{1,0:T(8,128)(2,1)S(1)} %collective-permute-done.1), channel_id=1, source_target_pairs={{0,480},{32,0},{64,32},{96,64},{128,96},{160,128},{192,160},{224,1... | collective-permute-start | bytes 589832 | tf_op jit(solution)/shard_map/ppermute | solution.py:63
  106.3 6.3 %collective-permute-start.4 = (bf16[192,512]{1,0:T(8,128)(2,1)S(1)}, bf16[192,512]{1,0:T(8,128)(2,1)S(1)}, u32[]{:S(2)}, u32[]{:S(2)}) collective-permute-start(bf16[192,512]{1,0:T(8,128)(2,1)S(1)} %collective-permute-done.2), channel_id=1, source_target_pairs={{0,32},{32,64},{64,96},{96,128},{128,160},{160,192},{192,224},{224... | collective-permute-start | bytes 589832 | tf_op jit(solution)/shard_map/ppermute | solution.py:60
  106.3 6.3 %collective-permute-start.5 = (bf16[192,512]{1,0:T(8,128)(2,1)S(1)}, bf16[192,512]{1,0:T(8,128)(2,1)S(1)}, u32[]{:S(2)}, u32[]{:S(2)}) collective-permute-start(bf16[192,512]{1,0:T(8,128)(2,1)S(1)} %collective-permute-done.3), channel_id=1, source_target_pairs={{0,480},{32,0},{64,32},{96,64},{128,96},{160,128},{192,160},{224,1... | collective-permute-start | bytes 589832 | tf_op jit(solution)/shard_map/ppermute | solution.py:63
  112.6 6.3 %collective-permute-start.6 = (bf16[192,512]{1,0:T(8,128)(2,1)S(1)}, bf16[192,512]{1,0:T(8,128)(2,1)S(1)}, u32[]{:S(2)}, u32[]{:S(2)}) collective-permute-start(bf16[192,512]{1,0:T(8,128)(2,1)S(1)} %collective-permute-done.4), channel_id=1, source_target_pairs={{0,32},{32,64},{64,96},{96,128},{128,160},{160,192},{192,224},{224... | collective-permute-start | bytes 589832 | tf_op jit(solution)/shard_map/ppermute | solution.py:60
  112.6 6.3 %collective-permute-start.7 = (bf16[192,512]{1,0:T(8,128)(2,1)S(1)}, bf16[192,512]{1,0:T(8,128)(2,1)S(1)}, u32[]{:S(2)}, u32[]{:S(2)}) collective-permute-start(bf16[192,512]{1,0:T(8,128)(2,1)S(1)} %collective-permute-done.5), channel_id=1, source_target_pairs={{0,480},{32,0},{64,32},{96,64},{128,96},{160,128},{192,160},{224,1... | collective-permute-start | bytes 589832 | tf_op jit(solution)/shard_map/ppermute | solution.py:63
  118.9 6.3 %collective-permute-start.8 = (bf16[192,512]{1,0:T(8,128)(2,1)S(1)}, bf16[192,512]{1,0:T(8,128)(2,1)S(1)}, u32[]{:S(2)}, u32[]{:S(2)}) collective-permute-start(bf16[192,512]{1,0:T(8,128)(2,1)S(1)} %collective-permute-done.6), channel_id=1, source_target_pairs={{0,32},{32,64},{64,96},{96,128},{128,160},{160,192},{192,224},{224... | collective-permute-start | bytes 589832 | tf_op jit(solution)/shard_map/ppermute | solution.py:60
  118.9 6.3 %collective-permute-start.9 = (bf16[192,512]{1,0:T(8,128)(2,1)S(1)}, bf16[192,512]{1,0:T(8,128)(2,1)S(1)}, u32[]{:S(2)}, u32[]{:S(2)}) collective-permute-start(bf16[192,512]{1,0:T(8,128)(2,1)S(1)} %collective-permute-done.7), channel_id=1, source_target_pairs={{0,480},{32,0},{64,32},{96,64},{128,96},{160,128},{192,160},{224,1... | collective-permute-start | bytes 589832 | tf_op jit(solution)/shard_map/ppermute | solution.py:63
  125.2 6.3 %collective-permute-start.10 = (bf16[192,512]{1,0:T(8,128)(2,1)S(1)}, bf16[192,512]{1,0:T(8,128)(2,1)S(1)}, u32[]{:S(2)}, u32[]{:S(2)}) collective-permute-start(bf16[192,512]{1,0:T(8,128)(2,1)S(1)} %collective-permute-done.8), channel_id=1, source_target_pairs={{0,32},{32,64},{64,96},{96,128},{128,160},{160,192},{192,224},{224... | collective-permute-start | bytes 589832 | tf_op jit(solution)/shard_map/ppermute | solution.py:60
  125.2 6.5 %collective-permute-start.11 = (bf16[192,512]{1,0:T(8,128)(2,1)S(1)}, bf16[192,512]{1,0:T(8,128)(2,1)S(1)}, u32[]{:S(2)}, u32[]{:S(2)}) collective-permute-start(bf16[192,512]{1,0:T(8,128)(2,1)S(1)} %collective-permute-done.9), channel_id=1, source_target_pairs={{0,480},{32,0},{64,32},{96,64},{128,96},{160,128},{192,160},{224,1... | collective-permute-start | bytes 589832 | tf_op jit(solution)/shard_map/ppermute | solution.py:63
  131.5 6.3 %collective-permute-start.12 = (bf16[192,512]{1,0:T(8,128)(2,1)S(1)}, bf16[192,512]{1,0:T(8,128)(2,1)S(1)}, u32[]{:S(2)}, u32[]{:S(2)}) collective-permute-start(bf16[192,512]{1,0:T(8,128)(2,1)S(1)} %collective-permute-done.10), channel_id=1, source_target_pairs={{0,32},{32,64},{64,96},{96,128},{128,160},{160,192},{192,224},{224... | collective-permute-start | bytes 589832 | tf_op jit(solution)/shard_map/ppermute | solution.py:60
  131.7 6.8 %collective-permute-start.13 = (bf16[192,512]{1,0:T(8,128)(2,1)S(1)}, bf16[192,512]{1,0:T(8,128)(2,1)S(1)}, u32[]{:S(2)}, u32[]{:S(2)}) collective-permute-start(bf16[192,512]{1,0:T(8,128)(2,1)S(1)} %collective-permute-done.11), channel_id=1, source_target_pairs={{0,480},{32,0},{64,32},{96,64},{128,96},{160,128},{192,160},{224,1... | collective-permute-start | bytes 589832 | tf_op jit(solution)/shard_map/ppermute | solution.py:63
  137.8 6.3 %collective-permute-start.14 = (bf16[192,512]{1,0:T(8,128)(2,1)S(1)}, bf16[192,512]{1,0:T(8,128)(2,1)S(1)}, u32[]{:S(2)}, u32[]{:S(2)}) collective-permute-start(bf16[192,512]{1,0:T(8,128)(2,1)S(1)} %collective-permute-done.12), channel_id=1, source_target_pairs={{0,32},{32,64},{64,96},{96,128},{128,160},{160,192},{192,224},{224... | collective-permute-start | bytes 589832 | tf_op jit(solution)/shard_map/ppermute | solution.py:60
Sparse Core Ops, SparseCore 0:
  70.7 88.3 all-gather.3

commit v13 on v1

--- a/solution.py
+++ b/solution.py
@@ -17,12 +17,13 @@
 def owned_errors(spikes, readout_weight, targets):
     npre = lax.axis_size("pre")
     b = lax.axis_index("pre")
-    partial_logits = jnp.dot(
-        spikes.astype(jnp.bfloat16), readout_weight, preferred_element_type=jnp.float32
+    rows = spikes.shape[0] // npre
+    spike_pieces = spikes.astype(jnp.bfloat16).reshape(npre, rows, -1)
+    partial_logits = lax.dot_general(
+        spike_pieces, readout_weight, (((2,), (0,)), ((), ())), preferred_element_type=jnp.float32
     )
-    rows = partial_logits.shape[0] // npre
     pieces = lax.all_to_all(partial_logits, "pre", 0, 0, tiled=True)
-    logits = pieces.reshape(npre, rows, -1).sum(0)
+    logits = pieces.sum(0)
     class_prob = jax.nn.softmax(logits, axis=-1)
     classes = lax.broadcasted_iota(jnp.int32, logits.shape, 1)
     mine = lax.dynamic_slice_in_dim(targets, b * rows, rows, 0)

time: 177 us -> 178 us (level)
  no operation moved by 1% of the time
where the time goes in v13:
time: 178 us; the launch traced here: 175 us
  waiting for transfers between devices  58.3 us (33%)
  starting transfers between devices  37 us (21%)
  blocking collectives  35.9 us (20%)
  local copies, waits for them, and re-layouts  15.3 us (9%)
  between operations  14.1 us (8%)
  matrix products  10.9 us (6%)
  other arithmetic  3.34 us (2%)
    ppermute x7, starting transfers between devices, ring_gather(): b = lax.ppermute(b, axis, bwd)  21.3 us
    ppermute x8, waiting for transfers between devices, ring_gather(): f = lax.ppermute(f, axis, fwd)  18.9 us
    all_gather x1, blocking collectives, route_errors(): return lax.all_gather(moved, 'tm', axis=0, tiled=True)  18.5 us
    all_gather x1, blocking collectives, shards(): ends = lax.all_gather(states[-1], 'tm', axis=0)  17.4 us
    all_to_all x1, waiting for transfers between devices, owned_errors(): pieces = lax.all_to_all(partial_logits, 'pre', 0, 0, tiled=True)  15.8 us
    all_gather x1, waiting for transfers between devices, shards(): weighted_all = lax.all_gather(weighted, 'pre', axis=0, tiled=True)  14.3 us
    all_to_all x1, starting transfers between devices, owned_errors(): pieces = lax.all_to_all(partial_logits, 'pre', 0, 0, tiled=True)  13.4 us
    ppermute x1, waiting for transfers between devices, route_errors(): moved = lax.ppermute(errors, ('tm', 'pre'), perm)  9.04 us
  transfers between devices with their start and end apart: 18, of which 12 were waited for; matrix products, arithmetic and copies ran while one was open for 9% of the time, Pallas kernels for 0%

profile of v13, /device:TPU:6, one launch (start us, length us, event | category | flops | bytes accessed | tf_op | source)
XLA Modules:
  0.0 175.4 jit_solution(9319874870876492088)
XLA Ops:
  6.5 1.1 convert_element_type.23
  7.7 0.1 reshape.34
  7.8 1.3 fusion.1
  9.1 1.0 copy.10
  10.1 13.4 %all-to-all-start = ((f32[32,6,512]{2,1,0:T(8,128)}), f32[32,6,512]{2,1,0:T(8,128)S(1)}, u32[]{:S(2)}, u32[]{:S(2)}) async-start(f32[32,6,512]{2,1,0:T(8,128)} %copy.10), calls=%async_computation | async-start | bytes 1048576 | tf_op jit(solution)/shard_map/all_to_all | solution.py:25
  23.6 0.0 all-gather.4.cloned.1.call-start
  23.7 0.1 slice.192
  23.8 0.1 slice.194
  24.5 0.1 dynamic_slice.10
  24.6 15.8 %all-to-all-done = f32[32,6,512]{2,1,0:T(8,128)S(1)} async-done(((f32[32,6,512]{2,1,0:T(8,128)}), f32[32,6,512]{2,1,0:T(8,128)S(1)}, u32[]{:S(2)}, u32[]{:S(2)}) %all-to-all-start) | async-done | bytes 393248 | tf_op jit(solution)/shard_map/all_to_all | solution.py:25
  40.4 0.1 reduce_sum.18
  40.4 0.1 reduce_max.9
  40.6 0.2 fusion.9
  40.8 0.1 subtract_convert_fusion
  40.9 1.9 %collective-permute-start.15 = (bf16[6,512]{1,0:T(8,128)(2,1)S(1)}, bf16[6,512]{1,0:T(8,128)(2,1)S(1)}, u32[]{:S(2)}, u32[]{:S(2)}) collective-permute-start(bf16[6,512]{1,0:T(8,128)(2,1)S(1)} %subtract_convert_fusion), channel_id=1, source_target_pairs={{0,0},{1,32},{2,64},{3,96},{4,128},{5,160},{6,192},{7,224},{8,256}... | collective-permute-start | bytes 18440 | tf_op jit(solution)/shard_map/ppermute | solution.py:45
  42.8 9.0 %collective-permute-done.15 = bf16[6,512]{1,0:T(8,128)(2,1)S(1)} collective-permute-done((bf16[6,512]{1,0:T(8,128)(2,1)S(1)}, bf16[6,512]{1,0:T(8,128)(2,1)S(1)}, u32[]{:S(2)}, u32[]{:S(2)}) %collective-permute-start.15) | collective-permute-done | bytes 6176 | tf_op jit(solution)/shard_map/ppermute | solution.py:45
  51.9 18.5 %all-gather.1 = bf16[16,6,512]{2,1,0:T(8,128)(2,1)S(1)} all-gather(bf16[1,6,512]{2,1,0:T(8,128)(2,1)S(1)} %bitcast.72), channel_id=1, replica_groups=mesh['tm'=16,'pre'=32] {'tm'}, dimensions={0}, use_global_device_ids=true | all-gather | bytes 104448 | tf_op jit(solution)/shard_map/all_gather | solution.py:47
  70.4 1.1 fusion
  71.6 0.0 all-gather.4.cloned.1.call-update
  71.8 0.2 slice.190
  72.8 0.1 pad.99
  73.0 0.1 fusion.3
  73.1 0.1 slice-done
  73.2 0.1 pad.98
  73.3 17.4 %all-gather = f32[16,1,512]{2,1,0:T(1,128)S(1)} all-gather(f32[1,1,512]{2,1,0:T(1,128)S(1)} %add_bitcast_fusion), channel_id=1, replica_groups=mesh['tm'=16,'pre'=32] {'tm'}, dimensions={0}, use_global_device_ids=true | all-gather | bytes 34816 | tf_op jit(solution)/shard_map/all_gather | solution.py:81
  90.7 0.1 pad.112
  90.8 0.1 pad.113
  90.9 0.9 while.14
  91.8 2.0 %broadcast_in_dim.65 = bf16[16,192,512]{2,1,0:T(8,128)(2,1)} broadcast(bf16[]{:T(256)} %constant.118.clone.1), dimensions={} | broadcast | bytes 3145730 | tf_op jit(solution)/shard_map/broadcast_in_dim | solution.py:54
  93.8 0.9 bitcast_dynamic-update-slice_fusion.15
  94.7 0.3 collective-permute-start
  95.0 2.6 %collective-permute-start.1 = (bf16[192,512]{1,0:T(8,128)(2,1)S(1)}, bf16[192,512]{1,0:T(8,128)(2,1)S(1)}, u32[]{:S(2)}, u32[]{:S(2)}) collective-permute-start(bf16[192,512]{1,0:T(8,128)(2,1)S(1)} %get-tuple-element.129), channel_id=1, source_target_pairs={{0,480},{32,0},{64,32},{96,64},{128,96},{160,128},{192,160},{224,1... | collective-permute-start | bytes 589832 | tf_op jit(solution)/shard_map/ppermute | solution.py:62
  97.6 3.3 %collective-permute-done = bf16[192,512]{1,0:T(8,128)(2,1)S(1)} collective-permute-done((bf16[192,512]{1,0:T(8,128)(2,1)S(1)}, bf16[192,512]{1,0:T(8,128)(2,1)S(1)}, u32[]{:S(2)}, u32[]{:S(2)}) %collective-permute-start) | collective-permute-done | bytes 196640 | tf_op jit(solution)/shard_map/ppermute | solution.py:59
  101.0 3.0 %collective-permute-start.3 = (bf16[192,512]{1,0:T(8,128)(2,1)S(1)}, bf16[192,512]{1,0:T(8,128)(2,1)S(1)}, u32[]{:S(2)}, u32[]{:S(2)}) collective-permute-start(bf16[192,512]{1,0:T(8,128)(2,1)S(1)} %collective-permute-done.1), channel_id=1, source_target_pairs={{0,480},{32,0},{64,32},{96,64},{128,96},{160,128},{192,160},{224,1... | collective-permute-start | bytes 589832 | tf_op jit(solution)/shard_map/ppermute | solution.py:62
  103.9 0.7 bitcast_dynamic-update-slice_fusion.14
  104.6 0.7 bitcast_dynamic-update-slice_fusion.13
  105.3 2.0 %collective-permute-done.2 = bf16[192,512]{1,0:T(8,128)(2,1)S(1)} collective-permute-done((bf16[192,512]{1,0:T(8,128)(2,1)S(1)}, bf16[192,512]{1,0:T(8,128)(2,1)S(1)}, u32[]{:S(2)}, u32[]{:S(2)}) %collective-permute-start.2) | collective-permute-done | bytes 196640 | tf_op jit(solution)/shard_map/ppermute | solution.py:59
  107.3 3.0 %collective-permute-start.5 = (bf16[192,512]{1,0:T(8,128)(2,1)S(1)}, bf16[192,512]{1,0:T(8,128)(2,1)S(1)}, u32[]{:S(2)}, u32[]{:S(2)}) collective-permute-start(bf16[192,512]{1,0:T(8,128)(2,1)S(1)} %collective-permute-done.3), channel_id=1, source_target_pairs={{0,480},{32,0},{64,32},{96,64},{128,96},{160,128},{192,160},{224,1... | collective-permute-start | bytes 589832 | tf_op jit(solution)/shard_map/ppermute | solution.py:62
  110.2 0.7 bitcast_dynamic-update-slice_fusion.12
  110.9 0.7 bitcast_dynamic-update-slice_fusion.11
  111.6 2.0 %collective-permute-done.4 = bf16[192,512]{1,0:T(8,128)(2,1)S(1)} collective-permute-done((bf16[192,512]{1,0:T(8,128)(2,1)S(1)}, bf16[192,512]{1,0:T(8,128)(2,1)S(1)}, u32[]{:S(2)}, u32[]{:S(2)}) %collective-permute-start.4) | collective-permute-done | bytes 196640 | tf_op jit(solution)/shard_map/ppermute | solution.py:59
  113.6 3.0 %collective-permute-start.7 = (bf16[192,512]{1,0:T(8,128)(2,1)S(1)}, bf16[192,512]{1,0:T(8,128)(2,1)S(1)}, u32[]{:S(2)}, u32[]{:S(2)}) collective-permute-start(bf16[192,512]{1,0:T(8,128)(2,1)S(1)} %collective-permute-done.5), channel_id=1, source_target_pairs={{0,480},{32,0},{64,32},{96,64},{128,96},{160,128},{192,160},{224,1... | collective-permute-start | bytes 589832 | tf_op jit(solution)/shard_map/ppermute | solution.py:62
  116.5 0.7 bitcast_dynamic-update-slice_fusion.10
  117.2 0.7 bitcast_dynamic-update-slice_fusion.9
  117.9 2.0 %collective-permute-done.6 = bf16[192,512]{1,0:T(8,128)(2,1)S(1)} collective-permute-done((bf16[192,512]{1,0:T(8,128)(2,1)S(1)}, bf16[192,512]{1,0:T(8,128)(2,1)S(1)}, u32[]{:S(2)}, u32[]{:S(2)}) %collective-permute-start.6) | collective-permute-done | bytes 196640 | tf_op jit(solution)/shard_map/ppermute | solution.py:59
  119.9 3.0 %collective-permute-start.9 = (bf16[192,512]{1,0:T(8,128)(2,1)S(1)}, bf16[192,512]{1,0:T(8,128)(2,1)S(1)}, u32[]{:S(2)}, u32[]{:S(2)}) collective-permute-start(bf16[192,512]{1,0:T(8,128)(2,1)S(1)} %collective-permute-done.7), channel_id=1, source_target_pairs={{0,480},{32,0},{64,32},{96,64},{128,96},{160,128},{192,160},{224,1... | collective-permute-start | bytes 589832 | tf_op jit(solution)/shard_map/ppermute | solution.py:62
  122.8 0.7 bitcast_dynamic-update-slice_fusion.8
  123.5 0.7 bitcast_dynamic-update-slice_fusion.7
  124.2 2.0 %collective-permute-done.8 = bf16[192,512]{1,0:T(8,128)(2,1)S(1)} collective-permute-done((bf16[192,512]{1,0:T(8,128)(2,1)S(1)}, bf16[192,512]{1,0:T(8,128)(2,1)S(1)}, u32[]{:S(2)}, u32[]{:S(2)}) %collective-permute-start.8) | collective-permute-done | bytes 196640 | tf_op jit(solution)/shard_map/ppermute | solution.py:59
  126.2 3.4 %collective-permute-start.11 = (bf16[192,512]{1,0:T(8,128)(2,1)S(1)}, bf16[192,512]{1,0:T(8,128)(2,1)S(1)}, u32[]{:S(2)}, u32[]{:S(2)}) collective-permute-start(bf16[192,512]{1,0:T(8,128)(2,1)S(1)} %collective-permute-done.9), channel_id=1, source_target_pairs={{0,480},{32,0},{64,32},{96,64},{128,96},{160,128},{192,160},{224,1... | collective-permute-start | bytes 589832 | tf_op jit(solution)/shard_map/ppermute | solution.py:62
  129.6 0.7 bitcast_dynamic-update-slice_fusion.6
  130.2 0.7 bitcast_dynamic-update-slice_fusion.5
  130.9 1.6 collective-permute-done.10
  132.5 0.2 collective-permute-done.11
  132.7 3.5 %collective-permute-start.13 = (bf16[192,512]{1,0:T(8,128)(2,1)S(1)}, bf16[192,512]{1,0:T(8,128)(2,1)S(1)}, u32[]{:S(2)}, u32[]{:S(2)}) collective-permute-start(bf16[192,512]{1,0:T(8,128)(2,1)S(1)} %collective-permute-done.11), channel_id=1, source_target_pairs={{0,480},{32,0},{64,32},{96,64},{128,96},{160,128},{192,160},{224,1... | collective-permute-start | bytes 589832 | tf_op jit(solution)/shard_map/ppermute | solution.py:62
  136.3 0.7 bitcast_dynamic-update-slice_fusion.4
  136.9 0.7 bitcast_dynamic-update-slice_fusion.3
  137.6 1.2 collective-permute-done.12
  138.8 0.7 bitcast_dynamic-update-slice_fusion.2
  139.5 0.7 bitcast_dynamic-update-slice_fusion.1
  140.2 4.9 %collective-permute-done.14 = bf16[192,512]{1,0:T(8,128)(2,1)S(1)} collective-permute-done((bf16[192,512]{1,0:T(8,128)(2,1)S(1)}, bf16[192,512]{1,0:T(8,128)(2,1)S(1)}, u32[]{:S(2)}, u32[]{:S(2)}) %collective-permute-start.14) | collective-permute-done | bytes 196640 | tf_op jit(solution)/shard_map/ppermute | solution.py:59
  145.1 0.7 bitcast_dynamic-update-slice_fusion
  145.8 14.3 %all-gather.4.cloned.1.call-done = bf16[3072,1024]{1,0:T(8,128)(2,1)} async-done(((bf16[96,1024]{1,0:T(8,128)(2,1)}), bf16[3072,1024]{1,0:T(8,128)(2,1)}) %all-gather.4.cloned.1.call-update) | async-done | bytes 6291472 | tf_op jit(solution)/shard_map/all_gather | solution.py:78
  160.1 8.5 %fusion.18 = f32[512,1024]{1,0:T(8,128)} fusion(bf16[3072,512]{1,0:T(8,128)(2,1)} %bitcast.27, bf16[3072,1024]{1,0:T(8,128)(2,1)} %all-gather.4.cloned.1.call-done), kind=kOutput, calls=%fused_computation.86 | convolution fusion | flops 3221225472 | bytes 11534336 | tf_op jit(solution)/shard_map/dot_general | solution.py:91
  (144 shorter events, 1.8 us)
Async XLA Ops:
  6.5 63.9 %copy-start = (bf16[1024,512]{1,0:T(8,128)(2,1)S(1)}, bf16[1024,512]{1,0:T(8,128)(2,1)}, u32[]{:S(2)}) copy-start(bf16[1024,512]{1,0:T(8,128)(2,1)} %param.12) | copy-start | bytes 3145732
  6.5 17.1 %copy-start.2 = (s32[192,512]{1,0:T(8,128)S(1)}, s32[192,512]{1,0:T(8,128)}, u32[]{:S(2)}) copy-start(s32[192,512]{1,0:T(8,128)} %param.8) | copy-start | bytes 1179652
  6.5 17.1 %copy-start.4 = (f32[512]{0:T(512)S(1)}, f32[512]{0:T(512)}, u32[]{:S(2)}) copy-start(f32[512]{0:T(512)} %param.9) | copy-start | bytes 6148
  7.8 16.7 %copy-start.5 = (s32[192]{0:T(256)S(1)}, s32[192]{0:T(256)}, u32[]{:S(2)}) copy-start(s32[192]{0:T(256)} %param.13) | copy-start | bytes 2308
  9.1 61.3 %copy-start.3 = (bf16[96,1024]{1,0:T(8,128)(2,1)S(1)}, bf16[96,1024]{1,0:T(8,128)(2,1)}, u32[]{:S(2)}) copy-start(bf16[96,1024]{1,0:T(8,128)(2,1)} %param.10) | copy-start | bytes 589828
  10.1 30.2 %all-to-all-start = ((f32[32,6,512]{2,1,0:T(8,128)}), f32[32,6,512]{2,1,0:T(8,128)S(1)}, u32[]{:S(2)}, u32[]{:S(2)}) async-start(f32[32,6,512]{2,1,0:T(8,128)} %copy.10), calls=%async_computation | async-start | bytes 1048576 | tf_op jit(solution)/shard_map/all_to_all | solution.py:25
  23.6 136.5 %all-gather.4.cloned.1.call-start = ((), (), s32[]{:S(2)}) async-start(), calls=%async_computation.1 | async-start | bytes 6488064 | tf_op jit(solution)/shard_map/all_gather | solution.py:78
  23.7 48.3 %copy-start.1 = (f32[192,512]{1,0:T(8,128)}, f32[192,512]{1,0:T(8,128)S(1)}, u32[]{:S(2)}) copy-start(f32[192,512]{1,0:T(8,128)S(1)} %convert_multiply_fusion) | copy-start | bytes 1179652
  40.9 11.0 %collective-permute-start.15 = (bf16[6,512]{1,0:T(8,128)(2,1)S(1)}, bf16[6,512]{1,0:T(8,128)(2,1)S(1)}, u32[]{:S(2)}, u32[]{:S(2)}) collective-permute-start(bf16[6,512]{1,0:T(8,128)(2,1)S(1)} %subtract_convert_fusion), channel_id=1, source_target_pairs={{0,0},{1,32},{2,64},{3,96},{4,128},{5,160},{6,192},{7,224},{8,256}... | collective-permute-start | bytes 18440 | tf_op jit(solution)/shard_map/ppermute | solution.py:45
  72.5 0.7 slice-start
  94.7 6.3 %collective-permute-start = (bf16[192,512]{1,0:T(8,128)(2,1)S(1)}, bf16[192,512]{1,0:T(8,128)(2,1)S(1)}, u32[]{:S(2)}, u32[]{:S(2)}) collective-permute-start(bf16[192,512]{1,0:T(8,128)(2,1)S(1)} %get-tuple-element.129), channel_id=1, source_target_pairs={{0,32},{32,64},{64,96},{96,128},{128,160},{160,192},{192,224},{224... | collective-permute-start | bytes 589832 | tf_op jit(solution)/shard_map/ppermute | solution.py:59
  95.0 6.0 %collective-permute-start.1 = (bf16[192,512]{1,0:T(8,128)(2,1)S(1)}, bf16[192,512]{1,0:T(8,128)(2,1)S(1)}, u32[]{:S(2)}, u32[]{:S(2)}) collective-permute-start(bf16[192,512]{1,0:T(8,128)(2,1)S(1)} %get-tuple-element.129), channel_id=1, source_target_pairs={{0,480},{32,0},{64,32},{96,64},{128,96},{160,128},{192,160},{224,1... | collective-permute-start | bytes 589832 | tf_op jit(solution)/shard_map/ppermute | solution.py:62
  101.0 6.3 %collective-permute-start.2 = (bf16[192,512]{1,0:T(8,128)(2,1)S(1)}, bf16[192,512]{1,0:T(8,128)(2,1)S(1)}, u32[]{:S(2)}, u32[]{:S(2)}) collective-permute-start(bf16[192,512]{1,0:T(8,128)(2,1)S(1)} %collective-permute-done), channel_id=1, source_target_pairs={{0,32},{32,64},{64,96},{96,128},{128,160},{160,192},{192,224},{224... | collective-permute-start | bytes 589832 | tf_op jit(solution)/shard_map/ppermute | solution.py:59
  101.0 6.3 %collective-permute-start.3 = (bf16[192,512]{1,0:T(8,128)(2,1)S(1)}, bf16[192,512]{1,0:T(8,128)(2,1)S(1)}, u32[]{:S(2)}, u32[]{:S(2)}) collective-permute-start(bf16[192,512]{1,0:T(8,128)(2,1)S(1)} %collective-permute-done.1), channel_id=1, source_target_pairs={{0,480},{32,0},{64,32},{96,64},{128,96},{160,128},{192,160},{224,1... | collective-permute-start | bytes 589832 | tf_op jit(solution)/shard_map/ppermute | solution.py:62
  107.3 6.3 %collective-permute-start.4 = (bf16[192,512]{1,0:T(8,128)(2,1)S(1)}, bf16[192,512]{1,0:T(8,128)(2,1)S(1)}, u32[]{:S(2)}, u32[]{:S(2)}) collective-permute-start(bf16[192,512]{1,0:T(8,128)(2,1)S(1)} %collective-permute-done.2), channel_id=1, source_target_pairs={{0,32},{32,64},{64,96},{96,128},{128,160},{160,192},{192,224},{224... | collective-permute-start | bytes 589832 | tf_op jit(solution)/shard_map/ppermute | solution.py:59
  107.3 6.3 %collective-permute-start.5 = (bf16[192,512]{1,0:T(8,128)(2,1)S(1)}, bf16[192,512]{1,0:T(8,128)(2,1)S(1)}, u32[]{:S(2)}, u32[]{:S(2)}) collective-permute-start(bf16[192,512]{1,0:T(8,128)(2,1)S(1)} %collective-permute-done.3), channel_id=1, source_target_pairs={{0,480},{32,0},{64,32},{96,64},{128,96},{160,128},{192,160},{224,1... | collective-permute-start | bytes 589832 | tf_op jit(solution)/shard_map/ppermute | solution.py:62
  113.6 6.3 %collective-permute-start.6 = (bf16[192,512]{1,0:T(8,128)(2,1)S(1)}, bf16[192,512]{1,0:T(8,128)(2,1)S(1)}, u32[]{:S(2)}, u32[]{:S(2)}) collective-permute-start(bf16[192,512]{1,0:T(8,128)(2,1)S(1)} %collective-permute-done.4), channel_id=1, source_target_pairs={{0,32},{32,64},{64,96},{96,128},{128,160},{160,192},{192,224},{224... | collective-permute-start | bytes 589832 | tf_op jit(solution)/shard_map/ppermute | solution.py:59
  113.6 6.3 %collective-permute-start.7 = (bf16[192,512]{1,0:T(8,128)(2,1)S(1)}, bf16[192,512]{1,0:T(8,128)(2,1)S(1)}, u32[]{:S(2)}, u32[]{:S(2)}) collective-permute-start(bf16[192,512]{1,0:T(8,128)(2,1)S(1)} %collective-permute-done.5), channel_id=1, source_target_pairs={{0,480},{32,0},{64,32},{96,64},{128,96},{160,128},{192,160},{224,1... | collective-permute-start | bytes 589832 | tf_op jit(solution)/shard_map/ppermute | solution.py:62
  119.9 6.3 %collective-permute-start.8 = (bf16[192,512]{1,0:T(8,128)(2,1)S(1)}, bf16[192,512]{1,0:T(8,128)(2,1)S(1)}, u32[]{:S(2)}, u32[]{:S(2)}) collective-permute-start(bf16[192,512]{1,0:T(8,128)(2,1)S(1)} %collective-permute-done.6), channel_id=1, source_target_pairs={{0,32},{32,64},{64,96},{96,128},{128,160},{160,192},{192,224},{224... | collective-permute-start | bytes 589832 | tf_op jit(solution)/shard_map/ppermute | solution.py:59
  119.9 6.3 %collective-permute-start.9 = (bf16[192,512]{1,0:T(8,128)(2,1)S(1)}, bf16[192,512]{1,0:T(8,128)(2,1)S(1)}, u32[]{:S(2)}, u32[]{:S(2)}) collective-permute-start(bf16[192,512]{1,0:T(8,128)(2,1)S(1)} %collective-permute-done.7), channel_id=1, source_target_pairs={{0,480},{32,0},{64,32},{96,64},{128,96},{160,128},{192,160},{224,1... | collective-permute-start | bytes 589832 | tf_op jit(solution)/shard_map/ppermute | solution.py:62
  126.2 6.3 %collective-permute-start.10 = (bf16[192,512]{1,0:T(8,128)(2,1)S(1)}, bf16[192,512]{1,0:T(8,128)(2,1)S(1)}, u32[]{:S(2)}, u32[]{:S(2)}) collective-permute-start(bf16[192,512]{1,0:T(8,128)(2,1)S(1)} %collective-permute-done.8), channel_id=1, source_target_pairs={{0,32},{32,64},{64,96},{96,128},{128,160},{160,192},{192,224},{224... | collective-permute-start | bytes 589832 | tf_op jit(solution)/shard_map/ppermute | solution.py:59
  126.2 6.5 %collective-permute-start.11 = (bf16[192,512]{1,0:T(8,128)(2,1)S(1)}, bf16[192,512]{1,0:T(8,128)(2,1)S(1)}, u32[]{:S(2)}, u32[]{:S(2)}) collective-permute-start(bf16[192,512]{1,0:T(8,128)(2,1)S(1)} %collective-permute-done.9), channel_id=1, source_target_pairs={{0,480},{32,0},{64,32},{96,64},{128,96},{160,128},{192,160},{224,1... | collective-permute-start | bytes 589832 | tf_op jit(solution)/shard_map/ppermute | solution.py:62
  132.5 6.3 %collective-permute-start.12 = (bf16[192,512]{1,0:T(8,128)(2,1)S(1)}, bf16[192,512]{1,0:T(8,128)(2,1)S(1)}, u32[]{:S(2)}, u32[]{:S(2)}) collective-permute-start(bf16[192,512]{1,0:T(8,128)(2,1)S(1)} %collective-permute-done.10), channel_id=1, source_target_pairs={{0,32},{32,64},{64,96},{96,128},{128,160},{160,192},{192,224},{224... | collective-permute-start | bytes 589832 | tf_op jit(solution)/shard_map/ppermute | solution.py:59
  132.7 6.8 %collective-permute-start.13 = (bf16[192,512]{1,0:T(8,128)(2,1)S(1)}, bf16[192,512]{1,0:T(8,128)(2,1)S(1)}, u32[]{:S(2)}, u32[]{:S(2)}) collective-permute-start(bf16[192,512]{1,0:T(8,128)(2,1)S(1)} %collective-permute-done.11), channel_id=1, source_target_pairs={{0,480},{32,0},{64,32},{96,64},{128,96},{160,128},{192,160},{224,1... | collective-permute-start | bytes 589832 | tf_op jit(solution)/shard_map/ppermute | solution.py:62
  138.8 6.3 %collective-permute-start.14 = (bf16[192,512]{1,0:T(8,128)(2,1)S(1)}, bf16[192,512]{1,0:T(8,128)(2,1)S(1)}, u32[]{:S(2)}, u32[]{:S(2)}) collective-permute-start(bf16[192,512]{1,0:T(8,128)(2,1)S(1)} %collective-permute-done.12), channel_id=1, source_target_pairs={{0,32},{32,64},{64,96},{96,128},{128,160},{160,192},{192,224},{224... | collective-permute-start | bytes 589832 | tf_op jit(solution)/shard_map/ppermute | solution.py:59
Sparse Core Ops, SparseCore 0:
  71.7 88.3 all-gather.3
